TPU v7x, 768 devices: a whole 4x8x12 slice. The times are simulated.
768 devices in a mesh: dp: 64 (over x, y, core), mp: 12 (over z).
Axes of the slice: x: 4, y: 8, z: 12, core: 2. Of those that a mesh axis runs over, the one named last changes fastest.
Arguments:
- hidden: bfloat16 [2, 4096, 4224], P(None, 'dp'), may hold values from 0 to 6, as said below
- proj_weight: bfloat16 [4224, 4224], P(None, 'mp'), may hold values from -0.09375 to 0.09375
Outputs:
- grad_first: bfloat16 [4096, 4224], P('dp', 'mp')
Inputs may be any that keep to these rules, and one draw needn't show every extreme that they name: `hidden`: rectified features of 4096 images in two views.
All inputs are finite; a program needn't handle non-finite values.
Results may differ from a plain program's by a relative error of at most 0.0057.
Values may be sent and summed in bfloat16 or wider, within the bound.
No kernel may reach another device: no remote copies, remote signals or barrier semaphores. Data moves between devices by JAX's collectives and lax.ppermute only.
A program may use at most 32 MiB of HBM per device.

v0:
```python
import jax
import jax.numpy as jnp
from jax import lax
from jax.sharding import PartitionSpec as P

off_weight = 0.0051
eps = 1e-05


def shards(hidden, proj_weight):
    mp_index = lax.axis_index("mp")
    dp_index = lax.axis_index("dp")
    dp_count = lax.axis_size("dp")
    rows = proj_weight.shape[1]
    total = hidden.shape[1] * dp_count
    feats = jnp.einsum("vbh,hc->vbc", hidden, proj_weight, preferred_element_type=jnp.float32)
    sums = lax.psum(jnp.sum(feats, axis=1, keepdims=True), "dp")
    mean = sums / total
    centered = feats - mean
    var = lax.psum(jnp.sum(centered * centered, axis=1, keepdims=True), "dp") / total
    normed = (centered / jnp.sqrt(var + eps)).astype(jnp.bfloat16)
    inv_std = 1.0 / jnp.sqrt(var + eps)
    first = normed[0]
    second = normed[1]
    second_full = lax.all_gather(second, "mp", axis=1, tiled=True)
    width = second_full.shape[1] // dp_count
    columns = lax.all_to_all(second_full, "dp", split_axis=1, concat_axis=0, tiled=True)
    corr = (
        jnp.einsum(
            "bi,bj->ij",
            lax.all_gather(first, "dp", axis=0, tiled=True),
            columns,
            preferred_element_type=jnp.float32,
        )
        / total
    )
    row_ids = mp_index * rows + lax.iota(jnp.int32, rows)[:, None]
    col_ids = dp_index * width + lax.iota(jnp.int32, width)[None, :]
    grad_block = jnp.where(row_ids == col_ids, 2.0 * (corr - 1.0), 2.0 * off_weight * corr).astype(
        jnp.bfloat16
    )
    grad_rows = lax.all_gather(grad_block, "dp", axis=1, tiled=True)
    grad_wide = grad_rows.astype(jnp.float32)
    all_cols = lax.iota(jnp.int32, grad_rows.shape[1])[None, :]
    diag_val = jnp.sum(jnp.where(all_cols == row_ids, grad_wide, 0.0), axis=1)
    scale_sum = (jnp.sum(grad_wide * grad_wide, axis=1) - diag_val * diag_val) / (
        2.0 * off_weight
    ) + diag_val * (1.0 + diag_val / 2.0)
    back = jnp.einsum("bj,ij->bi", second_full, grad_rows, preferred_element_type=jnp.float32)
    result = (back - first.astype(jnp.float32) * scale_sum[None, :]) * inv_std[0]
    return result.astype(jnp.bfloat16)


def solution(mesh):
    return jax.shard_map(
        shards,
        mesh=mesh,
        in_specs=(P(None, "dp", None), P(None, "mp")),
        out_specs=P("dp", "mp"),
        check_vma=False,
    )
```

profile of v0, /device:TPU:1, one launch (start us, length us, event | category | flops | bytes accessed | tf_op | source)
XLA Modules:
  0.0 482.0 jit_solution(5282712484925071352)
XLA Ops:
  6.5 0.0 copy-start
  6.5 0.0 all-gather.6.cloned.1.call-start
  6.5 1.8 copy-done
  8.4 2.3 fusion.16
  10.7 133.9 %psum.14 = f32[2,1,352]{2,0,1:T(2,128)S(1)} all-reduce(f32[2,1,352]{2,0,1:T(2,128)S(1)} %bitcast.43), channel_id=1, replica_groups=mesh['dp'=64,'mp'=12] {'dp'}, use_global_device_ids=true, to_apply=%region_1.0 | all-reduce | flops 704 | bytes 5632 | tf_op jit(solution)/shard_map/psum | solution.py:17
  144.7 124.1 %psum.15 = f32[2,1,352]{2,0,1:T(2,128)S(1)} all-reduce(f32[2,1,352]{2,0,1:T(2,128)S(1)} %bitcast.44), channel_id=1, replica_groups=mesh['dp'=64,'mp'=12] {'dp'}, use_global_device_ids=true, to_apply=%region_3.0 | all-reduce | flops 704 | bytes 5632 | tf_op jit(solution)/shard_map/psum | solution.py:20
  268.8 0.0 copy-start.2
  268.8 0.6 copy-done.2
  269.4 0.6 fusion.15
  270.1 0.0 all-gather.6.cloned.1.call-update
  270.1 0.2 copy.7
  270.3 39.5 %all-gather = bf16[1,64,4224]{1,0,2:T(2,128)(2,1)} all-gather(bf16[1,64,352]{1,0,2:T(2,128)(2,1)S(1)} %copy.7), channel_id=2, replica_groups=mesh['dp'=64,'mp'=12] {'mp'}, dimensions={2}, use_global_device_ids=true | all-gather | bytes 585728 | tf_op jit(solution)/shard_map/all_gather | solution.py:25
  309.8 24.4 %reduce = bf16[64,4224]{0,1:T(8,128)(2,1)} reduce(bf16[1,64,4224]{1,0,2:T(2,128)(2,1)} %all-gather, bf16[]{:T(256)} %constant.38), dimensions={0}, to_apply=%all-gather.reduce_sub_computation | reduce | bytes 1081346 | tf_op jit(solution)/shard_map/all_gather | solution.py:25
  334.2 2.2 reshape.32
  336.5 2.4 copy.10
  338.9 11.6 %all-to-all-start = ((bf16[64,64,66]{2,0,1:T(8,128)(2,1)}), bf16[64,64,66]{2,0,1:T(8,128)(2,1)}, u32[]{:S(2)}, u32[]{:S(2)}) async-start(bf16[64,64,66]{2,0,1:T(8,128)(2,1)} %copy.10), calls=%async_computation | async-start | bytes 2097152 | tf_op jit(solution)/shard_map/all_to_all | solution.py:27
  350.5 0.0 all-gather.8.cloned.1.call-start
  350.6 28.4 %all-to-all-done = bf16[64,64,66]{2,0,1:T(8,128)(2,1)} async-done(((bf16[64,64,66]{2,0,1:T(8,128)(2,1)}), bf16[64,64,66]{2,0,1:T(8,128)(2,1)}, u32[]{:S(2)}, u32[]{:S(2)}) %all-to-all-start) | async-done | bytes 540704 | tf_op jit(solution)/shard_map/all_to_all | solution.py:27
  379.0 0.0 all-gather.6.cloned.1.call-done
  379.0 3.4 fusion.11
  382.4 0.0 all-gather.8.cloned.1.call-update
  382.5 4.6 copy.8
  387.1 75.8 %all-gather.8.cloned.1.call-done = bf16[64,66,352]{2,1,0:T(8,128)(2,1)} async-done(((bf16[1,66,352]{2,1,0:T(8,128)(2,1)}), bf16[64,66,352]{2,1,0:T(8,128)(2,1)}) %all-gather.8.cloned.1.call-update) | async-done | bytes 2973712 | tf_op jit(solution)/shard_map/all_gather | solution.py:42
  462.9 5.8 %reshape.30 = bf16[4224,352]{1,0:T(8,128)(2,1)} reshape(bf16[64,66,352]{2,1,0:T(8,128)(2,1)} %all-gather.8.cloned.1.call-done) | data formatting | bytes 5947392
  468.8 0.0 copy-start.1
  468.8 4.3 fusion
  473.1 0.0 copy-done.1
  473.1 2.1 fusion.7
  (8 shorter events, 0.1 us)
Async XLA Ops:
  6.5 1.8 copy-start
  6.5 372.5 %all-gather.6.cloned.1.call-start = ((), (), s32[]{:S(2)}) async-start(), calls=%async_computation.1 | async-start | bytes 3194880 | tf_op jit(solution)/shard_map/all_gather | solution.py:31
  268.8 0.6 copy-start.2
  338.9 40.1 %all-to-all-start = ((bf16[64,64,66]{2,0,1:T(8,128)(2,1)}), bf16[64,64,66]{2,0,1:T(8,128)(2,1)}, u32[]{:S(2)}, u32[]{:S(2)}) async-start(bf16[64,64,66]{2,0,1:T(8,128)(2,1)} %copy.10), calls=%async_computation | async-start | bytes 2097152 | tf_op jit(solution)/shard_map/all_to_all | solution.py:27
  350.5 112.4 %all-gather.8.cloned.1.call-start = ((), (), s32[]{:S(2)}) async-start(), calls=%async_computation.2 | async-start | bytes 3594240 | tf_op jit(solution)/shard_map/all_gather | solution.py:42
  468.8 4.4 copy-start.1
Sparse Core Ops, SparseCore 0:
  270.2 84.4 all-gather.5
  382.6 80.3 all-gather.7
where the time goes:
time: 483 us; the launch traced here: 482 us
  blocking collectives  298 us (62%)
  waiting for transfers between devices  104 us (22%)
  other arithmetic  28.9 us (6%)
  local copies, waits for them, and re-layouts  18.3 us (4%)
  between operations  13.5 us (3%)
  starting transfers between devices  11.7 us (2%)
  matrix products  7.8 us (2%)
    psum x1, blocking collectives, shards(): sums = lax.psum(jnp.sum(feats, axis=1, keepdims=True), 'dp')  134 us
    psum x1, blocking collectives, shards(): lax.psum(jnp.sum(centered * centered, axis=1, keepdims=True), 'dp') / total  124 us
    all_gather x1, waiting for transfers between devices, shards(): grad_rows = lax.all_gather(grad_block, 'dp', axis=1, tiled=True)  75.8 us
    all_gather x1, blocking collectives, shards(): second_full = lax.all_gather(second, 'mp', axis=1, tiled=True)  39.5 us
    all_to_all x1, waiting for transfers between devices, shards(): lax.all_to_all(second_full, 'dp', split_axis=1, concat_axis=0, tiled=True)  28.4 us
    all_gather x1, other arithmetic, shards(): second_full = lax.all_gather(second, 'mp', axis=1, tiled=True)  24.4 us
    all_to_all x1, starting transfers between devices, shards(): lax.all_to_all(second_full, 'dp', split_axis=1, concat_axis=0, tiled=True)  11.6 us
  transfers between devices with their start and end apart: 3, of which 2 were waited for; matrix products, arithmetic and copies ran while one was open for 7% of the time, Pallas kernels for 0%

commit v1 on v0

v1 whole, which is shorter than its diff:
```python
import jax
import jax.numpy as jnp
from jax import lax
from jax.sharding import Mesh
from jax.sharding import PartitionSpec as P

off_weight = 0.0051
eps = 1e-05
DP = ("x", "y", "c")


def dp_sum(v):
    v = lax.psum(v, "c")
    v = lax.psum(v, "y")
    return lax.psum(v, "x")


def shards(hidden, proj_weight):
    mp_index = lax.axis_index("mp")
    dp_index = lax.axis_index(DP)
    dp_count = lax.axis_size(DP)
    rows = proj_weight.shape[1]
    total = hidden.shape[1] * dp_count
    feats = jnp.einsum("vbh,hc->vbc", hidden, proj_weight, preferred_element_type=jnp.float32)
    sums = dp_sum(jnp.sum(feats, axis=1, keepdims=True))
    mean = sums / total
    centered = feats - mean
    var = dp_sum(jnp.sum(centered * centered, axis=1, keepdims=True)) / total
    normed = (centered / jnp.sqrt(var + eps)).astype(jnp.bfloat16)
    inv_std = 1.0 / jnp.sqrt(var + eps)
    first = normed[0]
    second = normed[1]
    second_full = lax.all_gather(second, "mp", axis=1, tiled=True)
    width = second_full.shape[1] // dp_count
    columns = lax.all_to_all(second_full, DP, split_axis=1, concat_axis=0, tiled=True)
    corr = (
        jnp.einsum(
            "bi,bj->ij",
            lax.all_gather(first, DP, axis=0, tiled=True),
            columns,
            preferred_element_type=jnp.float32,
        )
        / total
    )
    row_ids = mp_index * rows + lax.iota(jnp.int32, rows)[:, None]
    col_ids = dp_index * width + lax.iota(jnp.int32, width)[None, :]
    grad_block = jnp.where(row_ids == col_ids, 2.0 * (corr - 1.0), 2.0 * off_weight * corr).astype(
        jnp.bfloat16
    )
    grad_rows = lax.all_gather(grad_block, DP, axis=1, tiled=True)
    grad_wide = grad_rows.astype(jnp.float32)
    all_cols = lax.iota(jnp.int32, grad_rows.shape[1])[None, :]
    diag_val = jnp.sum(jnp.where(all_cols == row_ids, grad_wide, 0.0), axis=1)
    scale_sum = (jnp.sum(grad_wide * grad_wide, axis=1) - diag_val * diag_val) / (
        2.0 * off_weight
    ) + diag_val * (1.0 + diag_val / 2.0)
    back = jnp.einsum("bj,ij->bi", second_full, grad_rows, preferred_element_type=jnp.float32)
    result = (back - first.astype(jnp.float32) * scale_sum[None, :]) * inv_std[0]
    return result.astype(jnp.bfloat16)


def solution(mesh):
    x, y, c = (4, 8, 2)
    sub = Mesh(mesh.devices.reshape(x, y, c, mesh.devices.shape[1]), DP + ("mp",))
    return jax.shard_map(
        shards,
        mesh=sub,
        in_specs=(P(None, DP, None), P(None, "mp")),
        out_specs=P(DP, "mp"),
        check_vma=False,
    )
```

time: 483 us -> 288 us (0.60)
  blocking collectives: 298 us -> 93.9 us
  starting transfers between devices: 11.7 us -> 17.7 us
    psum x2 -> x6, blocking collectives: 258 us -> 57.2 us  [the longest x2 23.3 us: dp_sum(): v = lax.psum(v, 'y')]
    all_to_all x1, starting transfers between devices: 11.6 us -> 17.5 us  [shards(): lax.all_to_all(second_full, DP, split_axis=1, concat_axis=0, tiled=True)]
  transfers between devices with their start and end apart: 3 -> 3, of which waited for: 2 -> 2; matrix products, arithmetic and copies ran while one was open for 7% -> 12% of each run, Pallas kernels for 0% -> 0%
where the time goes in v1:
time: 288 us; the launch traced here: 287 us
  waiting for transfers between devices  107 us (37%)
  blocking collectives  93.9 us (33%)
  other arithmetic  28.9 us (10%)
  local copies, waits for them, and re-layouts  18.3 us (6%)
  starting transfers between devices  17.7 us (6%)
  between operations  13.5 us (5%)
  matrix products  7.81 us (3%)
    all_gather x1, waiting for transfers between devices, shards(): grad_rows = lax.all_gather(grad_block, DP, axis=1, tiled=True)  78.3 us
    all_gather x1, blocking collectives, shards(): second_full = lax.all_gather(second, 'mp', axis=1, tiled=True)  36.7 us
    all_to_all x1, waiting for transfers between devices, shards(): lax.all_to_all(second_full, DP, split_axis=1, concat_axis=0, tiled=True)  28.8 us
    all_gather x1, other arithmetic, shards(): second_full = lax.all_gather(second, 'mp', axis=1, tiled=True)  24.4 us
    psum x2, blocking collectives, dp_sum(): v = lax.psum(v, 'y')  23.3 us
    psum x2, blocking collectives, dp_sum(): v = lax.psum(v, 'c')  20.2 us
    all_to_all x1, starting transfers between devices, shards(): lax.all_to_all(second_full, DP, split_axis=1, concat_axis=0, tiled=True)  17.5 us
    psum x2, blocking collectives, dp_sum(): return lax.psum(v, 'x')  13.7 us
  transfers between devices with their start and end apart: 3, of which 2 were waited for; matrix products, arithmetic and copies ran while one was open for 12% of the time, Pallas kernels for 0%

profile of v1, /device:TPU:1, one launch (start us, length us, event | category | flops | bytes accessed | tf_op | source)
XLA Modules:
  0.0 287.2 jit_solution(5387997776880344517)
XLA Ops:
  6.5 0.0 copy-start
  6.5 0.0 all-gather.6.cloned.1.call-start
  6.5 1.8 copy-done
  8.4 2.3 fusion.16
  10.7 12.6 %psum.42 = f32[2,1,352]{2,0,1:T(2,128)S(1)} all-reduce(f32[2,1,352]{2,0,1:T(2,128)S(1)} %bitcast.43), channel_id=1, replica_groups=mesh['x'=4,'y'=8,'c'=2,'mp'=12] {'c'}, use_global_device_ids=true, to_apply=%region_1.0 | all-reduce | flops 704 | bytes 5632 | tf_op jit(solution)/shard_map/psum | solution.py:13
  23.3 10.8 %psum.43 = f32[2,1,352]{2,0,1:T(2,128)S(1)} all-reduce(f32[2,1,352]{2,0,1:T(2,128)S(1)} %psum.42), channel_id=1, replica_groups=mesh['x'=4,'y'=8,'c'=2,'mp'=12] {'y'}, use_global_device_ids=true, to_apply=%region_2.0 | all-reduce | flops 704 | bytes 5632 | tf_op jit(solution)/shard_map/psum | solution.py:14
  34.1 6.0 %psum.44 = f32[2,1,352]{2,0,1:T(2,128)S(1)} all-reduce(f32[2,1,352]{2,0,1:T(2,128)S(1)} %psum.43), channel_id=1, replica_groups=mesh['x'=4,'y'=8,'c'=2,'mp'=12] {'x'}, use_global_device_ids=true, to_apply=%region_3.0 | all-reduce | flops 704 | bytes 5632 | tf_op jit(solution)/shard_map/psum | solution.py:15
  40.1 7.6 %psum.45 = f32[2,1,352]{2,0,1:T(2,128)S(1)} all-reduce(f32[2,1,352]{2,0,1:T(2,128)S(1)} %bitcast.44), channel_id=1, replica_groups=mesh['x'=4,'y'=8,'c'=2,'mp'=12] {'c'}, use_global_device_ids=true, to_apply=%region_5.0 | all-reduce | flops 704 | bytes 5632 | tf_op jit(solution)/shard_map/psum | solution.py:13
  47.8 12.5 %psum.46 = f32[2,1,352]{2,0,1:T(2,128)S(1)} all-reduce(f32[2,1,352]{2,0,1:T(2,128)S(1)} %psum.45), channel_id=1, replica_groups=mesh['x'=4,'y'=8,'c'=2,'mp'=12] {'y'}, use_global_device_ids=true, to_apply=%region_6.0 | all-reduce | flops 704 | bytes 5632 | tf_op jit(solution)/shard_map/psum | solution.py:14
  60.3 7.7 %psum.47 = f32[2,1,352]{2,0,1:T(2,128)S(1)} all-reduce(f32[2,1,352]{2,0,1:T(2,128)S(1)} %psum.46), channel_id=1, replica_groups=mesh['x'=4,'y'=8,'c'=2,'mp'=12] {'x'}, use_global_device_ids=true, to_apply=%region_7.0 | all-reduce | flops 704 | bytes 5632 | tf_op jit(solution)/shard_map/psum | solution.py:15
  68.0 0.0 copy-start.2
  68.0 0.6 copy-done.2
  68.7 0.6 fusion.15
  69.3 0.0 all-gather.6.cloned.1.call-update
  69.3 0.2 copy.7
  69.5 36.7 %all-gather = bf16[1,64,4224]{1,0,2:T(2,128)(2,1)} all-gather(bf16[1,64,352]{1,0,2:T(2,128)(2,1)S(1)} %copy.7), channel_id=2, replica_groups=mesh['x'=4,'y'=8,'c'=2,'mp'=12] {'mp'}, dimensions={2}, use_global_device_ids=true | all-gather | bytes 585728 | tf_op jit(solution)/shard_map/all_gather | solution.py:33
  106.1 24.4 %reduce = bf16[64,4224]{0,1:T(8,128)(2,1)} reduce(bf16[1,64,4224]{1,0,2:T(2,128)(2,1)} %all-gather, bf16[]{:T(256)} %constant.52), dimensions={0}, to_apply=%all-gather.reduce_sub_computation | reduce | bytes 1081346 | tf_op jit(solution)/shard_map/all_gather | solution.py:33
  130.6 2.2 reshape.32
  132.8 2.4 copy.10
  135.2 17.5 %all-to-all-start = ((bf16[64,64,66]{2,0,1:T(8,128)(2,1)}), bf16[64,64,66]{2,0,1:T(8,128)(2,1)}, u32[]{:S(2)}, u32[]{:S(2)}) async-start(bf16[64,64,66]{2,0,1:T(8,128)(2,1)} %copy.10), calls=%async_computation | async-start | bytes 2097152 | tf_op jit(solution)/shard_map/all_to_all | solution.py:35
  152.7 0.2 all-gather.8.cloned.1.call-start
  152.9 28.8 %all-to-all-done = bf16[64,64,66]{2,0,1:T(8,128)(2,1)} async-done(((bf16[64,64,66]{2,0,1:T(8,128)(2,1)}), bf16[64,64,66]{2,0,1:T(8,128)(2,1)}, u32[]{:S(2)}, u32[]{:S(2)}) %all-to-all-start) | async-done | bytes 540704 | tf_op jit(solution)/shard_map/all_to_all | solution.py:35
  181.8 0.0 all-gather.6.cloned.1.call-done
  181.8 3.4 %fusion.11 = bf16[1,66,352]{2,1,0:T(8,128)(2,1)} fusion(bf16[4096,66]{1,0:T(8,128)(2,1)} %bitcast.8, bf16[1,4096,352]{2,1,0:T(8,128)(2,1)} %all-gather.6.cloned.1.call-done, s32[352]{0:T(512)S(1)} %iota_add_fusion, s32[66]{0:T(128)S(1)} %iota_add_fusion.1), kind=kOutput, calls=%fused_computation.16 | convolution fusion | flops 190479168 | bytes 3472392 | tf_op jit(solution)/shard_map/bi,bj->ij/dot_general | solution.py:37
  185.2 0.0 all-gather.8.cloned.1.call-update
  185.2 4.6 %copy.8 = bf16[1,64,4224]{2,1,0:T(8,128)(2,1)S(1)} copy(bf16[1,64,4224]{1,0,2:T(2,128)(2,1)} %all-gather) | data formatting | bytes 1081344 | tf_op jit(solution)/shard_map/all_gather | solution.py:33
  189.9 78.3 %all-gather.8.cloned.1.call-done = bf16[64,66,352]{2,1,0:T(8,128)(2,1)} async-done(((bf16[1,66,352]{2,1,0:T(8,128)(2,1)}), bf16[64,66,352]{2,1,0:T(8,128)(2,1)}) %all-gather.8.cloned.1.call-update) | async-done | bytes 2973712 | tf_op jit(solution)/shard_map/all_gather | solution.py:50
  268.1 5.8 %reshape.30 = bf16[4224,352]{1,0:T(8,128)(2,1)} reshape(bf16[64,66,352]{2,1,0:T(8,128)(2,1)} %all-gather.8.cloned.1.call-done) | data formatting | bytes 5947392
  274.0 0.0 copy-start.1
  274.0 4.3 %fusion = (f32[352]{0:T(512)S(1)}, f32[352]{0:T(512)S(1)}) fusion(bf16[4224,352]{1,0:T(8,128)(2,1)} %reshape.30, s32[352]{0:T(512)S(1)} %iota_add_fusion), kind=kLoop, calls=%fused_computation.2 | loop fusion | flops 8920384 | bytes 2977920 | tf_op jit(solution)/shard_map/reduce_sum | solution.py:54
  278.3 0.0 copy-done.1
  278.3 2.1 fusion.7
  (8 shorter events, 0.1 us)
Async XLA Ops:
  6.5 1.8 copy-start
  6.5 175.2 %all-gather.6.cloned.1.call-start = ((), (), s32[]{:S(2)}) async-start(), calls=%async_computation.1 | async-start | bytes 3194880 | tf_op jit(solution)/shard_map/all_gather | solution.py:39
  68.0 0.6 copy-start.2
  135.2 46.6 %all-to-all-start = ((bf16[64,64,66]{2,0,1:T(8,128)(2,1)}), bf16[64,64,66]{2,0,1:T(8,128)(2,1)}, u32[]{:S(2)}, u32[]{:S(2)}) async-start(bf16[64,64,66]{2,0,1:T(8,128)(2,1)} %copy.10), calls=%async_computation | async-start | bytes 2097152 | tf_op jit(solution)/shard_map/all_to_all | solution.py:35
  152.7 115.5 %all-gather.8.cloned.1.call-start = ((), (), s32[]{:S(2)}) async-start(), calls=%async_computation.2 | async-start | bytes 3594240 | tf_op jit(solution)/shard_map/all_gather | solution.py:50
  274.0 4.4 %copy-start.1 = (bf16[4224,352]{1,0:T(8,128)(2,1)S(1)}, bf16[4224,352]{1,0:T(8,128)(2,1)}, u32[]{:S(2)}) copy-start(bf16[4224,352]{1,0:T(8,128)(2,1)} %reshape.30) | copy-start | bytes 8921092
Sparse Core Ops, SparseCore 0:
  69.4 93.4 all-gather.5
  185.3 82.7 all-gather.7

commit v2 on v1

v2 whole, which is shorter than its diff:
```python
import jax
import jax.numpy as jnp
from jax import lax
from jax.sharding import Mesh
from jax.sharding import PartitionSpec as P

off_weight = 0.0051
eps = 1e-05
DP = ("x", "y", "c")


def dp_sum(v):
    v = lax.psum(v, "c")
    v = lax.psum(v, "y")
    return lax.psum(v, "x")


def dp_gather(v):
    v = lax.all_gather(v, "x", axis=0)
    v = lax.all_gather(v, "y", axis=0)
    return lax.all_gather(v, "c", axis=0)


def shards(hidden, proj_weight):
    mp_index = lax.axis_index("mp")
    dp_index = lax.axis_index(DP)
    dp_count = lax.axis_size(DP)
    nx, ny, nc = lax.axis_size("x"), lax.axis_size("y"), lax.axis_size("c")
    rows = proj_weight.shape[1]
    local = hidden.shape[1]
    total = local * dp_count
    feats = jnp.einsum("vbh,hc->vbc", hidden, proj_weight, preferred_element_type=jnp.float32)
    sums = dp_sum(jnp.sum(feats, axis=1, keepdims=True))
    mean = sums / total
    centered = feats - mean
    var = dp_sum(jnp.sum(centered * centered, axis=1, keepdims=True)) / total
    normed = (centered / jnp.sqrt(var + eps)).astype(jnp.bfloat16)
    inv_std = 1.0 / jnp.sqrt(var + eps)
    first = normed[0]
    second = normed[1]
    n_mp = lax.axis_size("mp")
    stacked = lax.all_gather(second, "mp", axis=0)
    second_full = jnp.transpose(stacked, (1, 0, 2)).reshape(local, n_mp * rows)
    width = second_full.shape[1] // dp_count
    columns = lax.all_to_all(second_full, DP, split_axis=1, concat_axis=0, tiled=True)
    first_all = dp_gather(first)
    first_all = jnp.transpose(first_all, (2, 1, 0, 3, 4)).reshape(total, rows)
    corr = (
        jnp.einsum("bi,bj->ij", first_all, columns, preferred_element_type=jnp.float32)
        / total
    )
    row_ids = mp_index * rows + lax.iota(jnp.int32, rows)[:, None]
    col_ids = dp_index * width + lax.iota(jnp.int32, width)[None, :]
    grad_block = jnp.where(row_ids == col_ids, 2.0 * (corr - 1.0), 2.0 * off_weight * corr).astype(
        jnp.bfloat16
    )
    grad_t = dp_gather(grad_block.T).reshape(dp_count * width, rows)
    t = lax.iota(jnp.int32, width)
    cc = lax.iota(jnp.int32, nc)[:, None, None, None]
    yy = lax.iota(jnp.int32, ny)[None, :, None, None]
    xx = lax.iota(jnp.int32, nx)[None, None, :, None]
    perm_cols = (((xx * ny + yy) * nc + cc) * width + t[None, None, None, :]).reshape(-1)
    grad_wide = grad_t.astype(jnp.float32)
    row_flat = mp_index * rows + lax.iota(jnp.int32, rows)
    diag_val = jnp.sum(jnp.where(perm_cols[:, None] == row_flat[None, :], grad_wide, 0.0), axis=0)
    scale_sum = (jnp.sum(grad_wide * grad_wide, axis=0) - diag_val * diag_val) / (
        2.0 * off_weight
    ) + diag_val * (1.0 + diag_val / 2.0)
    second_perm = second_full.reshape(local, nx, ny, nc, width)
    second_perm = jnp.transpose(second_perm, (0, 3, 2, 1, 4)).reshape(local, dp_count * width)
    back = jnp.dot(second_perm, grad_t, preferred_element_type=jnp.float32)
    result = (back - first.astype(jnp.float32) * scale_sum[None, :]) * inv_std[0]
    return result.astype(jnp.bfloat16)


def solution(mesh):
    x, y, c = (4, 8, 2)
    sub = Mesh(mesh.devices.reshape(x, y, c, mesh.devices.shape[1]), DP + ("mp",))
    return jax.shard_map(
        shards,
        mesh=sub,
        in_specs=(P(None, DP, None), P(None, "mp")),
        out_specs=P(DP, "mp"),
        check_vma=False,
    )
```

time: 288 us -> 298 us (1.035)
  other arithmetic: 28.9 us -> 1.93 us
  waiting for transfers between devices: 107 us -> 130 us
  local copies, waits for them, and re-layouts: 18.3 us -> 25.9 us
  blocking collectives: 93.9 us -> 100 us
    all_gather x2 -> x4, waiting for transfers between devices: 78.3 us -> 106 us  [the longest x2 83.8 us: dp_gather(): v = lax.all_gather(v, 'y', axis=0)]
    all_gather x1 -> x0, other arithmetic: 24.4 us -> none  [shards(): second_full = lax.all_gather(second, 'mp', axis=1, tiled=True)]
    unnamed x7 -> x4, local copies, waits for them, and re-layouts: 8.3 us -> 1.84 us
    all_gather x1 -> x3, blocking collectives: 36.7 us -> 43 us  [the longest x1 22 us: shards(): stacked = lax.all_gather(second, 'mp', axis=0)]
    another operation x0 -> x1, local copies, waits for them, and re-layouts: none -> 6.11 us  [shards(): second_perm = second_full.reshape(local, nx, ny, nc, width)]
    transpose x0 -> x2, local copies, waits for them, and re-layouts: none -> 5.33 us  [the longest x1 4.04 us: shards(): first_all = jnp.transpose(first_all, (2, 1, 0, 3, 4)).reshape(total, rows)]
    all_to_all x1, waiting for transfers between devices: 28.8 us -> 24.3 us  [shards(): lax.all_to_all(second_full, DP, split_axis=1, concat_axis=0, tiled=True)]
  transfers between devices with their start and end apart: 3 -> 5, of which waited for: 2 -> 4; matrix products, arithmetic and copies ran while one was open for 12% -> 5% of each run, Pallas kernels for 0% -> 0%
where the time goes in v2:
time: 298 us; the launch traced here: 297 us
  waiting for transfers between devices  130 us (44%)
  blocking collectives  100 us (34%)
  local copies, waits for them, and re-layouts  25.9 us (9%)
  starting transfers between devices  18.3 us (6%)
  between operations  13.3 us (4%)
  matrix products  7.64 us (3%)
    all_gather x2, waiting for transfers between devices, dp_gather(): v = lax.all_gather(v, 'y', axis=0)  83.8 us
    all_to_all x1, waiting for transfers between devices, shards(): lax.all_to_all(second_full, DP, split_axis=1, concat_axis=0, tiled=True)  24.3 us
    psum x2, blocking collectives, dp_sum(): v = lax.psum(v, 'y')  23.3 us
    all_gather x1, blocking collectives, shards(): stacked = lax.all_gather(second, 'mp', axis=0)  22 us
    all_gather x2, waiting for transfers between devices, dp_gather(): return lax.all_gather(v, 'c', axis=0)  21.9 us
    all_gather x2, blocking collectives, dp_gather(): v = lax.all_gather(v, 'x', axis=0)  21 us
    psum x2, blocking collectives, dp_sum(): v = lax.psum(v, 'c')  20.2 us
    all_to_all x1, starting transfers between devices, shards(): lax.all_to_all(second_full, DP, split_axis=1, concat_axis=0, tiled=True)  18 us
  transfers between devices with their start and end apart: 5, of which 4 were waited for; matrix products, arithmetic and copies ran while one was open for 5% of the time, Pallas kernels for 0%

profile of v2, /device:TPU:1, one launch (start us, length us, event | category | flops | bytes accessed | tf_op | source)
XLA Modules:
  0.0 297.2 jit_solution(4308003901882238685)
XLA Ops:
  6.5 0.0 copy-start
  6.5 0.0 all-gather.11.cloned.1.call-start
  6.5 1.8 copy-done
  8.4 2.3 fusion.12
  10.7 12.6 %psum.42 = f32[2,1,352]{2,0,1:T(2,128)S(1)} all-reduce(f32[2,1,352]{2,0,1:T(2,128)S(1)} %bitcast.51), channel_id=1, replica_groups=mesh['x'=4,'y'=8,'c'=2,'mp'=12] {'c'}, use_global_device_ids=true, to_apply=%region_1.0 | all-reduce | flops 704 | bytes 5632 | tf_op jit(solution)/shard_map/psum | solution.py:13
  23.3 10.8 %psum.43 = f32[2,1,352]{2,0,1:T(2,128)S(1)} all-reduce(f32[2,1,352]{2,0,1:T(2,128)S(1)} %psum.42), channel_id=1, replica_groups=mesh['x'=4,'y'=8,'c'=2,'mp'=12] {'y'}, use_global_device_ids=true, to_apply=%region_2.0 | all-reduce | flops 704 | bytes 5632 | tf_op jit(solution)/shard_map/psum | solution.py:14
  34.1 6.0 %psum.44 = f32[2,1,352]{2,0,1:T(2,128)S(1)} all-reduce(f32[2,1,352]{2,0,1:T(2,128)S(1)} %psum.43), channel_id=1, replica_groups=mesh['x'=4,'y'=8,'c'=2,'mp'=12] {'x'}, use_global_device_ids=true, to_apply=%region_3.0 | all-reduce | flops 704 | bytes 5632 | tf_op jit(solution)/shard_map/psum | solution.py:15
  40.1 7.6 %psum.45 = f32[2,1,352]{2,0,1:T(2,128)S(1)} all-reduce(f32[2,1,352]{2,0,1:T(2,128)S(1)} %bitcast.52), channel_id=1, replica_groups=mesh['x'=4,'y'=8,'c'=2,'mp'=12] {'c'}, use_global_device_ids=true, to_apply=%region_5.0 | all-reduce | flops 704 | bytes 5632 | tf_op jit(solution)/shard_map/psum | solution.py:13
  47.8 12.5 %psum.46 = f32[2,1,352]{2,0,1:T(2,128)S(1)} all-reduce(f32[2,1,352]{2,0,1:T(2,128)S(1)} %psum.45), channel_id=1, replica_groups=mesh['x'=4,'y'=8,'c'=2,'mp'=12] {'y'}, use_global_device_ids=true, to_apply=%region_6.0 | all-reduce | flops 704 | bytes 5632 | tf_op jit(solution)/shard_map/psum | solution.py:14
  60.3 7.7 %psum.47 = f32[2,1,352]{2,0,1:T(2,128)S(1)} all-reduce(f32[2,1,352]{2,0,1:T(2,128)S(1)} %psum.46), channel_id=1, replica_groups=mesh['x'=4,'y'=8,'c'=2,'mp'=12] {'x'}, use_global_device_ids=true, to_apply=%region_7.0 | all-reduce | flops 704 | bytes 5632 | tf_op jit(solution)/shard_map/psum | solution.py:15
  68.0 10.0 %all_gather.37 = bf16[4,64,352]{2,1,0:T(8,128)(2,1)} all-gather(bf16[1,64,352]{2,1,0:T(8,128)(2,1)S(1)} %get-tuple-element.7), channel_id=1, replica_groups=mesh['x'=4,'y'=8,'c'=2,'mp'=12] {'x'}, dimensions={0}, use_global_device_ids=true | all-gather | bytes 225280 | tf_op jit(solution)/shard_map/all_gather | solution.py:19
  78.0 0.0 all-gather.11.cloned.1.call-update
  78.0 0.0 all-gather.13.cloned.1.call-start
  78.1 47.0 %all-gather.11.cloned.1.call-done = bf16[32,64,352]{2,1,0:T(8,128)(2,1)} async-done(((bf16[4,64,352]{2,1,0:T(8,128)(2,1)}), bf16[32,64,352]{2,1,0:T(8,128)(2,1)}) %all-gather.11.cloned.1.call-update) | async-done | bytes 1441808 | tf_op jit(solution)/shard_map/all_gather | solution.py:20
  125.1 0.0 all-gather.13.cloned.1.call-update
  125.1 22.0 %all_gather.36 = bf16[12,64,352]{2,1,0:T(8,128)(2,1)S(1)} all-gather(bf16[1,64,352]{2,1,0:T(8,128)(2,1)S(1)} %get-tuple-element.8), channel_id=1, replica_groups=mesh['x'=4,'y'=8,'c'=2,'mp'=12] {'mp'}, dimensions={0}, use_global_device_ids=true | all-gather | bytes 585728 | tf_op jit(solution)/shard_map/all_gather | solution.py:42
  147.1 1.3 copy.12
  148.4 4.0 %all_to_all.14 = bf16[64,64,66]{2,1,0:T(8,128)(2,1)} reshape(bf16[64,12,352]{2,1,0:T(8,128)(2,1)} %copy.12) | data formatting | bytes 1081344 | tf_op jit(solution)/shard_map/all_to_all | solution.py:45
  152.4 2.9 copy.15
  155.3 18.0 %all-to-all-start = ((bf16[64,64,66]{2,0,1:T(8,128)(2,1)}), bf16[64,64,66]{2,0,1:T(8,128)(2,1)}, u32[]{:S(2)}, u32[]{:S(2)}) async-start(bf16[64,64,66]{2,0,1:T(8,128)(2,1)} %copy.15), calls=%async_computation | async-start | bytes 2097152 | tf_op jit(solution)/shard_map/all_to_all | solution.py:45
  173.3 0.0 all-gather.15.cloned.1.call-start
  173.4 0.0 all-gather.13.cloned.1.call-done
  173.5 4.0 %copy.17 = bf16[4,8,2,64,352]{4,3,2,1,0:T(8,128)(2,1)} copy(bf16[4,8,2,64,352]{4,3,0,1,2:T(8,128)(2,1)} %bitcast.47) | data formatting | bytes 5767168 | tf_op jit(solution)/shard_map/transpose | solution.py:47
  177.5 24.3 %all-to-all-done = bf16[64,64,66]{2,0,1:T(8,128)(2,1)} async-done(((bf16[64,64,66]{2,0,1:T(8,128)(2,1)}), bf16[64,64,66]{2,0,1:T(8,128)(2,1)}, u32[]{:S(2)}, u32[]{:S(2)}) %all-to-all-start) | async-done | bytes 540704 | tf_op jit(solution)/shard_map/all_to_all | solution.py:45
  201.8 2.9 fusion.9
  204.7 11.0 %all-gather.5 = bf16[4,66,352]{2,1,0:T(8,128)(2,1)} all-gather(bf16[1,66,352]{2,1,0:T(8,128)(2,1)S(1)} %fusion.9), channel_id=4, replica_groups=mesh['x'=4,'y'=8,'c'=2,'mp'=12] {'x'}, dimensions={0}, use_global_device_ids=true | all-gather | bytes 232320 | tf_op jit(solution)/shard_map/all_gather | solution.py:19
  215.7 0.0 all-gather.15.cloned.1.call-update
  215.7 0.2 all-gather.17.cloned.1.call-start
  215.9 36.8 %all-gather.15.cloned.1.call-done = bf16[32,66,352]{2,1,0:T(8,128)(2,1)} async-done(((bf16[4,66,352]{2,1,0:T(8,128)(2,1)}), bf16[32,66,352]{2,1,0:T(8,128)(2,1)}) %all-gather.15.cloned.1.call-update) | async-done | bytes 1486864 | tf_op jit(solution)/shard_map/all_gather | solution.py:20
  252.8 3.3 %copy.18 = bf16[8,4,66,352]{3,1,2,0:T(4,128)(2,1)} copy(bf16[8,4,66,352]{3,2,1,0:T(8,128)(2,1)} %bitcast.49) | data formatting | bytes 2973696 | tf_op jit(solution)/shard_map/all_gather | solution.py:20
  256.0 0.0 all-gather.17.cloned.1.call-update
  256.1 6.1 %reshape_reshape.3 = bf16[64,4,8,2,66]{4,3,2,1,0:T(2,128)(2,1)} reshape(bf16[64,12,352]{2,1,0:T(8,128)(2,1)} %copy.12) | data formatting | bytes 1081344 | tf_op jit(solution)/shard_map/reshape;reshape | solution.py:69
  262.2 0.1 iota_add_fusion
  262.3 21.8 %all-gather.17.cloned.1.call-done = bf16[16,4,66,352]{3,1,2,0:T(4,128)(2,1)} async-done(((bf16[8,4,66,352]{3,1,2,0:T(4,128)(2,1)}), bf16[16,4,66,352]{3,1,2,0:T(4,128)(2,1)}) %all-gather.17.cloned.1.call-update) | async-done | bytes 2973712 | tf_op jit(solution)/shard_map/all_gather | solution.py:21
  284.1 2.4 copy.19
  286.5 0.0 copy-start.1
  286.5 1.7 fusion
  288.3 0.0 copy-done.1
  288.3 2.4 fusion.6
  (12 shorter events, 0.2 us)
Async XLA Ops:
  6.5 1.8 copy-start
  6.5 118.5 %all-gather.11.cloned.1.call-start = ((), (), s32[]{:S(2)}) async-start(), calls=%async_computation.1 | async-start | bytes 1769472 | tf_op jit(solution)/shard_map/all_gather | solution.py:20
  78.0 95.4 %all-gather.13.cloned.1.call-start = ((), (), s32[]{:S(2)}) async-start(), calls=%async_computation.2 | async-start | bytes 4718592 | tf_op jit(solution)/shard_map/all_gather | solution.py:21
  155.3 46.5 %all-to-all-start = ((bf16[64,64,66]{2,0,1:T(8,128)(2,1)}), bf16[64,64,66]{2,0,1:T(8,128)(2,1)}, u32[]{:S(2)}, u32[]{:S(2)}) async-start(bf16[64,64,66]{2,0,1:T(8,128)(2,1)} %copy.15), calls=%async_computation | async-start | bytes 2097152 | tf_op jit(solution)/shard_map/all_to_all | solution.py:45
  173.3 79.4 %all-gather.15.cloned.1.call-start = ((), (), s32[]{:S(2)}) async-start(), calls=%async_computation.3 | async-start | bytes 1990656 | tf_op jit(solution)/shard_map/all_gather | solution.py:20
  215.7 68.4 %all-gather.17.cloned.1.call-start = ((), (), s32[]{:S(2)}) async-start(), calls=%async_computation.4 | async-start | bytes 4866048 | tf_op jit(solution)/shard_map/all_gather | solution.py:21
  286.5 1.7 copy-start.1
Sparse Core Ops, SparseCore 0:
  78.2 46.8 all-gather.10
  127.4 28.1 all-gather.12
  215.8 36.8 all-gather.14
  256.2 27.9 all-gather.16

commit v3 on v2

v3 whole, which is shorter than its diff:
```python
import jax
import jax.numpy as jnp
from jax import lax
from jax.sharding import Mesh
from jax.sharding import PartitionSpec as P

off_weight = 0.0051
eps = 1e-05
DP = ("x", "y", "c")


def shift(v, axis, n, step):
    return lax.ppermute(v, axis, [(i, (i + step) % n) for i in range(n)])


def ring_gather(v, axis):
    n = lax.axis_size(axis)
    if n == 1:
        return v[None]
    right = n // 2
    left = n - 1 - right
    got = {0: v}
    cur = v
    for s in range(1, right + 1):
        cur = shift(cur, axis, n, 1)
        got[n - s] = cur
    cur = v
    for s in range(1, left + 1):
        cur = shift(cur, axis, n, -1)
        got[s] = cur
    return jnp.stack([got[t] for t in range(n)])


def dp_ring_gather(v):
    return ring_gather(ring_gather(ring_gather(v, "x"), "y"), "c")


def combine(mean, m2, count, axis, k):
    n = lax.axis_size(axis)
    pairs = [(i, i ^ k) for i in range(n)]
    other_mean = lax.ppermute(mean, axis, pairs)
    other_m2 = lax.ppermute(m2, axis, pairs)
    delta = other_mean - mean
    new_mean = (mean + other_mean) * 0.5
    new_m2 = (m2 + other_m2) + delta * delta * (count * 0.5)
    return new_mean, new_m2, count * 2


def dp_stats(feats):
    local = feats.shape[1]
    mean = jnp.sum(feats, axis=1, keepdims=True) / local
    dev = feats - mean
    m2 = jnp.sum(dev * dev, axis=1, keepdims=True)
    count = float(local)
    for axis in ("c", "y", "x"):
        k = 1
        while k < lax.axis_size(axis):
            mean, m2, count = combine(mean, m2, count, axis, k)
            k *= 2
    return mean, m2 / count


def relative_order(v, axes):
    for dim, axis in enumerate(axes, start=1):
        v = jnp.roll(v, -lax.axis_index(axis), axis=dim)
    return v


def shards(hidden, proj_weight):
    mp_index = lax.axis_index("mp")
    dp_index = lax.axis_index(DP)
    dp_count = lax.axis_size(DP)
    nx, ny, nc = lax.axis_size("x"), lax.axis_size("y"), lax.axis_size("c")
    ix, iy, ic = lax.axis_index("x"), lax.axis_index("y"), lax.axis_index("c")
    rows = proj_weight.shape[1]
    local = hidden.shape[1]
    total = local * dp_count
    feats = jnp.einsum("vbh,hc->vbc", hidden, proj_weight, preferred_element_type=jnp.float32)
    mean, var = dp_stats(feats)
    centered = feats - mean
    normed = (centered / jnp.sqrt(var + eps)).astype(jnp.bfloat16)
    inv_std = 1.0 / jnp.sqrt(var + eps)
    first = normed[0]
    second = normed[1]
    n_mp = lax.axis_size("mp")
    stacked = lax.all_gather(second, "mp", axis=0)
    second_full = jnp.transpose(stacked, (1, 0, 2)).reshape(local, n_mp * rows)
    width = second_full.shape[1] // dp_count
    columns = lax.all_to_all(second_full, DP, split_axis=1, concat_axis=0, tiled=True)
    columns = relative_order(columns.reshape(1, nx, ny, nc, local, width), ("x", "y", "c"))
    columns = jnp.transpose(columns[0], (2, 1, 0, 3, 4)).reshape(total, width)
    first_all = dp_ring_gather(first).reshape(total, rows)
    corr = (
        jnp.einsum("bi,bj->ij", first_all, columns, preferred_element_type=jnp.float32)
        / total
    )
    row_ids = mp_index * rows + lax.iota(jnp.int32, rows)[:, None]
    col_ids = dp_index * width + lax.iota(jnp.int32, width)[None, :]
    grad_block = jnp.where(row_ids == col_ids, 2.0 * (corr - 1.0), 2.0 * off_weight * corr).astype(
        jnp.bfloat16
    )
    grad_t = dp_ring_gather(grad_block.T).reshape(dp_count * width, rows)
    t = lax.iota(jnp.int32, width)
    cc = (lax.iota(jnp.int32, nc) + ic) % nc
    yy = (lax.iota(jnp.int32, ny) + iy) % ny
    xx = (lax.iota(jnp.int32, nx) + ix) % nx
    perm_cols = (
        ((xx[None, None, :, None] * ny + yy[None, :, None, None]) * nc + cc[:, None, None, None]) * width
        + t[None, None, None, :]
    ).reshape(-1)
    grad_wide = grad_t.astype(jnp.float32)
    row_flat = mp_index * rows + lax.iota(jnp.int32, rows)
    diag_val = jnp.sum(jnp.where(perm_cols[:, None] == row_flat[None, :], grad_wide, 0.0), axis=0)
    scale_sum = (jnp.sum(grad_wide * grad_wide, axis=0) - diag_val * diag_val) / (
        2.0 * off_weight
    ) + diag_val * (1.0 + diag_val / 2.0)
    second_perm = relative_order(second_full.reshape(local, nx, ny, nc, width), ("x", "y", "c"))
    second_perm = jnp.transpose(second_perm, (0, 3, 2, 1, 4)).reshape(local, dp_count * width)
    back = jnp.dot(second_perm, grad_t, preferred_element_type=jnp.float32)
    result = (back - first.astype(jnp.float32) * scale_sum[None, :]) * inv_std[0]
    return result.astype(jnp.bfloat16)


def solution(mesh):
    x, y, c = (4, 8, 2)
    sub = Mesh(mesh.devices.reshape(x, y, c, mesh.devices.shape[1]), DP + ("mp",))
    return jax.shard_map(
        shards,
        mesh=sub,
        in_specs=(P(None, DP, None), P(None, "mp")),
        out_specs=P(DP, "mp"),
        check_vma=False,
    )
```

time: 298 us -> 285 us (0.956)
  starting transfers between devices: 18.3 us -> 146 us
  blocking collectives: 100 us -> 24.6 us
  waiting for transfers between devices: 130 us -> 69.4 us
  between operations: 13.3 us -> 0.7 us
  other arithmetic: 1.93 us -> 6.39 us
    ppermute x0 -> x34, starting transfers between devices: none -> 134 us  [the longest x22 87 us: shift(): return lax.ppermute(v, axis, [(i, (i + step) % n) for i in range(n)])]
    all_gather x4 -> x0, waiting for transfers between devices: 106 us -> none  [the longest x2 83.8 us: dp_gather(): v = lax.all_gather(v, 'y', axis=0)]
    psum x6 -> x0, blocking collectives: 57.2 us -> none  [the longest x2 23.3 us: dp_sum(): v = lax.psum(v, 'y')]
    ppermute x0 -> x34, waiting for transfers between devices: none -> 41.1 us  [the longest x22 34.1 us: shift(): return lax.ppermute(v, axis, [(i, (i + step) % n) for i in range(n)])]
    all_gather x2 -> x0, blocking collectives: 21 us -> none  [dp_gather(): v = lax.all_gather(v, 'x', axis=0)]
    unnamed x4 -> x18, local copies, waits for them, and re-layouts: 1.84 us -> 7.67 us
    all_gather x2 -> x0, local copies, waits for them, and re-layouts: 5.66 us -> none  [the longest x1 3.28 us: dp_gather(): v = lax.all_gather(v, 'y', axis=0)]
    all_to_all x1, starting transfers between devices: 18 us -> 12.4 us  [shards(): lax.all_to_all(second_full, DP, split_axis=1, concat_axis=0, tiled=True)]
  transfers between devices with their start and end apart: 5 -> 35, of which waited for: 4 -> 17; matrix products, arithmetic and copies ran while one was open for 5% -> 7% of each run, Pallas kernels for 0% -> 0%
where the time goes in v3:
time: 285 us; the launch traced here: 284 us
  starting transfers between devices  146 us (51%)
  waiting for transfers between devices  69.4 us (24%)
  local copies, waits for them, and re-layouts  28.1 us (10%)
  blocking collectives  24.6 us (9%)
  matrix products  7.99 us (3%)
  other arithmetic  6.39 us (2%)
    ppermute x22, starting transfers between devices, shift(): return lax.ppermute(v, axis, [(i, (i + step) % n) for i in range(n)])  87 us
    ppermute x22, waiting for transfers between devices, shift(): return lax.ppermute(v, axis, [(i, (i + step) % n) for i in range(n)])  34.1 us
    ppermute x6, starting transfers between devices, combine(): other_m2 = lax.ppermute(m2, axis, pairs)  32.1 us
    all_to_all x1, waiting for transfers between devices, shards(): lax.all_to_all(second_full, DP, split_axis=1, concat_axis=0, tiled=True)  28.4 us
    all_gather x1, blocking collectives, shards(): stacked = lax.all_gather(second, 'mp', axis=0)  24.6 us
    ppermute x6, starting transfers between devices, combine(): other_mean = lax.ppermute(mean, axis, pairs)  15 us
    all_to_all x1, starting transfers between devices, shards(): lax.all_to_all(second_full, DP, split_axis=1, concat_axis=0, tiled=True)  12.4 us
    another operation x2, local copies, waits for them, and re-layouts, shards(): second_full.reshape(local, nx, ny, nc, width)  7.98 us
  transfers between devices with their start and end apart: 35, of which 17 were waited for; matrix products, arithmetic and copies ran while one was open for 7% of the time, Pallas kernels for 0%

profile of v3, /device:TPU:1, one launch (start us, length us, event | category | flops | bytes accessed | tf_op | source)
XLA Modules:
  0.0 283.5 jit_solution(15080898708272857608)
XLA Ops:
  0.0 1.8 copy-done
  1.8 2.3 fusion.37
  4.2 12.4 %collective-permute-start.6 = (f32[2,1,352]{2,0,1:T(2,128)S(1)}, f32[2,1,352]{2,0,1:T(2,128)S(1)}, u32[]{:S(2)}, u32[]{:S(2)}) collective-permute-start(f32[2,1,352]{2,0,1:T(2,128)S(1)} %bitcast.113), channel_id=1, source_target_pairs={{0,12},{12,0},{1,13},{13,1},{2,14},{14,2},{3,15},{15,3},{4,16},{16... | collective-permute-start | bytes 8456 | tf_op jit(solution)/shard_map/ppermute | solution.py:42
  16.7 1.9 collective-permute-start
  18.6 1.1 collective-permute-done
  19.7 1.9 collective-permute-start.1
  21.7 3.4 %collective-permute-start.7 = (f32[2,1,352]{2,0,1:T(2,128)S(1)}, f32[2,1,352]{2,0,1:T(2,128)S(1)}, u32[]{:S(2)}, u32[]{:S(2)}) collective-permute-start(f32[2,1,352]{2,0,1:T(2,128)S(1)} %get-tuple-element.20), channel_id=1, source_target_pairs={{0,24},{24,0},{48,72},{72,48},{96,120},{120,96},{144,168},{168,144... | collective-permute-start | bytes 8456 | tf_op jit(solution)/shard_map/ppermute | solution.py:42
  25.0 1.0 collective-permute-done.7
  26.0 1.9 collective-permute-start.2
  27.9 4.3 %collective-permute-start.8 = (f32[2,1,352]{2,0,1:T(2,128)S(1)}, f32[2,1,352]{2,0,1:T(2,128)S(1)}, u32[]{:S(2)}, u32[]{:S(2)}) collective-permute-start(f32[2,1,352]{2,0,1:T(2,128)S(1)} %get-tuple-element.18), channel_id=1, source_target_pairs={{0,48},{24,72},{48,0},{72,24},{96,144},{120,168},{144,96},{168,120... | collective-permute-start | bytes 8456 | tf_op jit(solution)/shard_map/ppermute | solution.py:42
  32.2 1.1 collective-permute-done.8
  33.3 1.9 collective-permute-start.3
  35.3 7.3 %collective-permute-start.9 = (f32[2,1,352]{2,0,1:T(2,128)S(1)}, f32[2,1,352]{2,0,1:T(2,128)S(1)}, u32[]{:S(2)}, u32[]{:S(2)}) collective-permute-start(f32[2,1,352]{2,0,1:T(2,128)S(1)} %get-tuple-element.16), channel_id=1, source_target_pairs={{0,96},{24,120},{48,144},{72,168},{96,0},{120,24},{144,48},{168,72... | collective-permute-start | bytes 8456 | tf_op jit(solution)/shard_map/ppermute | solution.py:42
  42.5 1.0 collective-permute-done.9
  43.5 1.9 collective-permute-start.10
  45.4 3.4 %collective-permute-start.4 = (f32[2,1,352]{2,0,1:T(2,128)S(1)}, f32[2,1,352]{2,0,1:T(2,128)S(1)}, u32[]{:S(2)}, u32[]{:S(2)}) collective-permute-start(f32[2,1,352]{2,0,1:T(2,128)S(1)} %get-tuple-element.15), channel_id=1, source_target_pairs={{0,192},{192,0},{384,576},{576,384},{1,193},{193,1},{385,577},{577... | collective-permute-start | bytes 8456 | tf_op jit(solution)/shard_map/ppermute | solution.py:41
  49.8 2.8 collective-permute-start.11
  52.6 4.0 %collective-permute-start.5 = (f32[2,1,352]{2,0,1:T(2,128)S(1)}, f32[2,1,352]{2,0,1:T(2,128)S(1)}, u32[]{:S(2)}, u32[]{:S(2)}) collective-permute-start(f32[2,1,352]{2,0,1:T(2,128)S(1)} %get-tuple-element.13), channel_id=1, source_target_pairs={{0,384},{192,576},{384,0},{576,192},{1,385},{193,577},{385,1},{577... | collective-permute-start | bytes 8456 | tf_op jit(solution)/shard_map/ppermute | solution.py:41
  56.6 1.9 collective-permute-done.5
  58.6 2.5 collective-permute-start.13
  61.0 4.3 %collective-permute-start.12 = (bf16[64,352]{1,0:T(8,128)(2,1)S(1)}, bf16[64,352]{1,0:T(8,128)(2,1)S(1)}, u32[]{:S(2)}, u32[]{:S(2)}) collective-permute-start(bf16[64,352]{1,0:T(8,128)(2,1)S(1)} %get-tuple-element.8), channel_id=1, source_target_pairs={{0,576},{192,0},{384,192},{576,384},{1,577},{193,1},{385,193},{577... | collective-permute-start | bytes 135176 | tf_op jit(solution)/shard_map/ppermute | solution.py:13
  65.3 1.9 collective-permute-start.14
  67.3 4.1 %collective-permute-done.14 = bf16[64,352]{1,0:T(8,128)(2,1)S(1)} collective-permute-done((bf16[64,352]{1,0:T(8,128)(2,1)S(1)}, bf16[64,352]{1,0:T(8,128)(2,1)S(1)}, u32[]{:S(2)}, u32[]{:S(2)}) %collective-permute-start.14) | collective-permute-done | bytes 45088 | tf_op jit(solution)/shard_map/ppermute | solution.py:13
  71.4 7.7 %collective-permute-start.15 = (bf16[4,64,352]{2,1,0:T(8,128)(2,1)S(1)}, bf16[4,64,352]{2,1,0:T(8,128)(2,1)S(1)}, u32[]{:S(2)}, u32[]{:S(2)}) collective-permute-start(bf16[4,64,352]{2,1,0:T(8,128)(2,1)S(1)} %pad_maximum_fusion.3), channel_id=1, source_target_pairs={{0,168},{24,0},{48,24},{72,48},{96,72},{120,96},{144,120},{168,144... | collective-permute-start | bytes 540680 | tf_op jit(solution)/shard_map/ppermute | solution.py:13
  79.1 1.9 collective-permute-start.18
  81.8 5.3 %collective-permute-start.16 = (bf16[4,64,352]{2,1,0:T(8,128)(2,1)S(1)}, bf16[4,64,352]{2,1,0:T(8,128)(2,1)S(1)}, u32[]{:S(2)}, u32[]{:S(2)}) collective-permute-start(bf16[4,64,352]{2,1,0:T(8,128)(2,1)S(1)} %collective-permute-done.15), channel_id=1, source_target_pairs={{0,168},{24,0},{48,24},{72,48},{96,72},{120,96},{144,120},{168,144... | collective-permute-start | bytes 540680 | tf_op jit(solution)/shard_map/ppermute | solution.py:13
  87.0 1.9 collective-permute-start.19
  90.2 5.3 %collective-permute-start.17 = (bf16[4,64,352]{2,1,0:T(8,128)(2,1)S(1)}, bf16[4,64,352]{2,1,0:T(8,128)(2,1)S(1)}, u32[]{:S(2)}, u32[]{:S(2)}) collective-permute-start(bf16[4,64,352]{2,1,0:T(8,128)(2,1)S(1)} %collective-permute-done.16), channel_id=1, source_target_pairs={{0,168},{24,0},{48,24},{72,48},{96,72},{120,96},{144,120},{168,144... | collective-permute-start | bytes 540680 | tf_op jit(solution)/shard_map/ppermute | solution.py:13
  95.6 1.9 collective-permute-start.20
  98.2 5.0 %collective-permute-done.20 = bf16[4,64,352]{2,1,0:T(8,128)(2,1)S(1)} collective-permute-done((bf16[4,64,352]{2,1,0:T(8,128)(2,1)S(1)}, bf16[4,64,352]{2,1,0:T(8,128)(2,1)S(1)}, u32[]{:S(2)}, u32[]{:S(2)}) %collective-permute-start.20) | collective-permute-done | bytes 180256 | tf_op jit(solution)/shard_map/ppermute | solution.py:13
  103.2 1.9 collective-permute-start.21
  105.8 5.0 %collective-permute-done.21 = bf16[4,64,352]{2,1,0:T(8,128)(2,1)S(1)} collective-permute-done((bf16[4,64,352]{2,1,0:T(8,128)(2,1)S(1)}, bf16[4,64,352]{2,1,0:T(8,128)(2,1)S(1)}, u32[]{:S(2)}, u32[]{:S(2)}) %collective-permute-start.21) | collective-permute-done | bytes 180256 | tf_op jit(solution)/shard_map/ppermute | solution.py:13
  113.6 15.1 %collective-permute-start.22 = (bf16[8,4,64,352]{3,2,1,0:T(8,128)(2,1)}, bf16[8,4,64,352]{3,2,1,0:T(8,128)(2,1)}, u32[]{:S(2)}, u32[]{:S(2)}) collective-permute-start(bf16[8,4,64,352]{3,2,1,0:T(8,128)(2,1)} %bitcast_dynamic-update-slice_fusion.8), channel_id=1, source_target_pairs={{0,12},{12,0},{1,13},{13,1},{2,14},{14,2},{3,15},{15,3},{4,16},{16... | collective-permute-start | bytes 4325384 | tf_op jit(solution)/shard_map/ppermute | solution.py:13
  128.7 24.6 %all_gather.3 = bf16[12,64,352]{2,1,0:T(8,128)(2,1)S(1)} all-gather(bf16[1,64,352]{2,1,0:T(8,128)(2,1)S(1)} %get-tuple-element.9), channel_id=1, replica_groups=mesh['x'=4,'y'=8,'c'=2,'mp'=12] {'mp'}, dimensions={0}, use_global_device_ids=true | all-gather | bytes 585728 | tf_op jit(solution)/shard_map/all_gather | solution.py:86
  153.3 1.3 copy.9
  154.6 4.0 %all_to_all.12 = bf16[64,64,66]{2,1,0:T(8,128)(2,1)} reshape(bf16[64,12,352]{2,1,0:T(8,128)(2,1)} %copy.9) | data formatting | bytes 1081344 | tf_op jit(solution)/shard_map/all_to_all | solution.py:89
  158.6 2.9 %copy.13 = bf16[64,64,66]{2,0,1:T(8,128)(2,1)} copy(bf16[64,64,66]{2,1,0:T(8,128)(2,1)} %all_to_all.12) | data formatting | bytes 1081344 | tf_op jit(solution)/shard_map/all_to_all | solution.py:89
  161.4 12.4 %all-to-all-start = ((bf16[64,64,66]{2,0,1:T(8,128)(2,1)}), bf16[64,64,66]{2,0,1:T(8,128)(2,1)}, u32[]{:S(2)}, u32[]{:S(2)}) async-start(bf16[64,64,66]{2,0,1:T(8,128)(2,1)} %copy.13), calls=%async_computation | async-start | bytes 2097152 | tf_op jit(solution)/shard_map/all_to_all | solution.py:89
  173.9 28.4 %all-to-all-done = bf16[64,64,66]{2,0,1:T(8,128)(2,1)} async-done(((bf16[64,64,66]{2,0,1:T(8,128)(2,1)}), bf16[64,64,66]{2,0,1:T(8,128)(2,1)}, u32[]{:S(2)}, u32[]{:S(2)}) %all-to-all-start) | async-done | bytes 540704 | tf_op jit(solution)/shard_map/all_to_all | solution.py:89
  202.3 1.7 fusion.16
  204.6 3.3 %select_convert_fusion = bf16[66,352]{1,0:T(8,128)(2,1)S(1)} fusion(bf16[1,8,4,64,352]{4,3,2,1,0:T(8,128)(2,1)} %bitcast.24, bf16[1,8,4,64,352]{4,3,2,1,0:T(8,128)(2,1)} %bitcast.23, s32[352]{0:T(512)S(1)} %iota_add_fusion.1, s32[66]{0:T(128)S(1)} %iota_add_fusion.2, s32[]{:T(128)S(6)} %select_n.96, bf16[1,4,8,2,64,66]{5,4,3,2,1,0:T(8,128)(2,1)S(1)} %fusion.15), kind=kOutput, calls=%fused_computation.58 | convolution fusion | flops 192191296 | bytes 3472396 | tf_op jit(solution)/shard_map/bi,bj->ij/dot_general | solution.py:94
  207.9 3.1 %collective-permute-start.24 = (bf16[66,352]{1,0:T(8,128)(2,1)S(1)}, bf16[66,352]{1,0:T(8,128)(2,1)S(1)}, u32[]{:S(2)}, u32[]{:S(2)}) collective-permute-start(bf16[66,352]{1,0:T(8,128)(2,1)S(1)} %select_convert_fusion), channel_id=1, source_target_pairs={{0,192},{192,384},{384,576},{576,0},{1,193},{193,385},{385,577},{5... | collective-permute-start | bytes 139400 | tf_op jit(solution)/shard_map/ppermute | solution.py:13
  211.0 3.4 %collective-permute-start.23 = (bf16[66,352]{1,0:T(8,128)(2,1)S(1)}, bf16[66,352]{1,0:T(8,128)(2,1)S(1)}, u32[]{:S(2)}, u32[]{:S(2)}) collective-permute-start(bf16[66,352]{1,0:T(8,128)(2,1)S(1)} %select_convert_fusion), channel_id=1, source_target_pairs={{0,576},{192,0},{384,192},{576,384},{1,577},{193,1},{385,193},{577... | collective-permute-start | bytes 139400 | tf_op jit(solution)/shard_map/ppermute | solution.py:13
  214.4 1.9 collective-permute-start.25
  216.5 4.1 %collective-permute-done.25 = bf16[66,352]{1,0:T(8,128)(2,1)S(1)} collective-permute-done((bf16[66,352]{1,0:T(8,128)(2,1)S(1)}, bf16[66,352]{1,0:T(8,128)(2,1)S(1)}, u32[]{:S(2)}, u32[]{:S(2)}) %collective-permute-start.25) | collective-permute-done | bytes 46496 | tf_op jit(solution)/shard_map/ppermute | solution.py:13
  220.6 2.0 collective-permute-start.26
  222.6 3.3 %collective-permute-start.29 = (bf16[4,66,352]{2,1,0:T(8,128)(2,1)S(1)}, bf16[4,66,352]{2,1,0:T(8,128)(2,1)S(1)}, u32[]{:S(2)}, u32[]{:S(2)}) collective-permute-start(bf16[4,66,352]{2,1,0:T(8,128)(2,1)S(1)} %pad_maximum_fusion.2), channel_id=1, source_target_pairs={{0,24},{24,48},{48,72},{72,96},{96,120},{120,144},{144,168},{168,0... | collective-permute-start | bytes 557576 | tf_op jit(solution)/shard_map/ppermute | solution.py:13
  225.9 1.3 collective-permute-done.26
  227.3 3.2 %collective-permute-start.27 = (bf16[4,66,352]{2,1,0:T(8,128)(2,1)S(1)}, bf16[4,66,352]{2,1,0:T(8,128)(2,1)S(1)}, u32[]{:S(2)}, u32[]{:S(2)}) collective-permute-start(bf16[4,66,352]{2,1,0:T(8,128)(2,1)S(1)} %collective-permute-done.26), channel_id=1, source_target_pairs={{0,168},{24,0},{48,24},{72,48},{96,72},{120,96},{144,120},{168,144... | collective-permute-start | bytes 557576 | tf_op jit(solution)/shard_map/ppermute | solution.py:13
  230.5 2.3 collective-permute-start.30
  232.9 1.3 collective-permute-done.27
  234.2 4.1 %collective-permute-start.28 = (bf16[4,66,352]{2,1,0:T(8,128)(2,1)S(1)}, bf16[4,66,352]{2,1,0:T(8,128)(2,1)S(1)}, u32[]{:S(2)}, u32[]{:S(2)}) collective-permute-start(bf16[4,66,352]{2,1,0:T(8,128)(2,1)S(1)} %collective-permute-done.27), channel_id=1, source_target_pairs={{0,168},{24,0},{48,24},{72,48},{96,72},{120,96},{144,120},{168,144... | collective-permute-start | bytes 557576 | tf_op jit(solution)/shard_map/ppermute | solution.py:13
  238.4 1.9 collective-permute-start.31
  240.4 5.9 %collective-permute-done.31 = bf16[4,66,352]{2,1,0:T(8,128)(2,1)S(1)} collective-permute-done((bf16[4,66,352]{2,1,0:T(8,128)(2,1)S(1)}, bf16[4,66,352]{2,1,0:T(8,128)(2,1)S(1)}, u32[]{:S(2)}, u32[]{:S(2)}) %collective-permute-start.31) | collective-permute-done | bytes 185888 | tf_op jit(solution)/shard_map/ppermute | solution.py:13
  246.3 1.9 collective-permute-start.32
  248.3 6.6 %collective-permute-done.32 = bf16[4,66,352]{2,1,0:T(8,128)(2,1)S(1)} collective-permute-done((bf16[4,66,352]{2,1,0:T(8,128)(2,1)S(1)}, bf16[4,66,352]{2,1,0:T(8,128)(2,1)S(1)}, u32[]{:S(2)}, u32[]{:S(2)}) %collective-permute-start.32) | collective-permute-done | bytes 185888 | tf_op jit(solution)/shard_map/ppermute | solution.py:13
  255.0 1.2 copy-done.1
  256.3 1.7 copy.15
  258.0 10.0 %collective-permute-start.33 = (bf16[8,4,66,352]{3,0,2,1:T(8,128)(2,1)}, bf16[8,4,66,352]{3,0,2,1:T(8,128)(2,1)}, u32[]{:S(2)}, u32[]{:S(2)}) collective-permute-start(bf16[8,4,66,352]{3,0,2,1:T(8,128)(2,1)} %copy.15), channel_id=1, source_target_pairs={{0,12},{12,0},{1,13},{13,1},{2,14},{14,2},{3,15},{15,3},{4,16},{16... | collective-permute-start | bytes 4460552 | tf_op jit(solution)/shard_map/ppermute | solution.py:13
  268.3 6.1 %reshape_reshape.3 = bf16[64,4,8,2,66]{4,3,2,1,0:T(2,128)(2,1)} reshape(bf16[64,12,352]{2,1,0:T(8,128)(2,1)} %copy.9) | data formatting | bytes 1081344 | tf_op jit(solution)/shard_map/reshape;reshape | solution.py:117
  274.4 1.9 copy.10
  277.4 1.8 copy.26
  279.4 1.8 fusion
  281.2 2.4 fusion.13
  (66 shorter events, 10.0 us)
Async XLA Ops:
  0.0 1.8 copy-start
  4.2 14.4 %collective-permute-start.6 = (f32[2,1,352]{2,0,1:T(2,128)S(1)}, f32[2,1,352]{2,0,1:T(2,128)S(1)}, u32[]{:S(2)}, u32[]{:S(2)}) collective-permute-start(f32[2,1,352]{2,0,1:T(2,128)S(1)} %bitcast.113), channel_id=1, source_target_pairs={{0,12},{12,0},{1,13},{13,1},{2,14},{14,2},{3,15},{15,3},{4,16},{16... | collective-permute-start | bytes 8456 | tf_op jit(solution)/shard_map/ppermute | solution.py:42
  16.7 3.1 %collective-permute-start = (f32[2,1,352]{2,0,1:T(2,128)S(1)}, f32[2,1,352]{2,0,1:T(2,128)S(1)}, u32[]{:S(2)}, u32[]{:S(2)}) collective-permute-start(f32[2,1,352]{2,0,1:T(2,128)S(1)} %get-tuple-element.23), channel_id=1, source_target_pairs={{0,12},{12,0},{1,13},{13,1},{2,14},{14,2},{3,15},{15,3},{4,16},{16... | collective-permute-start | bytes 8456 | tf_op jit(solution)/shard_map/ppermute | solution.py:41
  19.7 5.3 %collective-permute-start.1 = (f32[2,1,352]{2,0,1:T(2,128)S(1)}, f32[2,1,352]{2,0,1:T(2,128)S(1)}, u32[]{:S(2)}, u32[]{:S(2)}) collective-permute-start(f32[2,1,352]{2,0,1:T(2,128)S(1)} %get-tuple-element.21), channel_id=1, source_target_pairs={{0,24},{24,0},{48,72},{72,48},{96,120},{120,96},{144,168},{168,144... | collective-permute-start | bytes 8456 | tf_op jit(solution)/shard_map/ppermute | solution.py:41
  21.7 4.3 %collective-permute-start.7 = (f32[2,1,352]{2,0,1:T(2,128)S(1)}, f32[2,1,352]{2,0,1:T(2,128)S(1)}, u32[]{:S(2)}, u32[]{:S(2)}) collective-permute-start(f32[2,1,352]{2,0,1:T(2,128)S(1)} %get-tuple-element.20), channel_id=1, source_target_pairs={{0,24},{24,0},{48,72},{72,48},{96,120},{120,96},{144,168},{168,144... | collective-permute-start | bytes 8456 | tf_op jit(solution)/shard_map/ppermute | solution.py:42
  26.0 6.2 %collective-permute-start.2 = (f32[2,1,352]{2,0,1:T(2,128)S(1)}, f32[2,1,352]{2,0,1:T(2,128)S(1)}, u32[]{:S(2)}, u32[]{:S(2)}) collective-permute-start(f32[2,1,352]{2,0,1:T(2,128)S(1)} %get-tuple-element.19), channel_id=1, source_target_pairs={{0,48},{24,72},{48,0},{72,24},{96,144},{120,168},{144,96},{168,120... | collective-permute-start | bytes 8456 | tf_op jit(solution)/shard_map/ppermute | solution.py:41
  27.9 5.4 %collective-permute-start.8 = (f32[2,1,352]{2,0,1:T(2,128)S(1)}, f32[2,1,352]{2,0,1:T(2,128)S(1)}, u32[]{:S(2)}, u32[]{:S(2)}) collective-permute-start(f32[2,1,352]{2,0,1:T(2,128)S(1)} %get-tuple-element.18), channel_id=1, source_target_pairs={{0,48},{24,72},{48,0},{72,24},{96,144},{120,168},{144,96},{168,120... | collective-permute-start | bytes 8456 | tf_op jit(solution)/shard_map/ppermute | solution.py:42
  33.3 9.2 %collective-permute-start.3 = (f32[2,1,352]{2,0,1:T(2,128)S(1)}, f32[2,1,352]{2,0,1:T(2,128)S(1)}, u32[]{:S(2)}, u32[]{:S(2)}) collective-permute-start(f32[2,1,352]{2,0,1:T(2,128)S(1)} %get-tuple-element.17), channel_id=1, source_target_pairs={{0,96},{24,120},{48,144},{72,168},{96,0},{120,24},{144,48},{168,72... | collective-permute-start | bytes 8456 | tf_op jit(solution)/shard_map/ppermute | solution.py:41
  35.3 8.2 %collective-permute-start.9 = (f32[2,1,352]{2,0,1:T(2,128)S(1)}, f32[2,1,352]{2,0,1:T(2,128)S(1)}, u32[]{:S(2)}, u32[]{:S(2)}) collective-permute-start(f32[2,1,352]{2,0,1:T(2,128)S(1)} %get-tuple-element.16), channel_id=1, source_target_pairs={{0,96},{24,120},{48,144},{72,168},{96,0},{120,24},{144,48},{168,72... | collective-permute-start | bytes 8456 | tf_op jit(solution)/shard_map/ppermute | solution.py:42
  43.5 5.3 %collective-permute-start.10 = (f32[2,1,352]{2,0,1:T(2,128)S(1)}, f32[2,1,352]{2,0,1:T(2,128)S(1)}, u32[]{:S(2)}, u32[]{:S(2)}) collective-permute-start(f32[2,1,352]{2,0,1:T(2,128)S(1)} %get-tuple-element.14), channel_id=1, source_target_pairs={{0,192},{192,0},{384,576},{576,384},{1,193},{193,1},{385,577},{577... | collective-permute-start | bytes 8456 | tf_op jit(solution)/shard_map/ppermute | solution.py:42
  45.4 4.3 %collective-permute-start.4 = (f32[2,1,352]{2,0,1:T(2,128)S(1)}, f32[2,1,352]{2,0,1:T(2,128)S(1)}, u32[]{:S(2)}, u32[]{:S(2)}) collective-permute-start(f32[2,1,352]{2,0,1:T(2,128)S(1)} %get-tuple-element.15), channel_id=1, source_target_pairs={{0,192},{192,0},{384,576},{576,384},{1,193},{193,1},{385,577},{577... | collective-permute-start | bytes 8456 | tf_op jit(solution)/shard_map/ppermute | solution.py:41
  49.8 6.8 %collective-permute-start.11 = (f32[2,1,352]{2,0,1:T(2,128)S(1)}, f32[2,1,352]{2,0,1:T(2,128)S(1)}, u32[]{:S(2)}, u32[]{:S(2)}) collective-permute-start(f32[2,1,352]{2,0,1:T(2,128)S(1)} %get-tuple-element.12), channel_id=1, source_target_pairs={{0,384},{192,576},{384,0},{576,192},{1,385},{193,577},{385,1},{577... | collective-permute-start | bytes 8456 | tf_op jit(solution)/shard_map/ppermute | solution.py:42
  52.6 5.8 %collective-permute-start.5 = (f32[2,1,352]{2,0,1:T(2,128)S(1)}, f32[2,1,352]{2,0,1:T(2,128)S(1)}, u32[]{:S(2)}, u32[]{:S(2)}) collective-permute-start(f32[2,1,352]{2,0,1:T(2,128)S(1)} %get-tuple-element.13), channel_id=1, source_target_pairs={{0,384},{192,576},{384,0},{576,192},{1,385},{193,577},{385,1},{577... | collective-permute-start | bytes 8456 | tf_op jit(solution)/shard_map/ppermute | solution.py:41
  58.6 6.8 %collective-permute-start.13 = (bf16[64,352]{1,0:T(8,128)(2,1)S(1)}, bf16[64,352]{1,0:T(8,128)(2,1)S(1)}, u32[]{:S(2)}, u32[]{:S(2)}) collective-permute-start(bf16[64,352]{1,0:T(8,128)(2,1)S(1)} %get-tuple-element.8), channel_id=1, source_target_pairs={{0,192},{192,384},{384,576},{576,0},{1,193},{193,385},{385,577},{5... | collective-permute-start | bytes 135176 | tf_op jit(solution)/shard_map/ppermute | solution.py:13
  61.0 6.3 %collective-permute-start.12 = (bf16[64,352]{1,0:T(8,128)(2,1)S(1)}, bf16[64,352]{1,0:T(8,128)(2,1)S(1)}, u32[]{:S(2)}, u32[]{:S(2)}) collective-permute-start(bf16[64,352]{1,0:T(8,128)(2,1)S(1)} %get-tuple-element.8), channel_id=1, source_target_pairs={{0,576},{192,0},{384,192},{576,384},{1,577},{193,1},{385,193},{577... | collective-permute-start | bytes 135176 | tf_op jit(solution)/shard_map/ppermute | solution.py:13
  65.3 6.0 %collective-permute-start.14 = (bf16[64,352]{1,0:T(8,128)(2,1)S(1)}, bf16[64,352]{1,0:T(8,128)(2,1)S(1)}, u32[]{:S(2)}, u32[]{:S(2)}) collective-permute-start(bf16[64,352]{1,0:T(8,128)(2,1)S(1)} %collective-permute-done.13), channel_id=1, source_target_pairs={{0,192},{192,384},{384,576},{576,0},{1,193},{193,385},{385,577},{5... | collective-permute-start | bytes 135176 | tf_op jit(solution)/shard_map/ppermute | solution.py:13
  71.4 10.3 %collective-permute-start.15 = (bf16[4,64,352]{2,1,0:T(8,128)(2,1)S(1)}, bf16[4,64,352]{2,1,0:T(8,128)(2,1)S(1)}, u32[]{:S(2)}, u32[]{:S(2)}) collective-permute-start(bf16[4,64,352]{2,1,0:T(8,128)(2,1)S(1)} %pad_maximum_fusion.3), channel_id=1, source_target_pairs={{0,168},{24,0},{48,24},{72,48},{96,72},{120,96},{144,120},{168,144... | collective-permute-start | bytes 540680 | tf_op jit(solution)/shard_map/ppermute | solution.py:13
  79.1 7.9 %collective-permute-start.18 = (bf16[4,64,352]{2,1,0:T(8,128)(2,1)S(1)}, bf16[4,64,352]{2,1,0:T(8,128)(2,1)S(1)}, u32[]{:S(2)}, u32[]{:S(2)}) collective-permute-start(bf16[4,64,352]{2,1,0:T(8,128)(2,1)S(1)} %pad_maximum_fusion.3), channel_id=1, source_target_pairs={{0,24},{24,48},{48,72},{72,96},{96,120},{120,144},{144,168},{168,0... | collective-permute-start | bytes 540680 | tf_op jit(solution)/shard_map/ppermute | solution.py:13
  81.8 8.5 %collective-permute-start.16 = (bf16[4,64,352]{2,1,0:T(8,128)(2,1)S(1)}, bf16[4,64,352]{2,1,0:T(8,128)(2,1)S(1)}, u32[]{:S(2)}, u32[]{:S(2)}) collective-permute-start(bf16[4,64,352]{2,1,0:T(8,128)(2,1)S(1)} %collective-permute-done.15), channel_id=1, source_target_pairs={{0,168},{24,0},{48,24},{72,48},{96,72},{120,96},{144,120},{168,144... | collective-permute-start | bytes 540680 | tf_op jit(solution)/shard_map/ppermute | solution.py:13
  87.0 8.5 %collective-permute-start.19 = (bf16[4,64,352]{2,1,0:T(8,128)(2,1)S(1)}, bf16[4,64,352]{2,1,0:T(8,128)(2,1)S(1)}, u32[]{:S(2)}, u32[]{:S(2)}) collective-permute-start(bf16[4,64,352]{2,1,0:T(8,128)(2,1)S(1)} %collective-permute-done.18), channel_id=1, source_target_pairs={{0,24},{24,48},{48,72},{72,96},{96,120},{120,144},{144,168},{168,0... | collective-permute-start | bytes 540680 | tf_op jit(solution)/shard_map/ppermute | solution.py:13
  90.2 14.9 %collective-permute-start.17 = (bf16[4,64,352]{2,1,0:T(8,128)(2,1)S(1)}, bf16[4,64,352]{2,1,0:T(8,128)(2,1)S(1)}, u32[]{:S(2)}, u32[]{:S(2)}) collective-permute-start(bf16[4,64,352]{2,1,0:T(8,128)(2,1)S(1)} %collective-permute-done.16), channel_id=1, source_target_pairs={{0,168},{24,0},{48,24},{72,48},{96,72},{120,96},{144,120},{168,144... | collective-permute-start | bytes 540680 | tf_op jit(solution)/shard_map/ppermute | solution.py:13
  95.6 7.6 %collective-permute-start.20 = (bf16[4,64,352]{2,1,0:T(8,128)(2,1)S(1)}, bf16[4,64,352]{2,1,0:T(8,128)(2,1)S(1)}, u32[]{:S(2)}, u32[]{:S(2)}) collective-permute-start(bf16[4,64,352]{2,1,0:T(8,128)(2,1)S(1)} %collective-permute-done.19), channel_id=1, source_target_pairs={{0,24},{24,48},{48,72},{72,96},{96,120},{120,144},{144,168},{168,0... | collective-permute-start | bytes 540680 | tf_op jit(solution)/shard_map/ppermute | solution.py:13
  103.2 7.6 %collective-permute-start.21 = (bf16[4,64,352]{2,1,0:T(8,128)(2,1)S(1)}, bf16[4,64,352]{2,1,0:T(8,128)(2,1)S(1)}, u32[]{:S(2)}, u32[]{:S(2)}) collective-permute-start(bf16[4,64,352]{2,1,0:T(8,128)(2,1)S(1)} %collective-permute-done.20), channel_id=1, source_target_pairs={{0,24},{24,48},{48,72},{72,96},{96,120},{120,144},{144,168},{168,0... | collective-permute-start | bytes 540680 | tf_op jit(solution)/shard_map/ppermute | solution.py:13
  113.6 91.0 %collective-permute-start.22 = (bf16[8,4,64,352]{3,2,1,0:T(8,128)(2,1)}, bf16[8,4,64,352]{3,2,1,0:T(8,128)(2,1)}, u32[]{:S(2)}, u32[]{:S(2)}) collective-permute-start(bf16[8,4,64,352]{3,2,1,0:T(8,128)(2,1)} %bitcast_dynamic-update-slice_fusion.8), channel_id=1, source_target_pairs={{0,12},{12,0},{1,13},{13,1},{2,14},{14,2},{3,15},{15,3},{4,16},{16... | collective-permute-start | bytes 4325384 | tf_op jit(solution)/shard_map/ppermute | solution.py:13
  161.4 40.8 %all-to-all-start = ((bf16[64,64,66]{2,0,1:T(8,128)(2,1)}), bf16[64,64,66]{2,0,1:T(8,128)(2,1)}, u32[]{:S(2)}, u32[]{:S(2)}) async-start(bf16[64,64,66]{2,0,1:T(8,128)(2,1)} %copy.13), calls=%async_computation | async-start | bytes 2097152 | tf_op jit(solution)/shard_map/all_to_all | solution.py:89
  207.9 6.5 %collective-permute-start.24 = (bf16[66,352]{1,0:T(8,128)(2,1)S(1)}, bf16[66,352]{1,0:T(8,128)(2,1)S(1)}, u32[]{:S(2)}, u32[]{:S(2)}) collective-permute-start(bf16[66,352]{1,0:T(8,128)(2,1)S(1)} %select_convert_fusion), channel_id=1, source_target_pairs={{0,192},{192,384},{384,576},{576,0},{1,193},{193,385},{385,577},{5... | collective-permute-start | bytes 139400 | tf_op jit(solution)/shard_map/ppermute | solution.py:13
  211.0 5.5 %collective-permute-start.23 = (bf16[66,352]{1,0:T(8,128)(2,1)S(1)}, bf16[66,352]{1,0:T(8,128)(2,1)S(1)}, u32[]{:S(2)}, u32[]{:S(2)}) collective-permute-start(bf16[66,352]{1,0:T(8,128)(2,1)S(1)} %select_convert_fusion), channel_id=1, source_target_pairs={{0,576},{192,0},{384,192},{576,384},{1,577},{193,1},{385,193},{577... | collective-permute-start | bytes 139400 | tf_op jit(solution)/shard_map/ppermute | solution.py:13
  214.4 6.1 %collective-permute-start.25 = (bf16[66,352]{1,0:T(8,128)(2,1)S(1)}, bf16[66,352]{1,0:T(8,128)(2,1)S(1)}, u32[]{:S(2)}, u32[]{:S(2)}) collective-permute-start(bf16[66,352]{1,0:T(8,128)(2,1)S(1)} %collective-permute-done.24), channel_id=1, source_target_pairs={{0,192},{192,384},{384,576},{576,0},{1,193},{193,385},{385,577},{5... | collective-permute-start | bytes 139400 | tf_op jit(solution)/shard_map/ppermute | solution.py:13
  220.6 6.7 %collective-permute-start.26 = (bf16[4,66,352]{2,1,0:T(8,128)(2,1)S(1)}, bf16[4,66,352]{2,1,0:T(8,128)(2,1)S(1)}, u32[]{:S(2)}, u32[]{:S(2)}) collective-permute-start(bf16[4,66,352]{2,1,0:T(8,128)(2,1)S(1)} %pad_maximum_fusion.2), channel_id=1, source_target_pairs={{0,168},{24,0},{48,24},{72,48},{96,72},{120,96},{144,120},{168,144... | collective-permute-start | bytes 557576 | tf_op jit(solution)/shard_map/ppermute | solution.py:13
  222.6 7.9 %collective-permute-start.29 = (bf16[4,66,352]{2,1,0:T(8,128)(2,1)S(1)}, bf16[4,66,352]{2,1,0:T(8,128)(2,1)S(1)}, u32[]{:S(2)}, u32[]{:S(2)}) collective-permute-start(bf16[4,66,352]{2,1,0:T(8,128)(2,1)S(1)} %pad_maximum_fusion.2), channel_id=1, source_target_pairs={{0,24},{24,48},{48,72},{72,96},{96,120},{120,144},{144,168},{168,0... | collective-permute-start | bytes 557576 | tf_op jit(solution)/shard_map/ppermute | solution.py:13
  227.3 7.0 %collective-permute-start.27 = (bf16[4,66,352]{2,1,0:T(8,128)(2,1)S(1)}, bf16[4,66,352]{2,1,0:T(8,128)(2,1)S(1)}, u32[]{:S(2)}, u32[]{:S(2)}) collective-permute-start(bf16[4,66,352]{2,1,0:T(8,128)(2,1)S(1)} %collective-permute-done.26), channel_id=1, source_target_pairs={{0,168},{24,0},{48,24},{72,48},{96,72},{120,96},{144,120},{168,144... | collective-permute-start | bytes 557576 | tf_op jit(solution)/shard_map/ppermute | solution.py:13
  230.5 7.9 %collective-permute-start.30 = (bf16[4,66,352]{2,1,0:T(8,128)(2,1)S(1)}, bf16[4,66,352]{2,1,0:T(8,128)(2,1)S(1)}, u32[]{:S(2)}, u32[]{:S(2)}) collective-permute-start(bf16[4,66,352]{2,1,0:T(8,128)(2,1)S(1)} %collective-permute-done.29), channel_id=1, source_target_pairs={{0,24},{24,48},{48,72},{72,96},{96,120},{120,144},{144,168},{168,0... | collective-permute-start | bytes 557576 | tf_op jit(solution)/shard_map/ppermute | solution.py:13
  234.2 14.0 %collective-permute-start.28 = (bf16[4,66,352]{2,1,0:T(8,128)(2,1)S(1)}, bf16[4,66,352]{2,1,0:T(8,128)(2,1)S(1)}, u32[]{:S(2)}, u32[]{:S(2)}) collective-permute-start(bf16[4,66,352]{2,1,0:T(8,128)(2,1)S(1)} %collective-permute-done.27), channel_id=1, source_target_pairs={{0,168},{24,0},{48,24},{72,48},{96,72},{120,96},{144,120},{168,144... | collective-permute-start | bytes 557576 | tf_op jit(solution)/shard_map/ppermute | solution.py:13
  238.4 7.9 %collective-permute-start.31 = (bf16[4,66,352]{2,1,0:T(8,128)(2,1)S(1)}, bf16[4,66,352]{2,1,0:T(8,128)(2,1)S(1)}, u32[]{:S(2)}, u32[]{:S(2)}) collective-permute-start(bf16[4,66,352]{2,1,0:T(8,128)(2,1)S(1)} %collective-permute-done.30), channel_id=1, source_target_pairs={{0,24},{24,48},{48,72},{72,96},{96,120},{120,144},{144,168},{168,0... | collective-permute-start | bytes 557576 | tf_op jit(solution)/shard_map/ppermute | solution.py:13
  246.3 8.6 %collective-permute-start.32 = (bf16[4,66,352]{2,1,0:T(8,128)(2,1)S(1)}, bf16[4,66,352]{2,1,0:T(8,128)(2,1)S(1)}, u32[]{:S(2)}, u32[]{:S(2)}) collective-permute-start(bf16[4,66,352]{2,1,0:T(8,128)(2,1)S(1)} %collective-permute-done.31), channel_id=1, source_target_pairs={{0,24},{24,48},{48,72},{72,96},{96,120},{120,144},{144,168},{168,0... | collective-permute-start | bytes 557576 | tf_op jit(solution)/shard_map/ppermute | solution.py:13
  255.0 1.2 copy-start.1
  258.0 19.4 %collective-permute-start.33 = (bf16[8,4,66,352]{3,0,2,1:T(8,128)(2,1)}, bf16[8,4,66,352]{3,0,2,1:T(8,128)(2,1)}, u32[]{:S(2)}, u32[]{:S(2)}) collective-permute-start(bf16[8,4,66,352]{3,0,2,1:T(8,128)(2,1)} %copy.15), channel_id=1, source_target_pairs={{0,12},{12,0},{1,13},{13,1},{2,14},{14,2},{3,15},{15,3},{4,16},{16... | collective-permute-start | bytes 4460552 | tf_op jit(solution)/shard_map/ppermute | solution.py:13
  277.4 2.0 copy-start.2

commit v4 on v3

--- a/solution.py
+++ b/solution.py
@@ -38,8 +38,8 @@
 def combine(mean, m2, count, axis, k):
     n = lax.axis_size(axis)
     pairs = [(i, i ^ k) for i in range(n)]
-    other_mean = lax.ppermute(mean, axis, pairs)
-    other_m2 = lax.ppermute(m2, axis, pairs)
+    other = lax.ppermute(jnp.stack([mean, m2]), axis, pairs)
+    other_mean, other_m2 = other[0], other[1]
     delta = other_mean - mean
     new_mean = (mean + other_mean) * 0.5
     new_m2 = (m2 + other_m2) + delta * delta * (count * 0.5)
@@ -87,9 +87,7 @@
     second_full = jnp.transpose(stacked, (1, 0, 2)).reshape(local, n_mp * rows)
     width = second_full.shape[1] // dp_count
     columns = lax.all_to_all(second_full, DP, split_axis=1, concat_axis=0, tiled=True)
-    columns = relative_order(columns.reshape(1, nx, ny, nc, local, width), ("x", "y", "c"))
-    columns = jnp.transpose(columns[0], (2, 1, 0, 3, 4)).reshape(total, width)
-    first_all = dp_ring_gather(first).reshape(total, rows)
+    first_all = lax.all_gather(first, DP, axis=0, tiled=True)
     corr = (
         jnp.einsum("bi,bj->ij", first_all, columns, preferred_element_type=jnp.float32)
         / total

time: 285 us -> 234 us (0.82)
  starting transfers between devices: 146 us -> 82.3 us
  between operations: 0.7 us -> 13.9 us
  waiting for transfers between devices: 69.4 us -> 81.3 us
  local copies, waits for them, and re-layouts: 28.1 us -> 23.7 us
  blocking collectives: 24.6 us -> 21.1 us
  other arithmetic: 6.39 us -> 3.47 us
    ppermute x22 -> x11, starting transfers between devices: 87 us -> 38.1 us  [shift(): return lax.ppermute(v, axis, [(i, (i + step) % n) for i in range(n)])]
    ppermute x12 -> x6, starting transfers between devices: 47.1 us -> 22 us  [combine(): other = lax.ppermute(jnp.stack([mean, m2]), axis, pairs)]
    ppermute x22 -> x11, waiting for transfers between devices: 34.1 us -> 18.1 us  [shift(): return lax.ppermute(v, axis, [(i, (i + step) % n) for i in range(n)])]
    ppermute x12 -> x6, waiting for transfers between devices: 6.98 us -> 19.3 us  [combine(): other = lax.ppermute(jnp.stack([mean, m2]), axis, pairs)]
    all_gather x0 -> x1, waiting for transfers between devices: none -> 11.6 us  [shards(): first_all = lax.all_gather(first, DP, axis=0, tiled=True)]
    all_to_all x1, starting transfers between devices: 12.4 us -> 22.2 us  [shards(): lax.all_to_all(second_full, DP, split_axis=1, concat_axis=0, tiled=True)]
    unnamed x18 -> x12, local copies, waits for them, and re-layouts: 7.67 us -> 3.45 us
    all_to_all x1, waiting for transfers between devices: 28.4 us -> 32.3 us  [shards(): lax.all_to_all(second_full, DP, split_axis=1, concat_axis=0, tiled=True)]
  transfers between devices with their start and end apart: 35 -> 19, of which waited for: 17 -> 13; matrix products, arithmetic and copies ran while one was open for 7% -> 6% of each run, Pallas kernels for 0% -> 0%
where the time goes in v4:
time: 234 us; the launch traced here: 233 us
  starting transfers between devices  82.3 us (35%)
  waiting for transfers between devices  81.3 us (35%)
  local copies, waits for them, and re-layouts  23.7 us (10%)
  blocking collectives  21.1 us (9%)
  between operations  13.9 us (6%)
  matrix products  7.57 us (3%)
  other arithmetic  3.47 us (1%)
    ppermute x11, starting transfers between devices, shift(): return lax.ppermute(v, axis, [(i, (i + step) % n) for i in range(n)])  38.1 us
    all_to_all x1, waiting for transfers between devices, shards(): lax.all_to_all(second_full, DP, split_axis=1, concat_axis=0, tiled=True)  32.3 us
    all_to_all x1, starting transfers between devices, shards(): lax.all_to_all(second_full, DP, split_axis=1, concat_axis=0, tiled=True)  22.2 us
    ppermute x6, starting transfers between devices, combine(): other = lax.ppermute(jnp.stack([mean, m2]), axis, pairs)  22 us
    all_gather x1, blocking collectives, shards(): stacked = lax.all_gather(second, 'mp', axis=0)  21.1 us
    ppermute x6, waiting for transfers between devices, combine(): other = lax.ppermute(jnp.stack([mean, m2]), axis, pairs)  19.3 us
    ppermute x11, waiting for transfers between devices, shift(): return lax.ppermute(v, axis, [(i, (i + step) % n) for i in range(n)])  18.1 us
    all_gather x1, waiting for transfers between devices, shards(): first_all = lax.all_gather(first, DP, axis=0, tiled=True)  11.6 us
  transfers between devices with their start and end apart: 19, of which 13 were waited for; matrix products, arithmetic and copies ran while one was open for 6% of the time, Pallas kernels for 0%

profile of v4, /device:TPU:1, one launch (start us, length us, event | category | flops | bytes accessed | tf_op | source)
XLA Modules:
  0.0 233.3 jit_solution(2269352993274979161)
XLA Ops:
  6.5 0.0 copy-start
  6.5 0.0 all-gather.3.cloned.1.call-start
  6.5 1.8 copy-done
  8.4 2.3 fusion.74
  10.8 12.4 %collective-permute-start = (f32[2,2,1,352]{3,1,2,0:T(2,128)S(1)}, f32[2,2,1,352]{3,1,2,0:T(2,128)S(1)}, u32[]{:S(2)}, u32[]{:S(2)}) collective-permute-start(f32[2,2,1,352]{3,1,2,0:T(2,128)S(1)} %pad_maximum_fusion.3), channel_id=1, source_target_pairs={{0,12},{12,0},{1,13},{13,1},{2,14},{14,2},{3,15},{15,3},{4,16},{16... | collective-permute-start | bytes 16904 | tf_op jit(solution)/shard_map/ppermute | solution.py:41
  23.2 0.8 collective-permute-done
  24.0 1.9 collective-permute-start.1
  26.0 2.4 %collective-permute-done.1 = f32[2,2,1,352]{3,1,2,0:T(2,128)S(1)} collective-permute-done((f32[2,2,1,352]{3,1,2,0:T(2,128)S(1)}, f32[2,2,1,352]{3,1,2,0:T(2,128)S(1)}, u32[]{:S(2)}, u32[]{:S(2)}) %collective-permute-start.1) | collective-permute-done | bytes 5664 | tf_op jit(solution)/shard_map/ppermute | solution.py:41
  28.4 1.9 collective-permute-start.2
  30.4 3.3 %collective-permute-done.2 = f32[2,2,1,352]{3,1,2,0:T(2,128)S(1)} collective-permute-done((f32[2,2,1,352]{3,1,2,0:T(2,128)S(1)}, f32[2,2,1,352]{3,1,2,0:T(2,128)S(1)}, u32[]{:S(2)}, u32[]{:S(2)}) %collective-permute-start.2) | collective-permute-done | bytes 5664 | tf_op jit(solution)/shard_map/ppermute | solution.py:41
  33.7 1.9 collective-permute-start.3
  35.7 6.4 %collective-permute-done.3 = f32[2,2,1,352]{3,1,2,0:T(2,128)S(1)} collective-permute-done((f32[2,2,1,352]{3,1,2,0:T(2,128)S(1)}, f32[2,2,1,352]{3,1,2,0:T(2,128)S(1)}, u32[]{:S(2)}, u32[]{:S(2)}) %collective-permute-start.3) | collective-permute-done | bytes 5664 | tf_op jit(solution)/shard_map/ppermute | solution.py:41
  42.0 1.9 collective-permute-start.4
  44.0 2.4 %collective-permute-done.4 = f32[2,2,1,352]{3,1,2,0:T(2,128)S(1)} collective-permute-done((f32[2,2,1,352]{3,1,2,0:T(2,128)S(1)}, f32[2,2,1,352]{3,1,2,0:T(2,128)S(1)}, u32[]{:S(2)}, u32[]{:S(2)}) %collective-permute-start.4) | collective-permute-done | bytes 5664 | tf_op jit(solution)/shard_map/ppermute | solution.py:41
  46.4 1.9 collective-permute-start.5
  48.4 3.9 %collective-permute-done.5 = f32[2,2,1,352]{3,1,2,0:T(2,128)S(1)} collective-permute-done((f32[2,2,1,352]{3,1,2,0:T(2,128)S(1)}, f32[2,2,1,352]{3,1,2,0:T(2,128)S(1)}, u32[]{:S(2)}, u32[]{:S(2)}) %collective-permute-start.5) | collective-permute-done | bytes 5664 | tf_op jit(solution)/shard_map/ppermute | solution.py:41
  52.4 0.6 fusion.73
  53.0 0.0 all-gather.3.cloned.1.call-update
  53.1 21.1 %all_gather.6 = bf16[12,64,352]{2,1,0:T(8,128)(2,1)S(1)} all-gather(bf16[1,64,352]{2,1,0:T(8,128)(2,1)S(1)} %get-tuple-element.12), channel_id=1, replica_groups=mesh['x'=4,'y'=8,'c'=2,'mp'=12] {'mp'}, dimensions={0}, use_global_device_ids=true | all-gather | bytes 585728 | tf_op jit(solution)/shard_map/all_gather | solution.py:86
  74.2 1.2 copy.8
  75.4 4.0 %all_to_all.14 = bf16[64,64,66]{2,1,0:T(8,128)(2,1)} reshape(bf16[64,12,352]{2,1,0:T(8,128)(2,1)} %copy.8) | data formatting | bytes 1081344 | tf_op jit(solution)/shard_map/all_to_all | solution.py:89
  79.4 2.9 %copy.12 = bf16[64,64,66]{2,0,1:T(8,128)(2,1)} copy(bf16[64,64,66]{2,1,0:T(8,128)(2,1)} %all_to_all.14) | data formatting | bytes 1081344 | tf_op jit(solution)/shard_map/all_to_all | solution.py:89
  82.2 22.2 %all-to-all-start = ((bf16[64,64,66]{2,0,1:T(8,128)(2,1)}), bf16[64,64,66]{2,0,1:T(8,128)(2,1)}, u32[]{:S(2)}, u32[]{:S(2)}) async-start(bf16[64,64,66]{2,0,1:T(8,128)(2,1)} %copy.12), calls=%async_computation | async-start | bytes 2097152 | tf_op jit(solution)/shard_map/all_to_all | solution.py:89
  104.5 32.3 %all-to-all-done = bf16[64,64,66]{2,0,1:T(8,128)(2,1)} async-done(((bf16[64,64,66]{2,0,1:T(8,128)(2,1)}), bf16[64,64,66]{2,0,1:T(8,128)(2,1)}, u32[]{:S(2)}, u32[]{:S(2)}) %all-to-all-start) | async-done | bytes 540704 | tf_op jit(solution)/shard_map/all_to_all | solution.py:89
  136.8 11.6 %all-gather.3.cloned.1.call-done = bf16[1,4096,352]{2,1,0:T(8,128)(2,1)} async-done(((bf16[1,64,352]{2,1,0:T(8,128)(2,1)}), bf16[1,4096,352]{2,1,0:T(8,128)(2,1)}) %all-gather.3.cloned.1.call-update) | async-done | bytes 2883600 | tf_op jit(solution)/shard_map/all_gather | solution.py:90
  148.3 2.9 %select_convert_fusion = bf16[66,352]{1,0:T(8,128)(2,1)S(1)} fusion(bf16[4096,66]{1,0:T(8,128)(2,1)} %bitcast.18, bf16[1,4096,352]{2,1,0:T(8,128)(2,1)} %all-gather.3.cloned.1.call-done, s32[352]{0:T(512)S(1)} %iota_add_fusion.1, s32[66]{0:T(128)S(1)} %iota_add_fusion.2), kind=kOutput, calls=%fused_computation.35 | convolution fusion | flops 190479168 | bytes 3472392 | tf_op jit(solution)/shard_map/bi,bj->ij/dot_general | solution.py:92
  151.2 3.0 %collective-permute-start.7 = (bf16[66,352]{1,0:T(8,128)(2,1)S(1)}, bf16[66,352]{1,0:T(8,128)(2,1)S(1)}, u32[]{:S(2)}, u32[]{:S(2)}) collective-permute-start(bf16[66,352]{1,0:T(8,128)(2,1)S(1)} %select_convert_fusion), channel_id=1, source_target_pairs={{0,192},{192,384},{384,576},{576,0},{1,193},{193,385},{385,577},{5... | collective-permute-start | bytes 139400 | tf_op jit(solution)/shard_map/ppermute | solution.py:13
  154.2 3.5 %collective-permute-start.6 = (bf16[66,352]{1,0:T(8,128)(2,1)S(1)}, bf16[66,352]{1,0:T(8,128)(2,1)S(1)}, u32[]{:S(2)}, u32[]{:S(2)}) collective-permute-start(bf16[66,352]{1,0:T(8,128)(2,1)S(1)} %select_convert_fusion), channel_id=1, source_target_pairs={{0,576},{192,0},{384,192},{576,384},{1,577},{193,1},{385,193},{577... | collective-permute-start | bytes 139400 | tf_op jit(solution)/shard_map/ppermute | solution.py:13
  157.8 0.0 collective-permute-done.7
  157.8 1.9 collective-permute-start.8
  159.7 0.1 add_multiply_fusion.1
  159.8 0.0 collective-permute-done.6
  159.8 4.1 %collective-permute-done.8 = bf16[66,352]{1,0:T(8,128)(2,1)S(1)} collective-permute-done((bf16[66,352]{1,0:T(8,128)(2,1)S(1)}, bf16[66,352]{1,0:T(8,128)(2,1)S(1)}, u32[]{:S(2)}, u32[]{:S(2)}) %collective-permute-start.8) | collective-permute-done | bytes 46496 | tf_op jit(solution)/shard_map/ppermute | solution.py:13
  163.9 0.1 pad_maximum_fusion.2
  163.9 3.4 %collective-permute-start.9 = (bf16[4,66,352]{2,1,0:T(8,128)(2,1)S(1)}, bf16[4,66,352]{2,1,0:T(8,128)(2,1)S(1)}, u32[]{:S(2)}, u32[]{:S(2)}) collective-permute-start(bf16[4,66,352]{2,1,0:T(8,128)(2,1)S(1)} %pad_maximum_fusion.2), channel_id=1, source_target_pairs={{0,168},{24,0},{48,24},{72,48},{96,72},{120,96},{144,120},{168,144... | collective-permute-start | bytes 557576 | tf_op jit(solution)/shard_map/ppermute | solution.py:13
  167.3 1.9 collective-permute-start.12
  169.3 1.3 collective-permute-done.9
  170.6 4.6 %collective-permute-start.10 = (bf16[4,66,352]{2,1,0:T(8,128)(2,1)S(1)}, bf16[4,66,352]{2,1,0:T(8,128)(2,1)S(1)}, u32[]{:S(2)}, u32[]{:S(2)}) collective-permute-start(bf16[4,66,352]{2,1,0:T(8,128)(2,1)S(1)} %collective-permute-done.9), channel_id=1, source_target_pairs={{0,168},{24,0},{48,24},{72,48},{96,72},{120,96},{144,120},{168,144... | collective-permute-start | bytes 557576 | tf_op jit(solution)/shard_map/ppermute | solution.py:13
  175.2 0.0 collective-permute-done.12
  175.2 1.9 collective-permute-start.13
  177.2 0.9 collective-permute-done.10
  178.1 5.0 %collective-permute-start.11 = (bf16[4,66,352]{2,1,0:T(8,128)(2,1)S(1)}, bf16[4,66,352]{2,1,0:T(8,128)(2,1)S(1)}, u32[]{:S(2)}, u32[]{:S(2)}) collective-permute-start(bf16[4,66,352]{2,1,0:T(8,128)(2,1)S(1)} %collective-permute-done.10), channel_id=1, source_target_pairs={{0,168},{24,0},{48,24},{72,48},{96,72},{120,96},{144,120},{168,144... | collective-permute-start | bytes 557576 | tf_op jit(solution)/shard_map/ppermute | solution.py:13
  183.1 0.0 collective-permute-done.13
  183.1 1.9 collective-permute-start.14
  185.1 5.9 %collective-permute-done.14 = bf16[4,66,352]{2,1,0:T(8,128)(2,1)S(1)} collective-permute-done((bf16[4,66,352]{2,1,0:T(8,128)(2,1)S(1)}, bf16[4,66,352]{2,1,0:T(8,128)(2,1)S(1)}, u32[]{:S(2)}, u32[]{:S(2)}) %collective-permute-start.14) | collective-permute-done | bytes 185888 | tf_op jit(solution)/shard_map/ppermute | solution.py:13
  191.0 1.9 collective-permute-start.15
  192.9 0.0 collective-permute-done.11
  192.9 5.9 %collective-permute-done.15 = bf16[4,66,352]{2,1,0:T(8,128)(2,1)S(1)} collective-permute-done((bf16[4,66,352]{2,1,0:T(8,128)(2,1)S(1)}, bf16[4,66,352]{2,1,0:T(8,128)(2,1)S(1)}, u32[]{:S(2)}, u32[]{:S(2)}) %collective-permute-start.15) | collective-permute-done | bytes 185888 | tf_op jit(solution)/shard_map/ppermute | solution.py:13
  199.0 0.0 copy-start.1
  199.0 1.2 copy-done.1
  200.3 1.7 copy.14
  202.0 9.1 %collective-permute-start.16 = (bf16[8,4,66,352]{3,0,2,1:T(8,128)(2,1)}, bf16[8,4,66,352]{3,0,2,1:T(8,128)(2,1)}, u32[]{:S(2)}, u32[]{:S(2)}) collective-permute-start(bf16[8,4,66,352]{3,0,2,1:T(8,128)(2,1)} %copy.14), channel_id=1, source_target_pairs={{0,12},{12,0},{1,13},{13,1},{2,14},{14,2},{3,15},{15,3},{4,16},{16... | collective-permute-start | bytes 4460552 | tf_op jit(solution)/shard_map/ppermute | solution.py:13
  211.0 0.1 add_multiply_fusion
  211.1 0.1 iota_add_fusion
  211.2 6.1 %reshape_reshape.3 = bf16[64,4,8,2,66]{4,3,2,1,0:T(2,128)(2,1)} reshape(bf16[64,12,352]{2,1,0:T(8,128)(2,1)} %copy.8) | data formatting | bytes 1081344 | tf_op jit(solution)/shard_map/reshape;reshape | solution.py:115
  217.3 1.9 copy.9
  219.3 0.5 fusion.13
  219.8 0.5 fusion.12
  220.3 0.0 copy-start.2
  220.4 0.0 collective-permute-done.16
  220.4 1.8 copy.19
  222.2 0.2 copy-done.2
  222.3 1.8 fusion
  224.1 2.4 %fusion.8 = bf16[64,352]{1,0:T(8,128)(2,1)} fusion(s32[]{:T(128)S(6)} %select_n.78, bf16[64,4,8,2,66]{4,0,1,2,3:T(8,128)(2,1)S(1)} %fusion.12, bf16[1,8,4,66,352]{4,3,2,1,0:T(8,128)(2,1)S(1)} %bitcast.302, bf16[1,8,4,66,352]{4,3,2,1,0:T(8,128)(2,1)S(1)} %bitcast.300, f32[352]{0:T(512)S(1)} %rsqrt_reduce_fusion, f32[352]{0:T(512)S(1)} %multiply_add_fusion.5, ...), kind=kOutput, calls=%fused_computation.19 | convolution fusion | flops 192186368 | bytes 3607300 | tf_op jit(solution)/shard_map/dot_general | solution.py:117
  (34 shorter events, 0.6 us)
Async XLA Ops:
  6.5 1.8 copy-start
  6.5 141.8 %all-gather.3.cloned.1.call-start = ((), (), s32[]{:S(2)}) async-start(), calls=%async_computation.1 | async-start | bytes 3194880 | tf_op jit(solution)/shard_map/all_gather | solution.py:90
  10.8 13.2 %collective-permute-start = (f32[2,2,1,352]{3,1,2,0:T(2,128)S(1)}, f32[2,2,1,352]{3,1,2,0:T(2,128)S(1)}, u32[]{:S(2)}, u32[]{:S(2)}) collective-permute-start(f32[2,2,1,352]{3,1,2,0:T(2,128)S(1)} %pad_maximum_fusion.3), channel_id=1, source_target_pairs={{0,12},{12,0},{1,13},{13,1},{2,14},{14,2},{3,15},{15,3},{4,16},{16... | collective-permute-start | bytes 16904 | tf_op jit(solution)/shard_map/ppermute | solution.py:41
  24.0 4.4 %collective-permute-start.1 = (f32[2,2,1,352]{3,1,2,0:T(2,128)S(1)}, f32[2,2,1,352]{3,1,2,0:T(2,128)S(1)}, u32[]{:S(2)}, u32[]{:S(2)}) collective-permute-start(f32[2,2,1,352]{3,1,2,0:T(2,128)S(1)} %pad_maximum_fusion.4), channel_id=1, source_target_pairs={{0,24},{24,0},{48,72},{72,48},{96,120},{120,96},{144,168},{168,144... | collective-permute-start | bytes 16904 | tf_op jit(solution)/shard_map/ppermute | solution.py:41
  28.4 5.3 %collective-permute-start.2 = (f32[2,2,1,352]{3,1,2,0:T(2,128)S(1)}, f32[2,2,1,352]{3,1,2,0:T(2,128)S(1)}, u32[]{:S(2)}, u32[]{:S(2)}) collective-permute-start(f32[2,2,1,352]{3,1,2,0:T(2,128)S(1)} %pad_maximum_fusion.5), channel_id=1, source_target_pairs={{0,48},{24,72},{48,0},{72,24},{96,144},{120,168},{144,96},{168,120... | collective-permute-start | bytes 16904 | tf_op jit(solution)/shard_map/ppermute | solution.py:41
  33.7 8.3 %collective-permute-start.3 = (f32[2,2,1,352]{3,1,2,0:T(2,128)S(1)}, f32[2,2,1,352]{3,1,2,0:T(2,128)S(1)}, u32[]{:S(2)}, u32[]{:S(2)}) collective-permute-start(f32[2,2,1,352]{3,1,2,0:T(2,128)S(1)} %pad_maximum_fusion.6), channel_id=1, source_target_pairs={{0,96},{24,120},{48,144},{72,168},{96,0},{120,24},{144,48},{168,72... | collective-permute-start | bytes 16904 | tf_op jit(solution)/shard_map/ppermute | solution.py:41
  42.0 4.4 %collective-permute-start.4 = (f32[2,2,1,352]{3,1,2,0:T(2,128)S(1)}, f32[2,2,1,352]{3,1,2,0:T(2,128)S(1)}, u32[]{:S(2)}, u32[]{:S(2)}) collective-permute-start(f32[2,2,1,352]{3,1,2,0:T(2,128)S(1)} %pad_maximum_fusion.7), channel_id=1, source_target_pairs={{0,192},{192,0},{384,576},{576,384},{1,193},{193,1},{385,577},{577... | collective-permute-start | bytes 16904 | tf_op jit(solution)/shard_map/ppermute | solution.py:41
  46.4 5.9 %collective-permute-start.5 = (f32[2,2,1,352]{3,1,2,0:T(2,128)S(1)}, f32[2,2,1,352]{3,1,2,0:T(2,128)S(1)}, u32[]{:S(2)}, u32[]{:S(2)}) collective-permute-start(f32[2,2,1,352]{3,1,2,0:T(2,128)S(1)} %pad_maximum_fusion.8), channel_id=1, source_target_pairs={{0,384},{192,576},{384,0},{576,192},{1,385},{193,577},{385,1},{577... | collective-permute-start | bytes 16904 | tf_op jit(solution)/shard_map/ppermute | solution.py:41
  82.2 54.5 %all-to-all-start = ((bf16[64,64,66]{2,0,1:T(8,128)(2,1)}), bf16[64,64,66]{2,0,1:T(8,128)(2,1)}, u32[]{:S(2)}, u32[]{:S(2)}) async-start(bf16[64,64,66]{2,0,1:T(8,128)(2,1)} %copy.12), calls=%async_computation | async-start | bytes 2097152 | tf_op jit(solution)/shard_map/all_to_all | solution.py:89
  151.2 6.5 %collective-permute-start.7 = (bf16[66,352]{1,0:T(8,128)(2,1)S(1)}, bf16[66,352]{1,0:T(8,128)(2,1)S(1)}, u32[]{:S(2)}, u32[]{:S(2)}) collective-permute-start(bf16[66,352]{1,0:T(8,128)(2,1)S(1)} %select_convert_fusion), channel_id=1, source_target_pairs={{0,192},{192,384},{384,576},{576,0},{1,193},{193,385},{385,577},{5... | collective-permute-start | bytes 139400 | tf_op jit(solution)/shard_map/ppermute | solution.py:13
  154.2 5.6 %collective-permute-start.6 = (bf16[66,352]{1,0:T(8,128)(2,1)S(1)}, bf16[66,352]{1,0:T(8,128)(2,1)S(1)}, u32[]{:S(2)}, u32[]{:S(2)}) collective-permute-start(bf16[66,352]{1,0:T(8,128)(2,1)S(1)} %select_convert_fusion), channel_id=1, source_target_pairs={{0,576},{192,0},{384,192},{576,384},{1,577},{193,1},{385,193},{577... | collective-permute-start | bytes 139400 | tf_op jit(solution)/shard_map/ppermute | solution.py:13
  157.8 6.1 %collective-permute-start.8 = (bf16[66,352]{1,0:T(8,128)(2,1)S(1)}, bf16[66,352]{1,0:T(8,128)(2,1)S(1)}, u32[]{:S(2)}, u32[]{:S(2)}) collective-permute-start(bf16[66,352]{1,0:T(8,128)(2,1)S(1)} %collective-permute-done.7), channel_id=1, source_target_pairs={{0,192},{192,384},{384,576},{576,0},{1,193},{193,385},{385,577},{5... | collective-permute-start | bytes 139400 | tf_op jit(solution)/shard_map/ppermute | solution.py:13
  163.9 6.7 %collective-permute-start.9 = (bf16[4,66,352]{2,1,0:T(8,128)(2,1)S(1)}, bf16[4,66,352]{2,1,0:T(8,128)(2,1)S(1)}, u32[]{:S(2)}, u32[]{:S(2)}) collective-permute-start(bf16[4,66,352]{2,1,0:T(8,128)(2,1)S(1)} %pad_maximum_fusion.2), channel_id=1, source_target_pairs={{0,168},{24,0},{48,24},{72,48},{96,72},{120,96},{144,120},{168,144... | collective-permute-start | bytes 557576 | tf_op jit(solution)/shard_map/ppermute | solution.py:13
  167.3 7.9 %collective-permute-start.12 = (bf16[4,66,352]{2,1,0:T(8,128)(2,1)S(1)}, bf16[4,66,352]{2,1,0:T(8,128)(2,1)S(1)}, u32[]{:S(2)}, u32[]{:S(2)}) collective-permute-start(bf16[4,66,352]{2,1,0:T(8,128)(2,1)S(1)} %pad_maximum_fusion.2), channel_id=1, source_target_pairs={{0,24},{24,48},{48,72},{72,96},{96,120},{120,144},{144,168},{168,0... | collective-permute-start | bytes 557576 | tf_op jit(solution)/shard_map/ppermute | solution.py:13
  170.6 7.4 %collective-permute-start.10 = (bf16[4,66,352]{2,1,0:T(8,128)(2,1)S(1)}, bf16[4,66,352]{2,1,0:T(8,128)(2,1)S(1)}, u32[]{:S(2)}, u32[]{:S(2)}) collective-permute-start(bf16[4,66,352]{2,1,0:T(8,128)(2,1)S(1)} %collective-permute-done.9), channel_id=1, source_target_pairs={{0,168},{24,0},{48,24},{72,48},{96,72},{120,96},{144,120},{168,144... | collective-permute-start | bytes 557576 | tf_op jit(solution)/shard_map/ppermute | solution.py:13
  175.2 7.9 %collective-permute-start.13 = (bf16[4,66,352]{2,1,0:T(8,128)(2,1)S(1)}, bf16[4,66,352]{2,1,0:T(8,128)(2,1)S(1)}, u32[]{:S(2)}, u32[]{:S(2)}) collective-permute-start(bf16[4,66,352]{2,1,0:T(8,128)(2,1)S(1)} %collective-permute-done.12), channel_id=1, source_target_pairs={{0,24},{24,48},{48,72},{72,96},{96,120},{120,144},{144,168},{168,0... | collective-permute-start | bytes 557576 | tf_op jit(solution)/shard_map/ppermute | solution.py:13
  178.1 14.8 %collective-permute-start.11 = (bf16[4,66,352]{2,1,0:T(8,128)(2,1)S(1)}, bf16[4,66,352]{2,1,0:T(8,128)(2,1)S(1)}, u32[]{:S(2)}, u32[]{:S(2)}) collective-permute-start(bf16[4,66,352]{2,1,0:T(8,128)(2,1)S(1)} %collective-permute-done.10), channel_id=1, source_target_pairs={{0,168},{24,0},{48,24},{72,48},{96,72},{120,96},{144,120},{168,144... | collective-permute-start | bytes 557576 | tf_op jit(solution)/shard_map/ppermute | solution.py:13
  183.1 7.9 %collective-permute-start.14 = (bf16[4,66,352]{2,1,0:T(8,128)(2,1)S(1)}, bf16[4,66,352]{2,1,0:T(8,128)(2,1)S(1)}, u32[]{:S(2)}, u32[]{:S(2)}) collective-permute-start(bf16[4,66,352]{2,1,0:T(8,128)(2,1)S(1)} %collective-permute-done.13), channel_id=1, source_target_pairs={{0,24},{24,48},{48,72},{72,96},{96,120},{120,144},{144,168},{168,0... | collective-permute-start | bytes 557576 | tf_op jit(solution)/shard_map/ppermute | solution.py:13
  191.0 7.9 %collective-permute-start.15 = (bf16[4,66,352]{2,1,0:T(8,128)(2,1)S(1)}, bf16[4,66,352]{2,1,0:T(8,128)(2,1)S(1)}, u32[]{:S(2)}, u32[]{:S(2)}) collective-permute-start(bf16[4,66,352]{2,1,0:T(8,128)(2,1)S(1)} %collective-permute-done.14), channel_id=1, source_target_pairs={{0,24},{24,48},{48,72},{72,96},{96,120},{120,144},{144,168},{168,0... | collective-permute-start | bytes 557576 | tf_op jit(solution)/shard_map/ppermute | solution.py:13
  199.0 1.2 copy-start.1
  202.0 18.4 %collective-permute-start.16 = (bf16[8,4,66,352]{3,0,2,1:T(8,128)(2,1)}, bf16[8,4,66,352]{3,0,2,1:T(8,128)(2,1)}, u32[]{:S(2)}, u32[]{:S(2)}) collective-permute-start(bf16[8,4,66,352]{3,0,2,1:T(8,128)(2,1)} %copy.14), channel_id=1, source_target_pairs={{0,12},{12,0},{1,13},{13,1},{2,14},{14,2},{3,15},{15,3},{4,16},{16... | collective-permute-start | bytes 4460552 | tf_op jit(solution)/shard_map/ppermute | solution.py:13
  220.3 2.0 copy-start.2
Sparse Core Ops, SparseCore 0:
  53.2 95.1 all-gather.2

commit v5 on v4

--- a/solution.py
+++ b/solution.py
@@ -87,7 +87,8 @@
     second_full = jnp.transpose(stacked, (1, 0, 2)).reshape(local, n_mp * rows)
     width = second_full.shape[1] // dp_count
     columns = lax.all_to_all(second_full, DP, split_axis=1, concat_axis=0, tiled=True)
-    first_all = lax.all_gather(first, DP, axis=0, tiled=True)
+    half = rows // 2
+    first_all = jnp.concatenate([lax.all_gather(first[:, :half], DP, axis=0, tiled=True), lax.all_gather(first[:, half:], DP, axis=0, tiled=True)], axis=1)
     corr = (
         jnp.einsum("bi,bj->ij", first_all, columns, preferred_element_type=jnp.float32)
         / total

time: 234 us -> 323 us (1.38)
  waiting for transfers between devices: 81.3 us -> 169 us
    all_gather x1 -> x2, waiting for transfers between devices: 11.6 us -> 99.6 us  [the longest x1 89.8 us: shards(): lax.all_gather(first[:, half:], DP, axis=0, tiled=True)]
  transfers between devices with their start and end apart: 19 -> 20, of which waited for: 13 -> 14; matrix products, arithmetic and copies ran while one was open for 6% -> 4% of each run, Pallas kernels for 0% -> 0%
where the time goes in v5:
time: 323 us; the launch traced here: 322 us
  waiting for transfers between devices  169 us (52%)
  starting transfers between devices  82.5 us (26%)
  local copies, waits for them, and re-layouts  23.8 us (7%)
  blocking collectives  21.1 us (7%)
  between operations  13.9 us (4%)
  matrix products  8.64 us (3%)
  other arithmetic  3.47 us (1%)
    all_gather x1, waiting for transfers between devices, shards(): lax.all_gather(first[:, half:], DP, axis=0, tiled=True)  89.8 us
    ppermute x11, starting transfers between devices, shift(): return lax.ppermute(v, axis, [(i, (i + step) % n) for i in range(n)])  38.2 us
    all_to_all x1, waiting for transfers between devices, shards(): lax.all_to_all(second_full, DP, split_axis=1, concat_axis=0, tiled=True)  31.2 us
    all_to_all x1, starting transfers between devices, shards(): lax.all_to_all(second_full, DP, split_axis=1, concat_axis=0, tiled=True)  22.2 us
    ppermute x6, starting transfers between devices, combine(): other = lax.ppermute(jnp.stack([mean, m2]), axis, pairs)  22 us
    all_gather x1, blocking collectives, shards(): stacked = lax.all_gather(second, 'mp', axis=0)  21.1 us
    ppermute x6, waiting for transfers between devices, combine(): other = lax.ppermute(jnp.stack([mean, m2]), axis, pairs)  19.3 us
    ppermute x11, waiting for transfers between devices, shift(): return lax.ppermute(v, axis, [(i, (i + step) % n) for i in range(n)])  18.1 us
  transfers between devices with their start and end apart: 20, of which 14 were waited for; matrix products, arithmetic and copies ran while one was open for 4% of the time, Pallas kernels for 0%

profile of v5, /device:TPU:1, one launch (start us, length us, event | category | flops | bytes accessed | tf_op | source)
XLA Modules:
  0.0 322.3 jit_solution(5564080142970709808)
XLA Ops:
  6.5 0.0 all-gather.3.cloned.1.call-start
  6.5 1.8 copy-done
  8.4 2.3 fusion.77
  10.8 12.4 %collective-permute-start = (f32[2,2,1,352]{3,1,2,0:T(2,128)S(1)}, f32[2,2,1,352]{3,1,2,0:T(2,128)S(1)}, u32[]{:S(2)}, u32[]{:S(2)}) collective-permute-start(f32[2,2,1,352]{3,1,2,0:T(2,128)S(1)} %pad_maximum_fusion.3), channel_id=1, source_target_pairs={{0,12},{12,0},{1,13},{13,1},{2,14},{14,2},{3,15},{15,3},{4,16},{16... | collective-permute-start | bytes 16904 | tf_op jit(solution)/shard_map/ppermute | solution.py:41
  23.2 0.8 collective-permute-done
  24.0 1.9 collective-permute-start.1
  26.0 2.4 collective-permute-done.1
  28.4 1.9 collective-permute-start.2
  30.4 3.3 %collective-permute-done.2 = f32[2,2,1,352]{3,1,2,0:T(2,128)S(1)} collective-permute-done((f32[2,2,1,352]{3,1,2,0:T(2,128)S(1)}, f32[2,2,1,352]{3,1,2,0:T(2,128)S(1)}, u32[]{:S(2)}, u32[]{:S(2)}) %collective-permute-start.2) | collective-permute-done | bytes 5664 | tf_op jit(solution)/shard_map/ppermute | solution.py:41
  33.7 1.9 collective-permute-start.3
  35.7 6.4 %collective-permute-done.3 = f32[2,2,1,352]{3,1,2,0:T(2,128)S(1)} collective-permute-done((f32[2,2,1,352]{3,1,2,0:T(2,128)S(1)}, f32[2,2,1,352]{3,1,2,0:T(2,128)S(1)}, u32[]{:S(2)}, u32[]{:S(2)}) %collective-permute-start.3) | collective-permute-done | bytes 5664 | tf_op jit(solution)/shard_map/ppermute | solution.py:41
  42.0 1.9 collective-permute-start.4
  44.0 2.4 collective-permute-done.4
  46.4 1.9 collective-permute-start.5
  48.4 3.9 %collective-permute-done.5 = f32[2,2,1,352]{3,1,2,0:T(2,128)S(1)} collective-permute-done((f32[2,2,1,352]{3,1,2,0:T(2,128)S(1)}, f32[2,2,1,352]{3,1,2,0:T(2,128)S(1)}, u32[]{:S(2)}, u32[]{:S(2)}) %collective-permute-start.5) | collective-permute-done | bytes 5664 | tf_op jit(solution)/shard_map/ppermute | solution.py:41
  52.4 0.7 fusion.76
  53.1 0.0 all-gather.3.cloned.1.call-update
  53.1 0.0 all-gather.5.cloned.1.call-start
  53.2 0.7 all-gather.5.cloned.1.call-update
  53.9 21.1 %all_gather.9 = bf16[12,64,352]{2,1,0:T(8,128)(2,1)S(1)} all-gather(bf16[1,64,352]{2,1,0:T(8,128)(2,1)S(1)} %get-tuple-element.12), channel_id=1, replica_groups=mesh['x'=4,'y'=8,'c'=2,'mp'=12] {'mp'}, dimensions={0}, use_global_device_ids=true | all-gather | bytes 585728 | tf_op jit(solution)/shard_map/all_gather | solution.py:86
  75.0 1.3 copy.8
  76.2 4.0 %all_to_all.14 = bf16[64,64,66]{2,1,0:T(8,128)(2,1)} reshape(bf16[64,12,352]{2,1,0:T(8,128)(2,1)} %copy.8) | data formatting | bytes 1081344 | tf_op jit(solution)/shard_map/all_to_all | solution.py:89
  80.2 2.9 copy.12
  83.1 22.2 %all-to-all-start = ((bf16[64,64,66]{2,0,1:T(8,128)(2,1)}), bf16[64,64,66]{2,0,1:T(8,128)(2,1)}, u32[]{:S(2)}, u32[]{:S(2)}) async-start(bf16[64,64,66]{2,0,1:T(8,128)(2,1)} %copy.12), calls=%async_computation | async-start | bytes 2097152 | tf_op jit(solution)/shard_map/all_to_all | solution.py:89
  105.4 31.2 %all-to-all-done = bf16[64,64,66]{2,0,1:T(8,128)(2,1)} async-done(((bf16[64,64,66]{2,0,1:T(8,128)(2,1)}), bf16[64,64,66]{2,0,1:T(8,128)(2,1)}, u32[]{:S(2)}, u32[]{:S(2)}) %all-to-all-start) | async-done | bytes 540704 | tf_op jit(solution)/shard_map/all_to_all | solution.py:89
  136.6 9.8 %all-gather.3.cloned.1.call-done = bf16[4096,176]{1,0:T(8,128)(2,1)} async-done(((bf16[64,176]{1,0:T(8,128)(2,1)}), bf16[4096,176]{1,0:T(8,128)(2,1)}) %all-gather.3.cloned.1.call-update) | async-done | bytes 1441808 | tf_op jit(solution)/shard_map/all_gather | solution.py:91
  146.4 89.8 %all-gather.5.cloned.1.call-done = bf16[4096,176]{1,0:T(8,128)(2,1)} async-done(((bf16[64,176]{1,0:T(8,128)(2,1)}), bf16[4096,176]{1,0:T(8,128)(2,1)}) %all-gather.5.cloned.1.call-update) | async-done | bytes 1441808 | tf_op jit(solution)/shard_map/all_gather | solution.py:91
  236.2 4.0 %select_convert_fusion = bf16[66,352]{1,0:T(8,128)(2,1)S(1)} fusion(bf16[4096,66]{1,0:T(8,128)(2,1)} %bitcast.18, bf16[4096,176]{1,0:T(8,128)(2,1)} %all-gather.5.cloned.1.call-done, bf16[4096,176]{1,0:T(8,128)(2,1)} %all-gather.3.cloned.1.call-done, s32[352]{0:T(512)S(1)} %iota_add_fusion.1, s32[66]{0:T(128)S(1)} %iota_add_fusion.2), kind=kOutput, calls=%fused_computation.37 | convolution fusion | flops 196246336 | bytes 3472392 | tf_op jit(solution)/shard_map/bi,bj->ij/dot_general | solution.py:93
  240.2 2.1 collective-permute-start.7
  242.3 4.4 %collective-permute-start.6 = (bf16[66,352]{1,0:T(8,128)(2,1)S(1)}, bf16[66,352]{1,0:T(8,128)(2,1)S(1)}, u32[]{:S(2)}, u32[]{:S(2)}) collective-permute-start(bf16[66,352]{1,0:T(8,128)(2,1)S(1)} %select_convert_fusion), channel_id=1, source_target_pairs={{0,576},{192,0},{384,192},{576,384},{1,577},{193,1},{385,193},{577... | collective-permute-start | bytes 139400 | tf_op jit(solution)/shard_map/ppermute | solution.py:13
  246.7 0.0 collective-permute-done.7
  246.7 1.9 collective-permute-start.8
  248.6 0.1 add_multiply_fusion.1
  248.7 0.0 collective-permute-done.6
  248.7 4.1 %collective-permute-done.8 = bf16[66,352]{1,0:T(8,128)(2,1)S(1)} collective-permute-done((bf16[66,352]{1,0:T(8,128)(2,1)S(1)}, bf16[66,352]{1,0:T(8,128)(2,1)S(1)}, u32[]{:S(2)}, u32[]{:S(2)}) %collective-permute-start.8) | collective-permute-done | bytes 46496 | tf_op jit(solution)/shard_map/ppermute | solution.py:13
  252.8 0.1 pad_maximum_fusion.2
  252.9 3.4 %collective-permute-start.9 = (bf16[4,66,352]{2,1,0:T(8,128)(2,1)S(1)}, bf16[4,66,352]{2,1,0:T(8,128)(2,1)S(1)}, u32[]{:S(2)}, u32[]{:S(2)}) collective-permute-start(bf16[4,66,352]{2,1,0:T(8,128)(2,1)S(1)} %pad_maximum_fusion.2), channel_id=1, source_target_pairs={{0,168},{24,0},{48,24},{72,48},{96,72},{120,96},{144,120},{168,144... | collective-permute-start | bytes 557576 | tf_op jit(solution)/shard_map/ppermute | solution.py:13
  256.3 1.9 collective-permute-start.12
  258.3 1.3 collective-permute-done.9
  259.5 4.6 %collective-permute-start.10 = (bf16[4,66,352]{2,1,0:T(8,128)(2,1)S(1)}, bf16[4,66,352]{2,1,0:T(8,128)(2,1)S(1)}, u32[]{:S(2)}, u32[]{:S(2)}) collective-permute-start(bf16[4,66,352]{2,1,0:T(8,128)(2,1)S(1)} %collective-permute-done.9), channel_id=1, source_target_pairs={{0,168},{24,0},{48,24},{72,48},{96,72},{120,96},{144,120},{168,144... | collective-permute-start | bytes 557576 | tf_op jit(solution)/shard_map/ppermute | solution.py:13
  264.2 0.0 collective-permute-done.12
  264.2 1.9 collective-permute-start.13
  266.2 0.9 collective-permute-done.10
  267.0 5.0 %collective-permute-start.11 = (bf16[4,66,352]{2,1,0:T(8,128)(2,1)S(1)}, bf16[4,66,352]{2,1,0:T(8,128)(2,1)S(1)}, u32[]{:S(2)}, u32[]{:S(2)}) collective-permute-start(bf16[4,66,352]{2,1,0:T(8,128)(2,1)S(1)} %collective-permute-done.10), channel_id=1, source_target_pairs={{0,168},{24,0},{48,24},{72,48},{96,72},{120,96},{144,120},{168,144... | collective-permute-start | bytes 557576 | tf_op jit(solution)/shard_map/ppermute | solution.py:13
  272.1 0.0 collective-permute-done.13
  272.1 1.9 collective-permute-start.14
  274.0 5.9 %collective-permute-done.14 = bf16[4,66,352]{2,1,0:T(8,128)(2,1)S(1)} collective-permute-done((bf16[4,66,352]{2,1,0:T(8,128)(2,1)S(1)}, bf16[4,66,352]{2,1,0:T(8,128)(2,1)S(1)}, u32[]{:S(2)}, u32[]{:S(2)}) %collective-permute-start.14) | collective-permute-done | bytes 185888 | tf_op jit(solution)/shard_map/ppermute | solution.py:13
  280.0 1.9 collective-permute-start.15
  281.9 0.0 collective-permute-done.11
  281.9 5.9 %collective-permute-done.15 = bf16[4,66,352]{2,1,0:T(8,128)(2,1)S(1)} collective-permute-done((bf16[4,66,352]{2,1,0:T(8,128)(2,1)S(1)}, bf16[4,66,352]{2,1,0:T(8,128)(2,1)S(1)}, u32[]{:S(2)}, u32[]{:S(2)}) %collective-permute-start.15) | collective-permute-done | bytes 185888 | tf_op jit(solution)/shard_map/ppermute | solution.py:13
  288.0 1.2 copy-done.1
  289.2 1.7 copy.14
  291.0 9.1 %collective-permute-start.16 = (bf16[8,4,66,352]{3,0,2,1:T(8,128)(2,1)}, bf16[8,4,66,352]{3,0,2,1:T(8,128)(2,1)}, u32[]{:S(2)}, u32[]{:S(2)}) collective-permute-start(bf16[8,4,66,352]{3,0,2,1:T(8,128)(2,1)} %copy.14), channel_id=1, source_target_pairs={{0,12},{12,0},{1,13},{13,1},{2,14},{14,2},{3,15},{15,3},{4,16},{16... | collective-permute-start | bytes 4460552 | tf_op jit(solution)/shard_map/ppermute | solution.py:13
  300.0 0.1 add_multiply_fusion
  300.1 0.1 iota_add_fusion
  300.2 6.1 %reshape_reshape.3 = bf16[64,4,8,2,66]{4,3,2,1,0:T(2,128)(2,1)} reshape(bf16[64,12,352]{2,1,0:T(8,128)(2,1)} %copy.8) | data formatting | bytes 1081344 | tf_op jit(solution)/shard_map/reshape;reshape | solution.py:116
  306.3 1.9 copy.9
  308.3 0.5 fusion.15
  308.8 0.5 fusion.14
  309.3 0.0 collective-permute-done.16
  309.4 1.8 copy.19
  311.2 0.2 copy-done.2
  311.3 1.8 fusion
  313.1 2.4 fusion.10
  (38 shorter events, 0.6 us)
Async XLA Ops:
  6.5 1.8 copy-start
  6.5 139.9 %all-gather.3.cloned.1.call-start = ((), (), s32[]{:S(2)}) async-start(), calls=%async_computation.1 | async-start | bytes 2129920 | tf_op jit(solution)/shard_map/all_gather | solution.py:91
  10.8 13.2 %collective-permute-start = (f32[2,2,1,352]{3,1,2,0:T(2,128)S(1)}, f32[2,2,1,352]{3,1,2,0:T(2,128)S(1)}, u32[]{:S(2)}, u32[]{:S(2)}) collective-permute-start(f32[2,2,1,352]{3,1,2,0:T(2,128)S(1)} %pad_maximum_fusion.3), channel_id=1, source_target_pairs={{0,12},{12,0},{1,13},{13,1},{2,14},{14,2},{3,15},{15,3},{4,16},{16... | collective-permute-start | bytes 16904 | tf_op jit(solution)/shard_map/ppermute | solution.py:41
  24.0 4.4 %collective-permute-start.1 = (f32[2,2,1,352]{3,1,2,0:T(2,128)S(1)}, f32[2,2,1,352]{3,1,2,0:T(2,128)S(1)}, u32[]{:S(2)}, u32[]{:S(2)}) collective-permute-start(f32[2,2,1,352]{3,1,2,0:T(2,128)S(1)} %pad_maximum_fusion.4), channel_id=1, source_target_pairs={{0,24},{24,0},{48,72},{72,48},{96,120},{120,96},{144,168},{168,144... | collective-permute-start | bytes 16904 | tf_op jit(solution)/shard_map/ppermute | solution.py:41
  28.4 5.3 %collective-permute-start.2 = (f32[2,2,1,352]{3,1,2,0:T(2,128)S(1)}, f32[2,2,1,352]{3,1,2,0:T(2,128)S(1)}, u32[]{:S(2)}, u32[]{:S(2)}) collective-permute-start(f32[2,2,1,352]{3,1,2,0:T(2,128)S(1)} %pad_maximum_fusion.5), channel_id=1, source_target_pairs={{0,48},{24,72},{48,0},{72,24},{96,144},{120,168},{144,96},{168,120... | collective-permute-start | bytes 16904 | tf_op jit(solution)/shard_map/ppermute | solution.py:41
  33.7 8.3 %collective-permute-start.3 = (f32[2,2,1,352]{3,1,2,0:T(2,128)S(1)}, f32[2,2,1,352]{3,1,2,0:T(2,128)S(1)}, u32[]{:S(2)}, u32[]{:S(2)}) collective-permute-start(f32[2,2,1,352]{3,1,2,0:T(2,128)S(1)} %pad_maximum_fusion.6), channel_id=1, source_target_pairs={{0,96},{24,120},{48,144},{72,168},{96,0},{120,24},{144,48},{168,72... | collective-permute-start | bytes 16904 | tf_op jit(solution)/shard_map/ppermute | solution.py:41
  42.0 4.4 %collective-permute-start.4 = (f32[2,2,1,352]{3,1,2,0:T(2,128)S(1)}, f32[2,2,1,352]{3,1,2,0:T(2,128)S(1)}, u32[]{:S(2)}, u32[]{:S(2)}) collective-permute-start(f32[2,2,1,352]{3,1,2,0:T(2,128)S(1)} %pad_maximum_fusion.7), channel_id=1, source_target_pairs={{0,192},{192,0},{384,576},{576,384},{1,193},{193,1},{385,577},{577... | collective-permute-start | bytes 16904 | tf_op jit(solution)/shard_map/ppermute | solution.py:41
  46.4 5.9 %collective-permute-start.5 = (f32[2,2,1,352]{3,1,2,0:T(2,128)S(1)}, f32[2,2,1,352]{3,1,2,0:T(2,128)S(1)}, u32[]{:S(2)}, u32[]{:S(2)}) collective-permute-start(f32[2,2,1,352]{3,1,2,0:T(2,128)S(1)} %pad_maximum_fusion.8), channel_id=1, source_target_pairs={{0,384},{192,576},{384,0},{576,192},{1,385},{193,577},{385,1},{577... | collective-permute-start | bytes 16904 | tf_op jit(solution)/shard_map/ppermute | solution.py:41
  53.1 183.1 %all-gather.5.cloned.1.call-start = ((), (), s32[]{:S(2)}) async-start(), calls=%async_computation.2 | async-start | bytes 2129920 | tf_op jit(solution)/shard_map/all_gather | solution.py:91
  83.1 53.5 %all-to-all-start = ((bf16[64,64,66]{2,0,1:T(8,128)(2,1)}), bf16[64,64,66]{2,0,1:T(8,128)(2,1)}, u32[]{:S(2)}, u32[]{:S(2)}) async-start(bf16[64,64,66]{2,0,1:T(8,128)(2,1)} %copy.12), calls=%async_computation | async-start | bytes 2097152 | tf_op jit(solution)/shard_map/all_to_all | solution.py:89
  240.2 6.5 %collective-permute-start.7 = (bf16[66,352]{1,0:T(8,128)(2,1)S(1)}, bf16[66,352]{1,0:T(8,128)(2,1)S(1)}, u32[]{:S(2)}, u32[]{:S(2)}) collective-permute-start(bf16[66,352]{1,0:T(8,128)(2,1)S(1)} %select_convert_fusion), channel_id=1, source_target_pairs={{0,192},{192,384},{384,576},{576,0},{1,193},{193,385},{385,577},{5... | collective-permute-start | bytes 139400 | tf_op jit(solution)/shard_map/ppermute | solution.py:13
  242.3 6.4 %collective-permute-start.6 = (bf16[66,352]{1,0:T(8,128)(2,1)S(1)}, bf16[66,352]{1,0:T(8,128)(2,1)S(1)}, u32[]{:S(2)}, u32[]{:S(2)}) collective-permute-start(bf16[66,352]{1,0:T(8,128)(2,1)S(1)} %select_convert_fusion), channel_id=1, source_target_pairs={{0,576},{192,0},{384,192},{576,384},{1,577},{193,1},{385,193},{577... | collective-permute-start | bytes 139400 | tf_op jit(solution)/shard_map/ppermute | solution.py:13
  246.7 6.1 %collective-permute-start.8 = (bf16[66,352]{1,0:T(8,128)(2,1)S(1)}, bf16[66,352]{1,0:T(8,128)(2,1)S(1)}, u32[]{:S(2)}, u32[]{:S(2)}) collective-permute-start(bf16[66,352]{1,0:T(8,128)(2,1)S(1)} %collective-permute-done.7), channel_id=1, source_target_pairs={{0,192},{192,384},{384,576},{576,0},{1,193},{193,385},{385,577},{5... | collective-permute-start | bytes 139400 | tf_op jit(solution)/shard_map/ppermute | solution.py:13
  252.9 6.7 %collective-permute-start.9 = (bf16[4,66,352]{2,1,0:T(8,128)(2,1)S(1)}, bf16[4,66,352]{2,1,0:T(8,128)(2,1)S(1)}, u32[]{:S(2)}, u32[]{:S(2)}) collective-permute-start(bf16[4,66,352]{2,1,0:T(8,128)(2,1)S(1)} %pad_maximum_fusion.2), channel_id=1, source_target_pairs={{0,168},{24,0},{48,24},{72,48},{96,72},{120,96},{144,120},{168,144... | collective-permute-start | bytes 557576 | tf_op jit(solution)/shard_map/ppermute | solution.py:13
  256.3 7.9 %collective-permute-start.12 = (bf16[4,66,352]{2,1,0:T(8,128)(2,1)S(1)}, bf16[4,66,352]{2,1,0:T(8,128)(2,1)S(1)}, u32[]{:S(2)}, u32[]{:S(2)}) collective-permute-start(bf16[4,66,352]{2,1,0:T(8,128)(2,1)S(1)} %pad_maximum_fusion.2), channel_id=1, source_target_pairs={{0,24},{24,48},{48,72},{72,96},{96,120},{120,144},{144,168},{168,0... | collective-permute-start | bytes 557576 | tf_op jit(solution)/shard_map/ppermute | solution.py:13
  259.5 7.5 %collective-permute-start.10 = (bf16[4,66,352]{2,1,0:T(8,128)(2,1)S(1)}, bf16[4,66,352]{2,1,0:T(8,128)(2,1)S(1)}, u32[]{:S(2)}, u32[]{:S(2)}) collective-permute-start(bf16[4,66,352]{2,1,0:T(8,128)(2,1)S(1)} %collective-permute-done.9), channel_id=1, source_target_pairs={{0,168},{24,0},{48,24},{72,48},{96,72},{120,96},{144,120},{168,144... | collective-permute-start | bytes 557576 | tf_op jit(solution)/shard_map/ppermute | solution.py:13
  264.2 7.9 %collective-permute-start.13 = (bf16[4,66,352]{2,1,0:T(8,128)(2,1)S(1)}, bf16[4,66,352]{2,1,0:T(8,128)(2,1)S(1)}, u32[]{:S(2)}, u32[]{:S(2)}) collective-permute-start(bf16[4,66,352]{2,1,0:T(8,128)(2,1)S(1)} %collective-permute-done.12), channel_id=1, source_target_pairs={{0,24},{24,48},{48,72},{72,96},{96,120},{120,144},{144,168},{168,0... | collective-permute-start | bytes 557576 | tf_op jit(solution)/shard_map/ppermute | solution.py:13
  267.0 14.8 %collective-permute-start.11 = (bf16[4,66,352]{2,1,0:T(8,128)(2,1)S(1)}, bf16[4,66,352]{2,1,0:T(8,128)(2,1)S(1)}, u32[]{:S(2)}, u32[]{:S(2)}) collective-permute-start(bf16[4,66,352]{2,1,0:T(8,128)(2,1)S(1)} %collective-permute-done.10), channel_id=1, source_target_pairs={{0,168},{24,0},{48,24},{72,48},{96,72},{120,96},{144,120},{168,144... | collective-permute-start | bytes 557576 | tf_op jit(solution)/shard_map/ppermute | solution.py:13
  272.1 7.9 %collective-permute-start.14 = (bf16[4,66,352]{2,1,0:T(8,128)(2,1)S(1)}, bf16[4,66,352]{2,1,0:T(8,128)(2,1)S(1)}, u32[]{:S(2)}, u32[]{:S(2)}) collective-permute-start(bf16[4,66,352]{2,1,0:T(8,128)(2,1)S(1)} %collective-permute-done.13), channel_id=1, source_target_pairs={{0,24},{24,48},{48,72},{72,96},{96,120},{120,144},{144,168},{168,0... | collective-permute-start | bytes 557576 | tf_op jit(solution)/shard_map/ppermute | solution.py:13
  280.0 7.9 %collective-permute-start.15 = (bf16[4,66,352]{2,1,0:T(8,128)(2,1)S(1)}, bf16[4,66,352]{2,1,0:T(8,128)(2,1)S(1)}, u32[]{:S(2)}, u32[]{:S(2)}) collective-permute-start(bf16[4,66,352]{2,1,0:T(8,128)(2,1)S(1)} %collective-permute-done.14), channel_id=1, source_target_pairs={{0,24},{24,48},{48,72},{72,96},{96,120},{120,144},{144,168},{168,0... | collective-permute-start | bytes 557576 | tf_op jit(solution)/shard_map/ppermute | solution.py:13
  288.0 1.2 copy-start.1
  291.0 18.4 %collective-permute-start.16 = (bf16[8,4,66,352]{3,0,2,1:T(8,128)(2,1)}, bf16[8,4,66,352]{3,0,2,1:T(8,128)(2,1)}, u32[]{:S(2)}, u32[]{:S(2)}) collective-permute-start(bf16[8,4,66,352]{3,0,2,1:T(8,128)(2,1)} %copy.14), channel_id=1, source_target_pairs={{0,12},{12,0},{1,13},{13,1},{2,14},{14,2},{3,15},{15,3},{4,16},{16... | collective-permute-start | bytes 4460552 | tf_op jit(solution)/shard_map/ppermute | solution.py:13
  309.3 2.0 copy-start.2
Sparse Core Ops, SparseCore 0:
  53.3 93.0 all-gather.2
  150.3 85.8 all-gather.4

commit v6 on v4

--- a/solution.py
+++ b/solution.py
@@ -87,6 +87,9 @@
     second_full = jnp.transpose(stacked, (1, 0, 2)).reshape(local, n_mp * rows)
     width = second_full.shape[1] // dp_count
     columns = lax.all_to_all(second_full, DP, split_axis=1, concat_axis=0, tiled=True)
+    second_perm = relative_order(second_full.reshape(local, nx, ny, nc, width), ("x", "y", "c"))
+    second_perm = jnp.transpose(second_perm, (0, 3, 2, 1, 4)).reshape(local, dp_count * width)
+    columns, second_perm = lax.optimization_barrier((columns, second_perm))
     first_all = lax.all_gather(first, DP, axis=0, tiled=True)
     corr = (
         jnp.einsum("bi,bj->ij", first_all, columns, preferred_element_type=jnp.float32)
@@ -112,8 +115,6 @@
     scale_sum = (jnp.sum(grad_wide * grad_wide, axis=0) - diag_val * diag_val) / (
         2.0 * off_weight
     ) + diag_val * (1.0 + diag_val / 2.0)
-    second_perm = relative_order(second_full.reshape(local, nx, ny, nc, width), ("x", "y", "c"))
-    second_perm = jnp.transpose(second_perm, (0, 3, 2, 1, 4)).reshape(local, dp_count * width)
     back = jnp.dot(second_perm, grad_t, preferred_element_type=jnp.float32)
     result = (back - first.astype(jnp.float32) * scale_sum[None, :]) * inv_std[0]
     return result.astype(jnp.bfloat16)

time: 234 us -> 234 us (level)
  waiting for transfers between devices: 81.3 us -> 57.5 us
  other arithmetic: 3.47 us -> 18.9 us
  local copies, waits for them, and re-layouts: 23.7 us -> 31 us
    all_to_all x1, waiting for transfers between devices: 32.3 us -> 8.05 us  [shards(): lax.all_to_all(second_full, DP, split_axis=1, concat_axis=0, tiled=True)]
    reshape x0 -> x2, local copies, waits for them, and re-layouts: none -> 8.32 us  [the longest x1 5.85 us: shards(): grad_t = dp_ring_gather(grad_block.T).reshape(dp_count * width, rows)]
    concatenate x2, other arithmetic: 1.06 us -> 8.29 us  [relative_order(): v = jnp.roll(v, -lax.axis_index(axis), axis=dim)]
    transpose x0 -> x1, other arithmetic: none -> 4.66 us  [shards(): jnp.transpose(second_perm, (0, 3, 2, 1, 4)).reshape(local, dp_count * width)]
    ppermute x11, waiting for transfers between devices: 18.1 us -> 20.8 us  [shift(): return lax.ppermute(v, axis, [(i, (i + step) % n) for i in range(n)])]
    another operation x1 -> x2, other arithmetic: 0.06 us -> 2.54 us  [ring_gather(): return jnp.stack([got[t] for t in range(n)])]
    all_to_all x2 -> x3, local copies, waits for them, and re-layouts: 6.83 us -> 9.12 us  [shards(): lax.all_to_all(second_full, DP, split_axis=1, concat_axis=0, tiled=True)]
    another operation x2 -> x1, local copies, waits for them, and re-layouts: 7.97 us -> 6.07 us  [shards(): second_full.reshape(local, nx, ny, nc, width)]
  transfers between devices with their start and end apart: 19 -> 19, of which waited for: 13 -> 14; matrix products, arithmetic and copies ran while one was open for 6% -> 13% of each run, Pallas kernels for 0% -> 0%
where the time goes in v6:
time: 234 us; the launch traced here: 233 us
  starting transfers between devices  82.4 us (35%)
  waiting for transfers between devices  57.5 us (25%)
  local copies, waits for them, and re-layouts  31 us (13%)
  blocking collectives  21.1 us (9%)
  other arithmetic  18.9 us (8%)
  between operations  14 us (6%)
  matrix products  8.15 us (3%)
    ppermute x11, starting transfers between devices, shift(): return lax.ppermute(v, axis, [(i, (i + step) % n) for i in range(n)])  38.2 us
    all_to_all x1, starting transfers between devices, shards(): lax.all_to_all(second_full, DP, split_axis=1, concat_axis=0, tiled=True)  22.2 us
    ppermute x6, starting transfers between devices, combine(): other = lax.ppermute(jnp.stack([mean, m2]), axis, pairs)  22 us
    all_gather x1, blocking collectives, shards(): stacked = lax.all_gather(second, 'mp', axis=0)  21.1 us
    ppermute x11, waiting for transfers between devices, shift(): return lax.ppermute(v, axis, [(i, (i + step) % n) for i in range(n)])  20.8 us
    ppermute x6, waiting for transfers between devices, combine(): other = lax.ppermute(jnp.stack([mean, m2]), axis, pairs)  19.3 us
    all_gather x1, waiting for transfers between devices, shards(): first_all = lax.all_gather(first, DP, axis=0, tiled=True)  9.29 us
    all_to_all x3, local copies, waits for them, and re-layouts, shards(): lax.all_to_all(second_full, DP, split_axis=1, concat_axis=0, tiled=True)  9.12 us
  transfers between devices with their start and end apart: 19, of which 14 were waited for; matrix products, arithmetic and copies ran while one was open for 13% of the time, Pallas kernels for 0%

profile of v6, /device:TPU:1, one launch (start us, length us, event | category | flops | bytes accessed | tf_op | source)
XLA Modules:
  0.0 233.0 jit_solution(8543910817479282313)
XLA Ops:
  6.5 1.8 copy-done
  8.4 2.3 fusion.70
  10.8 12.4 %collective-permute-start = (f32[2,2,1,352]{3,1,2,0:T(2,128)S(1)}, f32[2,2,1,352]{3,1,2,0:T(2,128)S(1)}, u32[]{:S(2)}, u32[]{:S(2)}) collective-permute-start(f32[2,2,1,352]{3,1,2,0:T(2,128)S(1)} %pad_maximum_fusion.2), channel_id=1, source_target_pairs={{0,12},{12,0},{1,13},{13,1},{2,14},{14,2},{3,15},{15,3},{4,16},{16... | collective-permute-start | bytes 16904 | tf_op jit(solution)/shard_map/ppermute | solution.py:41
  23.2 0.8 collective-permute-done
  24.0 1.9 collective-permute-start.1
  26.0 2.4 %collective-permute-done.1 = f32[2,2,1,352]{3,1,2,0:T(2,128)S(1)} collective-permute-done((f32[2,2,1,352]{3,1,2,0:T(2,128)S(1)}, f32[2,2,1,352]{3,1,2,0:T(2,128)S(1)}, u32[]{:S(2)}, u32[]{:S(2)}) %collective-permute-start.1) | collective-permute-done | bytes 5664 | tf_op jit(solution)/shard_map/ppermute | solution.py:41
  28.4 1.9 collective-permute-start.2
  30.4 3.3 %collective-permute-done.2 = f32[2,2,1,352]{3,1,2,0:T(2,128)S(1)} collective-permute-done((f32[2,2,1,352]{3,1,2,0:T(2,128)S(1)}, f32[2,2,1,352]{3,1,2,0:T(2,128)S(1)}, u32[]{:S(2)}, u32[]{:S(2)}) %collective-permute-start.2) | collective-permute-done | bytes 5664 | tf_op jit(solution)/shard_map/ppermute | solution.py:41
  33.7 1.9 collective-permute-start.3
  35.7 6.4 %collective-permute-done.3 = f32[2,2,1,352]{3,1,2,0:T(2,128)S(1)} collective-permute-done((f32[2,2,1,352]{3,1,2,0:T(2,128)S(1)}, f32[2,2,1,352]{3,1,2,0:T(2,128)S(1)}, u32[]{:S(2)}, u32[]{:S(2)}) %collective-permute-start.3) | collective-permute-done | bytes 5664 | tf_op jit(solution)/shard_map/ppermute | solution.py:41
  42.0 1.9 collective-permute-start.4
  44.0 2.4 %collective-permute-done.4 = f32[2,2,1,352]{3,1,2,0:T(2,128)S(1)} collective-permute-done((f32[2,2,1,352]{3,1,2,0:T(2,128)S(1)}, f32[2,2,1,352]{3,1,2,0:T(2,128)S(1)}, u32[]{:S(2)}, u32[]{:S(2)}) %collective-permute-start.4) | collective-permute-done | bytes 5664 | tf_op jit(solution)/shard_map/ppermute | solution.py:41
  46.4 1.9 collective-permute-start.5
  48.4 3.9 %collective-permute-done.5 = f32[2,2,1,352]{3,1,2,0:T(2,128)S(1)} collective-permute-done((f32[2,2,1,352]{3,1,2,0:T(2,128)S(1)}, f32[2,2,1,352]{3,1,2,0:T(2,128)S(1)}, u32[]{:S(2)}, u32[]{:S(2)}) %collective-permute-start.5) | collective-permute-done | bytes 5664 | tf_op jit(solution)/shard_map/ppermute | solution.py:41
  52.4 0.5 copy-done.4
  52.9 0.6 copy-done.1
  53.6 0.6 fusion.69
  54.2 0.0 all-gather.3.cloned.1.call-update
  54.2 21.1 %all_gather.6 = bf16[12,64,352]{2,1,0:T(8,128)(2,1)S(1)} all-gather(bf16[1,64,352]{2,1,0:T(8,128)(2,1)S(1)} %get-tuple-element.16), channel_id=1, replica_groups=mesh['x'=4,'y'=8,'c'=2,'mp'=12] {'mp'}, dimensions={0}, use_global_device_ids=true | all-gather | bytes 585728 | tf_op jit(solution)/shard_map/all_gather | solution.py:86
  75.3 1.3 copy.7
  76.6 4.0 %all_to_all.14 = bf16[64,64,66]{2,1,0:T(8,128)(2,1)} reshape(bf16[64,12,352]{2,1,0:T(8,128)(2,1)} %copy.7) | data formatting | bytes 1081344 | tf_op jit(solution)/shard_map/all_to_all | solution.py:89
  80.5 2.9 %copy.8 = bf16[64,64,66]{2,0,1:T(8,128)(2,1)} copy(bf16[64,64,66]{2,1,0:T(8,128)(2,1)} %all_to_all.14) | data formatting | bytes 1081344 | tf_op jit(solution)/shard_map/all_to_all | solution.py:89
  83.4 22.2 %all-to-all-start = ((bf16[64,64,66]{2,0,1:T(8,128)(2,1)}), bf16[64,64,66]{2,0,1:T(8,128)(2,1)}, u32[]{:S(2)}, u32[]{:S(2)}) async-start(bf16[64,64,66]{2,0,1:T(8,128)(2,1)} %copy.8), calls=%async_computation | async-start | bytes 2097152 | tf_op jit(solution)/shard_map/all_to_all | solution.py:89
  105.7 0.5 iota_add_fusion.2
  106.2 0.6 iota_add_fusion.1
  106.8 6.1 %reshape_reshape.3 = bf16[64,4,8,2,66]{4,3,2,1,0:T(2,128)(2,1)} reshape(bf16[64,12,352]{2,1,0:T(8,128)(2,1)} %copy.7) | data formatting | bytes 1081344 | tf_op jit(solution)/shard_map/reshape;reshape | solution.py:90
  112.9 4.2 %fusion.9 = bf16[64,4,8,2,66]{4,3,2,1,0:T(2,128)(2,1)S(1)} fusion(s32[]{:T(128)S(6)} %select_n.74, bf16[64,4,8,2,66]{4,3,2,1,0:T(2,128)(2,1)} %reshape_reshape.3), kind=kLoop, calls=%fused_computation.20 | loop fusion | flops 270336 | bytes 1081348 | tf_op jit(solution)/shard_map/jit(_roll_dynamic)/concatenate | solution.py:65
  117.1 4.1 %fusion.8 = bf16[64,4,8,2,66]{4,3,2,1,0:T(2,128)(2,1)S(1)} fusion(s32[]{:T(128)S(6)} %select_n.76, bf16[64,4,8,2,66]{4,3,2,1,0:T(2,128)(2,1)S(1)} %fusion.9), kind=kLoop, calls=%fused_computation.19 | loop fusion | flops 270336 | bytes 1081348 | tf_op jit(solution)/shard_map/jit(_roll_dynamic)/concatenate | solution.py:65
  121.2 4.7 %fusion.11 = bf16[64,2,8,4,66]{4,1,2,3,0:T(2,128)(2,1)S(1)} fusion(s32[]{:T(128)S(6)} %select_n.78, bf16[64,4,8,2,66]{4,3,2,1,0:T(2,128)(2,1)S(1)} %fusion.8), kind=kLoop, calls=%fused_computation.22 | loop fusion | flops 1081344 | bytes 1081348 | tf_op jit(solution)/shard_map/transpose | solution.py:91
  125.9 1.5 copy.11
  127.4 2.5 %reshape.652 = bf16[64,4224]{1,0:T(8,128)(2,1)S(1)} reshape(bf16[64,2,8,4,66]{4,3,2,1,0:T(4,128)(2,1)} %copy.11) | data formatting | bytes 1081344 | tf_op jit(solution)/shard_map/reshape | solution.py:91
  129.9 8.1 %all-to-all-done = bf16[64,64,66]{2,0,1:T(8,128)(2,1)} async-done(((bf16[64,64,66]{2,0,1:T(8,128)(2,1)}), bf16[64,64,66]{2,0,1:T(8,128)(2,1)}, u32[]{:S(2)}, u32[]{:S(2)}) %all-to-all-start) | async-done | bytes 540704 | tf_op jit(solution)/shard_map/all_to_all | solution.py:89
  137.9 2.3 copy.14
  140.2 9.3 %all-gather.3.cloned.1.call-done = bf16[1,4096,352]{2,1,0:T(8,128)(2,1)} async-done(((bf16[1,64,352]{2,1,0:T(8,128)(2,1)}), bf16[1,4096,352]{2,1,0:T(8,128)(2,1)}) %all-gather.3.cloned.1.call-update) | async-done | bytes 2883600 | tf_op jit(solution)/shard_map/all_gather | solution.py:93
  149.5 2.7 %select_convert_fusion = bf16[66,352]{1,0:T(8,128)(2,1)S(1)} fusion(bf16[4096,66]{0,1:T(8,128)(2,1)} %copy.14, bf16[1,4096,352]{2,1,0:T(8,128)(2,1)} %all-gather.3.cloned.1.call-done, s32[352]{0:T(512)} %iota_add_fusion.1, s32[66]{0:T(128)} %iota_add_fusion.2), kind=kOutput, calls=%fused_computation.34 | convolution fusion | flops 190479168 | bytes 3472392 | tf_op jit(solution)/shard_map/bi,bj->ij/dot_general | solution.py:95
  152.1 3.0 %collective-permute-start.7 = (bf16[66,352]{1,0:T(8,128)(2,1)S(1)}, bf16[66,352]{1,0:T(8,128)(2,1)S(1)}, u32[]{:S(2)}, u32[]{:S(2)}) collective-permute-start(bf16[66,352]{1,0:T(8,128)(2,1)S(1)} %select_convert_fusion), channel_id=1, source_target_pairs={{0,192},{192,384},{384,576},{576,0},{1,193},{193,385},{385,577},{5... | collective-permute-start | bytes 139400 | tf_op jit(solution)/shard_map/ppermute | solution.py:13
  155.2 3.7 %collective-permute-start.6 = (bf16[66,352]{1,0:T(8,128)(2,1)S(1)}, bf16[66,352]{1,0:T(8,128)(2,1)S(1)}, u32[]{:S(2)}, u32[]{:S(2)}) collective-permute-start(bf16[66,352]{1,0:T(8,128)(2,1)S(1)} %select_convert_fusion), channel_id=1, source_target_pairs={{0,576},{192,0},{384,192},{576,384},{1,577},{193,1},{385,193},{577... | collective-permute-start | bytes 139400 | tf_op jit(solution)/shard_map/ppermute | solution.py:13
  158.9 1.9 collective-permute-start.8
  160.8 4.2 %collective-permute-done.8 = bf16[66,352]{1,0:T(8,128)(2,1)S(1)} collective-permute-done((bf16[66,352]{1,0:T(8,128)(2,1)S(1)}, bf16[66,352]{1,0:T(8,128)(2,1)S(1)}, u32[]{:S(2)}, u32[]{:S(2)}) %collective-permute-start.8) | collective-permute-done | bytes 46496 | tf_op jit(solution)/shard_map/ppermute | solution.py:13
  165.0 0.1 pad_maximum_fusion.1
  165.0 3.5 %collective-permute-start.9 = (bf16[4,66,352]{2,1,0:T(8,128)(2,1)S(1)}, bf16[4,66,352]{2,1,0:T(8,128)(2,1)S(1)}, u32[]{:S(2)}, u32[]{:S(2)}) collective-permute-start(bf16[4,66,352]{2,1,0:T(8,128)(2,1)S(1)} %pad_maximum_fusion.1), channel_id=1, source_target_pairs={{0,168},{24,0},{48,24},{72,48},{96,72},{120,96},{144,120},{168,144... | collective-permute-start | bytes 557576 | tf_op jit(solution)/shard_map/ppermute | solution.py:13
  168.5 1.9 collective-permute-start.12
  170.5 1.2 collective-permute-done.9
  171.7 4.7 %collective-permute-start.10 = (bf16[4,66,352]{2,1,0:T(8,128)(2,1)S(1)}, bf16[4,66,352]{2,1,0:T(8,128)(2,1)S(1)}, u32[]{:S(2)}, u32[]{:S(2)}) collective-permute-start(bf16[4,66,352]{2,1,0:T(8,128)(2,1)S(1)} %collective-permute-done.9), channel_id=1, source_target_pairs={{0,168},{24,0},{48,24},{72,48},{96,72},{120,96},{144,120},{168,144... | collective-permute-start | bytes 557576 | tf_op jit(solution)/shard_map/ppermute | solution.py:13
  176.4 0.0 collective-permute-done.12
  176.4 1.9 collective-permute-start.13
  178.4 0.9 collective-permute-done.10
  179.2 5.0 %collective-permute-start.11 = (bf16[4,66,352]{2,1,0:T(8,128)(2,1)S(1)}, bf16[4,66,352]{2,1,0:T(8,128)(2,1)S(1)}, u32[]{:S(2)}, u32[]{:S(2)}) collective-permute-start(bf16[4,66,352]{2,1,0:T(8,128)(2,1)S(1)} %collective-permute-done.10), channel_id=1, source_target_pairs={{0,168},{24,0},{48,24},{72,48},{96,72},{120,96},{144,120},{168,144... | collective-permute-start | bytes 557576 | tf_op jit(solution)/shard_map/ppermute | solution.py:13
  184.3 0.0 collective-permute-done.13
  184.3 1.9 collective-permute-start.14
  186.2 5.9 %collective-permute-done.14 = bf16[4,66,352]{2,1,0:T(8,128)(2,1)S(1)} collective-permute-done((bf16[4,66,352]{2,1,0:T(8,128)(2,1)S(1)}, bf16[4,66,352]{2,1,0:T(8,128)(2,1)S(1)}, u32[]{:S(2)}, u32[]{:S(2)}) %collective-permute-start.14) | collective-permute-done | bytes 185888 | tf_op jit(solution)/shard_map/ppermute | solution.py:13
  192.2 1.9 collective-permute-start.15
  194.1 5.9 %collective-permute-done.15 = bf16[4,66,352]{2,1,0:T(8,128)(2,1)S(1)} collective-permute-done((bf16[4,66,352]{2,1,0:T(8,128)(2,1)S(1)}, bf16[4,66,352]{2,1,0:T(8,128)(2,1)S(1)}, u32[]{:S(2)}, u32[]{:S(2)}) %collective-permute-start.15) | collective-permute-done | bytes 185888 | tf_op jit(solution)/shard_map/ppermute | solution.py:13
  200.2 0.6 copy.12
  200.8 8.7 %collective-permute-start.16 = (bf16[8,4,66,352]{3,0,2,1:T(8,128)(2,1)S(1)}, bf16[8,4,66,352]{3,0,2,1:T(8,128)(2,1)S(1)}, u32[]{:S(2)}, u32[]{:S(2)}) collective-permute-start(bf16[8,4,66,352]{3,0,2,1:T(8,128)(2,1)S(1)} %copy.12), channel_id=1, source_target_pairs={{0,12},{12,0},{1,13},{13,1},{2,14},{14,2},{3,15},{15,3},{4,16},{16... | collective-permute-start | bytes 4460552 | tf_op jit(solution)/shard_map/ppermute | solution.py:13
  209.6 0.1 add_multiply_fusion.1
  209.7 0.1 add_multiply_fusion
  209.7 0.1 iota_add_fusion
  209.9 2.7 %collective-permute-done.16 = bf16[8,4,66,352]{3,0,2,1:T(8,128)(2,1)S(1)} collective-permute-done((bf16[8,4,66,352]{3,0,2,1:T(8,128)(2,1)S(1)}, bf16[8,4,66,352]{3,0,2,1:T(8,128)(2,1)S(1)}, u32[]{:S(2)}, u32[]{:S(2)}) %collective-permute-start.16) | collective-permute-done | bytes 1486880 | tf_op jit(solution)/shard_map/ppermute | solution.py:13
  212.7 0.2 copy.16
  212.9 2.5 %pad_maximum_fusion = bf16[2,8,4,66,352]{4,3,2,1,0:T(8,128)(2,1)} fusion(bf16[1,8,4,66,352]{4,3,2,1,0:T(8,128)(2,1)S(1)} %bitcast.292, bf16[1,8,4,66,352]{4,3,2,1,0:T(8,128)(2,1)S(1)} %bitcast.290), kind=kLoop, calls=%fused_computation.4 | loop fusion | flops 1486848 | bytes 5947392 | tf_op jit(solution)/shard_map/stack | solution.py:31
  215.4 1.8 fusion
  217.2 5.8 %reshape.653 = bf16[4224,352]{1,0:T(8,128)(2,1)} reshape(bf16[2,8,4,66,352]{4,3,2,1,0:T(8,128)(2,1)} %pad_maximum_fusion) | data formatting | bytes 5947392 | tf_op jit(solution)/shard_map/reshape | solution.py:103
  223.0 3.2 %fusion.7 = bf16[64,352]{1,0:T(8,128)(2,1)} fusion(bf16[64,4224]{1,0:T(8,128)(2,1)S(1)} %reshape.652, bf16[4224,352]{1,0:T(8,128)(2,1)} %reshape.653, f32[352]{0:T(512)S(1)} %rsqrt_reduce_fusion, f32[352]{0:T(512)S(1)} %multiply_add_fusion.5, bf16[2,64,352]{2,1,0:T(8,128)(2,1)} %copy-done.1), kind=kOutput, calls=%fused_computation.18 | convolution fusion | flops 190429184 | bytes 3607296 | tf_op jit(solution)/shard_map/dot_general | solution.py:118
  (47 shorter events, 0.6 us)
Async XLA Ops:
  6.5 1.8 copy-start
  6.5 142.9 %all-gather.3.cloned.1.call-start = ((), (), s32[]{:S(2)}) async-start(), calls=%async_computation.1 | async-start | bytes 3194880 | tf_op jit(solution)/shard_map/all_gather | solution.py:93
  10.8 13.2 %collective-permute-start = (f32[2,2,1,352]{3,1,2,0:T(2,128)S(1)}, f32[2,2,1,352]{3,1,2,0:T(2,128)S(1)}, u32[]{:S(2)}, u32[]{:S(2)}) collective-permute-start(f32[2,2,1,352]{3,1,2,0:T(2,128)S(1)} %pad_maximum_fusion.2), channel_id=1, source_target_pairs={{0,12},{12,0},{1,13},{13,1},{2,14},{14,2},{3,15},{15,3},{4,16},{16... | collective-permute-start | bytes 16904 | tf_op jit(solution)/shard_map/ppermute | solution.py:41
  24.0 4.4 %collective-permute-start.1 = (f32[2,2,1,352]{3,1,2,0:T(2,128)S(1)}, f32[2,2,1,352]{3,1,2,0:T(2,128)S(1)}, u32[]{:S(2)}, u32[]{:S(2)}) collective-permute-start(f32[2,2,1,352]{3,1,2,0:T(2,128)S(1)} %pad_maximum_fusion.3), channel_id=1, source_target_pairs={{0,24},{24,0},{48,72},{72,48},{96,120},{120,96},{144,168},{168,144... | collective-permute-start | bytes 16904 | tf_op jit(solution)/shard_map/ppermute | solution.py:41
  28.4 5.3 %collective-permute-start.2 = (f32[2,2,1,352]{3,1,2,0:T(2,128)S(1)}, f32[2,2,1,352]{3,1,2,0:T(2,128)S(1)}, u32[]{:S(2)}, u32[]{:S(2)}) collective-permute-start(f32[2,2,1,352]{3,1,2,0:T(2,128)S(1)} %pad_maximum_fusion.4), channel_id=1, source_target_pairs={{0,48},{24,72},{48,0},{72,24},{96,144},{120,168},{144,96},{168,120... | collective-permute-start | bytes 16904 | tf_op jit(solution)/shard_map/ppermute | solution.py:41
  33.7 8.3 %collective-permute-start.3 = (f32[2,2,1,352]{3,1,2,0:T(2,128)S(1)}, f32[2,2,1,352]{3,1,2,0:T(2,128)S(1)}, u32[]{:S(2)}, u32[]{:S(2)}) collective-permute-start(f32[2,2,1,352]{3,1,2,0:T(2,128)S(1)} %pad_maximum_fusion.5), channel_id=1, source_target_pairs={{0,96},{24,120},{48,144},{72,168},{96,0},{120,24},{144,48},{168,72... | collective-permute-start | bytes 16904 | tf_op jit(solution)/shard_map/ppermute | solution.py:41
  42.0 10.4 %copy-start.2 = (f32[2,2,1,352]{3,1,2,0:T(2,128)}, f32[2,2,1,352]{3,1,2,0:T(2,128)S(1)}, u32[]{:S(2)}) copy-start(f32[2,2,1,352]{3,1,2,0:T(2,128)S(1)} %collective-permute-done.3) | copy-start | bytes 16900
  42.0 4.4 %collective-permute-start.4 = (f32[2,2,1,352]{3,1,2,0:T(2,128)S(1)}, f32[2,2,1,352]{3,1,2,0:T(2,128)S(1)}, u32[]{:S(2)}, u32[]{:S(2)}) collective-permute-start(f32[2,2,1,352]{3,1,2,0:T(2,128)S(1)} %pad_maximum_fusion.6), channel_id=1, source_target_pairs={{0,192},{192,0},{384,576},{576,384},{1,193},{193,1},{385,577},{577... | collective-permute-start | bytes 16904 | tf_op jit(solution)/shard_map/ppermute | solution.py:41
  46.4 5.9 %collective-permute-start.5 = (f32[2,2,1,352]{3,1,2,0:T(2,128)S(1)}, f32[2,2,1,352]{3,1,2,0:T(2,128)S(1)}, u32[]{:S(2)}, u32[]{:S(2)}) collective-permute-start(f32[2,2,1,352]{3,1,2,0:T(2,128)S(1)} %pad_maximum_fusion.7), channel_id=1, source_target_pairs={{0,384},{192,576},{384,0},{576,192},{1,385},{193,577},{385,1},{577... | collective-permute-start | bytes 16904 | tf_op jit(solution)/shard_map/ppermute | solution.py:41
  52.3 0.6 copy-start.4
  52.9 0.6 copy-start.1
  83.4 54.5 %all-to-all-start = ((bf16[64,64,66]{2,0,1:T(8,128)(2,1)}), bf16[64,64,66]{2,0,1:T(8,128)(2,1)}, u32[]{:S(2)}, u32[]{:S(2)}) async-start(bf16[64,64,66]{2,0,1:T(8,128)(2,1)} %copy.8), calls=%async_computation | async-start | bytes 2097152 | tf_op jit(solution)/shard_map/all_to_all | solution.py:89
  152.1 6.7 %collective-permute-start.7 = (bf16[66,352]{1,0:T(8,128)(2,1)S(1)}, bf16[66,352]{1,0:T(8,128)(2,1)S(1)}, u32[]{:S(2)}, u32[]{:S(2)}) collective-permute-start(bf16[66,352]{1,0:T(8,128)(2,1)S(1)} %select_convert_fusion), channel_id=1, source_target_pairs={{0,192},{192,384},{384,576},{576,0},{1,193},{193,385},{385,577},{5... | collective-permute-start | bytes 139400 | tf_op jit(solution)/shard_map/ppermute | solution.py:13
  155.2 5.7 %collective-permute-start.6 = (bf16[66,352]{1,0:T(8,128)(2,1)S(1)}, bf16[66,352]{1,0:T(8,128)(2,1)S(1)}, u32[]{:S(2)}, u32[]{:S(2)}) collective-permute-start(bf16[66,352]{1,0:T(8,128)(2,1)S(1)} %select_convert_fusion), channel_id=1, source_target_pairs={{0,576},{192,0},{384,192},{576,384},{1,577},{193,1},{385,193},{577... | collective-permute-start | bytes 139400 | tf_op jit(solution)/shard_map/ppermute | solution.py:13
  158.9 6.1 %collective-permute-start.8 = (bf16[66,352]{1,0:T(8,128)(2,1)S(1)}, bf16[66,352]{1,0:T(8,128)(2,1)S(1)}, u32[]{:S(2)}, u32[]{:S(2)}) collective-permute-start(bf16[66,352]{1,0:T(8,128)(2,1)S(1)} %collective-permute-done.7), channel_id=1, source_target_pairs={{0,192},{192,384},{384,576},{576,0},{1,193},{193,385},{385,577},{5... | collective-permute-start | bytes 139400 | tf_op jit(solution)/shard_map/ppermute | solution.py:13
  165.0 6.7 %collective-permute-start.9 = (bf16[4,66,352]{2,1,0:T(8,128)(2,1)S(1)}, bf16[4,66,352]{2,1,0:T(8,128)(2,1)S(1)}, u32[]{:S(2)}, u32[]{:S(2)}) collective-permute-start(bf16[4,66,352]{2,1,0:T(8,128)(2,1)S(1)} %pad_maximum_fusion.1), channel_id=1, source_target_pairs={{0,168},{24,0},{48,24},{72,48},{96,72},{120,96},{144,120},{168,144... | collective-permute-start | bytes 557576 | tf_op jit(solution)/shard_map/ppermute | solution.py:13
  168.5 7.9 %collective-permute-start.12 = (bf16[4,66,352]{2,1,0:T(8,128)(2,1)S(1)}, bf16[4,66,352]{2,1,0:T(8,128)(2,1)S(1)}, u32[]{:S(2)}, u32[]{:S(2)}) collective-permute-start(bf16[4,66,352]{2,1,0:T(8,128)(2,1)S(1)} %pad_maximum_fusion.1), channel_id=1, source_target_pairs={{0,24},{24,48},{48,72},{72,96},{96,120},{120,144},{144,168},{168,0... | collective-permute-start | bytes 557576 | tf_op jit(solution)/shard_map/ppermute | solution.py:13
  171.7 7.5 %collective-permute-start.10 = (bf16[4,66,352]{2,1,0:T(8,128)(2,1)S(1)}, bf16[4,66,352]{2,1,0:T(8,128)(2,1)S(1)}, u32[]{:S(2)}, u32[]{:S(2)}) collective-permute-start(bf16[4,66,352]{2,1,0:T(8,128)(2,1)S(1)} %collective-permute-done.9), channel_id=1, source_target_pairs={{0,168},{24,0},{48,24},{72,48},{96,72},{120,96},{144,120},{168,144... | collective-permute-start | bytes 557576 | tf_op jit(solution)/shard_map/ppermute | solution.py:13
  176.4 7.9 %collective-permute-start.13 = (bf16[4,66,352]{2,1,0:T(8,128)(2,1)S(1)}, bf16[4,66,352]{2,1,0:T(8,128)(2,1)S(1)}, u32[]{:S(2)}, u32[]{:S(2)}) collective-permute-start(bf16[4,66,352]{2,1,0:T(8,128)(2,1)S(1)} %collective-permute-done.12), channel_id=1, source_target_pairs={{0,24},{24,48},{48,72},{72,96},{96,120},{120,144},{144,168},{168,0... | collective-permute-start | bytes 557576 | tf_op jit(solution)/shard_map/ppermute | solution.py:13
  179.2 14.8 %collective-permute-start.11 = (bf16[4,66,352]{2,1,0:T(8,128)(2,1)S(1)}, bf16[4,66,352]{2,1,0:T(8,128)(2,1)S(1)}, u32[]{:S(2)}, u32[]{:S(2)}) collective-permute-start(bf16[4,66,352]{2,1,0:T(8,128)(2,1)S(1)} %collective-permute-done.10), channel_id=1, source_target_pairs={{0,168},{24,0},{48,24},{72,48},{96,72},{120,96},{144,120},{168,144... | collective-permute-start | bytes 557576 | tf_op jit(solution)/shard_map/ppermute | solution.py:13
  184.3 7.9 %collective-permute-start.14 = (bf16[4,66,352]{2,1,0:T(8,128)(2,1)S(1)}, bf16[4,66,352]{2,1,0:T(8,128)(2,1)S(1)}, u32[]{:S(2)}, u32[]{:S(2)}) collective-permute-start(bf16[4,66,352]{2,1,0:T(8,128)(2,1)S(1)} %collective-permute-done.13), channel_id=1, source_target_pairs={{0,24},{24,48},{48,72},{72,96},{96,120},{120,144},{144,168},{168,0... | collective-permute-start | bytes 557576 | tf_op jit(solution)/shard_map/ppermute | solution.py:13
  192.2 7.9 %collective-permute-start.15 = (bf16[4,66,352]{2,1,0:T(8,128)(2,1)S(1)}, bf16[4,66,352]{2,1,0:T(8,128)(2,1)S(1)}, u32[]{:S(2)}, u32[]{:S(2)}) collective-permute-start(bf16[4,66,352]{2,1,0:T(8,128)(2,1)S(1)} %collective-permute-done.14), channel_id=1, source_target_pairs={{0,24},{24,48},{48,72},{72,96},{96,120},{120,144},{144,168},{168,0... | collective-permute-start | bytes 557576 | tf_op jit(solution)/shard_map/ppermute | solution.py:13
  200.2 9.6 %copy-start.3 = (f32[2,2,1,352]{3,1,2,0:T(2,128)S(1)}, f32[2,2,1,352]{3,1,2,0:T(2,128)}, u32[]{:S(2)}) copy-start(f32[2,2,1,352]{3,1,2,0:T(2,128)} %copy-done.2) | copy-start | bytes 16900
  200.2 9.6 %copy-start.5 = (f32[2,2,1,352]{3,1,2,0:T(2,128)S(1)}, f32[2,2,1,352]{3,1,2,0:T(2,128)}, u32[]{:S(2)}) copy-start(f32[2,2,1,352]{3,1,2,0:T(2,128)} %copy-done.4) | copy-start | bytes 16900
  200.8 11.8 %collective-permute-start.16 = (bf16[8,4,66,352]{3,0,2,1:T(8,128)(2,1)S(1)}, bf16[8,4,66,352]{3,0,2,1:T(8,128)(2,1)S(1)}, u32[]{:S(2)}, u32[]{:S(2)}) collective-permute-start(bf16[8,4,66,352]{3,0,2,1:T(8,128)(2,1)S(1)} %copy.12), channel_id=1, source_target_pairs={{0,12},{12,0},{1,13},{13,1},{2,14},{14,2},{3,15},{15,3},{4,16},{16... | collective-permute-start | bytes 4460552 | tf_op jit(solution)/shard_map/ppermute | solution.py:13
  212.9 2.5 %copy-start.6 = (s32[352]{0:T(512)S(1)}, s32[352]{0:T(512)}, u32[]{:S(2)}) copy-start(s32[352]{0:T(512)} %iota_add_fusion.1) | copy-start | bytes 4228
Sparse Core Ops, SparseCore 0:
  54.3 95.0 all-gather.2

commit v7 on v6

--- a/solution.py
+++ b/solution.py
@@ -76,12 +76,15 @@
     local = hidden.shape[1]
     total = local * dp_count
     feats = jnp.einsum("vbh,hc->vbc", hidden, proj_weight, preferred_element_type=jnp.float32)
-    mean, var = dp_stats(feats)
-    centered = feats - mean
-    normed = (centered / jnp.sqrt(var + eps)).astype(jnp.bfloat16)
-    inv_std = 1.0 / jnp.sqrt(var + eps)
-    first = normed[0]
-    second = normed[1]
+    feats0_all = lax.all_gather(feats[0], DP, axis=0, tiled=True)
+    mean0 = jnp.sum(feats0_all, axis=0, keepdims=True) / total
+    centered0 = feats0_all - mean0
+    var0 = jnp.sum(centered0 * centered0, axis=0, keepdims=True) / total
+    first_all = (centered0 / jnp.sqrt(var0 + eps)).astype(jnp.bfloat16)
+    first = ((feats[0] - mean0) / jnp.sqrt(var0 + eps)).astype(jnp.bfloat16)
+    inv_std0 = 1.0 / jnp.sqrt(var0 + eps)
+    mean1, var1 = dp_stats(feats[1:])
+    second = ((feats[1] - mean1[0]) / jnp.sqrt(var1[0] + eps)).astype(jnp.bfloat16)
     n_mp = lax.axis_size("mp")
     stacked = lax.all_gather(second, "mp", axis=0)
     second_full = jnp.transpose(stacked, (1, 0, 2)).reshape(local, n_mp * rows)
@@ -90,7 +93,6 @@
     second_perm = relative_order(second_full.reshape(local, nx, ny, nc, width), ("x", "y", "c"))
     second_perm = jnp.transpose(second_perm, (0, 3, 2, 1, 4)).reshape(local, dp_count * width)
     columns, second_perm = lax.optimization_barrier((columns, second_perm))
-    first_all = lax.all_gather(first, DP, axis=0, tiled=True)
     corr = (
         jnp.einsum("bi,bj->ij", first_all, columns, preferred_element_type=jnp.float32)
         / total
@@ -116,7 +118,7 @@
         2.0 * off_weight
     ) + diag_val * (1.0 + diag_val / 2.0)
     back = jnp.dot(second_perm, grad_t, preferred_element_type=jnp.float32)
-    result = (back - first.astype(jnp.float32) * scale_sum[None, :]) * inv_std[0]
+    result = (back - first.astype(jnp.float32) * scale_sum[None, :]) * inv_std0
     return result.astype(jnp.bfloat16)
 
 

time: 234 us -> 226 us (0.966)
  waiting for transfers between devices: 57.5 us -> 46.4 us
  other arithmetic: 18.9 us -> 25.6 us
  starting transfers between devices: 82.4 us -> 78.3 us
    all_gather x1, waiting for transfers between devices: 9.29 us -> 0.01 us  [shards(): feats0_all = lax.all_gather(feats[0], DP, axis=0, tiled=True)]
    reduce_sum x1 -> x3, other arithmetic: 0.04 us -> 7.12 us  [the longest x1 3.74 us: shards(): var0 = jnp.sum(centered0 * centered0, axis=0, keepdims=True) / total]
    all_to_all x1, waiting for transfers between devices: 8.05 us -> 4.93 us  [shards(): lax.all_to_all(second_full, DP, split_axis=1, concat_axis=0, tiled=True)]
  transfers between devices with their start and end apart: 19 -> 19, of which waited for: 14 -> 14; matrix products, arithmetic and copies ran while one was open for 13% -> 14% of each run, Pallas kernels for 0% -> 0%
where the time goes in v7:
time: 226 us; the launch traced here: 225 us
  starting transfers between devices  78.3 us (35%)
  waiting for transfers between devices  46.4 us (21%)
  local copies, waits for them, and re-layouts  30.9 us (14%)
  other arithmetic  25.6 us (11%)
  blocking collectives  22.7 us (10%)
  between operations  13.9 us (6%)
  matrix products  7.53 us (3%)
    ppermute x11, starting transfers between devices, shift(): return lax.ppermute(v, axis, [(i, (i + step) % n) for i in range(n)])  35.9 us
    all_gather x1, blocking collectives, shards(): stacked = lax.all_gather(second, 'mp', axis=0)  22.7 us
    ppermute x11, waiting for transfers between devices, shift(): return lax.ppermute(v, axis, [(i, (i + step) % n) for i in range(n)])  22.2 us
    ppermute x6, starting transfers between devices, combine(): other = lax.ppermute(jnp.stack([mean, m2]), axis, pairs)  22 us
    all_to_all x1, starting transfers between devices, shards(): lax.all_to_all(second_full, DP, split_axis=1, concat_axis=0, tiled=True)  20.4 us
    ppermute x6, waiting for transfers between devices, combine(): other = lax.ppermute(jnp.stack([mean, m2]), axis, pairs)  19.2 us
    all_to_all x3, local copies, waits for them, and re-layouts, shards(): lax.all_to_all(second_full, DP, split_axis=1, concat_axis=0, tiled=True)  9.12 us
    concatenate x2, other arithmetic, relative_order(): v = jnp.roll(v, -lax.axis_index(axis), axis=dim)  8.29 us
  transfers between devices with their start and end apart: 19, of which 14 were waited for; matrix products, arithmetic and copies ran while one was open for 14% of the time, Pallas kernels for 0%

profile of v7, /device:TPU:1, one launch (start us, length us, event | category | flops | bytes accessed | tf_op | source)
XLA Modules:
  0.0 225.3 jit_solution(8128383188779477859)
XLA Ops:
  6.5 1.8 copy-done
  8.4 2.3 %fusion.3 = f32[2,64,352]{2,1,0:T(8,128)S(1)} fusion(bf16[2,64,4224]{2,1,0:T(8,128)(2,1)} %param.2, bf16[4224,352]{0,1:T(8,128)(2,1)S(1)} %copy-done), kind=kOutput, calls=%fused_computation.9 | convolution fusion | flops 380633088 | bytes 4235264 | tf_op jit(solution)/shard_map/vbh,hc->vbc/dot_general | solution.py:78
  10.7 0.7 fusion.19
  11.4 0.0 all-gather.3.cloned.1.call-update
  11.4 12.4 %collective-permute-start = (f32[2,1,1,352]{3,2,1,0:T(1,128)S(1)}, f32[2,1,1,352]{3,2,1,0:T(1,128)S(1)}, u32[]{:S(2)}, u32[]{:S(2)}) collective-permute-start(f32[2,1,1,352]{3,2,1,0:T(1,128)S(1)} %pad_maximum_fusion.2), channel_id=1, source_target_pairs={{0,12},{12,0},{1,13},{13,1},{2,14},{14,2},{3,15},{15,3},{4,16},{16... | collective-permute-start | bytes 8456 | tf_op jit(solution)/shard_map/ppermute | solution.py:41
  23.9 0.8 collective-permute-done
  24.7 1.9 collective-permute-start.1
  26.6 2.4 %collective-permute-done.1 = f32[2,1,1,352]{3,2,1,0:T(1,128)S(1)} collective-permute-done((f32[2,1,1,352]{3,2,1,0:T(1,128)S(1)}, f32[2,1,1,352]{3,2,1,0:T(1,128)S(1)}, u32[]{:S(2)}, u32[]{:S(2)}) %collective-permute-start.1) | collective-permute-done | bytes 2848 | tf_op jit(solution)/shard_map/ppermute | solution.py:41
  29.1 1.9 collective-permute-start.2
  31.0 3.3 %collective-permute-done.2 = f32[2,1,1,352]{3,2,1,0:T(1,128)S(1)} collective-permute-done((f32[2,1,1,352]{3,2,1,0:T(1,128)S(1)}, f32[2,1,1,352]{3,2,1,0:T(1,128)S(1)}, u32[]{:S(2)}, u32[]{:S(2)}) %collective-permute-start.2) | collective-permute-done | bytes 2848 | tf_op jit(solution)/shard_map/ppermute | solution.py:41
  34.4 1.9 collective-permute-start.3
  36.3 6.4 %collective-permute-done.3 = f32[2,1,1,352]{3,2,1,0:T(1,128)S(1)} collective-permute-done((f32[2,1,1,352]{3,2,1,0:T(1,128)S(1)}, f32[2,1,1,352]{3,2,1,0:T(1,128)S(1)}, u32[]{:S(2)}, u32[]{:S(2)}) %collective-permute-start.3) | collective-permute-done | bytes 2848 | tf_op jit(solution)/shard_map/ppermute | solution.py:41
  42.7 1.9 collective-permute-start.4
  44.7 2.4 %collective-permute-done.4 = f32[2,1,1,352]{3,2,1,0:T(1,128)S(1)} collective-permute-done((f32[2,1,1,352]{3,2,1,0:T(1,128)S(1)}, f32[2,1,1,352]{3,2,1,0:T(1,128)S(1)}, u32[]{:S(2)}, u32[]{:S(2)}) %collective-permute-start.4) | collective-permute-done | bytes 2848 | tf_op jit(solution)/shard_map/ppermute | solution.py:41
  47.1 1.9 collective-permute-start.5
  49.0 3.9 %collective-permute-done.5 = f32[2,1,1,352]{3,2,1,0:T(1,128)S(1)} collective-permute-done((f32[2,1,1,352]{3,2,1,0:T(1,128)S(1)}, f32[2,1,1,352]{3,2,1,0:T(1,128)S(1)}, u32[]{:S(2)}, u32[]{:S(2)}) %collective-permute-start.5) | collective-permute-done | bytes 2848 | tf_op jit(solution)/shard_map/ppermute | solution.py:41
  53.0 22.7 %all_gather.7 = bf16[12,64,352]{2,1,0:T(8,128)(2,1)S(1)} all-gather(bf16[1,64,352]{2,1,0:T(8,128)(2,1)S(1)} %divide_convert_fusion.4), channel_id=1, replica_groups=mesh['x'=4,'y'=8,'c'=2,'mp'=12] {'mp'}, dimensions={0}, use_global_device_ids=true | all-gather | bytes 585728 | tf_op jit(solution)/shard_map/all_gather | solution.py:89
  75.7 1.2 copy.7
  77.0 4.0 %all_to_all.14 = bf16[64,64,66]{2,1,0:T(8,128)(2,1)} reshape(bf16[64,12,352]{2,1,0:T(8,128)(2,1)} %copy.7) | data formatting | bytes 1081344 | tf_op jit(solution)/shard_map/all_to_all | solution.py:92
  81.0 2.9 %copy.8 = bf16[64,64,66]{2,0,1:T(8,128)(2,1)} copy(bf16[64,64,66]{2,1,0:T(8,128)(2,1)} %all_to_all.14) | data formatting | bytes 1081344 | tf_op jit(solution)/shard_map/all_to_all | solution.py:92
  83.8 20.4 %all-to-all-start = ((bf16[64,64,66]{2,0,1:T(8,128)(2,1)}), bf16[64,64,66]{2,0,1:T(8,128)(2,1)}, u32[]{:S(2)}, u32[]{:S(2)}) async-start(bf16[64,64,66]{2,0,1:T(8,128)(2,1)} %copy.8), calls=%async_computation | async-start | bytes 2097152 | tf_op jit(solution)/shard_map/all_to_all | solution.py:92
  104.4 6.1 %reshape_reshape.3 = bf16[64,4,8,2,66]{4,3,2,1,0:T(2,128)(2,1)} reshape(bf16[64,12,352]{2,1,0:T(8,128)(2,1)} %copy.7) | data formatting | bytes 1081344 | tf_op jit(solution)/shard_map/reshape;reshape | solution.py:93
  110.5 4.2 %fusion.8 = bf16[64,4,8,2,66]{4,3,2,1,0:T(2,128)(2,1)S(1)} fusion(s32[]{:T(128)S(6)} %select_n.74, bf16[64,4,8,2,66]{4,3,2,1,0:T(2,128)(2,1)} %reshape_reshape.3), kind=kLoop, calls=%fused_computation.22 | loop fusion | flops 270336 | bytes 1081348 | tf_op jit(solution)/shard_map/jit(_roll_dynamic)/concatenate | solution.py:65
  114.7 4.1 %fusion.7 = bf16[64,4,8,2,66]{4,3,2,1,0:T(2,128)(2,1)S(1)} fusion(s32[]{:T(128)S(6)} %select_n.76, bf16[64,4,8,2,66]{4,3,2,1,0:T(2,128)(2,1)S(1)} %fusion.8), kind=kLoop, calls=%fused_computation.21 | loop fusion | flops 270336 | bytes 1081348 | tf_op jit(solution)/shard_map/jit(_roll_dynamic)/concatenate | solution.py:65
  118.8 4.7 %fusion.10 = bf16[64,2,8,4,66]{4,1,2,3,0:T(2,128)(2,1)S(1)} fusion(s32[]{:T(128)S(6)} %select_n.78, bf16[64,4,8,2,66]{4,3,2,1,0:T(2,128)(2,1)S(1)} %fusion.7), kind=kLoop, calls=%fused_computation.24 | loop fusion | flops 1081344 | bytes 1081348 | tf_op jit(solution)/shard_map/transpose | solution.py:94
  123.5 1.6 copy.11
  125.1 3.1 %reshape.545 = bf16[64,4224]{1,0:T(8,128)(2,1)} reshape(bf16[64,2,8,4,66]{4,3,2,1,0:T(4,128)(2,1)} %copy.11) | data formatting | bytes 1081344 | tf_op jit(solution)/shard_map/reshape | solution.py:94
  128.2 4.9 %all-to-all-done = bf16[64,64,66]{2,0,1:T(8,128)(2,1)} async-done(((bf16[64,64,66]{2,0,1:T(8,128)(2,1)}), bf16[64,64,66]{2,0,1:T(8,128)(2,1)}, u32[]{:S(2)}, u32[]{:S(2)}) %all-to-all-start) | async-done | bytes 540704 | tf_op jit(solution)/shard_map/all_to_all | solution.py:92
  133.2 2.3 %copy.14 = bf16[4096,66]{0,1:T(8,128)(2,1)} copy(bf16[4096,66]{1,0:T(8,128)(2,1)} %bitcast.3) | data formatting | bytes 1081344 | tf_op jit(solution)/shard_map/all_to_all | solution.py:92
  135.4 3.4 %reduce_sum.56 = f32[352]{0:T(512)S(1)} reduce(f32[1,4096,352]{2,1,0:T(8,128)} %all-gather.3.cloned.1.call-done, f32[]{:T(128)} %constant.121.clone.1), dimensions={0,1}, to_apply=%region_2.0 | reduce | flops 1441440 | bytes 5768580 | tf_op jit(solution)/shard_map/reduce_sum | solution.py:80
  138.8 3.7 %multiply_reduce_fusion = f32[352]{0:T(512)S(1)} fusion(f32[1,4096,352]{2,1,0:T(8,128)} %all-gather.3.cloned.1.call-done, f32[352]{0:T(512)S(1)} %broadcast_multiply_fusion), kind=kLoop, calls=%fused_computation.6 | loop fusion | flops 4325024 | bytes 5769984 | tf_op jit(solution)/shard_map/reduce_sum | solution.py:82
  142.6 0.8 copy-done.1
  143.4 1.9 select_convert_fusion
  145.3 2.2 collective-permute-start.7
  147.5 4.3 %collective-permute-start.6 = (bf16[66,352]{1,0:T(8,128)(2,1)S(1)}, bf16[66,352]{1,0:T(8,128)(2,1)S(1)}, u32[]{:S(2)}, u32[]{:S(2)}) collective-permute-start(bf16[66,352]{1,0:T(8,128)(2,1)S(1)} %select_convert_fusion), channel_id=1, source_target_pairs={{0,576},{192,0},{384,192},{576,384},{1,577},{193,1},{385,193},{577... | collective-permute-start | bytes 139400 | tf_op jit(solution)/shard_map/ppermute | solution.py:13
  151.8 0.3 collective-permute-done.7
  152.1 1.9 collective-permute-start.8
  154.0 0.0 collective-permute-done.6
  154.0 4.2 %collective-permute-done.8 = bf16[66,352]{1,0:T(8,128)(2,1)S(1)} collective-permute-done((bf16[66,352]{1,0:T(8,128)(2,1)S(1)}, bf16[66,352]{1,0:T(8,128)(2,1)S(1)}, u32[]{:S(2)}, u32[]{:S(2)}) %collective-permute-start.8) | collective-permute-done | bytes 46496 | tf_op jit(solution)/shard_map/ppermute | solution.py:13
  158.2 0.1 pad_maximum_fusion.1
  158.3 1.9 collective-permute-start.9
  160.2 3.4 %collective-permute-start.12 = (bf16[4,66,352]{2,1,0:T(8,128)(2,1)S(1)}, bf16[4,66,352]{2,1,0:T(8,128)(2,1)S(1)}, u32[]{:S(2)}, u32[]{:S(2)}) collective-permute-start(bf16[4,66,352]{2,1,0:T(8,128)(2,1)S(1)} %pad_maximum_fusion.1), channel_id=1, source_target_pairs={{0,24},{24,48},{48,72},{72,96},{96,120},{120,144},{144,168},{168,0... | collective-permute-start | bytes 557576 | tf_op jit(solution)/shard_map/ppermute | solution.py:13
  163.6 1.7 collective-permute-done.9
  165.4 2.7 %collective-permute-start.10 = (bf16[4,66,352]{2,1,0:T(8,128)(2,1)S(1)}, bf16[4,66,352]{2,1,0:T(8,128)(2,1)S(1)}, u32[]{:S(2)}, u32[]{:S(2)}) collective-permute-start(bf16[4,66,352]{2,1,0:T(8,128)(2,1)S(1)} %collective-permute-done.9), channel_id=1, source_target_pairs={{0,168},{24,0},{48,24},{72,48},{96,72},{120,96},{144,120},{168,144... | collective-permute-start | bytes 557576 | tf_op jit(solution)/shard_map/ppermute | solution.py:13
  168.1 0.0 collective-permute-done.12
  168.1 2.6 %collective-permute-start.13 = (bf16[4,66,352]{2,1,0:T(8,128)(2,1)S(1)}, bf16[4,66,352]{2,1,0:T(8,128)(2,1)S(1)}, u32[]{:S(2)}, u32[]{:S(2)}) collective-permute-start(bf16[4,66,352]{2,1,0:T(8,128)(2,1)S(1)} %collective-permute-done.12), channel_id=1, source_target_pairs={{0,24},{24,48},{48,72},{72,96},{96,120},{120,144},{144,168},{168,0... | collective-permute-start | bytes 557576 | tf_op jit(solution)/shard_map/ppermute | solution.py:13
  170.7 1.3 collective-permute-done.10
  172.0 3.9 %collective-permute-start.11 = (bf16[4,66,352]{2,1,0:T(8,128)(2,1)S(1)}, bf16[4,66,352]{2,1,0:T(8,128)(2,1)S(1)}, u32[]{:S(2)}, u32[]{:S(2)}) collective-permute-start(bf16[4,66,352]{2,1,0:T(8,128)(2,1)S(1)} %collective-permute-done.10), channel_id=1, source_target_pairs={{0,168},{24,0},{48,24},{72,48},{96,72},{120,96},{144,120},{168,144... | collective-permute-start | bytes 557576 | tf_op jit(solution)/shard_map/ppermute | solution.py:13
  176.0 0.0 collective-permute-done.13
  176.0 1.9 collective-permute-start.14
  177.9 5.9 %collective-permute-done.14 = bf16[4,66,352]{2,1,0:T(8,128)(2,1)S(1)} collective-permute-done((bf16[4,66,352]{2,1,0:T(8,128)(2,1)S(1)}, bf16[4,66,352]{2,1,0:T(8,128)(2,1)S(1)}, u32[]{:S(2)}, u32[]{:S(2)}) %collective-permute-start.14) | collective-permute-done | bytes 185888 | tf_op jit(solution)/shard_map/ppermute | solution.py:13
  183.9 1.9 collective-permute-start.15
  185.8 5.9 %collective-permute-done.15 = bf16[4,66,352]{2,1,0:T(8,128)(2,1)S(1)} collective-permute-done((bf16[4,66,352]{2,1,0:T(8,128)(2,1)S(1)}, bf16[4,66,352]{2,1,0:T(8,128)(2,1)S(1)}, u32[]{:S(2)}, u32[]{:S(2)}) %collective-permute-start.15) | collective-permute-done | bytes 185888 | tf_op jit(solution)/shard_map/ppermute | solution.py:13
  191.9 0.6 copy.12
  192.5 9.2 %collective-permute-start.16 = (bf16[8,4,66,352]{3,0,2,1:T(8,128)(2,1)S(1)}, bf16[8,4,66,352]{3,0,2,1:T(8,128)(2,1)S(1)}, u32[]{:S(2)}, u32[]{:S(2)}) collective-permute-start(bf16[8,4,66,352]{3,0,2,1:T(8,128)(2,1)S(1)} %copy.12), channel_id=1, source_target_pairs={{0,12},{12,0},{1,13},{13,1},{2,14},{14,2},{3,15},{15,3},{4,16},{16... | collective-permute-start | bytes 4460552 | tf_op jit(solution)/shard_map/ppermute | solution.py:13
  201.7 0.1 add_multiply_fusion.1
  201.8 0.1 add_multiply_fusion
  201.9 0.1 iota_add_fusion
  202.0 2.8 %collective-permute-done.16 = bf16[8,4,66,352]{3,0,2,1:T(8,128)(2,1)S(1)} collective-permute-done((bf16[8,4,66,352]{3,0,2,1:T(8,128)(2,1)S(1)}, bf16[8,4,66,352]{3,0,2,1:T(8,128)(2,1)S(1)}, u32[]{:S(2)}, u32[]{:S(2)}) %collective-permute-start.16) | collective-permute-done | bytes 1486880 | tf_op jit(solution)/shard_map/ppermute | solution.py:13
  204.8 0.2 copy.16
  205.0 2.5 %pad_maximum_fusion = bf16[2,8,4,66,352]{4,3,2,1,0:T(8,128)(2,1)} fusion(bf16[1,8,4,66,352]{4,3,2,1,0:T(8,128)(2,1)S(1)} %bitcast.56, bf16[1,8,4,66,352]{4,3,2,1,0:T(8,128)(2,1)S(1)} %bitcast.54), kind=kLoop, calls=%fused_computation.7 | loop fusion | flops 1486848 | bytes 5947392 | tf_op jit(solution)/shard_map/stack | solution.py:31
  207.5 1.8 fusion
  209.3 5.8 %reshape.546 = bf16[4224,352]{1,0:T(8,128)(2,1)} reshape(bf16[2,8,4,66,352]{4,3,2,1,0:T(8,128)(2,1)} %pad_maximum_fusion) | data formatting | bytes 5947392 | tf_op jit(solution)/shard_map/reshape | solution.py:105
  215.1 3.3 %fusion.6 = bf16[64,352]{1,0:T(8,128)(2,1)} fusion(bf16[64,4224]{1,0:T(8,128)(2,1)} %reshape.545, bf16[4224,352]{1,0:T(8,128)(2,1)} %reshape.546, f32[352]{0:T(512)S(1)} %get-tuple-element.47, f32[352]{0:T(512)S(1)} %multiply_add_fusion, f32[352]{0:T(512)S(1)} %get-tuple-element.48, f32[352]{0:T(512)S(1)} %broadcast_multiply_fusion, ...), kind=kOutput, calls=%fused_computation.20 | convolution fusion | flops 190496768 | bytes 3655168 | tf_op jit(solution)/shard_map/dot_general | solution.py:120
  (39 shorter events, 0.6 us)
Async XLA Ops:
  6.5 1.8 copy-start
  6.5 128.9 %all-gather.3.cloned.1.call-start = ((), (), s32[]{:S(2)}) async-start(), calls=%async_computation.1 | async-start | bytes 6389760 | tf_op jit(solution)/shard_map/all_gather | solution.py:79
  11.4 13.2 %collective-permute-start = (f32[2,1,1,352]{3,2,1,0:T(1,128)S(1)}, f32[2,1,1,352]{3,2,1,0:T(1,128)S(1)}, u32[]{:S(2)}, u32[]{:S(2)}) collective-permute-start(f32[2,1,1,352]{3,2,1,0:T(1,128)S(1)} %pad_maximum_fusion.2), channel_id=1, source_target_pairs={{0,12},{12,0},{1,13},{13,1},{2,14},{14,2},{3,15},{15,3},{4,16},{16... | collective-permute-start | bytes 8456 | tf_op jit(solution)/shard_map/ppermute | solution.py:41
  24.7 4.3 %collective-permute-start.1 = (f32[2,1,1,352]{3,2,1,0:T(1,128)S(1)}, f32[2,1,1,352]{3,2,1,0:T(1,128)S(1)}, u32[]{:S(2)}, u32[]{:S(2)}) collective-permute-start(f32[2,1,1,352]{3,2,1,0:T(1,128)S(1)} %pad_maximum_fusion.3), channel_id=1, source_target_pairs={{0,24},{24,0},{48,72},{72,48},{96,120},{120,96},{144,168},{168,144... | collective-permute-start | bytes 8456 | tf_op jit(solution)/shard_map/ppermute | solution.py:41
  29.1 5.2 %collective-permute-start.2 = (f32[2,1,1,352]{3,2,1,0:T(1,128)S(1)}, f32[2,1,1,352]{3,2,1,0:T(1,128)S(1)}, u32[]{:S(2)}, u32[]{:S(2)}) collective-permute-start(f32[2,1,1,352]{3,2,1,0:T(1,128)S(1)} %pad_maximum_fusion.4), channel_id=1, source_target_pairs={{0,48},{24,72},{48,0},{72,24},{96,144},{120,168},{144,96},{168,120... | collective-permute-start | bytes 8456 | tf_op jit(solution)/shard_map/ppermute | solution.py:41
  34.4 8.3 %collective-permute-start.3 = (f32[2,1,1,352]{3,2,1,0:T(1,128)S(1)}, f32[2,1,1,352]{3,2,1,0:T(1,128)S(1)}, u32[]{:S(2)}, u32[]{:S(2)}) collective-permute-start(f32[2,1,1,352]{3,2,1,0:T(1,128)S(1)} %pad_maximum_fusion.5), channel_id=1, source_target_pairs={{0,96},{24,120},{48,144},{72,168},{96,0},{120,24},{144,48},{168,72... | collective-permute-start | bytes 8456 | tf_op jit(solution)/shard_map/ppermute | solution.py:41
  42.7 4.3 %collective-permute-start.4 = (f32[2,1,1,352]{3,2,1,0:T(1,128)S(1)}, f32[2,1,1,352]{3,2,1,0:T(1,128)S(1)}, u32[]{:S(2)}, u32[]{:S(2)}) collective-permute-start(f32[2,1,1,352]{3,2,1,0:T(1,128)S(1)} %pad_maximum_fusion.6), channel_id=1, source_target_pairs={{0,192},{192,0},{384,576},{576,384},{1,193},{193,1},{385,577},{577... | collective-permute-start | bytes 8456 | tf_op jit(solution)/shard_map/ppermute | solution.py:41
  47.1 5.8 %collective-permute-start.5 = (f32[2,1,1,352]{3,2,1,0:T(1,128)S(1)}, f32[2,1,1,352]{3,2,1,0:T(1,128)S(1)}, u32[]{:S(2)}, u32[]{:S(2)}) collective-permute-start(f32[2,1,1,352]{3,2,1,0:T(1,128)S(1)} %pad_maximum_fusion.7), channel_id=1, source_target_pairs={{0,384},{192,576},{384,0},{576,192},{1,385},{193,577},{385,1},{577... | collective-permute-start | bytes 8456 | tf_op jit(solution)/shard_map/ppermute | solution.py:41
  83.8 49.3 %all-to-all-start = ((bf16[64,64,66]{2,0,1:T(8,128)(2,1)}), bf16[64,64,66]{2,0,1:T(8,128)(2,1)}, u32[]{:S(2)}, u32[]{:S(2)}) async-start(bf16[64,64,66]{2,0,1:T(8,128)(2,1)} %copy.8), calls=%async_computation | async-start | bytes 2097152 | tf_op jit(solution)/shard_map/all_to_all | solution.py:92
  138.8 4.6 %copy-start.1 = (f32[1,4096,352]{2,1,0:T(8,128)S(1)}, f32[1,4096,352]{2,1,0:T(8,128)}, u32[]{:S(2)}) copy-start(f32[1,4096,352]{2,1,0:T(8,128)} %all-gather.3.cloned.1.call-done) | copy-start | bytes 17301508
  145.3 6.8 %collective-permute-start.7 = (bf16[66,352]{1,0:T(8,128)(2,1)S(1)}, bf16[66,352]{1,0:T(8,128)(2,1)S(1)}, u32[]{:S(2)}, u32[]{:S(2)}) collective-permute-start(bf16[66,352]{1,0:T(8,128)(2,1)S(1)} %select_convert_fusion), channel_id=1, source_target_pairs={{0,192},{192,384},{384,576},{576,0},{1,193},{193,385},{385,577},{5... | collective-permute-start | bytes 139400 | tf_op jit(solution)/shard_map/ppermute | solution.py:13
  147.5 6.5 %collective-permute-start.6 = (bf16[66,352]{1,0:T(8,128)(2,1)S(1)}, bf16[66,352]{1,0:T(8,128)(2,1)S(1)}, u32[]{:S(2)}, u32[]{:S(2)}) collective-permute-start(bf16[66,352]{1,0:T(8,128)(2,1)S(1)} %select_convert_fusion), channel_id=1, source_target_pairs={{0,576},{192,0},{384,192},{576,384},{1,577},{193,1},{385,193},{577... | collective-permute-start | bytes 139400 | tf_op jit(solution)/shard_map/ppermute | solution.py:13
  152.1 6.1 %collective-permute-start.8 = (bf16[66,352]{1,0:T(8,128)(2,1)S(1)}, bf16[66,352]{1,0:T(8,128)(2,1)S(1)}, u32[]{:S(2)}, u32[]{:S(2)}) collective-permute-start(bf16[66,352]{1,0:T(8,128)(2,1)S(1)} %collective-permute-done.7), channel_id=1, source_target_pairs={{0,192},{192,384},{384,576},{576,0},{1,193},{193,385},{385,577},{5... | collective-permute-start | bytes 139400 | tf_op jit(solution)/shard_map/ppermute | solution.py:13
  158.3 7.1 %collective-permute-start.9 = (bf16[4,66,352]{2,1,0:T(8,128)(2,1)S(1)}, bf16[4,66,352]{2,1,0:T(8,128)(2,1)S(1)}, u32[]{:S(2)}, u32[]{:S(2)}) collective-permute-start(bf16[4,66,352]{2,1,0:T(8,128)(2,1)S(1)} %pad_maximum_fusion.1), channel_id=1, source_target_pairs={{0,168},{24,0},{48,24},{72,48},{96,72},{120,96},{144,120},{168,144... | collective-permute-start | bytes 557576 | tf_op jit(solution)/shard_map/ppermute | solution.py:13
  160.2 7.9 %collective-permute-start.12 = (bf16[4,66,352]{2,1,0:T(8,128)(2,1)S(1)}, bf16[4,66,352]{2,1,0:T(8,128)(2,1)S(1)}, u32[]{:S(2)}, u32[]{:S(2)}) collective-permute-start(bf16[4,66,352]{2,1,0:T(8,128)(2,1)S(1)} %pad_maximum_fusion.1), channel_id=1, source_target_pairs={{0,24},{24,48},{48,72},{72,96},{96,120},{120,144},{144,168},{168,0... | collective-permute-start | bytes 557576 | tf_op jit(solution)/shard_map/ppermute | solution.py:13
  165.4 6.7 %collective-permute-start.10 = (bf16[4,66,352]{2,1,0:T(8,128)(2,1)S(1)}, bf16[4,66,352]{2,1,0:T(8,128)(2,1)S(1)}, u32[]{:S(2)}, u32[]{:S(2)}) collective-permute-start(bf16[4,66,352]{2,1,0:T(8,128)(2,1)S(1)} %collective-permute-done.9), channel_id=1, source_target_pairs={{0,168},{24,0},{48,24},{72,48},{96,72},{120,96},{144,120},{168,144... | collective-permute-start | bytes 557576 | tf_op jit(solution)/shard_map/ppermute | solution.py:13
  168.1 7.9 %collective-permute-start.13 = (bf16[4,66,352]{2,1,0:T(8,128)(2,1)S(1)}, bf16[4,66,352]{2,1,0:T(8,128)(2,1)S(1)}, u32[]{:S(2)}, u32[]{:S(2)}) collective-permute-start(bf16[4,66,352]{2,1,0:T(8,128)(2,1)S(1)} %collective-permute-done.12), channel_id=1, source_target_pairs={{0,24},{24,48},{48,72},{72,96},{96,120},{120,144},{144,168},{168,0... | collective-permute-start | bytes 557576 | tf_op jit(solution)/shard_map/ppermute | solution.py:13
  172.0 13.8 %collective-permute-start.11 = (bf16[4,66,352]{2,1,0:T(8,128)(2,1)S(1)}, bf16[4,66,352]{2,1,0:T(8,128)(2,1)S(1)}, u32[]{:S(2)}, u32[]{:S(2)}) collective-permute-start(bf16[4,66,352]{2,1,0:T(8,128)(2,1)S(1)} %collective-permute-done.10), channel_id=1, source_target_pairs={{0,168},{24,0},{48,24},{72,48},{96,72},{120,96},{144,120},{168,144... | collective-permute-start | bytes 557576 | tf_op jit(solution)/shard_map/ppermute | solution.py:13
  176.0 7.9 %collective-permute-start.14 = (bf16[4,66,352]{2,1,0:T(8,128)(2,1)S(1)}, bf16[4,66,352]{2,1,0:T(8,128)(2,1)S(1)}, u32[]{:S(2)}, u32[]{:S(2)}) collective-permute-start(bf16[4,66,352]{2,1,0:T(8,128)(2,1)S(1)} %collective-permute-done.13), channel_id=1, source_target_pairs={{0,24},{24,48},{48,72},{72,96},{96,120},{120,144},{144,168},{168,0... | collective-permute-start | bytes 557576 | tf_op jit(solution)/shard_map/ppermute | solution.py:13
  183.9 7.9 %collective-permute-start.15 = (bf16[4,66,352]{2,1,0:T(8,128)(2,1)S(1)}, bf16[4,66,352]{2,1,0:T(8,128)(2,1)S(1)}, u32[]{:S(2)}, u32[]{:S(2)}) collective-permute-start(bf16[4,66,352]{2,1,0:T(8,128)(2,1)S(1)} %collective-permute-done.14), channel_id=1, source_target_pairs={{0,24},{24,48},{48,72},{72,96},{96,120},{120,144},{144,168},{168,0... | collective-permute-start | bytes 557576 | tf_op jit(solution)/shard_map/ppermute | solution.py:13
  192.5 12.3 %collective-permute-start.16 = (bf16[8,4,66,352]{3,0,2,1:T(8,128)(2,1)S(1)}, bf16[8,4,66,352]{3,0,2,1:T(8,128)(2,1)S(1)}, u32[]{:S(2)}, u32[]{:S(2)}) collective-permute-start(bf16[8,4,66,352]{3,0,2,1:T(8,128)(2,1)S(1)} %copy.12), channel_id=1, source_target_pairs={{0,12},{12,0},{1,13},{13,1},{2,14},{14,2},{3,15},{15,3},{4,16},{16... | collective-permute-start | bytes 4460552 | tf_op jit(solution)/shard_map/ppermute | solution.py:13
Sparse Core Ops, SparseCore 0:
  11.5 102.5 all-gather.2

commit v8 on v7

--- a/solution.py
+++ b/solution.py
@@ -31,8 +31,13 @@
     return jnp.stack([got[t] for t in range(n)])
 
 
+def ring_gather_abs(v, axis):
+    return jnp.roll(ring_gather(v, axis), lax.axis_index(axis), axis=0)
+
+
 def dp_ring_gather(v):
-    return ring_gather(ring_gather(ring_gather(v, "x"), "y"), "c")
+    g = ring_gather_abs(ring_gather_abs(ring_gather_abs(v, "x"), "y"), "c")
+    return jnp.transpose(g, (2, 1, 0) + tuple(range(3, g.ndim)))
 
 
 def combine(mean, m2, count, axis, k):
@@ -60,18 +65,10 @@
     return mean, m2 / count
 
 
-def relative_order(v, axes):
-    for dim, axis in enumerate(axes, start=1):
-        v = jnp.roll(v, -lax.axis_index(axis), axis=dim)
-    return v
-
-
 def shards(hidden, proj_weight):
     mp_index = lax.axis_index("mp")
     dp_index = lax.axis_index(DP)
     dp_count = lax.axis_size(DP)
-    nx, ny, nc = lax.axis_size("x"), lax.axis_size("y"), lax.axis_size("c")
-    ix, iy, ic = lax.axis_index("x"), lax.axis_index("y"), lax.axis_index("c")
     rows = proj_weight.shape[1]
     local = hidden.shape[1]
     total = local * dp_count
@@ -90,9 +87,6 @@
     second_full = jnp.transpose(stacked, (1, 0, 2)).reshape(local, n_mp * rows)
     width = second_full.shape[1] // dp_count
     columns = lax.all_to_all(second_full, DP, split_axis=1, concat_axis=0, tiled=True)
-    second_perm = relative_order(second_full.reshape(local, nx, ny, nc, width), ("x", "y", "c"))
-    second_perm = jnp.transpose(second_perm, (0, 3, 2, 1, 4)).reshape(local, dp_count * width)
-    columns, second_perm = lax.optimization_barrier((columns, second_perm))
     corr = (
         jnp.einsum("bi,bj->ij", first_all, columns, preferred_element_type=jnp.float32)
         / total
@@ -103,21 +97,14 @@
         jnp.bfloat16
     )
     grad_t = dp_ring_gather(grad_block.T).reshape(dp_count * width, rows)
-    t = lax.iota(jnp.int32, width)
-    cc = (lax.iota(jnp.int32, nc) + ic) % nc
-    yy = (lax.iota(jnp.int32, ny) + iy) % ny
-    xx = (lax.iota(jnp.int32, nx) + ix) % nx
-    perm_cols = (
-        ((xx[None, None, :, None] * ny + yy[None, :, None, None]) * nc + cc[:, None, None, None]) * width
-        + t[None, None, None, :]
-    ).reshape(-1)
     grad_wide = grad_t.astype(jnp.float32)
+    all_cols = lax.iota(jnp.int32, dp_count * width)
     row_flat = mp_index * rows + lax.iota(jnp.int32, rows)
-    diag_val = jnp.sum(jnp.where(perm_cols[:, None] == row_flat[None, :], grad_wide, 0.0), axis=0)
+    diag_val = jnp.sum(jnp.where(all_cols[:, None] == row_flat[None, :], grad_wide, 0.0), axis=0)
     scale_sum = (jnp.sum(grad_wide * grad_wide, axis=0) - diag_val * diag_val) / (
         2.0 * off_weight
     ) + diag_val * (1.0 + diag_val / 2.0)
-    back = jnp.dot(second_perm, grad_t, preferred_element_type=jnp.float32)
+    back = jnp.dot(second_full, grad_t, preferred_element_type=jnp.float32)
     result = (back - first.astype(jnp.float32) * scale_sum[None, :]) * inv_std0
     return result.astype(jnp.bfloat16)
 

time: 226 us -> 243 us (1.075)
  local copies, waits for them, and re-layouts: 30.9 us -> 46.8 us
  other arithmetic: 25.6 us -> 12.8 us
  waiting for transfers between devices: 46.4 us -> 57.7 us
  matrix products: 7.53 us -> 10.2 us
    unnamed x10 -> x25, local copies, waits for them, and re-layouts: 2.91 us -> 21.3 us
    all_gather x1, waiting for transfers between devices: 0.01 us -> 9.73 us  [shards(): feats0_all = lax.all_gather(feats[0], DP, axis=0, tiled=True)]
    concatenate x2 -> x0, other arithmetic: 8.29 us -> none  [relative_order(): v = jnp.roll(v, -lax.axis_index(axis), axis=dim)]
    all_to_all x1, waiting for transfers between devices: 4.93 us -> 12.2 us  [shards(): lax.all_to_all(second_full, DP, split_axis=1, concat_axis=0, tiled=True)]
    another operation x3 -> x0, local copies, waits for them, and re-layouts: 6.75 us -> none  [the longest x1 6.12 us: shards(): second_full.reshape(local, nx, ny, nc, width)]
    ppermute x11, waiting for transfers between devices: 22.2 us -> 16.5 us  [shift(): return lax.ppermute(v, axis, [(i, (i + step) % n) for i in range(n)])]
    dynamic_slice x0 -> x3, local copies, waits for them, and re-layouts: none -> 5.41 us  [ring_gather_abs(): return jnp.roll(ring_gather(v, axis), lax.axis_index(axis), axis=0)]
    transpose x1 -> x0, other arithmetic: 4.66 us -> none  [shards(): jnp.transpose(second_perm, (0, 3, 2, 1, 4)).reshape(local, dp_count * width)]
  transfers between devices with their start and end apart: 19 -> 19, of which waited for: 14 -> 13; matrix products, arithmetic and copies ran while one was open for 14% -> 8% of each run, Pallas kernels for 0% -> 0%
where the time goes in v8:
time: 243 us; the launch traced here: 242 us
  starting transfers between devices  78.2 us (32%)
  waiting for transfers between devices  57.7 us (24%)
  local copies, waits for them, and re-layouts  46.8 us (19%)
  blocking collectives  22.7 us (9%)
  between operations  13.8 us (6%)
  other arithmetic  12.8 us (5%)
  matrix products  10.2 us (4%)
    ppermute x11, starting transfers between devices, shift(): return lax.ppermute(v, axis, [(i, (i + step) % n) for i in range(n)])  35.8 us
    all_gather x1, blocking collectives, shards(): stacked = lax.all_gather(second, 'mp', axis=0)  22.7 us
    ppermute x6, starting transfers between devices, combine(): other = lax.ppermute(jnp.stack([mean, m2]), axis, pairs)  22 us
    unnamed x25, local copies, waits for them, and re-layouts  21.3 us
    all_to_all x1, starting transfers between devices, shards(): lax.all_to_all(second_full, DP, split_axis=1, concat_axis=0, tiled=True)  20.4 us
    ppermute x6, waiting for transfers between devices, combine(): other = lax.ppermute(jnp.stack([mean, m2]), axis, pairs)  19.2 us
    ppermute x11, waiting for transfers between devices, shift(): return lax.ppermute(v, axis, [(i, (i + step) % n) for i in range(n)])  16.5 us
    all_to_all x1, waiting for transfers between devices, shards(): lax.all_to_all(second_full, DP, split_axis=1, concat_axis=0, tiled=True)  12.2 us
  transfers between devices with their start and end apart: 19, of which 13 were waited for; matrix products, arithmetic and copies ran while one was open for 8% of the time, Pallas kernels for 0%

profile of v8, /device:TPU:1, one launch (start us, length us, event | category | flops | bytes accessed | tf_op | source)
XLA Modules:
  0.0 242.2 jit_solution(2061429140245801381)
XLA Ops:
  6.5 1.8 copy-done
  8.4 2.3 fusion.7
  11.4 12.4 %collective-permute-start = (f32[2,1,1,352]{3,2,1,0:T(1,128)S(1)}, f32[2,1,1,352]{3,2,1,0:T(1,128)S(1)}, u32[]{:S(2)}, u32[]{:S(2)}) collective-permute-start(f32[2,1,1,352]{3,2,1,0:T(1,128)S(1)} %pad_maximum_fusion), channel_id=1, source_target_pairs={{0,12},{12,0},{1,13},{13,1},{2,14},{14,2},{3,15},{15,3},{4,16},{16... | collective-permute-start | bytes 8456 | tf_op jit(solution)/shard_map/ppermute | solution.py:46
  23.9 0.8 collective-permute-done
  24.7 1.9 collective-permute-start.1
  26.6 2.4 collective-permute-done.1
  29.1 1.9 collective-permute-start.2
  31.0 3.3 %collective-permute-done.2 = f32[2,1,1,352]{3,2,1,0:T(1,128)S(1)} collective-permute-done((f32[2,1,1,352]{3,2,1,0:T(1,128)S(1)}, f32[2,1,1,352]{3,2,1,0:T(1,128)S(1)}, u32[]{:S(2)}, u32[]{:S(2)}) %collective-permute-start.2) | collective-permute-done | bytes 2848 | tf_op jit(solution)/shard_map/ppermute | solution.py:46
  34.4 1.9 collective-permute-start.3
  36.3 6.4 %collective-permute-done.3 = f32[2,1,1,352]{3,2,1,0:T(1,128)S(1)} collective-permute-done((f32[2,1,1,352]{3,2,1,0:T(1,128)S(1)}, f32[2,1,1,352]{3,2,1,0:T(1,128)S(1)}, u32[]{:S(2)}, u32[]{:S(2)}) %collective-permute-start.3) | collective-permute-done | bytes 2848 | tf_op jit(solution)/shard_map/ppermute | solution.py:46
  42.7 1.9 collective-permute-start.4
  44.6 2.4 collective-permute-done.4
  47.1 1.9 collective-permute-start.5
  49.0 3.9 %collective-permute-done.5 = f32[2,1,1,352]{3,2,1,0:T(1,128)S(1)} collective-permute-done((f32[2,1,1,352]{3,2,1,0:T(1,128)S(1)}, f32[2,1,1,352]{3,2,1,0:T(1,128)S(1)}, u32[]{:S(2)}, u32[]{:S(2)}) %collective-permute-start.5) | collective-permute-done | bytes 2848 | tf_op jit(solution)/shard_map/ppermute | solution.py:46
  53.0 22.7 %all_gather.7 = bf16[12,64,352]{2,1,0:T(8,128)(2,1)S(1)} all-gather(bf16[1,64,352]{2,1,0:T(8,128)(2,1)S(1)} %divide_convert_fusion.4), channel_id=1, replica_groups=mesh['x'=4,'y'=8,'c'=2,'mp'=12] {'mp'}, dimensions={0}, use_global_device_ids=true | all-gather | bytes 585728 | tf_op jit(solution)/shard_map/all_gather | solution.py:86
  75.7 1.3 copy.13
  77.0 4.0 %all_to_all.14 = bf16[64,64,66]{2,1,0:T(8,128)(2,1)} reshape(bf16[64,12,352]{2,1,0:T(8,128)(2,1)} %copy.13) | data formatting | bytes 1081344 | tf_op jit(solution)/shard_map/all_to_all | solution.py:89
  81.0 2.9 %copy.15 = bf16[64,64,66]{2,0,1:T(8,128)(2,1)} copy(bf16[64,64,66]{2,1,0:T(8,128)(2,1)} %all_to_all.14) | data formatting | bytes 1081344 | tf_op jit(solution)/shard_map/all_to_all | solution.py:89
  83.9 20.4 %all-to-all-start = ((bf16[64,64,66]{2,0,1:T(8,128)(2,1)}), bf16[64,64,66]{2,0,1:T(8,128)(2,1)}, u32[]{:S(2)}, u32[]{:S(2)}) async-start(bf16[64,64,66]{2,0,1:T(8,128)(2,1)} %copy.15), calls=%async_computation | async-start | bytes 2097152 | tf_op jit(solution)/shard_map/all_to_all | solution.py:89
  104.4 9.7 %all-gather.3.cloned.1.call-done = f32[1,4096,352]{2,1,0:T(8,128)} async-done(((f32[1,64,352]{2,1,0:T(8,128)}), f32[1,4096,352]{2,1,0:T(8,128)}) %all-gather.3.cloned.1.call-update) | async-done | bytes 5767184 | tf_op jit(solution)/shard_map/all_gather | solution.py:76
  114.1 3.4 %reduce_sum.56 = f32[352]{0:T(512)S(1)} reduce(f32[1,4096,352]{2,1,0:T(8,128)} %all-gather.3.cloned.1.call-done, f32[]{:T(128)} %constant.95.clone.1), dimensions={0,1}, to_apply=%region_2.0 | reduce | flops 1441440 | bytes 5768580 | tf_op jit(solution)/shard_map/reduce_sum | solution.py:77
  117.5 3.6 %multiply_reduce_fusion = f32[352]{0:T(512)S(1)} fusion(f32[1,4096,352]{2,1,0:T(8,128)} %all-gather.3.cloned.1.call-done, f32[352]{0:T(512)S(1)} %broadcast_multiply_fusion), kind=kLoop, calls=%fused_computation.10 | loop fusion | flops 4325024 | bytes 5769984 | tf_op jit(solution)/shard_map/reduce_sum | solution.py:79
  121.1 12.2 %all-to-all-done = bf16[64,64,66]{2,0,1:T(8,128)(2,1)} async-done(((bf16[64,64,66]{2,0,1:T(8,128)(2,1)}), bf16[64,64,66]{2,0,1:T(8,128)(2,1)}, u32[]{:S(2)}, u32[]{:S(2)}) %all-to-all-start) | async-done | bytes 540704 | tf_op jit(solution)/shard_map/all_to_all | solution.py:89
  133.2 4.5 %bitcast_dynamic-update-slice_fusion.22 = (bf16[8,66,352]{2,1,0:T(8,128)(2,1)}, bf16[66,352]{1,0:T(8,128)(2,1)S(1)}) fusion(bf16[4096,66]{1,0:T(8,128)(2,1)} %bitcast.3, f32[1,4096,352]{2,1,0:T(8,128)} %all-gather.3.cloned.1.call-done, f32[352]{0:T(512)S(1)} %get-tuple-element.47, f32[352]{0:T(512)S(1)} %broadcast_multiply_fusion, ...), kind=kOutput, calls=%fused_computation.51 | convolution fusion | flops 194804544 | bytes 6414088 | tf_op jit(solution)/shard_map/bi,bj->ij/dot_general | solution.py:91
  137.8 2.3 collective-permute-start.7
  140.0 4.2 %collective-permute-start.6 = (bf16[66,352]{1,0:T(8,128)(2,1)S(1)}, bf16[66,352]{1,0:T(8,128)(2,1)S(1)}, u32[]{:S(2)}, u32[]{:S(2)}) collective-permute-start(bf16[66,352]{1,0:T(8,128)(2,1)S(1)} %get-tuple-element.49), channel_id=1, source_target_pairs={{0,576},{192,0},{384,192},{576,384},{1,577},{193,1},{385,193},{577... | collective-permute-start | bytes 139400 | tf_op jit(solution)/shard_map/ppermute | solution.py:13
  144.6 1.9 collective-permute-start.8
  147.2 3.5 %collective-permute-done.8 = bf16[66,352]{1,0:T(8,128)(2,1)S(1)} collective-permute-done((bf16[66,352]{1,0:T(8,128)(2,1)S(1)}, bf16[66,352]{1,0:T(8,128)(2,1)S(1)}, u32[]{:S(2)}, u32[]{:S(2)}) %collective-permute-start.8) | collective-permute-done | bytes 46496 | tf_op jit(solution)/shard_map/ppermute | solution.py:13
  154.4 1.7 bitcast_dynamic-update-slice_fusion.14
  156.2 1.9 collective-permute-start.9
  158.1 3.4 %collective-permute-start.12 = (bf16[4,66,352]{2,1,0:T(8,128)(2,1)}, bf16[4,66,352]{2,1,0:T(8,128)(2,1)S(1)}, u32[]{:S(2)}, u32[]{:S(2)}) collective-permute-start(bf16[4,66,352]{2,1,0:T(8,128)(2,1)} %get-tuple-element.21), channel_id=1, source_target_pairs={{0,24},{24,48},{48,72},{72,96},{96,120},{120,144},{144,168},{168,0... | collective-permute-start | bytes 557576 | tf_op jit(solution)/shard_map/ppermute | solution.py:13
  161.5 2.1 collective-permute-done.9
  163.6 2.7 %collective-permute-start.10 = (bf16[4,66,352]{2,1,0:T(8,128)(2,1)}, bf16[4,66,352]{2,1,0:T(8,128)(2,1)S(1)}, u32[]{:S(2)}, u32[]{:S(2)}) collective-permute-start(bf16[4,66,352]{2,1,0:T(8,128)(2,1)} %collective-permute-done.9), channel_id=1, source_target_pairs={{0,168},{24,0},{48,24},{72,48},{96,72},{120,96},{144,120},{168,144... | collective-permute-start | bytes 557576 | tf_op jit(solution)/shard_map/ppermute | solution.py:13
  166.3 2.6 %collective-permute-start.13 = (bf16[4,66,352]{2,1,0:T(8,128)(2,1)S(1)}, bf16[4,66,352]{2,1,0:T(8,128)(2,1)S(1)}, u32[]{:S(2)}, u32[]{:S(2)}) collective-permute-start(bf16[4,66,352]{2,1,0:T(8,128)(2,1)S(1)} %collective-permute-done.12), channel_id=1, source_target_pairs={{0,24},{24,48},{48,72},{72,96},{96,120},{120,144},{144,168},{168,0... | collective-permute-start | bytes 557576 | tf_op jit(solution)/shard_map/ppermute | solution.py:13
  168.9 1.7 bitcast_dynamic-update-slice_fusion.12
  170.6 3.9 %collective-permute-start.11 = (bf16[4,66,352]{2,1,0:T(8,128)(2,1)S(1)}, bf16[4,66,352]{2,1,0:T(8,128)(2,1)S(1)}, u32[]{:S(2)}, u32[]{:S(2)}) collective-permute-start(bf16[4,66,352]{2,1,0:T(8,128)(2,1)S(1)} %collective-permute-done.10), channel_id=1, source_target_pairs={{0,168},{24,0},{48,24},{72,48},{96,72},{120,96},{144,120},{168,144... | collective-permute-start | bytes 557576 | tf_op jit(solution)/shard_map/ppermute | solution.py:13
  174.5 1.9 collective-permute-start.14
  176.4 0.7 bitcast_dynamic-update-slice_fusion.10
  177.1 5.3 %collective-permute-done.14 = bf16[4,66,352]{2,1,0:T(8,128)(2,1)S(1)} collective-permute-done((bf16[4,66,352]{2,1,0:T(8,128)(2,1)S(1)}, bf16[4,66,352]{2,1,0:T(8,128)(2,1)S(1)}, u32[]{:S(2)}, u32[]{:S(2)}) %collective-permute-start.14) | collective-permute-done | bytes 185888 | tf_op jit(solution)/shard_map/ppermute | solution.py:13
  182.4 1.9 collective-permute-start.15
  184.3 0.7 bitcast_dynamic-update-slice_fusion.8
  185.0 5.2 %collective-permute-done.15 = bf16[4,66,352]{2,1,0:T(8,128)(2,1)S(1)} collective-permute-done((bf16[4,66,352]{2,1,0:T(8,128)(2,1)S(1)}, bf16[4,66,352]{2,1,0:T(8,128)(2,1)S(1)}, u32[]{:S(2)}, u32[]{:S(2)}) %collective-permute-start.15) | collective-permute-done | bytes 185888 | tf_op jit(solution)/shard_map/ppermute | solution.py:13
  190.2 0.7 bitcast_dynamic-update-slice_fusion.6
  190.9 0.7 bitcast_dynamic-update-slice_fusion.4
  191.6 0.7 bitcast_dynamic-update-slice_fusion.2
  192.4 0.7 bitcast_dynamic-update-slice_fusion
  193.1 1.6 bitcast_dynamic-update-slice_fusion.15
  194.7 1.6 bitcast_dynamic-update-slice_fusion.13
  196.3 0.7 bitcast_dynamic-update-slice_fusion.11
  197.1 0.7 bitcast_dynamic-update-slice_fusion.9
  197.8 0.7 bitcast_dynamic-update-slice_fusion.7
  198.5 0.7 bitcast_dynamic-update-slice_fusion.5
  199.2 0.7 bitcast_dynamic-update-slice_fusion.3
  199.9 0.7 bitcast_dynamic-update-slice_fusion.1
  200.6 1.7 constant_dynamic-slice_fusion
  202.3 1.2 copy-done.1
  203.5 1.7 copy.17
  205.2 9.1 %collective-permute-start.16 = (bf16[8,4,66,352]{3,0,2,1:T(8,128)(2,1)}, bf16[8,4,66,352]{3,0,2,1:T(8,128)(2,1)}, u32[]{:S(2)}, u32[]{:S(2)}) collective-permute-start(bf16[8,4,66,352]{3,0,2,1:T(8,128)(2,1)} %copy.17), channel_id=1, source_target_pairs={{0,12},{12,0},{1,13},{13,1},{2,14},{14,2},{3,15},{15,3},{4,16},{16... | collective-permute-start | bytes 4460552 | tf_op jit(solution)/shard_map/ppermute | solution.py:13
  214.4 2.5 %reshape.452 = bf16[64,4224]{1,0:T(8,128)(2,1)} reshape(bf16[64,12,352]{2,1,0:T(8,128)(2,1)} %copy.13) | data formatting | bytes 1081344 | tf_op jit(solution)/shard_map/reshape | solution.py:87
  216.9 2.0 copy.22
  219.0 4.9 %fusion = (f32[352]{0:T(512)S(1)}, f32[352]{0:T(512)S(1)}, bf16[4,8,2,66,352]{4,1,3,0,2:T(8,128)(2,1)S(1)}) fusion(s32[352]{0:T(512)S(1)} %iota_add_fusion, s32[4,8,2,66]{1,3,0,2:T(8,128)S(1)} %multiply_add_fusion, s32[]{:T(128)S(6)} %select_n.49, bf16[1,8,4,66,352]{4,1,3,2,0:T(8,128)(2,1)} %bitcast.18, bf16[1,8,4,66,352]{4,1,3,2,0:T(8,128)(2,1)S(1)} %bitcast.73), kind=kLoop, calls=%fused_computation.2 | loop fusion | flops 13380928 | bytes 5968516 | tf_op jit(solution)/shard_map/reduce_sum | solution.py:104
  223.9 2.2 copy.19
  226.2 5.8 %reshape.453 = bf16[4224,352]{1,0:T(8,128)(2,1)} reshape(bf16[4,8,2,66,352]{4,3,2,1,0:T(8,128)(2,1)} %copy.19) | data formatting | bytes 5947392 | tf_op jit(solution)/shard_map/reshape | solution.py:99
  232.0 3.3 %fusion.10 = bf16[64,352]{1,0:T(8,128)(2,1)} fusion(bf16[64,4224]{1,0:T(8,128)(2,1)} %reshape.452, bf16[4224,352]{1,0:T(8,128)(2,1)} %reshape.453, f32[352]{0:T(512)S(1)} %get-tuple-element.46, f32[352]{0:T(512)S(1)} %multiply_add_fusion.1, f32[352]{0:T(512)S(1)} %get-tuple-element.47, f32[352]{0:T(512)S(1)} %broadcast_multiply_fusion, ...), kind=kOutput, calls=%fused_computation.20 | convolution fusion | flops 190496768 | bytes 3655168 | tf_op jit(solution)/shard_map/dot_general | solution.py:107
  (43 shorter events, 5.7 us)
Async XLA Ops:
  6.5 1.8 copy-start
  6.5 107.6 %all-gather.3.cloned.1.call-start = ((), (), s32[]{:S(2)}) async-start(), calls=%async_computation.1 | async-start | bytes 6389760 | tf_op jit(solution)/shard_map/all_gather | solution.py:76
  11.4 13.2 %collective-permute-start = (f32[2,1,1,352]{3,2,1,0:T(1,128)S(1)}, f32[2,1,1,352]{3,2,1,0:T(1,128)S(1)}, u32[]{:S(2)}, u32[]{:S(2)}) collective-permute-start(f32[2,1,1,352]{3,2,1,0:T(1,128)S(1)} %pad_maximum_fusion), channel_id=1, source_target_pairs={{0,12},{12,0},{1,13},{13,1},{2,14},{14,2},{3,15},{15,3},{4,16},{16... | collective-permute-start | bytes 8456 | tf_op jit(solution)/shard_map/ppermute | solution.py:46
  24.7 4.3 %collective-permute-start.1 = (f32[2,1,1,352]{3,2,1,0:T(1,128)S(1)}, f32[2,1,1,352]{3,2,1,0:T(1,128)S(1)}, u32[]{:S(2)}, u32[]{:S(2)}) collective-permute-start(f32[2,1,1,352]{3,2,1,0:T(1,128)S(1)} %pad_maximum_fusion.1), channel_id=1, source_target_pairs={{0,24},{24,0},{48,72},{72,48},{96,120},{120,96},{144,168},{168,144... | collective-permute-start | bytes 8456 | tf_op jit(solution)/shard_map/ppermute | solution.py:46
  29.1 5.2 %collective-permute-start.2 = (f32[2,1,1,352]{3,2,1,0:T(1,128)S(1)}, f32[2,1,1,352]{3,2,1,0:T(1,128)S(1)}, u32[]{:S(2)}, u32[]{:S(2)}) collective-permute-start(f32[2,1,1,352]{3,2,1,0:T(1,128)S(1)} %pad_maximum_fusion.2), channel_id=1, source_target_pairs={{0,48},{24,72},{48,0},{72,24},{96,144},{120,168},{144,96},{168,120... | collective-permute-start | bytes 8456 | tf_op jit(solution)/shard_map/ppermute | solution.py:46
  34.4 8.3 %collective-permute-start.3 = (f32[2,1,1,352]{3,2,1,0:T(1,128)S(1)}, f32[2,1,1,352]{3,2,1,0:T(1,128)S(1)}, u32[]{:S(2)}, u32[]{:S(2)}) collective-permute-start(f32[2,1,1,352]{3,2,1,0:T(1,128)S(1)} %pad_maximum_fusion.3), channel_id=1, source_target_pairs={{0,96},{24,120},{48,144},{72,168},{96,0},{120,24},{144,48},{168,72... | collective-permute-start | bytes 8456 | tf_op jit(solution)/shard_map/ppermute | solution.py:46
  42.7 4.3 %collective-permute-start.4 = (f32[2,1,1,352]{3,2,1,0:T(1,128)S(1)}, f32[2,1,1,352]{3,2,1,0:T(1,128)S(1)}, u32[]{:S(2)}, u32[]{:S(2)}) collective-permute-start(f32[2,1,1,352]{3,2,1,0:T(1,128)S(1)} %pad_maximum_fusion.4), channel_id=1, source_target_pairs={{0,192},{192,0},{384,576},{576,384},{1,193},{193,1},{385,577},{577... | collective-permute-start | bytes 8456 | tf_op jit(solution)/shard_map/ppermute | solution.py:46
  47.1 5.8 %collective-permute-start.5 = (f32[2,1,1,352]{3,2,1,0:T(1,128)S(1)}, f32[2,1,1,352]{3,2,1,0:T(1,128)S(1)}, u32[]{:S(2)}, u32[]{:S(2)}) collective-permute-start(f32[2,1,1,352]{3,2,1,0:T(1,128)S(1)} %pad_maximum_fusion.5), channel_id=1, source_target_pairs={{0,384},{192,576},{384,0},{576,192},{1,385},{193,577},{385,1},{577... | collective-permute-start | bytes 8456 | tf_op jit(solution)/shard_map/ppermute | solution.py:46
  83.9 49.4 %all-to-all-start = ((bf16[64,64,66]{2,0,1:T(8,128)(2,1)}), bf16[64,64,66]{2,0,1:T(8,128)(2,1)}, u32[]{:S(2)}, u32[]{:S(2)}) async-start(bf16[64,64,66]{2,0,1:T(8,128)(2,1)} %copy.15), calls=%async_computation | async-start | bytes 2097152 | tf_op jit(solution)/shard_map/all_to_all | solution.py:89
  137.8 6.8 %collective-permute-start.7 = (bf16[66,352]{1,0:T(8,128)(2,1)S(1)}, bf16[66,352]{1,0:T(8,128)(2,1)S(1)}, u32[]{:S(2)}, u32[]{:S(2)}) collective-permute-start(bf16[66,352]{1,0:T(8,128)(2,1)S(1)} %get-tuple-element.49), channel_id=1, source_target_pairs={{0,192},{192,384},{384,576},{576,0},{1,193},{193,385},{385,577},{5... | collective-permute-start | bytes 139400 | tf_op jit(solution)/shard_map/ppermute | solution.py:13
  140.0 6.5 %collective-permute-start.6 = (bf16[66,352]{1,0:T(8,128)(2,1)S(1)}, bf16[66,352]{1,0:T(8,128)(2,1)S(1)}, u32[]{:S(2)}, u32[]{:S(2)}) collective-permute-start(bf16[66,352]{1,0:T(8,128)(2,1)S(1)} %get-tuple-element.49), channel_id=1, source_target_pairs={{0,576},{192,0},{384,192},{576,384},{1,577},{193,1},{385,193},{577... | collective-permute-start | bytes 139400 | tf_op jit(solution)/shard_map/ppermute | solution.py:13
  144.6 6.1 %collective-permute-start.8 = (bf16[66,352]{1,0:T(8,128)(2,1)S(1)}, bf16[66,352]{1,0:T(8,128)(2,1)S(1)}, u32[]{:S(2)}, u32[]{:S(2)}) collective-permute-start(bf16[66,352]{1,0:T(8,128)(2,1)S(1)} %collective-permute-done.7), channel_id=1, source_target_pairs={{0,192},{192,384},{384,576},{576,0},{1,193},{193,385},{385,577},{5... | collective-permute-start | bytes 139400 | tf_op jit(solution)/shard_map/ppermute | solution.py:13
  156.2 7.4 %collective-permute-start.9 = (bf16[4,66,352]{2,1,0:T(8,128)(2,1)}, bf16[4,66,352]{2,1,0:T(8,128)(2,1)}, u32[]{:S(2)}, u32[]{:S(2)}) collective-permute-start(bf16[4,66,352]{2,1,0:T(8,128)(2,1)} %get-tuple-element.21), channel_id=1, source_target_pairs={{0,168},{24,0},{48,24},{72,48},{96,72},{120,96},{144,120},{168,144... | collective-permute-start | bytes 557576 | tf_op jit(solution)/shard_map/ppermute | solution.py:13
  158.1 8.2 %collective-permute-start.12 = (bf16[4,66,352]{2,1,0:T(8,128)(2,1)}, bf16[4,66,352]{2,1,0:T(8,128)(2,1)S(1)}, u32[]{:S(2)}, u32[]{:S(2)}) collective-permute-start(bf16[4,66,352]{2,1,0:T(8,128)(2,1)} %get-tuple-element.21), channel_id=1, source_target_pairs={{0,24},{24,48},{48,72},{72,96},{96,120},{120,144},{144,168},{168,0... | collective-permute-start | bytes 557576 | tf_op jit(solution)/shard_map/ppermute | solution.py:13
  163.6 7.0 %collective-permute-start.10 = (bf16[4,66,352]{2,1,0:T(8,128)(2,1)}, bf16[4,66,352]{2,1,0:T(8,128)(2,1)S(1)}, u32[]{:S(2)}, u32[]{:S(2)}) collective-permute-start(bf16[4,66,352]{2,1,0:T(8,128)(2,1)} %collective-permute-done.9), channel_id=1, source_target_pairs={{0,168},{24,0},{48,24},{72,48},{96,72},{120,96},{144,120},{168,144... | collective-permute-start | bytes 557576 | tf_op jit(solution)/shard_map/ppermute | solution.py:13
  166.3 8.2 %collective-permute-start.13 = (bf16[4,66,352]{2,1,0:T(8,128)(2,1)S(1)}, bf16[4,66,352]{2,1,0:T(8,128)(2,1)S(1)}, u32[]{:S(2)}, u32[]{:S(2)}) collective-permute-start(bf16[4,66,352]{2,1,0:T(8,128)(2,1)S(1)} %collective-permute-done.12), channel_id=1, source_target_pairs={{0,24},{24,48},{48,72},{72,96},{96,120},{120,144},{144,168},{168,0... | collective-permute-start | bytes 557576 | tf_op jit(solution)/shard_map/ppermute | solution.py:13
  170.6 13.7 %collective-permute-start.11 = (bf16[4,66,352]{2,1,0:T(8,128)(2,1)S(1)}, bf16[4,66,352]{2,1,0:T(8,128)(2,1)S(1)}, u32[]{:S(2)}, u32[]{:S(2)}) collective-permute-start(bf16[4,66,352]{2,1,0:T(8,128)(2,1)S(1)} %collective-permute-done.10), channel_id=1, source_target_pairs={{0,168},{24,0},{48,24},{72,48},{96,72},{120,96},{144,120},{168,144... | collective-permute-start | bytes 557576 | tf_op jit(solution)/shard_map/ppermute | solution.py:13
  174.5 7.9 %collective-permute-start.14 = (bf16[4,66,352]{2,1,0:T(8,128)(2,1)S(1)}, bf16[4,66,352]{2,1,0:T(8,128)(2,1)S(1)}, u32[]{:S(2)}, u32[]{:S(2)}) collective-permute-start(bf16[4,66,352]{2,1,0:T(8,128)(2,1)S(1)} %collective-permute-done.13), channel_id=1, source_target_pairs={{0,24},{24,48},{48,72},{72,96},{96,120},{120,144},{144,168},{168,0... | collective-permute-start | bytes 557576 | tf_op jit(solution)/shard_map/ppermute | solution.py:13
  182.4 7.9 %collective-permute-start.15 = (bf16[4,66,352]{2,1,0:T(8,128)(2,1)S(1)}, bf16[4,66,352]{2,1,0:T(8,128)(2,1)S(1)}, u32[]{:S(2)}, u32[]{:S(2)}) collective-permute-start(bf16[4,66,352]{2,1,0:T(8,128)(2,1)S(1)} %collective-permute-done.14), channel_id=1, source_target_pairs={{0,24},{24,48},{48,72},{72,96},{96,120},{120,144},{144,168},{168,0... | collective-permute-start | bytes 557576 | tf_op jit(solution)/shard_map/ppermute | solution.py:13
  202.3 1.2 copy-start.1
  205.2 13.8 %collective-permute-start.16 = (bf16[8,4,66,352]{3,0,2,1:T(8,128)(2,1)}, bf16[8,4,66,352]{3,0,2,1:T(8,128)(2,1)}, u32[]{:S(2)}, u32[]{:S(2)}) collective-permute-start(bf16[8,4,66,352]{3,0,2,1:T(8,128)(2,1)} %copy.17), channel_id=1, source_target_pairs={{0,12},{12,0},{1,13},{13,1},{2,14},{14,2},{3,15},{15,3},{4,16},{16... | collective-permute-start | bytes 4460552 | tf_op jit(solution)/shard_map/ppermute | solution.py:13
Sparse Core Ops, SparseCore 0:
  11.5 102.5 all-gather.2

commit v9 on v7

--- a/solution.py
+++ b/solution.py
@@ -83,16 +83,19 @@
     first_all = (centered0 / jnp.sqrt(var0 + eps)).astype(jnp.bfloat16)
     first = ((feats[0] - mean0) / jnp.sqrt(var0 + eps)).astype(jnp.bfloat16)
     inv_std0 = 1.0 / jnp.sqrt(var0 + eps)
-    mean1, var1 = dp_stats(feats[1:])
-    second = ((feats[1] - mean1[0]) / jnp.sqrt(var1[0] + eps)).astype(jnp.bfloat16)
     n_mp = lax.axis_size("mp")
-    stacked = lax.all_gather(second, "mp", axis=0)
-    second_full = jnp.transpose(stacked, (1, 0, 2)).reshape(local, n_mp * rows)
-    width = second_full.shape[1] // dp_count
-    columns = lax.all_to_all(second_full, DP, split_axis=1, concat_axis=0, tiled=True)
+    stacked = lax.all_gather(feats[1], "mp", axis=0)
+    raw_full = jnp.transpose(stacked, (1, 0, 2)).reshape(local, n_mp * rows)
+    width = raw_full.shape[1] // dp_count
+    raw_cols = lax.all_to_all(raw_full, DP, split_axis=1, concat_axis=0, tiled=True)
+    mean_c = jnp.sum(raw_cols, axis=0, keepdims=True) / total
+    centered_c = raw_cols - mean_c
+    var_c = jnp.sum(centered_c * centered_c, axis=0, keepdims=True) / total
+    columns = (centered_c / jnp.sqrt(var_c + eps)).astype(jnp.bfloat16)
+    mean1, var1 = dp_stats(raw_full[None])
+    second_full = ((raw_full - mean1[0]) / jnp.sqrt(var1[0] + eps)).astype(jnp.bfloat16)
     second_perm = relative_order(second_full.reshape(local, nx, ny, nc, width), ("x", "y", "c"))
     second_perm = jnp.transpose(second_perm, (0, 3, 2, 1, 4)).reshape(local, dp_count * width)
-    columns, second_perm = lax.optimization_barrier((columns, second_perm))
     corr = (
         jnp.einsum("bi,bj->ij", first_all, columns, preferred_element_type=jnp.float32)
         / total
@@ -102,6 +105,7 @@
     grad_block = jnp.where(row_ids == col_ids, 2.0 * (corr - 1.0), 2.0 * off_weight * corr).astype(
         jnp.bfloat16
     )
+    grad_block, second_perm = lax.optimization_barrier((grad_block, second_perm))
     grad_t = dp_ring_gather(grad_block.T).reshape(dp_count * width, rows)
     t = lax.iota(jnp.int32, width)
     cc = (lax.iota(jnp.int32, nc) + ic) % nc

time: 226 us -> 308 us (1.36)
  waiting for transfers between devices: 46.4 us -> 132 us
  blocking collectives: 22.7 us -> 0 us
  other arithmetic: 25.6 us -> 34.7 us
  local copies, waits for them, and re-layouts: 30.9 us -> 37.6 us
    all_gather x0 -> x1, waiting for transfers between devices: none -> 59.9 us  [shards(): stacked = lax.all_gather(feats[1], 'mp', axis=0)]
    all_to_all x1, waiting for transfers between devices: 4.93 us -> 41.6 us  [shards(): lax.all_to_all(raw_full, DP, split_axis=1, concat_axis=0, tiled=True)]
    all_gather x1 -> x0, blocking collectives: 22.7 us -> none  [shards(): stacked = lax.all_gather(second, 'mp', axis=0)]
    ppermute x6, waiting for transfers between devices: 19.2 us -> 7.75 us  [combine(): other = lax.ppermute(jnp.stack([mean, m2]), axis, pairs)]
    ppermute x6, starting transfers between devices: 22 us -> 31.9 us  [combine(): other = lax.ppermute(jnp.stack([mean, m2]), axis, pairs)]
    all_to_all x1, starting transfers between devices: 20.4 us -> 12.9 us  [shards(): lax.all_to_all(raw_full, DP, split_axis=1, concat_axis=0, tiled=True)]
    reshape x0 -> x1, local copies, waits for them, and re-layouts: none -> 6.22 us  [shards(): raw_full = jnp.transpose(stacked, (1, 0, 2)).reshape(local, n_mp * rows)]
    another operation x1 -> x0, local copies, waits for them, and re-layouts: 6.12 us -> none  [shards(): second_full.reshape(local, nx, ny, nc, width)]
  transfers between devices with their start and end apart: 19 -> 20, of which waited for: 14 -> 14; matrix products, arithmetic and copies ran while one was open for 14% -> 15% of each run, Pallas kernels for 0% -> 0%
where the time goes in v9:
time: 308 us; the launch traced here: 306 us
  waiting for transfers between devices  132 us (43%)
  starting transfers between devices  80.2 us (26%)
  local copies, waits for them, and re-layouts  37.6 us (12%)
  other arithmetic  34.7 us (11%)
  between operations  14 us (5%)
  matrix products  7.66 us (2%)
    all_gather x1, waiting for transfers between devices, shards(): stacked = lax.all_gather(feats[1], 'mp', axis=0)  59.9 us
    all_to_all x1, waiting for transfers between devices, shards(): lax.all_to_all(raw_full, DP, split_axis=1, concat_axis=0, tiled=True)  41.6 us
    ppermute x11, starting transfers between devices, shift(): return lax.ppermute(v, axis, [(i, (i + step) % n) for i in range(n)])  35.3 us
    ppermute x6, starting transfers between devices, combine(): other = lax.ppermute(jnp.stack([mean, m2]), axis, pairs)  31.9 us
    ppermute x11, waiting for transfers between devices, shift(): return lax.ppermute(v, axis, [(i, (i + step) % n) for i in range(n)])  22.4 us
    all_to_all x1, starting transfers between devices, shards(): lax.all_to_all(raw_full, DP, split_axis=1, concat_axis=0, tiled=True)  12.9 us
    all_to_all x3, local copies, waits for them, and re-layouts, shards(): lax.all_to_all(raw_full, DP, split_axis=1, concat_axis=0, tiled=True)  10.9 us
    ppermute x6, waiting for transfers between devices, combine(): other = lax.ppermute(jnp.stack([mean, m2]), axis, pairs)  7.75 us
  transfers between devices with their start and end apart: 20, of which 14 were waited for; matrix products, arithmetic and copies ran while one was open for 15% of the time, Pallas kernels for 0%

profile of v9, /device:TPU:1, one launch (start us, length us, event | category | flops | bytes accessed | tf_op | source)
XLA Modules:
  0.0 306.5 jit_solution(1098180580440082735)
XLA Ops:
  6.5 1.8 copy-done
  8.4 2.3 fusion.3
  10.7 0.7 copy-done.2
  11.4 0.7 fusion.24
  12.1 0.7 all-gather.6.cloned.1.call-update
  12.8 59.9 %all-gather.4.cloned.1.call-done = f32[12,64,352]{2,1,0:T(8,128)} async-done(((f32[1,64,352]{2,1,0:T(8,128)}), f32[12,64,352]{2,1,0:T(8,128)}) %all-gather.4.cloned.1.call-update) | async-done | bytes 1081360 | tf_op jit(solution)/shard_map/all_gather | solution.py:87
  72.7 1.4 bitcast_reduce_fusion
  74.2 1.4 multiply_reduce_fusion.1
  75.8 9.7 %collective-permute-start = (f32[2,1,1,4224]{3,2,1,0:T(1,128)S(1)}, f32[2,1,1,4224]{3,2,1,0:T(1,128)S(1)}, u32[]{:S(2)}, u32[]{:S(2)}) collective-permute-start(f32[2,1,1,4224]{3,2,1,0:T(1,128)S(1)} %pad_maximum_fusion.2), channel_id=1, source_target_pairs={{0,12},{12,0},{1,13},{13,1},{2,14},{14,2},{3,15},{15,3},{4,16},{16... | collective-permute-start | bytes 101384 | tf_op jit(solution)/shard_map/ppermute | solution.py:41
  85.4 0.8 collective-permute-done
  86.4 3.1 %collective-permute-start.1 = (f32[2,1,1,4224]{3,2,1,0:T(1,128)S(1)}, f32[2,1,1,4224]{3,2,1,0:T(1,128)S(1)}, u32[]{:S(2)}, u32[]{:S(2)}) collective-permute-start(f32[2,1,1,4224]{3,2,1,0:T(1,128)S(1)} %pad_maximum_fusion.3), channel_id=1, source_target_pairs={{0,24},{24,0},{48,72},{72,48},{96,120},{120,96},{144,168},{168,144... | collective-permute-start | bytes 101384 | tf_op jit(solution)/shard_map/ppermute | solution.py:41
  89.6 1.5 collective-permute-done.1
  91.3 4.0 %collective-permute-start.2 = (f32[2,1,1,4224]{3,2,1,0:T(1,128)S(1)}, f32[2,1,1,4224]{3,2,1,0:T(1,128)S(1)}, u32[]{:S(2)}, u32[]{:S(2)}) collective-permute-start(f32[2,1,1,4224]{3,2,1,0:T(1,128)S(1)} %pad_maximum_fusion.4), channel_id=1, source_target_pairs={{0,48},{24,72},{48,0},{72,24},{96,144},{120,168},{144,96},{168,120... | collective-permute-start | bytes 101384 | tf_op jit(solution)/shard_map/ppermute | solution.py:41
  95.3 1.5 collective-permute-done.2
  97.0 7.5 %collective-permute-start.3 = (f32[2,1,1,4224]{3,2,1,0:T(1,128)S(1)}, f32[2,1,1,4224]{3,2,1,0:T(1,128)S(1)}, u32[]{:S(2)}, u32[]{:S(2)}) collective-permute-start(f32[2,1,1,4224]{3,2,1,0:T(1,128)S(1)} %pad_maximum_fusion.5), channel_id=1, source_target_pairs={{0,96},{24,120},{48,144},{72,168},{96,0},{120,24},{144,48},{168,72... | collective-permute-start | bytes 101384 | tf_op jit(solution)/shard_map/ppermute | solution.py:41
  104.5 1.7 collective-permute-done.3
  106.4 3.1 %collective-permute-start.4 = (f32[2,1,1,4224]{3,2,1,0:T(1,128)S(1)}, f32[2,1,1,4224]{3,2,1,0:T(1,128)S(1)}, u32[]{:S(2)}, u32[]{:S(2)}) collective-permute-start(f32[2,1,1,4224]{3,2,1,0:T(1,128)S(1)} %pad_maximum_fusion.6), channel_id=1, source_target_pairs={{0,192},{192,0},{384,576},{576,384},{1,193},{193,1},{385,577},{577... | collective-permute-start | bytes 101384 | tf_op jit(solution)/shard_map/ppermute | solution.py:41
  109.5 2.1 collective-permute-done.4
  111.8 4.5 %collective-permute-start.5 = (f32[2,1,1,4224]{3,2,1,0:T(1,128)S(1)}, f32[2,1,1,4224]{3,2,1,0:T(1,128)S(1)}, u32[]{:S(2)}, u32[]{:S(2)}) collective-permute-start(f32[2,1,1,4224]{3,2,1,0:T(1,128)S(1)} %pad_maximum_fusion.7), channel_id=1, source_target_pairs={{0,384},{192,576},{384,0},{576,192},{1,385},{193,577},{385,1},{577... | collective-permute-start | bytes 101384 | tf_op jit(solution)/shard_map/ppermute | solution.py:41
  116.6 3.1 %copy.7 = f32[64,12,352]{2,1,0:T(8,128)} copy(f32[64,12,352]{2,0,1:T(8,128)} %bitcast.66) | data formatting | bytes 2162688 | tf_op jit(solution)/shard_map/transpose | solution.py:88
  119.7 6.2 %reshape.592 = f32[64,4,8,2,66]{4,3,2,1,0:T(2,128)} reshape(f32[64,12,352]{2,1,0:T(8,128)} %copy.7) | data formatting | bytes 2162688 | tf_op jit(solution)/shard_map/reshape | solution.py:88
  126.0 4.0 %all_to_all.14 = f32[64,64,66]{2,1,0:T(8,128)} reshape(f32[64,12,352]{2,1,0:T(8,128)} %copy.7) | data formatting | bytes 2162688 | tf_op jit(solution)/shard_map/all_to_all | solution.py:90
  130.0 4.1 %copy.8 = f32[64,64,66]{2,0,1:T(8,128)} copy(f32[64,64,66]{2,1,0:T(8,128)} %all_to_all.14) | data formatting | bytes 2162688 | tf_op jit(solution)/shard_map/all_to_all | solution.py:90
  134.1 12.9 %all-to-all-start = ((f32[64,64,66]{2,0,1:T(8,128)}), f32[64,64,66]{2,0,1:T(8,128)}, u32[]{:S(2)}, u32[]{:S(2)}) async-start(f32[64,64,66]{2,0,1:T(8,128)} %copy.8), calls=%async_computation | async-start | bytes 4194304 | tf_op jit(solution)/shard_map/all_to_all | solution.py:90
  147.6 0.2 squeeze.45
  148.9 0.2 add_multiply_fusion
  149.2 2.9 fusion.7
  152.1 3.2 %fusion.11 = bf16[64,4,8,2,66]{4,3,2,1,0:T(2,128)(2,1)S(1)} fusion(s32[]{:T(128)S(6)} %select_n.74, bf16[64,4,8,2,66]{4,3,2,1,0:T(2,128)(2,1)S(1)} %fusion.7), kind=kLoop, calls=%fused_computation.29 | loop fusion | flops 270336 | bytes 1081348 | tf_op jit(solution)/shard_map/jit(_roll_dynamic)/concatenate | solution.py:65
  155.3 4.1 %fusion.10 = bf16[64,4,8,2,66]{4,3,2,1,0:T(2,128)(2,1)S(1)} fusion(s32[]{:T(128)S(6)} %select_n.76, bf16[64,4,8,2,66]{4,3,2,1,0:T(2,128)(2,1)S(1)} %fusion.11), kind=kLoop, calls=%fused_computation.28 | loop fusion | flops 270336 | bytes 1081348 | tf_op jit(solution)/shard_map/jit(_roll_dynamic)/concatenate | solution.py:65
  159.4 4.7 %fusion.13 = bf16[64,2,8,4,66]{4,1,2,3,0:T(2,128)(2,1)S(1)} fusion(s32[]{:T(128)S(6)} %select_n.78, bf16[64,4,8,2,66]{4,3,2,1,0:T(2,128)(2,1)S(1)} %fusion.10), kind=kLoop, calls=%fused_computation.31 | loop fusion | flops 1081344 | bytes 1081348 | tf_op jit(solution)/shard_map/transpose | solution.py:98
  164.1 1.6 copy.11
  165.7 2.5 reshape.593
  168.2 41.6 %all-to-all-done = f32[64,64,66]{2,0,1:T(8,128)} async-done(((f32[64,64,66]{2,0,1:T(8,128)}), f32[64,64,66]{2,0,1:T(8,128)}, u32[]{:S(2)}, u32[]{:S(2)}) %all-to-all-start) | async-done | bytes 1081376 | tf_op jit(solution)/shard_map/all_to_all | solution.py:90
  209.8 2.8 copy.14
  212.6 2.1 reduce_sum.76
  214.7 2.1 fusion.6
  216.9 3.4 %reduce_sum.74 = f32[352]{0:T(512)S(1)} reduce(f32[1,4096,352]{2,1,0:T(8,128)} %all-gather.6.cloned.1.call-done, f32[]{:T(128)} %constant.136.clone.1), dimensions={0,1}, to_apply=%region_0.0 | reduce | flops 1441440 | bytes 5768580 | tf_op jit(solution)/shard_map/reduce_sum | solution.py:80
  220.3 3.7 %multiply_reduce_fusion = f32[352]{0:T(512)S(1)} fusion(f32[1,4096,352]{2,1,0:T(8,128)} %all-gather.6.cloned.1.call-done, f32[352]{0:T(512)S(1)} %broadcast_multiply_fusion.1), kind=kLoop, calls=%fused_computation.6 | loop fusion | flops 4325024 | bytes 5769984 | tf_op jit(solution)/shard_map/reduce_sum | solution.py:82
  224.0 0.8 copy-done.1
  224.9 2.2 select_convert_fusion
  227.1 2.4 collective-permute-start.7
  229.4 4.1 %collective-permute-start.6 = (bf16[66,352]{1,0:T(8,128)(2,1)S(1)}, bf16[66,352]{1,0:T(8,128)(2,1)S(1)}, u32[]{:S(2)}, u32[]{:S(2)}) collective-permute-start(bf16[66,352]{1,0:T(8,128)(2,1)S(1)} %bitcast.68), channel_id=1, source_target_pairs={{0,576},{192,0},{384,192},{576,384},{1,577},{193,1},{385,193},{577... | collective-permute-start | bytes 139400 | tf_op jit(solution)/shard_map/ppermute | solution.py:13
  233.6 0.4 collective-permute-done.7
  234.0 1.9 collective-permute-start.8
  235.9 4.2 %collective-permute-done.8 = bf16[66,352]{1,0:T(8,128)(2,1)S(1)} collective-permute-done((bf16[66,352]{1,0:T(8,128)(2,1)S(1)}, bf16[66,352]{1,0:T(8,128)(2,1)S(1)}, u32[]{:S(2)}, u32[]{:S(2)}) %collective-permute-start.8) | collective-permute-done | bytes 46496 | tf_op jit(solution)/shard_map/ppermute | solution.py:13
  240.1 1.9 collective-permute-start.9
  242.1 3.4 %collective-permute-start.12 = (bf16[4,66,352]{2,1,0:T(8,128)(2,1)S(1)}, bf16[4,66,352]{2,1,0:T(8,128)(2,1)S(1)}, u32[]{:S(2)}, u32[]{:S(2)}) collective-permute-start(bf16[4,66,352]{2,1,0:T(8,128)(2,1)S(1)} %pad_maximum_fusion.1), channel_id=1, source_target_pairs={{0,24},{24,48},{48,72},{72,96},{96,120},{120,144},{144,168},{168,0... | collective-permute-start | bytes 557576 | tf_op jit(solution)/shard_map/ppermute | solution.py:13
  245.5 1.8 collective-permute-done.9
  247.3 3.3 %collective-permute-start.10 = (bf16[4,66,352]{2,1,0:T(8,128)(2,1)S(1)}, bf16[4,66,352]{2,1,0:T(8,128)(2,1)S(1)}, u32[]{:S(2)}, u32[]{:S(2)}) collective-permute-start(bf16[4,66,352]{2,1,0:T(8,128)(2,1)S(1)} %collective-permute-done.9), channel_id=1, source_target_pairs={{0,168},{24,0},{48,24},{72,48},{96,72},{120,96},{144,120},{168,144... | collective-permute-start | bytes 557576 | tf_op jit(solution)/shard_map/ppermute | solution.py:13
  250.6 2.0 collective-permute-start.13
  252.6 1.3 collective-permute-done.10
  254.0 4.5 %collective-permute-start.11 = (bf16[4,66,352]{2,1,0:T(8,128)(2,1)S(1)}, bf16[4,66,352]{2,1,0:T(8,128)(2,1)S(1)}, u32[]{:S(2)}, u32[]{:S(2)}) collective-permute-start(bf16[4,66,352]{2,1,0:T(8,128)(2,1)S(1)} %collective-permute-done.10), channel_id=1, source_target_pairs={{0,168},{24,0},{48,24},{72,48},{96,72},{120,96},{144,120},{168,144... | collective-permute-start | bytes 557576 | tf_op jit(solution)/shard_map/ppermute | solution.py:13
  258.5 1.9 collective-permute-start.14
  260.4 5.9 %collective-permute-done.14 = bf16[4,66,352]{2,1,0:T(8,128)(2,1)S(1)} collective-permute-done((bf16[4,66,352]{2,1,0:T(8,128)(2,1)S(1)}, bf16[4,66,352]{2,1,0:T(8,128)(2,1)S(1)}, u32[]{:S(2)}, u32[]{:S(2)}) %collective-permute-start.14) | collective-permute-done | bytes 185888 | tf_op jit(solution)/shard_map/ppermute | solution.py:13
  266.4 1.9 collective-permute-start.15
  268.3 5.9 %collective-permute-done.15 = bf16[4,66,352]{2,1,0:T(8,128)(2,1)S(1)} collective-permute-done((bf16[4,66,352]{2,1,0:T(8,128)(2,1)S(1)}, bf16[4,66,352]{2,1,0:T(8,128)(2,1)S(1)}, u32[]{:S(2)}, u32[]{:S(2)}) %collective-permute-start.15) | collective-permute-done | bytes 185888 | tf_op jit(solution)/shard_map/ppermute | solution.py:13
  274.4 0.6 copy.12
  275.0 8.0 %collective-permute-start.16 = (bf16[8,4,66,352]{3,0,2,1:T(8,128)(2,1)S(1)}, bf16[8,4,66,352]{3,0,2,1:T(8,128)(2,1)S(1)}, u32[]{:S(2)}, u32[]{:S(2)}) collective-permute-start(bf16[8,4,66,352]{3,0,2,1:T(8,128)(2,1)S(1)} %copy.12), channel_id=1, source_target_pairs={{0,12},{12,0},{1,13},{13,1},{2,14},{14,2},{3,15},{15,3},{4,16},{16... | collective-permute-start | bytes 4460552 | tf_op jit(solution)/shard_map/ppermute | solution.py:13
  283.3 2.8 collective-permute-done.16
  286.1 0.2 copy.16
  286.4 2.5 pad_maximum_fusion
  288.9 1.8 fusion
  290.6 5.8 %reshape.594 = bf16[4224,352]{1,0:T(8,128)(2,1)} reshape(bf16[2,8,4,66,352]{4,3,2,1,0:T(8,128)(2,1)} %pad_maximum_fusion) | data formatting | bytes 5947392 | tf_op jit(solution)/shard_map/reshape | solution.py:109
  296.5 3.2 %fusion.9 = bf16[64,352]{1,0:T(8,128)(2,1)} fusion(bf16[64,4224]{1,0:T(8,128)(2,1)S(1)} %reshape.593, bf16[4224,352]{1,0:T(8,128)(2,1)} %reshape.594, f32[352]{0:T(512)S(1)} %get-tuple-element.47, f32[352]{0:T(512)S(1)} %multiply_add_fusion.5, f32[352]{0:T(512)S(1)} %get-tuple-element.48, f32[352]{0:T(512)S(1)} %broadcast_multiply_fusion.1, ...), kind=kOutput, calls=%fused_computation.27 | convolution fusion | flops 190496768 | bytes 3655168 | tf_op jit(solution)/shard_map/dot_general | solution.py:124
  (62 shorter events, 3.7 us)
Async XLA Ops:
  6.5 1.8 copy-start
  6.5 66.2 %all-gather.4.cloned.1.call-start = ((), (), s32[]{:S(2)}) async-start(), calls=%async_computation.1 | async-start | bytes 1277952 | tf_op jit(solution)/shard_map/all_gather | solution.py:87
  10.7 0.7 copy-start.2
  12.1 204.8 %all-gather.6.cloned.1.call-start = ((), (), s32[]{:S(2)}) async-start(), calls=%async_computation.2 | async-start | bytes 6389760 | tf_op jit(solution)/shard_map/all_gather | solution.py:79
  75.8 10.5 %collective-permute-start = (f32[2,1,1,4224]{3,2,1,0:T(1,128)S(1)}, f32[2,1,1,4224]{3,2,1,0:T(1,128)S(1)}, u32[]{:S(2)}, u32[]{:S(2)}) collective-permute-start(f32[2,1,1,4224]{3,2,1,0:T(1,128)S(1)} %pad_maximum_fusion.2), channel_id=1, source_target_pairs={{0,12},{12,0},{1,13},{13,1},{2,14},{14,2},{3,15},{15,3},{4,16},{16... | collective-permute-start | bytes 101384 | tf_op jit(solution)/shard_map/ppermute | solution.py:41
  86.4 4.7 %collective-permute-start.1 = (f32[2,1,1,4224]{3,2,1,0:T(1,128)S(1)}, f32[2,1,1,4224]{3,2,1,0:T(1,128)S(1)}, u32[]{:S(2)}, u32[]{:S(2)}) collective-permute-start(f32[2,1,1,4224]{3,2,1,0:T(1,128)S(1)} %pad_maximum_fusion.3), channel_id=1, source_target_pairs={{0,24},{24,0},{48,72},{72,48},{96,120},{120,96},{144,168},{168,144... | collective-permute-start | bytes 101384 | tf_op jit(solution)/shard_map/ppermute | solution.py:41
  91.3 5.6 %collective-permute-start.2 = (f32[2,1,1,4224]{3,2,1,0:T(1,128)S(1)}, f32[2,1,1,4224]{3,2,1,0:T(1,128)S(1)}, u32[]{:S(2)}, u32[]{:S(2)}) collective-permute-start(f32[2,1,1,4224]{3,2,1,0:T(1,128)S(1)} %pad_maximum_fusion.4), channel_id=1, source_target_pairs={{0,48},{24,72},{48,0},{72,24},{96,144},{120,168},{144,96},{168,120... | collective-permute-start | bytes 101384 | tf_op jit(solution)/shard_map/ppermute | solution.py:41
  97.0 9.2 %collective-permute-start.3 = (f32[2,1,1,4224]{3,2,1,0:T(1,128)S(1)}, f32[2,1,1,4224]{3,2,1,0:T(1,128)S(1)}, u32[]{:S(2)}, u32[]{:S(2)}) collective-permute-start(f32[2,1,1,4224]{3,2,1,0:T(1,128)S(1)} %pad_maximum_fusion.5), channel_id=1, source_target_pairs={{0,96},{24,120},{48,144},{72,168},{96,0},{120,24},{144,48},{168,72... | collective-permute-start | bytes 101384 | tf_op jit(solution)/shard_map/ppermute | solution.py:41
  106.4 5.3 %collective-permute-start.4 = (f32[2,1,1,4224]{3,2,1,0:T(1,128)S(1)}, f32[2,1,1,4224]{3,2,1,0:T(1,128)S(1)}, u32[]{:S(2)}, u32[]{:S(2)}) collective-permute-start(f32[2,1,1,4224]{3,2,1,0:T(1,128)S(1)} %pad_maximum_fusion.6), channel_id=1, source_target_pairs={{0,192},{192,0},{384,576},{576,384},{1,193},{193,1},{385,577},{577... | collective-permute-start | bytes 101384 | tf_op jit(solution)/shard_map/ppermute | solution.py:41
  111.8 36.8 %collective-permute-start.5 = (f32[2,1,1,4224]{3,2,1,0:T(1,128)S(1)}, f32[2,1,1,4224]{3,2,1,0:T(1,128)S(1)}, u32[]{:S(2)}, u32[]{:S(2)}) collective-permute-start(f32[2,1,1,4224]{3,2,1,0:T(1,128)S(1)} %pad_maximum_fusion.7), channel_id=1, source_target_pairs={{0,384},{192,576},{384,0},{576,192},{1,385},{193,577},{385,1},{577... | collective-permute-start | bytes 101384 | tf_op jit(solution)/shard_map/ppermute | solution.py:41
  134.1 75.7 %all-to-all-start = ((f32[64,64,66]{2,0,1:T(8,128)}), f32[64,64,66]{2,0,1:T(8,128)}, u32[]{:S(2)}, u32[]{:S(2)}) async-start(f32[64,64,66]{2,0,1:T(8,128)} %copy.8), calls=%async_computation | async-start | bytes 4194304 | tf_op jit(solution)/shard_map/all_to_all | solution.py:90
  220.3 4.6 %copy-start.1 = (f32[1,4096,352]{2,1,0:T(8,128)S(1)}, f32[1,4096,352]{2,1,0:T(8,128)}, u32[]{:S(2)}) copy-start(f32[1,4096,352]{2,1,0:T(8,128)} %all-gather.6.cloned.1.call-done) | copy-start | bytes 17301508
  227.1 6.9 %collective-permute-start.7 = (bf16[66,352]{1,0:T(8,128)(2,1)S(1)}, bf16[66,352]{1,0:T(8,128)(2,1)S(1)}, u32[]{:S(2)}, u32[]{:S(2)}) collective-permute-start(bf16[66,352]{1,0:T(8,128)(2,1)S(1)} %bitcast.67), channel_id=1, source_target_pairs={{0,192},{192,384},{384,576},{576,0},{1,193},{193,385},{385,577},{5... | collective-permute-start | bytes 139400 | tf_op jit(solution)/shard_map/ppermute | solution.py:13
  229.4 6.4 %collective-permute-start.6 = (bf16[66,352]{1,0:T(8,128)(2,1)S(1)}, bf16[66,352]{1,0:T(8,128)(2,1)S(1)}, u32[]{:S(2)}, u32[]{:S(2)}) collective-permute-start(bf16[66,352]{1,0:T(8,128)(2,1)S(1)} %bitcast.68), channel_id=1, source_target_pairs={{0,576},{192,0},{384,192},{576,384},{1,577},{193,1},{385,193},{577... | collective-permute-start | bytes 139400 | tf_op jit(solution)/shard_map/ppermute | solution.py:13
  234.0 6.1 %collective-permute-start.8 = (bf16[66,352]{1,0:T(8,128)(2,1)S(1)}, bf16[66,352]{1,0:T(8,128)(2,1)S(1)}, u32[]{:S(2)}, u32[]{:S(2)}) collective-permute-start(bf16[66,352]{1,0:T(8,128)(2,1)S(1)} %collective-permute-done.7), channel_id=1, source_target_pairs={{0,192},{192,384},{384,576},{576,0},{1,193},{193,385},{385,577},{5... | collective-permute-start | bytes 139400 | tf_op jit(solution)/shard_map/ppermute | solution.py:13
  240.1 7.2 %collective-permute-start.9 = (bf16[4,66,352]{2,1,0:T(8,128)(2,1)S(1)}, bf16[4,66,352]{2,1,0:T(8,128)(2,1)S(1)}, u32[]{:S(2)}, u32[]{:S(2)}) collective-permute-start(bf16[4,66,352]{2,1,0:T(8,128)(2,1)S(1)} %pad_maximum_fusion.1), channel_id=1, source_target_pairs={{0,168},{24,0},{48,24},{72,48},{96,72},{120,96},{144,120},{168,144... | collective-permute-start | bytes 557576 | tf_op jit(solution)/shard_map/ppermute | solution.py:13
  242.1 8.5 %collective-permute-start.12 = (bf16[4,66,352]{2,1,0:T(8,128)(2,1)S(1)}, bf16[4,66,352]{2,1,0:T(8,128)(2,1)S(1)}, u32[]{:S(2)}, u32[]{:S(2)}) collective-permute-start(bf16[4,66,352]{2,1,0:T(8,128)(2,1)S(1)} %pad_maximum_fusion.1), channel_id=1, source_target_pairs={{0,24},{24,48},{48,72},{72,96},{96,120},{120,144},{144,168},{168,0... | collective-permute-start | bytes 557576 | tf_op jit(solution)/shard_map/ppermute | solution.py:13
  247.3 6.7 %collective-permute-start.10 = (bf16[4,66,352]{2,1,0:T(8,128)(2,1)S(1)}, bf16[4,66,352]{2,1,0:T(8,128)(2,1)S(1)}, u32[]{:S(2)}, u32[]{:S(2)}) collective-permute-start(bf16[4,66,352]{2,1,0:T(8,128)(2,1)S(1)} %collective-permute-done.9), channel_id=1, source_target_pairs={{0,168},{24,0},{48,24},{72,48},{96,72},{120,96},{144,120},{168,144... | collective-permute-start | bytes 557576 | tf_op jit(solution)/shard_map/ppermute | solution.py:13
  250.6 7.9 %collective-permute-start.13 = (bf16[4,66,352]{2,1,0:T(8,128)(2,1)S(1)}, bf16[4,66,352]{2,1,0:T(8,128)(2,1)S(1)}, u32[]{:S(2)}, u32[]{:S(2)}) collective-permute-start(bf16[4,66,352]{2,1,0:T(8,128)(2,1)S(1)} %collective-permute-done.12), channel_id=1, source_target_pairs={{0,24},{24,48},{48,72},{72,96},{96,120},{120,144},{144,168},{168,0... | collective-permute-start | bytes 557576 | tf_op jit(solution)/shard_map/ppermute | solution.py:13
  254.0 14.3 %collective-permute-start.11 = (bf16[4,66,352]{2,1,0:T(8,128)(2,1)S(1)}, bf16[4,66,352]{2,1,0:T(8,128)(2,1)S(1)}, u32[]{:S(2)}, u32[]{:S(2)}) collective-permute-start(bf16[4,66,352]{2,1,0:T(8,128)(2,1)S(1)} %collective-permute-done.10), channel_id=1, source_target_pairs={{0,168},{24,0},{48,24},{72,48},{96,72},{120,96},{144,120},{168,144... | collective-permute-start | bytes 557576 | tf_op jit(solution)/shard_map/ppermute | solution.py:13
  258.5 7.9 %collective-permute-start.14 = (bf16[4,66,352]{2,1,0:T(8,128)(2,1)S(1)}, bf16[4,66,352]{2,1,0:T(8,128)(2,1)S(1)}, u32[]{:S(2)}, u32[]{:S(2)}) collective-permute-start(bf16[4,66,352]{2,1,0:T(8,128)(2,1)S(1)} %collective-permute-done.13), channel_id=1, source_target_pairs={{0,24},{24,48},{48,72},{72,96},{96,120},{120,144},{144,168},{168,0... | collective-permute-start | bytes 557576 | tf_op jit(solution)/shard_map/ppermute | solution.py:13
  266.4 7.9 %collective-permute-start.15 = (bf16[4,66,352]{2,1,0:T(8,128)(2,1)S(1)}, bf16[4,66,352]{2,1,0:T(8,128)(2,1)S(1)}, u32[]{:S(2)}, u32[]{:S(2)}) collective-permute-start(bf16[4,66,352]{2,1,0:T(8,128)(2,1)S(1)} %collective-permute-done.14), channel_id=1, source_target_pairs={{0,24},{24,48},{48,72},{72,96},{96,120},{120,144},{144,168},{168,0... | collective-permute-start | bytes 557576 | tf_op jit(solution)/shard_map/ppermute | solution.py:13
  275.0 11.1 %collective-permute-start.16 = (bf16[8,4,66,352]{3,0,2,1:T(8,128)(2,1)S(1)}, bf16[8,4,66,352]{3,0,2,1:T(8,128)(2,1)S(1)}, u32[]{:S(2)}, u32[]{:S(2)}) collective-permute-start(bf16[8,4,66,352]{3,0,2,1:T(8,128)(2,1)S(1)} %copy.12), channel_id=1, source_target_pairs={{0,12},{12,0},{1,13},{13,1},{2,14},{14,2},{3,15},{15,3},{4,16},{16... | collective-permute-start | bytes 4460552 | tf_op jit(solution)/shard_map/ppermute | solution.py:13
Sparse Core Ops, SparseCore 0:
  12.2 60.4 all-gather.3
  76.6 117.7 all-gather.5

commit v10 on v7

--- a/solution.py
+++ b/solution.py
@@ -11,6 +11,14 @@
 
 def shift(v, axis, n, step):
     return lax.ppermute(v, axis, [(i, (i + step) % n) for i in range(n)])
+
+
+def direct_gather(v, axis):
+    n = lax.axis_size(axis)
+    got = {0: v}
+    for t in range(1, n):
+        got[t] = lax.ppermute(v, axis, [(i, (i - t) % n) for i in range(n)])
+    return jnp.stack([got[t] for t in range(n)])
 
 
 def ring_gather(v, axis):
@@ -32,7 +40,7 @@
 
 
 def dp_ring_gather(v):
-    return ring_gather(ring_gather(ring_gather(v, "x"), "y"), "c")
+    return ring_gather(ring_gather(direct_gather(v, "x"), "y"), "c")
 
 
 def combine(mean, m2, count, axis, k):
@@ -46,17 +54,33 @@
     return new_mean, new_m2, count * 2
 
 
+def combine_all(mean, m2, count, axis):
+    n = lax.axis_size(axis)
+    got = jnp.roll(direct_gather(jnp.stack([mean, m2]), axis), lax.axis_index(axis), axis=0)
+    means = [got[j, 0] for j in range(n)]
+    m2s = [got[j, 1] for j in range(n)]
+    while len(means) > 1:
+        new_means, new_m2s = [], []
+        for a in range(0, len(means), 2):
+            delta = means[a + 1] - means[a]
+            new_means.append((means[a] + means[a + 1]) * 0.5)
+            new_m2s.append((m2s[a] + m2s[a + 1]) + delta * delta * (count * 0.5))
+        means, m2s, count = new_means, new_m2s, count * 2
+    return means[0], m2s[0], count
+
+
 def dp_stats(feats):
     local = feats.shape[1]
     mean = jnp.sum(feats, axis=1, keepdims=True) / local
     dev = feats - mean
     m2 = jnp.sum(dev * dev, axis=1, keepdims=True)
     count = float(local)
-    for axis in ("c", "y", "x"):
+    for axis in ("c", "y"):
         k = 1
         while k < lax.axis_size(axis):
             mean, m2, count = combine(mean, m2, count, axis, k)
             k *= 2
+    mean, m2, count = combine_all(mean, m2, count, "x")
     return mean, m2 / count
 
 

time: 226 us -> 226 us (level)
    ppermute x0 -> x6, starting transfers between devices: none -> 15.9 us  [direct_gather(): got[t] = lax.ppermute(v, axis, [(i, (i - t) % n) for i in range(n)])]
    ppermute x11 -> x8, starting transfers between devices: 35.9 us -> 26.1 us  [shift(): return lax.ppermute(v, axis, [(i, (i + step) % n) for i in range(n)])]
    ppermute x0 -> x6, waiting for transfers between devices: none -> 7.58 us  [direct_gather(): got[t] = lax.ppermute(v, axis, [(i, (i - t) % n) for i in range(n)])]
    ppermute x6 -> x4, waiting for transfers between devices: 19.2 us -> 12.9 us  [combine(): other = lax.ppermute(jnp.stack([mean, m2]), axis, pairs)]
    ppermute x6 -> x4, starting transfers between devices: 22 us -> 18.2 us  [combine(): other = lax.ppermute(jnp.stack([mean, m2]), axis, pairs)]
    ppermute x11 -> x8, waiting for transfers between devices: 22.2 us -> 18.6 us  [shift(): return lax.ppermute(v, axis, [(i, (i + step) % n) for i in range(n)])]
  transfers between devices with their start and end apart: 19 -> 20, of which waited for: 14 -> 14; matrix products, arithmetic and copies ran while one was open for 14% -> 14% of each run, Pallas kernels for 0% -> 0%
where the time goes in v10:
time: 226 us; the launch traced here: 225 us
  starting transfers between devices  79.6 us (35%)
  waiting for transfers between devices  44.2 us (20%)
  local copies, waits for them, and re-layouts  30.9 us (14%)
  other arithmetic  25.5 us (11%)
  blocking collectives  23.4 us (10%)
  between operations  13.9 us (6%)
  matrix products  7.54 us (3%)
    ppermute x8, starting transfers between devices, shift(): return lax.ppermute(v, axis, [(i, (i + step) % n) for i in range(n)])  26.1 us
    all_gather x1, blocking collectives, shards(): stacked = lax.all_gather(second, 'mp', axis=0)  23.4 us
    all_to_all x1, starting transfers between devices, shards(): lax.all_to_all(second_full, DP, split_axis=1, concat_axis=0, tiled=True)  19.4 us
    ppermute x8, waiting for transfers between devices, shift(): return lax.ppermute(v, axis, [(i, (i + step) % n) for i in range(n)])  18.6 us
    ppermute x4, starting transfers between devices, combine(): other = lax.ppermute(jnp.stack([mean, m2]), axis, pairs)  18.2 us
    ppermute x6, starting transfers between devices, direct_gather(): got[t] = lax.ppermute(v, axis, [(i, (i - t) % n) for i in range(n)])  15.9 us
    ppermute x4, waiting for transfers between devices, combine(): other = lax.ppermute(jnp.stack([mean, m2]), axis, pairs)  12.9 us
    all_to_all x3, local copies, waits for them, and re-layouts, shards(): lax.all_to_all(second_full, DP, split_axis=1, concat_axis=0, tiled=True)  9.14 us
  transfers between devices with their start and end apart: 20, of which 14 were waited for; matrix products, arithmetic and copies ran while one was open for 14% of the time, Pallas kernels for 0%

profile of v10, /device:TPU:1, one launch (start us, length us, event | category | flops | bytes accessed | tf_op | source)
XLA Modules:
  0.0 225.0 jit_solution(10563504385321620739)
XLA Ops:
  6.5 1.8 copy-done
  8.4 2.3 %fusion.3 = f32[2,64,352]{2,1,0:T(8,128)S(1)} fusion(bf16[2,64,4224]{2,1,0:T(8,128)(2,1)} %param.2, bf16[4224,352]{0,1:T(8,128)(2,1)S(1)} %copy-done), kind=kOutput, calls=%fused_computation.9 | convolution fusion | flops 380633088 | bytes 4235264 | tf_op jit(solution)/shard_map/vbh,hc->vbc/dot_general | solution.py:102
  10.7 0.6 fusion.28
  11.4 0.0 all-gather.3.cloned.1.call-update
  11.4 12.4 %collective-permute-start = (f32[2,1,1,352]{3,2,1,0:T(1,128)S(1)}, f32[2,1,1,352]{3,2,1,0:T(1,128)S(1)}, u32[]{:S(2)}, u32[]{:S(2)}) collective-permute-start(f32[2,1,1,352]{3,2,1,0:T(1,128)S(1)} %pad_maximum_fusion.2), channel_id=1, source_target_pairs={{0,12},{12,0},{1,13},{13,1},{2,14},{14,2},{3,15},{15,3},{4,16},{16... | collective-permute-start | bytes 8456 | tf_op jit(solution)/shard_map/ppermute | solution.py:49
  23.9 0.8 collective-permute-done
  24.7 1.9 collective-permute-start.1
  26.6 2.4 %collective-permute-done.1 = f32[2,1,1,352]{3,2,1,0:T(1,128)S(1)} collective-permute-done((f32[2,1,1,352]{3,2,1,0:T(1,128)S(1)}, f32[2,1,1,352]{3,2,1,0:T(1,128)S(1)}, u32[]{:S(2)}, u32[]{:S(2)}) %collective-permute-start.1) | collective-permute-done | bytes 2848 | tf_op jit(solution)/shard_map/ppermute | solution.py:49
  29.1 1.9 collective-permute-start.2
  31.0 3.3 %collective-permute-done.2 = f32[2,1,1,352]{3,2,1,0:T(1,128)S(1)} collective-permute-done((f32[2,1,1,352]{3,2,1,0:T(1,128)S(1)}, f32[2,1,1,352]{3,2,1,0:T(1,128)S(1)}, u32[]{:S(2)}, u32[]{:S(2)}) %collective-permute-start.2) | collective-permute-done | bytes 2848 | tf_op jit(solution)/shard_map/ppermute | solution.py:49
  34.3 1.9 collective-permute-start.3
  36.3 6.3 %collective-permute-done.3 = f32[2,1,1,352]{3,2,1,0:T(1,128)S(1)} collective-permute-done((f32[2,1,1,352]{3,2,1,0:T(1,128)S(1)}, f32[2,1,1,352]{3,2,1,0:T(1,128)S(1)}, u32[]{:S(2)}, u32[]{:S(2)}) %collective-permute-start.3) | collective-permute-done | bytes 2848 | tf_op jit(solution)/shard_map/ppermute | solution.py:49
  42.6 1.9 collective-permute-start.4
  44.6 1.9 collective-permute-start.5
  46.5 3.4 %collective-permute-start.6 = (f32[2,1,1,352]{3,2,1,0:T(1,128)S(1)}, f32[2,1,1,352]{3,2,1,0:T(1,128)S(1)}, u32[]{:S(2)}, u32[]{:S(2)}) collective-permute-start(f32[2,1,1,352]{3,2,1,0:T(1,128)S(1)} %pad_maximum_fusion.6), channel_id=1, source_target_pairs={{0,192},{192,384},{384,576},{576,0},{1,193},{193,385},{385,577},{5... | collective-permute-start | bytes 8456 | tf_op jit(solution)/shard_map/ppermute | solution.py:20
  49.9 0.6 collective-permute-done.5
  50.5 2.9 %collective-permute-done.6 = f32[2,1,1,352]{3,2,1,0:T(1,128)S(1)} collective-permute-done((f32[2,1,1,352]{3,2,1,0:T(1,128)S(1)}, f32[2,1,1,352]{3,2,1,0:T(1,128)S(1)}, u32[]{:S(2)}, u32[]{:S(2)}) %collective-permute-start.6) | collective-permute-done | bytes 2848 | tf_op jit(solution)/shard_map/ppermute | solution.py:20
  53.5 0.1 multiply_reduce_fusion.2
  53.5 23.4 %all_gather.7 = bf16[12,64,352]{2,1,0:T(8,128)(2,1)S(1)} all-gather(bf16[1,64,352]{2,1,0:T(8,128)(2,1)S(1)} %divide_convert_fusion.4), channel_id=1, replica_groups=mesh['x'=4,'y'=8,'c'=2,'mp'=12] {'mp'}, dimensions={0}, use_global_device_ids=true | all-gather | bytes 585728 | tf_op jit(solution)/shard_map/all_gather | solution.py:113
  77.0 1.2 copy.7
  78.2 4.0 %all_to_all.14 = bf16[64,64,66]{2,1,0:T(8,128)(2,1)} reshape(bf16[64,12,352]{2,1,0:T(8,128)(2,1)} %copy.7) | data formatting | bytes 1081344 | tf_op jit(solution)/shard_map/all_to_all | solution.py:116
  82.2 2.9 %copy.8 = bf16[64,64,66]{2,0,1:T(8,128)(2,1)} copy(bf16[64,64,66]{2,1,0:T(8,128)(2,1)} %all_to_all.14) | data formatting | bytes 1081344 | tf_op jit(solution)/shard_map/all_to_all | solution.py:116
  85.1 19.4 %all-to-all-start = ((bf16[64,64,66]{2,0,1:T(8,128)(2,1)}), bf16[64,64,66]{2,0,1:T(8,128)(2,1)}, u32[]{:S(2)}, u32[]{:S(2)}) async-start(bf16[64,64,66]{2,0,1:T(8,128)(2,1)} %copy.8), calls=%async_computation | async-start | bytes 2097152 | tf_op jit(solution)/shard_map/all_to_all | solution.py:116
  104.6 6.1 %reshape_reshape.3 = bf16[64,4,8,2,66]{4,3,2,1,0:T(2,128)(2,1)} reshape(bf16[64,12,352]{2,1,0:T(8,128)(2,1)} %copy.7) | data formatting | bytes 1081344 | tf_op jit(solution)/shard_map/reshape;reshape | solution.py:117
  110.7 4.2 %fusion.8 = bf16[64,4,8,2,66]{4,3,2,1,0:T(2,128)(2,1)S(1)} fusion(s32[]{:T(128)S(6)} %select_n.86, bf16[64,4,8,2,66]{4,3,2,1,0:T(2,128)(2,1)} %reshape_reshape.3), kind=kLoop, calls=%fused_computation.22 | loop fusion | flops 270336 | bytes 1081348 | tf_op jit(solution)/shard_map/jit(_roll_dynamic)/concatenate | solution.py:89
  114.9 4.1 %fusion.7 = bf16[64,4,8,2,66]{4,3,2,1,0:T(2,128)(2,1)S(1)} fusion(s32[]{:T(128)S(6)} %select_n.88, bf16[64,4,8,2,66]{4,3,2,1,0:T(2,128)(2,1)S(1)} %fusion.8), kind=kLoop, calls=%fused_computation.21 | loop fusion | flops 270336 | bytes 1081348 | tf_op jit(solution)/shard_map/jit(_roll_dynamic)/concatenate | solution.py:89
  119.0 4.7 %fusion.10 = bf16[64,2,8,4,66]{4,1,2,3,0:T(2,128)(2,1)S(1)} fusion(s32[]{:T(128)S(6)} %select_n.90, bf16[64,4,8,2,66]{4,3,2,1,0:T(2,128)(2,1)S(1)} %fusion.7), kind=kLoop, calls=%fused_computation.24 | loop fusion | flops 1081344 | bytes 1081348 | tf_op jit(solution)/shard_map/transpose | solution.py:118
  123.7 1.6 copy.11
  125.3 3.1 %reshape.484 = bf16[64,4224]{1,0:T(8,128)(2,1)} reshape(bf16[64,2,8,4,66]{4,3,2,1,0:T(4,128)(2,1)} %copy.11) | data formatting | bytes 1081344 | tf_op jit(solution)/shard_map/reshape | solution.py:118
  128.4 5.1 %all-to-all-done = bf16[64,64,66]{2,0,1:T(8,128)(2,1)} async-done(((bf16[64,64,66]{2,0,1:T(8,128)(2,1)}), bf16[64,64,66]{2,0,1:T(8,128)(2,1)}, u32[]{:S(2)}, u32[]{:S(2)}) %all-to-all-start) | async-done | bytes 540704 | tf_op jit(solution)/shard_map/all_to_all | solution.py:116
  133.5 2.3 %copy.14 = bf16[4096,66]{0,1:T(8,128)(2,1)} copy(bf16[4096,66]{1,0:T(8,128)(2,1)} %bitcast.7) | data formatting | bytes 1081344 | tf_op jit(solution)/shard_map/all_to_all | solution.py:116
  135.8 3.4 %reduce_sum.56 = f32[352]{0:T(512)S(1)} reduce(f32[1,4096,352]{2,1,0:T(8,128)} %all-gather.3.cloned.1.call-done, f32[]{:T(128)} %constant.134.clone.1), dimensions={0,1}, to_apply=%region_2.0 | reduce | flops 1441440 | bytes 5768580 | tf_op jit(solution)/shard_map/reduce_sum | solution.py:104
  139.1 3.7 %multiply_reduce_fusion = f32[352]{0:T(512)S(1)} fusion(f32[1,4096,352]{2,1,0:T(8,128)} %all-gather.3.cloned.1.call-done, f32[352]{0:T(512)S(1)} %broadcast_multiply_fusion), kind=kLoop, calls=%fused_computation.6 | loop fusion | flops 4325024 | bytes 5769984 | tf_op jit(solution)/shard_map/reduce_sum | solution.py:106
  142.9 0.8 copy-done.1
  143.7 1.9 select_convert_fusion
  145.6 3.8 %collective-permute-start.7 = (bf16[66,352]{1,0:T(8,128)(2,1)S(1)}, bf16[66,352]{1,0:T(8,128)(2,1)S(1)}, u32[]{:S(2)}, u32[]{:S(2)}) collective-permute-start(bf16[66,352]{1,0:T(8,128)(2,1)S(1)} %select_convert_fusion), channel_id=1, source_target_pairs={{0,576},{192,0},{384,192},{576,384},{1,577},{193,1},{385,193},{577... | collective-permute-start | bytes 139400 | tf_op jit(solution)/shard_map/ppermute | solution.py:20
  149.4 2.3 %collective-permute-start.8 = (bf16[66,352]{1,0:T(8,128)(2,1)S(1)}, bf16[66,352]{1,0:T(8,128)(2,1)S(1)}, u32[]{:S(2)}, u32[]{:S(2)}) collective-permute-start(bf16[66,352]{1,0:T(8,128)(2,1)S(1)} %select_convert_fusion), channel_id=1, source_target_pairs={{0,384},{192,576},{384,0},{576,192},{1,385},{193,577},{385,1},{577... | collective-permute-start | bytes 139400 | tf_op jit(solution)/shard_map/ppermute | solution.py:20
  151.7 2.6 %collective-permute-start.9 = (bf16[66,352]{1,0:T(8,128)(2,1)S(1)}, bf16[66,352]{1,0:T(8,128)(2,1)S(1)}, u32[]{:S(2)}, u32[]{:S(2)}) collective-permute-start(bf16[66,352]{1,0:T(8,128)(2,1)S(1)} %select_convert_fusion), channel_id=1, source_target_pairs={{0,192},{192,384},{384,576},{576,0},{1,193},{193,385},{385,577},{5... | collective-permute-start | bytes 139400 | tf_op jit(solution)/shard_map/ppermute | solution.py:20
  154.3 2.3 %collective-permute-done.8 = bf16[66,352]{1,0:T(8,128)(2,1)S(1)} collective-permute-done((bf16[66,352]{1,0:T(8,128)(2,1)S(1)}, bf16[66,352]{1,0:T(8,128)(2,1)S(1)}, u32[]{:S(2)}, u32[]{:S(2)}) %collective-permute-start.8) | collective-permute-done | bytes 46496 | tf_op jit(solution)/shard_map/ppermute | solution.py:20
  156.7 1.7 collective-permute-done.9
  158.4 0.1 pad_maximum_fusion.1
  158.5 1.9 collective-permute-start.10
  160.4 3.4 %collective-permute-start.13 = (bf16[4,66,352]{2,1,0:T(8,128)(2,1)S(1)}, bf16[4,66,352]{2,1,0:T(8,128)(2,1)S(1)}, u32[]{:S(2)}, u32[]{:S(2)}) collective-permute-start(bf16[4,66,352]{2,1,0:T(8,128)(2,1)S(1)} %pad_maximum_fusion.1), channel_id=1, source_target_pairs={{0,24},{24,48},{48,72},{72,96},{96,120},{120,144},{144,168},{168,0... | collective-permute-start | bytes 557576 | tf_op jit(solution)/shard_map/ppermute | solution.py:13
  163.8 2.8 %collective-permute-done.10 = bf16[4,66,352]{2,1,0:T(8,128)(2,1)S(1)} collective-permute-done((bf16[4,66,352]{2,1,0:T(8,128)(2,1)S(1)}, bf16[4,66,352]{2,1,0:T(8,128)(2,1)S(1)}, u32[]{:S(2)}, u32[]{:S(2)}) %collective-permute-start.10) | collective-permute-done | bytes 185888 | tf_op jit(solution)/shard_map/ppermute | solution.py:13
  166.6 2.0 collective-permute-start.11
  168.6 3.3 %collective-permute-start.14 = (bf16[4,66,352]{2,1,0:T(8,128)(2,1)S(1)}, bf16[4,66,352]{2,1,0:T(8,128)(2,1)S(1)}, u32[]{:S(2)}, u32[]{:S(2)}) collective-permute-start(bf16[4,66,352]{2,1,0:T(8,128)(2,1)S(1)} %collective-permute-done.13), channel_id=1, source_target_pairs={{0,24},{24,48},{48,72},{72,96},{96,120},{120,144},{144,168},{168,0... | collective-permute-start | bytes 557576 | tf_op jit(solution)/shard_map/ppermute | solution.py:13
  172.0 1.9 collective-permute-done.11
  173.9 2.6 %collective-permute-start.12 = (bf16[4,66,352]{2,1,0:T(8,128)(2,1)S(1)}, bf16[4,66,352]{2,1,0:T(8,128)(2,1)S(1)}, u32[]{:S(2)}, u32[]{:S(2)}) collective-permute-start(bf16[4,66,352]{2,1,0:T(8,128)(2,1)S(1)} %collective-permute-done.11), channel_id=1, source_target_pairs={{0,168},{24,0},{48,24},{72,48},{96,72},{120,96},{144,120},{168,144... | collective-permute-start | bytes 557576 | tf_op jit(solution)/shard_map/ppermute | solution.py:13
  176.5 0.0 collective-permute-done.14
  176.5 2.6 %collective-permute-start.15 = (bf16[4,66,352]{2,1,0:T(8,128)(2,1)S(1)}, bf16[4,66,352]{2,1,0:T(8,128)(2,1)S(1)}, u32[]{:S(2)}, u32[]{:S(2)}) collective-permute-start(bf16[4,66,352]{2,1,0:T(8,128)(2,1)S(1)} %collective-permute-done.14), channel_id=1, source_target_pairs={{0,24},{24,48},{48,72},{72,96},{96,120},{120,144},{144,168},{168,0... | collective-permute-start | bytes 557576 | tf_op jit(solution)/shard_map/ppermute | solution.py:13
  179.2 5.2 %collective-permute-done.15 = bf16[4,66,352]{2,1,0:T(8,128)(2,1)S(1)} collective-permute-done((bf16[4,66,352]{2,1,0:T(8,128)(2,1)S(1)}, bf16[4,66,352]{2,1,0:T(8,128)(2,1)S(1)}, u32[]{:S(2)}, u32[]{:S(2)}) %collective-permute-start.15) | collective-permute-done | bytes 185888 | tf_op jit(solution)/shard_map/ppermute | solution.py:13
  184.4 1.9 collective-permute-start.16
  186.4 5.9 %collective-permute-done.16 = bf16[4,66,352]{2,1,0:T(8,128)(2,1)S(1)} collective-permute-done((bf16[4,66,352]{2,1,0:T(8,128)(2,1)S(1)}, bf16[4,66,352]{2,1,0:T(8,128)(2,1)S(1)}, u32[]{:S(2)}, u32[]{:S(2)}) %collective-permute-start.16) | collective-permute-done | bytes 185888 | tf_op jit(solution)/shard_map/ppermute | solution.py:13
  192.5 0.6 copy.12
  193.0 8.3 %collective-permute-start.17 = (bf16[8,4,66,352]{3,0,2,1:T(8,128)(2,1)S(1)}, bf16[8,4,66,352]{3,0,2,1:T(8,128)(2,1)S(1)}, u32[]{:S(2)}, u32[]{:S(2)}) collective-permute-start(bf16[8,4,66,352]{3,0,2,1:T(8,128)(2,1)S(1)} %copy.12), channel_id=1, source_target_pairs={{0,12},{12,0},{1,13},{13,1},{2,14},{14,2},{3,15},{15,3},{4,16},{16... | collective-permute-start | bytes 4460552 | tf_op jit(solution)/shard_map/ppermute | solution.py:13
  201.4 0.1 add_multiply_fusion.1
  201.5 0.1 add_multiply_fusion
  201.6 0.1 iota_add_fusion
  201.7 2.8 %collective-permute-done.17 = bf16[8,4,66,352]{3,0,2,1:T(8,128)(2,1)S(1)} collective-permute-done((bf16[8,4,66,352]{3,0,2,1:T(8,128)(2,1)S(1)}, bf16[8,4,66,352]{3,0,2,1:T(8,128)(2,1)S(1)}, u32[]{:S(2)}, u32[]{:S(2)}) %collective-permute-start.17) | collective-permute-done | bytes 1486880 | tf_op jit(solution)/shard_map/ppermute | solution.py:13
  204.5 0.2 copy.16
  204.7 2.5 %pad_maximum_fusion = bf16[2,8,4,66,352]{4,3,2,1,0:T(8,128)(2,1)} fusion(bf16[1,8,4,66,352]{4,3,2,1,0:T(8,128)(2,1)S(1)} %bitcast.68, bf16[1,8,4,66,352]{4,3,2,1,0:T(8,128)(2,1)S(1)} %bitcast.66), kind=kLoop, calls=%fused_computation.7 | loop fusion | flops 1486848 | bytes 5947392 | tf_op jit(solution)/shard_map/stack | solution.py:39
  207.2 1.8 fusion
  209.0 5.8 %reshape.485 = bf16[4224,352]{1,0:T(8,128)(2,1)} reshape(bf16[2,8,4,66,352]{4,3,2,1,0:T(8,128)(2,1)} %pad_maximum_fusion) | data formatting | bytes 5947392 | tf_op jit(solution)/shard_map/reshape | solution.py:129
  214.8 3.3 %fusion.6 = bf16[64,352]{1,0:T(8,128)(2,1)} fusion(bf16[64,4224]{1,0:T(8,128)(2,1)} %reshape.484, bf16[4224,352]{1,0:T(8,128)(2,1)} %reshape.485, f32[352]{0:T(512)S(1)} %get-tuple-element.23, f32[352]{0:T(512)S(1)} %multiply_add_fusion, f32[352]{0:T(512)S(1)} %get-tuple-element.24, f32[352]{0:T(512)S(1)} %broadcast_multiply_fusion, ...), kind=kOutput, calls=%fused_computation.20 | convolution fusion | flops 190496768 | bytes 3655168 | tf_op jit(solution)/shard_map/dot_general | solution.py:144
  (46 shorter events, 0.6 us)
Async XLA Ops:
  6.5 1.8 copy-start
  6.5 129.2 %all-gather.3.cloned.1.call-start = ((), (), s32[]{:S(2)}) async-start(), calls=%async_computation.1 | async-start | bytes 6389760 | tf_op jit(solution)/shard_map/all_gather | solution.py:103
  11.4 13.2 %collective-permute-start = (f32[2,1,1,352]{3,2,1,0:T(1,128)S(1)}, f32[2,1,1,352]{3,2,1,0:T(1,128)S(1)}, u32[]{:S(2)}, u32[]{:S(2)}) collective-permute-start(f32[2,1,1,352]{3,2,1,0:T(1,128)S(1)} %pad_maximum_fusion.2), channel_id=1, source_target_pairs={{0,12},{12,0},{1,13},{13,1},{2,14},{14,2},{3,15},{15,3},{4,16},{16... | collective-permute-start | bytes 8456 | tf_op jit(solution)/shard_map/ppermute | solution.py:49
  24.7 4.3 %collective-permute-start.1 = (f32[2,1,1,352]{3,2,1,0:T(1,128)S(1)}, f32[2,1,1,352]{3,2,1,0:T(1,128)S(1)}, u32[]{:S(2)}, u32[]{:S(2)}) collective-permute-start(f32[2,1,1,352]{3,2,1,0:T(1,128)S(1)} %pad_maximum_fusion.3), channel_id=1, source_target_pairs={{0,24},{24,0},{48,72},{72,48},{96,120},{120,96},{144,168},{168,144... | collective-permute-start | bytes 8456 | tf_op jit(solution)/shard_map/ppermute | solution.py:49
  29.1 5.2 %collective-permute-start.2 = (f32[2,1,1,352]{3,2,1,0:T(1,128)S(1)}, f32[2,1,1,352]{3,2,1,0:T(1,128)S(1)}, u32[]{:S(2)}, u32[]{:S(2)}) collective-permute-start(f32[2,1,1,352]{3,2,1,0:T(1,128)S(1)} %pad_maximum_fusion.4), channel_id=1, source_target_pairs={{0,48},{24,72},{48,0},{72,24},{96,144},{120,168},{144,96},{168,120... | collective-permute-start | bytes 8456 | tf_op jit(solution)/shard_map/ppermute | solution.py:49
  34.3 8.3 %collective-permute-start.3 = (f32[2,1,1,352]{3,2,1,0:T(1,128)S(1)}, f32[2,1,1,352]{3,2,1,0:T(1,128)S(1)}, u32[]{:S(2)}, u32[]{:S(2)}) collective-permute-start(f32[2,1,1,352]{3,2,1,0:T(1,128)S(1)} %pad_maximum_fusion.5), channel_id=1, source_target_pairs={{0,96},{24,120},{48,144},{72,168},{96,0},{120,24},{144,48},{168,72... | collective-permute-start | bytes 8456 | tf_op jit(solution)/shard_map/ppermute | solution.py:49
  42.6 7.2 %collective-permute-start.4 = (f32[2,1,1,352]{3,2,1,0:T(1,128)S(1)}, f32[2,1,1,352]{3,2,1,0:T(1,128)S(1)}, u32[]{:S(2)}, u32[]{:S(2)}) collective-permute-start(f32[2,1,1,352]{3,2,1,0:T(1,128)S(1)} %pad_maximum_fusion.6), channel_id=1, source_target_pairs={{0,576},{192,0},{384,192},{576,384},{1,577},{193,1},{385,193},{577... | collective-permute-start | bytes 8456 | tf_op jit(solution)/shard_map/ppermute | solution.py:20
  44.6 5.9 %collective-permute-start.5 = (f32[2,1,1,352]{3,2,1,0:T(1,128)S(1)}, f32[2,1,1,352]{3,2,1,0:T(1,128)S(1)}, u32[]{:S(2)}, u32[]{:S(2)}) collective-permute-start(f32[2,1,1,352]{3,2,1,0:T(1,128)S(1)} %pad_maximum_fusion.6), channel_id=1, source_target_pairs={{0,384},{192,576},{384,0},{576,192},{1,385},{193,577},{385,1},{577... | collective-permute-start | bytes 8456 | tf_op jit(solution)/shard_map/ppermute | solution.py:20
  46.5 6.9 %collective-permute-start.6 = (f32[2,1,1,352]{3,2,1,0:T(1,128)S(1)}, f32[2,1,1,352]{3,2,1,0:T(1,128)S(1)}, u32[]{:S(2)}, u32[]{:S(2)}) collective-permute-start(f32[2,1,1,352]{3,2,1,0:T(1,128)S(1)} %pad_maximum_fusion.6), channel_id=1, source_target_pairs={{0,192},{192,384},{384,576},{576,0},{1,193},{193,385},{385,577},{5... | collective-permute-start | bytes 8456 | tf_op jit(solution)/shard_map/ppermute | solution.py:20
  85.1 48.4 %all-to-all-start = ((bf16[64,64,66]{2,0,1:T(8,128)(2,1)}), bf16[64,64,66]{2,0,1:T(8,128)(2,1)}, u32[]{:S(2)}, u32[]{:S(2)}) async-start(bf16[64,64,66]{2,0,1:T(8,128)(2,1)} %copy.8), calls=%async_computation | async-start | bytes 2097152 | tf_op jit(solution)/shard_map/all_to_all | solution.py:116
  139.1 4.6 %copy-start.1 = (f32[1,4096,352]{2,1,0:T(8,128)S(1)}, f32[1,4096,352]{2,1,0:T(8,128)}, u32[]{:S(2)}) copy-start(f32[1,4096,352]{2,1,0:T(8,128)} %all-gather.3.cloned.1.call-done) | copy-start | bytes 17301508
  145.6 8.7 %collective-permute-start.7 = (bf16[66,352]{1,0:T(8,128)(2,1)S(1)}, bf16[66,352]{1,0:T(8,128)(2,1)S(1)}, u32[]{:S(2)}, u32[]{:S(2)}) collective-permute-start(bf16[66,352]{1,0:T(8,128)(2,1)S(1)} %select_convert_fusion), channel_id=1, source_target_pairs={{0,576},{192,0},{384,192},{576,384},{1,577},{193,1},{385,193},{577... | collective-permute-start | bytes 139400 | tf_op jit(solution)/shard_map/ppermute | solution.py:20
  149.4 7.3 %collective-permute-start.8 = (bf16[66,352]{1,0:T(8,128)(2,1)S(1)}, bf16[66,352]{1,0:T(8,128)(2,1)S(1)}, u32[]{:S(2)}, u32[]{:S(2)}) collective-permute-start(bf16[66,352]{1,0:T(8,128)(2,1)S(1)} %select_convert_fusion), channel_id=1, source_target_pairs={{0,384},{192,576},{384,0},{576,192},{1,385},{193,577},{385,1},{577... | collective-permute-start | bytes 139400 | tf_op jit(solution)/shard_map/ppermute | solution.py:20
  151.7 6.7 %collective-permute-start.9 = (bf16[66,352]{1,0:T(8,128)(2,1)S(1)}, bf16[66,352]{1,0:T(8,128)(2,1)S(1)}, u32[]{:S(2)}, u32[]{:S(2)}) collective-permute-start(bf16[66,352]{1,0:T(8,128)(2,1)S(1)} %select_convert_fusion), channel_id=1, source_target_pairs={{0,192},{192,384},{384,576},{576,0},{1,193},{193,385},{385,577},{5... | collective-permute-start | bytes 139400 | tf_op jit(solution)/shard_map/ppermute | solution.py:20
  158.5 8.2 %collective-permute-start.10 = (bf16[4,66,352]{2,1,0:T(8,128)(2,1)S(1)}, bf16[4,66,352]{2,1,0:T(8,128)(2,1)S(1)}, u32[]{:S(2)}, u32[]{:S(2)}) collective-permute-start(bf16[4,66,352]{2,1,0:T(8,128)(2,1)S(1)} %pad_maximum_fusion.1), channel_id=1, source_target_pairs={{0,168},{24,0},{48,24},{72,48},{96,72},{120,96},{144,120},{168,144... | collective-permute-start | bytes 557576 | tf_op jit(solution)/shard_map/ppermute | solution.py:13
  160.4 8.2 %collective-permute-start.13 = (bf16[4,66,352]{2,1,0:T(8,128)(2,1)S(1)}, bf16[4,66,352]{2,1,0:T(8,128)(2,1)S(1)}, u32[]{:S(2)}, u32[]{:S(2)}) collective-permute-start(bf16[4,66,352]{2,1,0:T(8,128)(2,1)S(1)} %pad_maximum_fusion.1), channel_id=1, source_target_pairs={{0,24},{24,48},{48,72},{72,96},{96,120},{120,144},{144,168},{168,0... | collective-permute-start | bytes 557576 | tf_op jit(solution)/shard_map/ppermute | solution.py:13
  166.6 7.2 %collective-permute-start.11 = (bf16[4,66,352]{2,1,0:T(8,128)(2,1)S(1)}, bf16[4,66,352]{2,1,0:T(8,128)(2,1)S(1)}, u32[]{:S(2)}, u32[]{:S(2)}) collective-permute-start(bf16[4,66,352]{2,1,0:T(8,128)(2,1)S(1)} %collective-permute-done.10), channel_id=1, source_target_pairs={{0,168},{24,0},{48,24},{72,48},{96,72},{120,96},{144,120},{168,144... | collective-permute-start | bytes 557576 | tf_op jit(solution)/shard_map/ppermute | solution.py:13
  168.6 7.9 %collective-permute-start.14 = (bf16[4,66,352]{2,1,0:T(8,128)(2,1)S(1)}, bf16[4,66,352]{2,1,0:T(8,128)(2,1)S(1)}, u32[]{:S(2)}, u32[]{:S(2)}) collective-permute-start(bf16[4,66,352]{2,1,0:T(8,128)(2,1)S(1)} %collective-permute-done.13), channel_id=1, source_target_pairs={{0,24},{24,48},{48,72},{72,96},{96,120},{120,144},{144,168},{168,0... | collective-permute-start | bytes 557576 | tf_op jit(solution)/shard_map/ppermute | solution.py:13
  173.9 12.5 %collective-permute-start.12 = (bf16[4,66,352]{2,1,0:T(8,128)(2,1)S(1)}, bf16[4,66,352]{2,1,0:T(8,128)(2,1)S(1)}, u32[]{:S(2)}, u32[]{:S(2)}) collective-permute-start(bf16[4,66,352]{2,1,0:T(8,128)(2,1)S(1)} %collective-permute-done.11), channel_id=1, source_target_pairs={{0,168},{24,0},{48,24},{72,48},{96,72},{120,96},{144,120},{168,144... | collective-permute-start | bytes 557576 | tf_op jit(solution)/shard_map/ppermute | solution.py:13
  176.5 7.9 %collective-permute-start.15 = (bf16[4,66,352]{2,1,0:T(8,128)(2,1)S(1)}, bf16[4,66,352]{2,1,0:T(8,128)(2,1)S(1)}, u32[]{:S(2)}, u32[]{:S(2)}) collective-permute-start(bf16[4,66,352]{2,1,0:T(8,128)(2,1)S(1)} %collective-permute-done.14), channel_id=1, source_target_pairs={{0,24},{24,48},{48,72},{72,96},{96,120},{120,144},{144,168},{168,0... | collective-permute-start | bytes 557576 | tf_op jit(solution)/shard_map/ppermute | solution.py:13
  184.4 7.9 %collective-permute-start.16 = (bf16[4,66,352]{2,1,0:T(8,128)(2,1)S(1)}, bf16[4,66,352]{2,1,0:T(8,128)(2,1)S(1)}, u32[]{:S(2)}, u32[]{:S(2)}) collective-permute-start(bf16[4,66,352]{2,1,0:T(8,128)(2,1)S(1)} %collective-permute-done.15), channel_id=1, source_target_pairs={{0,24},{24,48},{48,72},{72,96},{96,120},{120,144},{144,168},{168,0... | collective-permute-start | bytes 557576 | tf_op jit(solution)/shard_map/ppermute | solution.py:13
  193.0 11.4 %collective-permute-start.17 = (bf16[8,4,66,352]{3,0,2,1:T(8,128)(2,1)S(1)}, bf16[8,4,66,352]{3,0,2,1:T(8,128)(2,1)S(1)}, u32[]{:S(2)}, u32[]{:S(2)}) collective-permute-start(bf16[8,4,66,352]{3,0,2,1:T(8,128)(2,1)S(1)} %copy.12), channel_id=1, source_target_pairs={{0,12},{12,0},{1,13},{13,1},{2,14},{14,2},{3,15},{15,3},{4,16},{16... | collective-permute-start | bytes 4460552 | tf_op jit(solution)/shard_map/ppermute | solution.py:13
Sparse Core Ops, SparseCore 0:
  11.5 102.5 all-gather.2

commit v11 on v10

--- a/solution.py
+++ b/solution.py
@@ -100,15 +100,13 @@
     local = hidden.shape[1]
     total = local * dp_count
     feats = jnp.einsum("vbh,hc->vbc", hidden, proj_weight, preferred_element_type=jnp.float32)
+    mean, var = dp_stats(feats)
+    inv_std = 1.0 / jnp.sqrt(var + eps)
     feats0_all = lax.all_gather(feats[0], DP, axis=0, tiled=True)
-    mean0 = jnp.sum(feats0_all, axis=0, keepdims=True) / total
-    centered0 = feats0_all - mean0
-    var0 = jnp.sum(centered0 * centered0, axis=0, keepdims=True) / total
-    first_all = (centered0 / jnp.sqrt(var0 + eps)).astype(jnp.bfloat16)
-    first = ((feats[0] - mean0) / jnp.sqrt(var0 + eps)).astype(jnp.bfloat16)
-    inv_std0 = 1.0 / jnp.sqrt(var0 + eps)
-    mean1, var1 = dp_stats(feats[1:])
-    second = ((feats[1] - mean1[0]) / jnp.sqrt(var1[0] + eps)).astype(jnp.bfloat16)
+    first_all = ((feats0_all - mean[0]) / jnp.sqrt(var[0] + eps)).astype(jnp.bfloat16)
+    first = ((feats[0] - mean[0]) / jnp.sqrt(var[0] + eps)).astype(jnp.bfloat16)
+    inv_std0 = inv_std[0]
+    second = ((feats[1] - mean[1]) / jnp.sqrt(var[1] + eps)).astype(jnp.bfloat16)
     n_mp = lax.axis_size("mp")
     stacked = lax.all_gather(second, "mp", axis=0)
     second_full = jnp.transpose(stacked, (1, 0, 2)).reshape(local, n_mp * rows)

time: 226 us -> 240 us (1.062)
  waiting for transfers between devices: 44.2 us -> 60.7 us
  other arithmetic: 25.5 us -> 18.4 us
  starting transfers between devices: 79.6 us -> 82.8 us
    all_gather x1, waiting for transfers between devices: 0.01 us -> 14.9 us  [shards(): feats0_all = lax.all_gather(feats[0], DP, axis=0, tiled=True)]
    reduce_sum x3 -> x1, other arithmetic: 7.12 us -> 0.04 us  [dp_stats(): m2 = jnp.sum(dev * dev, axis=1, keepdims=True)]
    all_to_all x1, waiting for transfers between devices: 5.08 us -> 9.07 us  [shards(): lax.all_to_all(second_full, DP, split_axis=1, concat_axis=0, tiled=True)]
    ppermute x8, starting transfers between devices: 26.1 us -> 28.9 us  [shift(): return lax.ppermute(v, axis, [(i, (i + step) % n) for i in range(n)])]
  transfers between devices with their start and end apart: 20 -> 20, of which waited for: 14 -> 15; matrix products, arithmetic and copies ran while one was open for 14% -> 13% of each run, Pallas kernels for 0% -> 0%
where the time goes in v11:
time: 240 us; the launch traced here: 239 us
  starting transfers between devices  82.8 us (34%)
  waiting for transfers between devices  60.7 us (25%)
  local copies, waits for them, and re-layouts  30 us (12%)
  blocking collectives  23.6 us (10%)
  other arithmetic  18.4 us (8%)
  between operations  13.9 us (6%)
  matrix products  9.42 us (4%)
    ppermute x8, starting transfers between devices, shift(): return lax.ppermute(v, axis, [(i, (i + step) % n) for i in range(n)])  28.9 us
    all_gather x1, blocking collectives, shards(): stacked = lax.all_gather(second, 'mp', axis=0)  23.6 us
    all_to_all x1, starting transfers between devices, shards(): lax.all_to_all(second_full, DP, split_axis=1, concat_axis=0, tiled=True)  19.1 us
    ppermute x4, starting transfers between devices, combine(): other = lax.ppermute(jnp.stack([mean, m2]), axis, pairs)  18.2 us
    ppermute x8, waiting for transfers between devices, shift(): return lax.ppermute(v, axis, [(i, (i + step) % n) for i in range(n)])  16.9 us
    ppermute x6, starting transfers between devices, direct_gather(): got[t] = lax.ppermute(v, axis, [(i, (i - t) % n) for i in range(n)])  16.5 us
    all_gather x1, waiting for transfers between devices, shards(): feats0_all = lax.all_gather(feats[0], DP, axis=0, tiled=True)  14.9 us
    ppermute x4, waiting for transfers between devices, combine(): other = lax.ppermute(jnp.stack([mean, m2]), axis, pairs)  12.9 us
  transfers between devices with their start and end apart: 20, of which 15 were waited for; matrix products, arithmetic and copies ran while one was open for 13% of the time, Pallas kernels for 0%

profile of v11, /device:TPU:1, one launch (start us, length us, event | category | flops | bytes accessed | tf_op | source)
XLA Modules:
  0.0 238.9 jit_solution(8375253307210543537)
XLA Ops:
  6.5 1.8 copy-done
  8.4 2.3 fusion.40
  10.8 12.4 %collective-permute-start = (f32[2,2,1,352]{3,1,2,0:T(2,128)S(1)}, f32[2,2,1,352]{3,1,2,0:T(2,128)S(1)}, u32[]{:S(2)}, u32[]{:S(2)}) collective-permute-start(f32[2,2,1,352]{3,1,2,0:T(2,128)S(1)} %pad_maximum_fusion.2), channel_id=1, source_target_pairs={{0,12},{12,0},{1,13},{13,1},{2,14},{14,2},{3,15},{15,3},{4,16},{16... | collective-permute-start | bytes 16904 | tf_op jit(solution)/shard_map/ppermute | solution.py:49
  23.2 0.8 collective-permute-done
  24.0 1.9 collective-permute-start.1
  26.0 2.4 %collective-permute-done.1 = f32[2,2,1,352]{3,1,2,0:T(2,128)S(1)} collective-permute-done((f32[2,2,1,352]{3,1,2,0:T(2,128)S(1)}, f32[2,2,1,352]{3,1,2,0:T(2,128)S(1)}, u32[]{:S(2)}, u32[]{:S(2)}) %collective-permute-start.1) | collective-permute-done | bytes 5664 | tf_op jit(solution)/shard_map/ppermute | solution.py:49
  28.4 1.9 collective-permute-start.2
  30.4 3.3 %collective-permute-done.2 = f32[2,2,1,352]{3,1,2,0:T(2,128)S(1)} collective-permute-done((f32[2,2,1,352]{3,1,2,0:T(2,128)S(1)}, f32[2,2,1,352]{3,1,2,0:T(2,128)S(1)}, u32[]{:S(2)}, u32[]{:S(2)}) %collective-permute-start.2) | collective-permute-done | bytes 5664 | tf_op jit(solution)/shard_map/ppermute | solution.py:49
  33.7 1.9 collective-permute-start.3
  35.7 6.3 %collective-permute-done.3 = f32[2,2,1,352]{3,1,2,0:T(2,128)S(1)} collective-permute-done((f32[2,2,1,352]{3,1,2,0:T(2,128)S(1)}, f32[2,2,1,352]{3,1,2,0:T(2,128)S(1)}, u32[]{:S(2)}, u32[]{:S(2)}) %collective-permute-start.3) | collective-permute-done | bytes 5664 | tf_op jit(solution)/shard_map/ppermute | solution.py:49
  42.0 1.9 collective-permute-start.4
  44.0 1.9 collective-permute-start.5
  45.9 3.4 %collective-permute-start.6 = (f32[2,2,1,352]{3,1,2,0:T(2,128)S(1)}, f32[2,2,1,352]{3,1,2,0:T(2,128)S(1)}, u32[]{:S(2)}, u32[]{:S(2)}) collective-permute-start(f32[2,2,1,352]{3,1,2,0:T(2,128)S(1)} %get-tuple-element.28), channel_id=1, source_target_pairs={{0,192},{192,384},{384,576},{576,0},{1,193},{193,385},{385,577},{5... | collective-permute-start | bytes 16904 | tf_op jit(solution)/shard_map/ppermute | solution.py:20
  49.3 0.6 collective-permute-done.5
  49.9 2.8 %collective-permute-done.6 = f32[2,2,1,352]{3,1,2,0:T(2,128)S(1)} collective-permute-done((f32[2,2,1,352]{3,1,2,0:T(2,128)S(1)}, f32[2,2,1,352]{3,1,2,0:T(2,128)S(1)}, u32[]{:S(2)}, u32[]{:S(2)}) %collective-permute-start.6) | collective-permute-done | bytes 5664 | tf_op jit(solution)/shard_map/ppermute | solution.py:20
  52.8 0.7 fusion.39
  53.5 0.0 all-gather.3.cloned.1.call-update
  53.5 23.6 %all_gather.7 = bf16[12,64,352]{2,1,0:T(8,128)(2,1)S(1)} all-gather(bf16[1,64,352]{2,1,0:T(8,128)(2,1)S(1)} %get-tuple-element.17), channel_id=1, replica_groups=mesh['x'=4,'y'=8,'c'=2,'mp'=12] {'mp'}, dimensions={0}, use_global_device_ids=true | all-gather | bytes 585728 | tf_op jit(solution)/shard_map/all_gather | solution.py:111
  77.1 1.2 copy.13
  78.3 4.0 %all_to_all.14 = bf16[64,64,66]{2,1,0:T(8,128)(2,1)} reshape(bf16[64,12,352]{2,1,0:T(8,128)(2,1)} %copy.13) | data formatting | bytes 1081344 | tf_op jit(solution)/shard_map/all_to_all | solution.py:114
  82.3 2.9 %copy.14 = bf16[64,64,66]{2,0,1:T(8,128)(2,1)} copy(bf16[64,64,66]{2,1,0:T(8,128)(2,1)} %all_to_all.14) | data formatting | bytes 1081344 | tf_op jit(solution)/shard_map/all_to_all | solution.py:114
  85.2 19.1 %all-to-all-start = ((bf16[64,64,66]{2,0,1:T(8,128)(2,1)}), bf16[64,64,66]{2,0,1:T(8,128)(2,1)}, u32[]{:S(2)}, u32[]{:S(2)}) async-start(bf16[64,64,66]{2,0,1:T(8,128)(2,1)} %copy.14), calls=%async_computation | async-start | bytes 2097152 | tf_op jit(solution)/shard_map/all_to_all | solution.py:114
  104.4 6.1 %reshape_reshape.3 = bf16[64,4,8,2,66]{4,3,2,1,0:T(2,128)(2,1)} reshape(bf16[64,12,352]{2,1,0:T(8,128)(2,1)} %copy.13) | data formatting | bytes 1081344 | tf_op jit(solution)/shard_map/reshape;reshape | solution.py:115
  110.5 4.2 %fusion.11 = bf16[64,4,8,2,66]{4,3,2,1,0:T(2,128)(2,1)S(1)} fusion(s32[]{:T(128)S(6)} %select_n.86, bf16[64,4,8,2,66]{4,3,2,1,0:T(2,128)(2,1)} %reshape_reshape.3), kind=kLoop, calls=%fused_computation.22 | loop fusion | flops 270336 | bytes 1081348 | tf_op jit(solution)/shard_map/jit(_roll_dynamic)/concatenate | solution.py:89
  114.7 4.1 %fusion.10 = bf16[64,4,8,2,66]{4,3,2,1,0:T(2,128)(2,1)S(1)} fusion(s32[]{:T(128)S(6)} %select_n.88, bf16[64,4,8,2,66]{4,3,2,1,0:T(2,128)(2,1)S(1)} %fusion.11), kind=kLoop, calls=%fused_computation.21 | loop fusion | flops 270336 | bytes 1081348 | tf_op jit(solution)/shard_map/jit(_roll_dynamic)/concatenate | solution.py:89
  118.9 4.7 %fusion.13 = bf16[64,2,8,4,66]{4,1,2,3,0:T(2,128)(2,1)S(1)} fusion(s32[]{:T(128)S(6)} %select_n.90, bf16[64,4,8,2,66]{4,3,2,1,0:T(2,128)(2,1)S(1)} %fusion.10), kind=kLoop, calls=%fused_computation.24 | loop fusion | flops 1081344 | bytes 1081348 | tf_op jit(solution)/shard_map/transpose | solution.py:116
  123.5 1.6 copy.17
  125.1 3.1 %reshape.586 = bf16[64,4224]{1,0:T(8,128)(2,1)} reshape(bf16[64,2,8,4,66]{4,3,2,1,0:T(4,128)(2,1)} %copy.17) | data formatting | bytes 1081344 | tf_op jit(solution)/shard_map/reshape | solution.py:116
  128.2 9.1 %all-to-all-done = bf16[64,64,66]{2,0,1:T(8,128)(2,1)} async-done(((bf16[64,64,66]{2,0,1:T(8,128)(2,1)}), bf16[64,64,66]{2,0,1:T(8,128)(2,1)}, u32[]{:S(2)}, u32[]{:S(2)}) %all-to-all-start) | async-done | bytes 540704 | tf_op jit(solution)/shard_map/all_to_all | solution.py:114
  137.3 2.3 copy.20
  139.6 14.9 %all-gather.3.cloned.1.call-done = f32[1,4096,352]{2,1,0:T(8,128)} async-done(((f32[1,64,352]{2,1,0:T(8,128)}), f32[1,4096,352]{2,1,0:T(8,128)}) %all-gather.3.cloned.1.call-update) | async-done | bytes 5767184 | tf_op jit(solution)/shard_map/all_gather | solution.py:105
  154.5 3.8 %select_convert_fusion = bf16[66,352]{1,0:T(8,128)(2,1)S(1)} fusion(bf16[4096,66]{0,1:T(8,128)(2,1)} %copy.20, f32[1,4096,352]{2,1,0:T(8,128)} %all-gather.3.cloned.1.call-done, f32[352]{0:T(512)S(1)} %get-tuple-element.34, f32[352]{0:T(512)S(1)} %get-tuple-element.14, s32[352]{0:T(512)S(1)} %iota_add_fusion.1, s32[66]{0:T(128)S(1)} %iota_add_fusion.2), kind=kOutput, calls=%fused_computation.35 | convolution fusion | flops 194804544 | bytes 6358792 | tf_op jit(solution)/shard_map/bi,bj->ij/dot_general | solution.py:119
  158.3 4.7 %collective-permute-start.7 = (bf16[66,352]{1,0:T(8,128)(2,1)S(1)}, bf16[66,352]{1,0:T(8,128)(2,1)S(1)}, u32[]{:S(2)}, u32[]{:S(2)}) collective-permute-start(bf16[66,352]{1,0:T(8,128)(2,1)S(1)} %select_convert_fusion), channel_id=1, source_target_pairs={{0,576},{192,0},{384,192},{576,384},{1,577},{193,1},{385,193},{577... | collective-permute-start | bytes 139400 | tf_op jit(solution)/shard_map/ppermute | solution.py:20
  162.9 2.1 collective-permute-start.8
  165.1 2.6 %collective-permute-start.9 = (bf16[66,352]{1,0:T(8,128)(2,1)S(1)}, bf16[66,352]{1,0:T(8,128)(2,1)S(1)}, u32[]{:S(2)}, u32[]{:S(2)}) collective-permute-start(bf16[66,352]{1,0:T(8,128)(2,1)S(1)} %select_convert_fusion), channel_id=1, source_target_pairs={{0,192},{192,384},{384,576},{576,0},{1,193},{193,385},{385,577},{5... | collective-permute-start | bytes 139400 | tf_op jit(solution)/shard_map/ppermute | solution.py:20
  167.6 0.0 collective-permute-done.7
  167.6 1.7 collective-permute-done.8
  169.4 1.8 collective-permute-done.9
  171.2 0.1 pad_maximum_fusion.1
  171.2 2.9 %collective-permute-start.10 = (bf16[4,66,352]{2,1,0:T(8,128)(2,1)S(1)}, bf16[4,66,352]{2,1,0:T(8,128)(2,1)S(1)}, u32[]{:S(2)}, u32[]{:S(2)}) collective-permute-start(bf16[4,66,352]{2,1,0:T(8,128)(2,1)S(1)} %pad_maximum_fusion.1), channel_id=1, source_target_pairs={{0,168},{24,0},{48,24},{72,48},{96,72},{120,96},{144,120},{168,144... | collective-permute-start | bytes 557576 | tf_op jit(solution)/shard_map/ppermute | solution.py:13
  174.2 2.4 collective-permute-start.13
  176.6 1.3 collective-permute-done.10
  177.9 4.1 %collective-permute-start.11 = (bf16[4,66,352]{2,1,0:T(8,128)(2,1)S(1)}, bf16[4,66,352]{2,1,0:T(8,128)(2,1)S(1)}, u32[]{:S(2)}, u32[]{:S(2)}) collective-permute-start(bf16[4,66,352]{2,1,0:T(8,128)(2,1)S(1)} %collective-permute-done.10), channel_id=1, source_target_pairs={{0,168},{24,0},{48,24},{72,48},{96,72},{120,96},{144,120},{168,144... | collective-permute-start | bytes 557576 | tf_op jit(solution)/shard_map/ppermute | solution.py:13
  182.0 0.0 collective-permute-done.13
  182.0 1.9 collective-permute-start.14
  184.0 0.9 collective-permute-done.11
  184.9 5.0 %collective-permute-start.12 = (bf16[4,66,352]{2,1,0:T(8,128)(2,1)S(1)}, bf16[4,66,352]{2,1,0:T(8,128)(2,1)S(1)}, u32[]{:S(2)}, u32[]{:S(2)}) collective-permute-start(bf16[4,66,352]{2,1,0:T(8,128)(2,1)S(1)} %collective-permute-done.11), channel_id=1, source_target_pairs={{0,168},{24,0},{48,24},{72,48},{96,72},{120,96},{144,120},{168,144... | collective-permute-start | bytes 557576 | tf_op jit(solution)/shard_map/ppermute | solution.py:13
  189.9 0.0 collective-permute-done.14
  189.9 1.9 collective-permute-start.15
  191.9 5.9 %collective-permute-done.15 = bf16[4,66,352]{2,1,0:T(8,128)(2,1)S(1)} collective-permute-done((bf16[4,66,352]{2,1,0:T(8,128)(2,1)S(1)}, bf16[4,66,352]{2,1,0:T(8,128)(2,1)S(1)}, u32[]{:S(2)}, u32[]{:S(2)}) %collective-permute-start.15) | collective-permute-done | bytes 185888 | tf_op jit(solution)/shard_map/ppermute | solution.py:13
  197.8 1.9 collective-permute-start.16
  199.7 0.0 collective-permute-done.12
  199.8 5.9 %collective-permute-done.16 = bf16[4,66,352]{2,1,0:T(8,128)(2,1)S(1)} collective-permute-done((bf16[4,66,352]{2,1,0:T(8,128)(2,1)S(1)}, bf16[4,66,352]{2,1,0:T(8,128)(2,1)S(1)}, u32[]{:S(2)}, u32[]{:S(2)}) %collective-permute-start.16) | collective-permute-done | bytes 185888 | tf_op jit(solution)/shard_map/ppermute | solution.py:13
  205.9 0.6 copy.18
  206.5 8.8 %collective-permute-start.17 = (bf16[8,4,66,352]{3,0,2,1:T(8,128)(2,1)S(1)}, bf16[8,4,66,352]{3,0,2,1:T(8,128)(2,1)S(1)}, u32[]{:S(2)}, u32[]{:S(2)}) collective-permute-start(bf16[8,4,66,352]{3,0,2,1:T(8,128)(2,1)S(1)} %copy.18), channel_id=1, source_target_pairs={{0,12},{12,0},{1,13},{13,1},{2,14},{14,2},{3,15},{15,3},{4,16},{16... | collective-permute-start | bytes 4460552 | tf_op jit(solution)/shard_map/ppermute | solution.py:13
  215.3 0.1 add_multiply_fusion.1
  215.3 0.1 add_multiply_fusion
  215.4 0.1 iota_add_fusion
  215.5 2.8 %collective-permute-done.17 = bf16[8,4,66,352]{3,0,2,1:T(8,128)(2,1)S(1)} collective-permute-done((bf16[8,4,66,352]{3,0,2,1:T(8,128)(2,1)S(1)}, bf16[8,4,66,352]{3,0,2,1:T(8,128)(2,1)S(1)}, u32[]{:S(2)}, u32[]{:S(2)}) %collective-permute-start.17) | collective-permute-done | bytes 1486880 | tf_op jit(solution)/shard_map/ppermute | solution.py:13
  218.3 0.2 copy.22
  218.5 2.5 %pad_maximum_fusion = bf16[2,8,4,66,352]{4,3,2,1,0:T(8,128)(2,1)} fusion(bf16[1,8,4,66,352]{4,3,2,1,0:T(8,128)(2,1)S(1)} %bitcast.79, bf16[1,8,4,66,352]{4,3,2,1,0:T(8,128)(2,1)S(1)} %bitcast.77), kind=kLoop, calls=%fused_computation.7 | loop fusion | flops 1486848 | bytes 5947392 | tf_op jit(solution)/shard_map/stack | solution.py:39
  221.0 1.8 fusion
  222.8 5.9 %reshape.587 = bf16[4224,352]{1,0:T(8,128)(2,1)} reshape(bf16[2,8,4,66,352]{4,3,2,1,0:T(8,128)(2,1)} %pad_maximum_fusion) | data formatting | bytes 5947392 | tf_op jit(solution)/shard_map/reshape | solution.py:127
  228.7 3.3 %fusion.9 = bf16[64,352]{1,0:T(8,128)(2,1)} fusion(bf16[64,4224]{1,0:T(8,128)(2,1)} %reshape.586, bf16[4224,352]{1,0:T(8,128)(2,1)} %reshape.587, f32[352]{0:T(512)S(1)} %get-tuple-element.36, f32[352]{0:T(512)S(1)} %multiply_add_fusion, f32[352]{0:T(512)S(1)} %get-tuple-element.34, f32[352]{0:T(512)S(1)} %get-tuple-element.14, ...), kind=kOutput, calls=%fused_computation.20 | convolution fusion | flops 190496768 | bytes 3655168 | tf_op jit(solution)/shard_map/dot_general | solution.py:142
  (38 shorter events, 0.6 us)
Async XLA Ops:
  6.5 1.8 copy-start
  6.5 148.0 %all-gather.3.cloned.1.call-start = ((), (), s32[]{:S(2)}) async-start(), calls=%async_computation.1 | async-start | bytes 6389760 | tf_op jit(solution)/shard_map/all_gather | solution.py:105
  10.8 13.2 %collective-permute-start = (f32[2,2,1,352]{3,1,2,0:T(2,128)S(1)}, f32[2,2,1,352]{3,1,2,0:T(2,128)S(1)}, u32[]{:S(2)}, u32[]{:S(2)}) collective-permute-start(f32[2,2,1,352]{3,1,2,0:T(2,128)S(1)} %pad_maximum_fusion.2), channel_id=1, source_target_pairs={{0,12},{12,0},{1,13},{13,1},{2,14},{14,2},{3,15},{15,3},{4,16},{16... | collective-permute-start | bytes 16904 | tf_op jit(solution)/shard_map/ppermute | solution.py:49
  24.0 4.4 %collective-permute-start.1 = (f32[2,2,1,352]{3,1,2,0:T(2,128)S(1)}, f32[2,2,1,352]{3,1,2,0:T(2,128)S(1)}, u32[]{:S(2)}, u32[]{:S(2)}) collective-permute-start(f32[2,2,1,352]{3,1,2,0:T(2,128)S(1)} %pad_maximum_fusion.3), channel_id=1, source_target_pairs={{0,24},{24,0},{48,72},{72,48},{96,120},{120,96},{144,168},{168,144... | collective-permute-start | bytes 16904 | tf_op jit(solution)/shard_map/ppermute | solution.py:49
  28.4 5.3 %collective-permute-start.2 = (f32[2,2,1,352]{3,1,2,0:T(2,128)S(1)}, f32[2,2,1,352]{3,1,2,0:T(2,128)S(1)}, u32[]{:S(2)}, u32[]{:S(2)}) collective-permute-start(f32[2,2,1,352]{3,1,2,0:T(2,128)S(1)} %pad_maximum_fusion.4), channel_id=1, source_target_pairs={{0,48},{24,72},{48,0},{72,24},{96,144},{120,168},{144,96},{168,120... | collective-permute-start | bytes 16904 | tf_op jit(solution)/shard_map/ppermute | solution.py:49
  33.7 8.3 %collective-permute-start.3 = (f32[2,2,1,352]{3,1,2,0:T(2,128)S(1)}, f32[2,2,1,352]{3,1,2,0:T(2,128)S(1)}, u32[]{:S(2)}, u32[]{:S(2)}) collective-permute-start(f32[2,2,1,352]{3,1,2,0:T(2,128)S(1)} %pad_maximum_fusion.5), channel_id=1, source_target_pairs={{0,96},{24,120},{48,144},{72,168},{96,0},{120,24},{144,48},{168,72... | collective-permute-start | bytes 16904 | tf_op jit(solution)/shard_map/ppermute | solution.py:49
  42.0 7.2 %collective-permute-start.4 = (f32[2,2,1,352]{3,1,0,2:T(2,128)S(1)}, f32[2,2,1,352]{3,1,0,2:T(2,128)S(1)}, u32[]{:S(2)}, u32[]{:S(2)}) collective-permute-start(f32[2,2,1,352]{3,1,0,2:T(2,128)S(1)} %get-tuple-element.29), channel_id=1, source_target_pairs={{0,576},{192,0},{384,192},{576,384},{1,577},{193,1},{385,193},{577... | collective-permute-start | bytes 16904 | tf_op jit(solution)/shard_map/ppermute | solution.py:20
  44.0 5.9 %collective-permute-start.5 = (f32[2,2,1,352]{3,1,0,2:T(2,128)S(1)}, f32[2,2,1,352]{3,1,0,2:T(2,128)S(1)}, u32[]{:S(2)}, u32[]{:S(2)}) collective-permute-start(f32[2,2,1,352]{3,1,0,2:T(2,128)S(1)} %get-tuple-element.29), channel_id=1, source_target_pairs={{0,384},{192,576},{384,0},{576,192},{1,385},{193,577},{385,1},{577... | collective-permute-start | bytes 16904 | tf_op jit(solution)/shard_map/ppermute | solution.py:20
  45.9 6.8 %collective-permute-start.6 = (f32[2,2,1,352]{3,1,2,0:T(2,128)S(1)}, f32[2,2,1,352]{3,1,2,0:T(2,128)S(1)}, u32[]{:S(2)}, u32[]{:S(2)}) collective-permute-start(f32[2,2,1,352]{3,1,2,0:T(2,128)S(1)} %get-tuple-element.28), channel_id=1, source_target_pairs={{0,192},{192,384},{384,576},{576,0},{1,193},{193,385},{385,577},{5... | collective-permute-start | bytes 16904 | tf_op jit(solution)/shard_map/ppermute | solution.py:20
  85.2 52.1 %all-to-all-start = ((bf16[64,64,66]{2,0,1:T(8,128)(2,1)}), bf16[64,64,66]{2,0,1:T(8,128)(2,1)}, u32[]{:S(2)}, u32[]{:S(2)}) async-start(bf16[64,64,66]{2,0,1:T(8,128)(2,1)} %copy.14), calls=%async_computation | async-start | bytes 2097152 | tf_op jit(solution)/shard_map/all_to_all | solution.py:114
  158.3 9.3 %collective-permute-start.7 = (bf16[66,352]{1,0:T(8,128)(2,1)S(1)}, bf16[66,352]{1,0:T(8,128)(2,1)S(1)}, u32[]{:S(2)}, u32[]{:S(2)}) collective-permute-start(bf16[66,352]{1,0:T(8,128)(2,1)S(1)} %select_convert_fusion), channel_id=1, source_target_pairs={{0,576},{192,0},{384,192},{576,384},{1,577},{193,1},{385,193},{577... | collective-permute-start | bytes 139400 | tf_op jit(solution)/shard_map/ppermute | solution.py:20
  162.9 6.4 %collective-permute-start.8 = (bf16[66,352]{1,0:T(8,128)(2,1)S(1)}, bf16[66,352]{1,0:T(8,128)(2,1)S(1)}, u32[]{:S(2)}, u32[]{:S(2)}) collective-permute-start(bf16[66,352]{1,0:T(8,128)(2,1)S(1)} %select_convert_fusion), channel_id=1, source_target_pairs={{0,384},{192,576},{384,0},{576,192},{1,385},{193,577},{385,1},{577... | collective-permute-start | bytes 139400 | tf_op jit(solution)/shard_map/ppermute | solution.py:20
  165.1 6.1 %collective-permute-start.9 = (bf16[66,352]{1,0:T(8,128)(2,1)S(1)}, bf16[66,352]{1,0:T(8,128)(2,1)S(1)}, u32[]{:S(2)}, u32[]{:S(2)}) collective-permute-start(bf16[66,352]{1,0:T(8,128)(2,1)S(1)} %select_convert_fusion), channel_id=1, source_target_pairs={{0,192},{192,384},{384,576},{576,0},{1,193},{193,385},{385,577},{5... | collective-permute-start | bytes 139400 | tf_op jit(solution)/shard_map/ppermute | solution.py:20
  171.2 6.7 %collective-permute-start.10 = (bf16[4,66,352]{2,1,0:T(8,128)(2,1)S(1)}, bf16[4,66,352]{2,1,0:T(8,128)(2,1)S(1)}, u32[]{:S(2)}, u32[]{:S(2)}) collective-permute-start(bf16[4,66,352]{2,1,0:T(8,128)(2,1)S(1)} %pad_maximum_fusion.1), channel_id=1, source_target_pairs={{0,168},{24,0},{48,24},{72,48},{96,72},{120,96},{144,120},{168,144... | collective-permute-start | bytes 557576 | tf_op jit(solution)/shard_map/ppermute | solution.py:13
  174.2 7.9 %collective-permute-start.13 = (bf16[4,66,352]{2,1,0:T(8,128)(2,1)S(1)}, bf16[4,66,352]{2,1,0:T(8,128)(2,1)S(1)}, u32[]{:S(2)}, u32[]{:S(2)}) collective-permute-start(bf16[4,66,352]{2,1,0:T(8,128)(2,1)S(1)} %pad_maximum_fusion.1), channel_id=1, source_target_pairs={{0,24},{24,48},{48,72},{72,96},{96,120},{120,144},{144,168},{168,0... | collective-permute-start | bytes 557576 | tf_op jit(solution)/shard_map/ppermute | solution.py:13
  177.9 7.0 %collective-permute-start.11 = (bf16[4,66,352]{2,1,0:T(8,128)(2,1)S(1)}, bf16[4,66,352]{2,1,0:T(8,128)(2,1)S(1)}, u32[]{:S(2)}, u32[]{:S(2)}) collective-permute-start(bf16[4,66,352]{2,1,0:T(8,128)(2,1)S(1)} %collective-permute-done.10), channel_id=1, source_target_pairs={{0,168},{24,0},{48,24},{72,48},{96,72},{120,96},{144,120},{168,144... | collective-permute-start | bytes 557576 | tf_op jit(solution)/shard_map/ppermute | solution.py:13
  182.0 7.9 %collective-permute-start.14 = (bf16[4,66,352]{2,1,0:T(8,128)(2,1)S(1)}, bf16[4,66,352]{2,1,0:T(8,128)(2,1)S(1)}, u32[]{:S(2)}, u32[]{:S(2)}) collective-permute-start(bf16[4,66,352]{2,1,0:T(8,128)(2,1)S(1)} %collective-permute-done.13), channel_id=1, source_target_pairs={{0,24},{24,48},{48,72},{72,96},{96,120},{120,144},{144,168},{168,0... | collective-permute-start | bytes 557576 | tf_op jit(solution)/shard_map/ppermute | solution.py:13
  184.9 14.8 %collective-permute-start.12 = (bf16[4,66,352]{2,1,0:T(8,128)(2,1)S(1)}, bf16[4,66,352]{2,1,0:T(8,128)(2,1)S(1)}, u32[]{:S(2)}, u32[]{:S(2)}) collective-permute-start(bf16[4,66,352]{2,1,0:T(8,128)(2,1)S(1)} %collective-permute-done.11), channel_id=1, source_target_pairs={{0,168},{24,0},{48,24},{72,48},{96,72},{120,96},{144,120},{168,144... | collective-permute-start | bytes 557576 | tf_op jit(solution)/shard_map/ppermute | solution.py:13
  189.9 7.9 %collective-permute-start.15 = (bf16[4,66,352]{2,1,0:T(8,128)(2,1)S(1)}, bf16[4,66,352]{2,1,0:T(8,128)(2,1)S(1)}, u32[]{:S(2)}, u32[]{:S(2)}) collective-permute-start(bf16[4,66,352]{2,1,0:T(8,128)(2,1)S(1)} %collective-permute-done.14), channel_id=1, source_target_pairs={{0,24},{24,48},{48,72},{72,96},{96,120},{120,144},{144,168},{168,0... | collective-permute-start | bytes 557576 | tf_op jit(solution)/shard_map/ppermute | solution.py:13
  197.8 7.9 %collective-permute-start.16 = (bf16[4,66,352]{2,1,0:T(8,128)(2,1)S(1)}, bf16[4,66,352]{2,1,0:T(8,128)(2,1)S(1)}, u32[]{:S(2)}, u32[]{:S(2)}) collective-permute-start(bf16[4,66,352]{2,1,0:T(8,128)(2,1)S(1)} %collective-permute-done.15), channel_id=1, source_target_pairs={{0,24},{24,48},{48,72},{72,96},{96,120},{120,144},{144,168},{168,0... | collective-permute-start | bytes 557576 | tf_op jit(solution)/shard_map/ppermute | solution.py:13
  206.5 11.8 %collective-permute-start.17 = (bf16[8,4,66,352]{3,0,2,1:T(8,128)(2,1)S(1)}, bf16[8,4,66,352]{3,0,2,1:T(8,128)(2,1)S(1)}, u32[]{:S(2)}, u32[]{:S(2)}) collective-permute-start(bf16[8,4,66,352]{3,0,2,1:T(8,128)(2,1)S(1)} %copy.18), channel_id=1, source_target_pairs={{0,12},{12,0},{1,13},{13,1},{2,14},{14,2},{3,15},{15,3},{4,16},{16... | collective-permute-start | bytes 4460552 | tf_op jit(solution)/shard_map/ppermute | solution.py:13
Sparse Core Ops, SparseCore 0:
  53.6 100.8 all-gather.2

commit v12 on v10

--- a/solution.py
+++ b/solution.py
@@ -126,22 +126,28 @@
     grad_block = jnp.where(row_ids == col_ids, 2.0 * (corr - 1.0), 2.0 * off_weight * corr).astype(
         jnp.bfloat16
     )
-    grad_t = dp_ring_gather(grad_block.T).reshape(dp_count * width, rows)
+    own = ring_gather(direct_gather(grad_block.T, "x"), "y")
+    other = shift(own, "c", nc, 1)
+    half = ny * nx * width
     t = lax.iota(jnp.int32, width)
-    cc = (lax.iota(jnp.int32, nc) + ic) % nc
     yy = (lax.iota(jnp.int32, ny) + iy) % ny
     xx = (lax.iota(jnp.int32, nx) + ix) % nx
-    perm_cols = (
-        ((xx[None, None, :, None] * ny + yy[None, :, None, None]) * nc + cc[:, None, None, None]) * width
-        + t[None, None, None, :]
-    ).reshape(-1)
-    grad_wide = grad_t.astype(jnp.float32)
     row_flat = mp_index * rows + lax.iota(jnp.int32, rows)
-    diag_val = jnp.sum(jnp.where(perm_cols[:, None] == row_flat[None, :], grad_wide, 0.0), axis=0)
-    scale_sum = (jnp.sum(grad_wide * grad_wide, axis=0) - diag_val * diag_val) / (
-        2.0 * off_weight
-    ) + diag_val * (1.0 + diag_val / 2.0)
-    back = jnp.dot(second_perm, grad_t, preferred_element_type=jnp.float32)
+    back = None
+    sq_sum = None
+    diag_val = None
+    for k, part in enumerate((own, other)):
+        cc = (ic + k) % nc
+        perm_cols = (((xx[None, :, None] * ny + yy[:, None, None]) * nc + cc) * width + t[None, None, :]).reshape(-1)
+        g = part.reshape(half, rows)
+        g_wide = g.astype(jnp.float32)
+        d = jnp.sum(jnp.where(perm_cols[:, None] == row_flat[None, :], g_wide, 0.0), axis=0)
+        q = jnp.sum(g_wide * g_wide, axis=0)
+        b = jnp.dot(second_perm[:, k * half:(k + 1) * half], g, preferred_element_type=jnp.float32)
+        back = b if back is None else back + b
+        sq_sum = q if sq_sum is None else sq_sum + q
+        diag_val = d if diag_val is None else diag_val + d
+    scale_sum = (sq_sum - diag_val * diag_val) / (2.0 * off_weight) + diag_val * (1.0 + diag_val / 2.0)
     result = (back - first.astype(jnp.float32) * scale_sum[None, :]) * inv_std0
     return result.astype(jnp.bfloat16)
 

time: 226 us -> 229 us (1.013)
  local copies, waits for them, and re-layouts: 30.9 us -> 37.4 us
  waiting for transfers between devices: 44.2 us -> 41.4 us
    ppermute x8, waiting for transfers between devices: 18.6 us -> 15.8 us  [shift(): return lax.ppermute(v, axis, [(i, (i + step) % n) for i in range(n)])]
    ppermute x1, local copies, waits for them, and re-layouts: 0.23 us -> 2.86 us  [shift(): return lax.ppermute(v, axis, [(i, (i + step) % n) for i in range(n)])]
    another operation x1 -> x0, other arithmetic: 2.48 us -> none  [ring_gather(): return jnp.stack([got[t] for t in range(n)])]
    reshape x1 -> x2, local copies, waits for them, and re-layouts: 5.85 us -> 7.38 us  [shards(): g = part.reshape(half, rows)]
  transfers between devices with their start and end apart: 20 -> 20, of which waited for: 14 -> 13; matrix products, arithmetic and copies ran while one was open for 14% -> 15% of each run, Pallas kernels for 0% -> 0%
where the time goes in v12:
time: 229 us; the launch traced here: 228 us
  starting transfers between devices  79.6 us (35%)
  waiting for transfers between devices  41.4 us (18%)
  local copies, waits for them, and re-layouts  37.4 us (16%)
  other arithmetic  24.7 us (11%)
  blocking collectives  23.4 us (10%)
  between operations  14 us (6%)
  matrix products  7.26 us (3%)
    ppermute x8, starting transfers between devices, shift(): return lax.ppermute(v, axis, [(i, (i + step) % n) for i in range(n)])  26.1 us
    all_gather x1, blocking collectives, shards(): stacked = lax.all_gather(second, 'mp', axis=0)  23.4 us
    all_to_all x1, starting transfers between devices, shards(): lax.all_to_all(second_full, DP, split_axis=1, concat_axis=0, tiled=True)  19.4 us
    ppermute x4, starting transfers between devices, combine(): other = lax.ppermute(jnp.stack([mean, m2]), axis, pairs)  18.2 us
    ppermute x6, starting transfers between devices, direct_gather(): got[t] = lax.ppermute(v, axis, [(i, (i - t) % n) for i in range(n)])  15.9 us
    ppermute x8, waiting for transfers between devices, shift(): return lax.ppermute(v, axis, [(i, (i + step) % n) for i in range(n)])  15.8 us
    ppermute x4, waiting for transfers between devices, combine(): other = lax.ppermute(jnp.stack([mean, m2]), axis, pairs)  12.9 us
    all_to_all x3, local copies, waits for them, and re-layouts, shards(): lax.all_to_all(second_full, DP, split_axis=1, concat_axis=0, tiled=True)  9.14 us
  transfers between devices with their start and end apart: 20, of which 13 were waited for; matrix products, arithmetic and copies ran while one was open for 15% of the time, Pallas kernels for 0%

profile of v12, /device:TPU:1, one launch (start us, length us, event | category | flops | bytes accessed | tf_op | source)
XLA Modules:
  0.0 227.7 jit_solution(10956053020475724082)
XLA Ops:
  6.5 1.8 copy-done
  8.4 2.3 %fusion.5 = f32[2,64,352]{2,1,0:T(8,128)S(1)} fusion(bf16[2,64,4224]{2,1,0:T(8,128)(2,1)} %param.2, bf16[4224,352]{0,1:T(8,128)(2,1)S(1)} %copy-done), kind=kOutput, calls=%fused_computation.12 | convolution fusion | flops 380633088 | bytes 4235264 | tf_op jit(solution)/shard_map/vbh,hc->vbc/dot_general | solution.py:102
  10.7 0.6 fusion.33
  11.4 0.0 all-gather.3.cloned.1.call-update
  11.4 12.4 %collective-permute-start = (f32[2,1,1,352]{3,2,1,0:T(1,128)S(1)}, f32[2,1,1,352]{3,2,1,0:T(1,128)S(1)}, u32[]{:S(2)}, u32[]{:S(2)}) collective-permute-start(f32[2,1,1,352]{3,2,1,0:T(1,128)S(1)} %pad_maximum_fusion.1), channel_id=1, source_target_pairs={{0,12},{12,0},{1,13},{13,1},{2,14},{14,2},{3,15},{15,3},{4,16},{16... | collective-permute-start | bytes 8456 | tf_op jit(solution)/shard_map/ppermute | solution.py:49
  23.9 0.8 collective-permute-done
  24.7 1.9 collective-permute-start.1
  26.6 2.4 %collective-permute-done.1 = f32[2,1,1,352]{3,2,1,0:T(1,128)S(1)} collective-permute-done((f32[2,1,1,352]{3,2,1,0:T(1,128)S(1)}, f32[2,1,1,352]{3,2,1,0:T(1,128)S(1)}, u32[]{:S(2)}, u32[]{:S(2)}) %collective-permute-start.1) | collective-permute-done | bytes 2848 | tf_op jit(solution)/shard_map/ppermute | solution.py:49
  29.1 1.9 collective-permute-start.2
  31.0 3.3 %collective-permute-done.2 = f32[2,1,1,352]{3,2,1,0:T(1,128)S(1)} collective-permute-done((f32[2,1,1,352]{3,2,1,0:T(1,128)S(1)}, f32[2,1,1,352]{3,2,1,0:T(1,128)S(1)}, u32[]{:S(2)}, u32[]{:S(2)}) %collective-permute-start.2) | collective-permute-done | bytes 2848 | tf_op jit(solution)/shard_map/ppermute | solution.py:49
  34.3 1.9 collective-permute-start.3
  36.3 6.3 %collective-permute-done.3 = f32[2,1,1,352]{3,2,1,0:T(1,128)S(1)} collective-permute-done((f32[2,1,1,352]{3,2,1,0:T(1,128)S(1)}, f32[2,1,1,352]{3,2,1,0:T(1,128)S(1)}, u32[]{:S(2)}, u32[]{:S(2)}) %collective-permute-start.3) | collective-permute-done | bytes 2848 | tf_op jit(solution)/shard_map/ppermute | solution.py:49
  42.6 1.9 collective-permute-start.4
  44.6 1.9 collective-permute-start.5
  46.5 3.4 %collective-permute-start.6 = (f32[2,1,1,352]{3,2,1,0:T(1,128)S(1)}, f32[2,1,1,352]{3,2,1,0:T(1,128)S(1)}, u32[]{:S(2)}, u32[]{:S(2)}) collective-permute-start(f32[2,1,1,352]{3,2,1,0:T(1,128)S(1)} %pad_maximum_fusion.5), channel_id=1, source_target_pairs={{0,192},{192,384},{384,576},{576,0},{1,193},{193,385},{385,577},{5... | collective-permute-start | bytes 8456 | tf_op jit(solution)/shard_map/ppermute | solution.py:20
  49.9 0.6 collective-permute-done.5
  50.5 2.9 %collective-permute-done.6 = f32[2,1,1,352]{3,2,1,0:T(1,128)S(1)} collective-permute-done((f32[2,1,1,352]{3,2,1,0:T(1,128)S(1)}, f32[2,1,1,352]{3,2,1,0:T(1,128)S(1)}, u32[]{:S(2)}, u32[]{:S(2)}) %collective-permute-start.6) | collective-permute-done | bytes 2848 | tf_op jit(solution)/shard_map/ppermute | solution.py:20
  53.5 0.1 multiply_reduce_fusion.2
  53.5 23.4 %all_gather.7 = bf16[12,64,352]{2,1,0:T(8,128)(2,1)S(1)} all-gather(bf16[1,64,352]{2,1,0:T(8,128)(2,1)S(1)} %divide_convert_fusion.4), channel_id=1, replica_groups=mesh['x'=4,'y'=8,'c'=2,'mp'=12] {'mp'}, dimensions={0}, use_global_device_ids=true | all-gather | bytes 585728 | tf_op jit(solution)/shard_map/all_gather | solution.py:113
  77.0 1.2 copy.7
  78.2 4.0 %all_to_all.14 = bf16[64,64,66]{2,1,0:T(8,128)(2,1)} reshape(bf16[64,12,352]{2,1,0:T(8,128)(2,1)} %copy.7) | data formatting | bytes 1081344 | tf_op jit(solution)/shard_map/all_to_all | solution.py:116
  82.2 2.9 %copy.8 = bf16[64,64,66]{2,0,1:T(8,128)(2,1)} copy(bf16[64,64,66]{2,1,0:T(8,128)(2,1)} %all_to_all.14) | data formatting | bytes 1081344 | tf_op jit(solution)/shard_map/all_to_all | solution.py:116
  85.1 19.4 %all-to-all-start = ((bf16[64,64,66]{2,0,1:T(8,128)(2,1)}), bf16[64,64,66]{2,0,1:T(8,128)(2,1)}, u32[]{:S(2)}, u32[]{:S(2)}) async-start(bf16[64,64,66]{2,0,1:T(8,128)(2,1)} %copy.8), calls=%async_computation | async-start | bytes 2097152 | tf_op jit(solution)/shard_map/all_to_all | solution.py:116
  104.6 6.1 %reshape_reshape.3 = bf16[64,4,8,2,66]{4,3,2,1,0:T(2,128)(2,1)} reshape(bf16[64,12,352]{2,1,0:T(8,128)(2,1)} %copy.7) | data formatting | bytes 1081344 | tf_op jit(solution)/shard_map/reshape;reshape | solution.py:117
  110.7 4.2 %fusion.11 = bf16[64,4,8,2,66]{4,3,2,1,0:T(2,128)(2,1)S(1)} fusion(s32[]{:T(128)S(6)} %select_n.90, bf16[64,4,8,2,66]{4,3,2,1,0:T(2,128)(2,1)} %reshape_reshape.3), kind=kLoop, calls=%fused_computation.25 | loop fusion | flops 270336 | bytes 1081348 | tf_op jit(solution)/shard_map/jit(_roll_dynamic)/concatenate | solution.py:89
  114.9 4.1 %fusion.10 = bf16[64,4,8,2,66]{4,3,2,1,0:T(2,128)(2,1)S(1)} fusion(s32[]{:T(128)S(6)} %select_n.92, bf16[64,4,8,2,66]{4,3,2,1,0:T(2,128)(2,1)S(1)} %fusion.11), kind=kLoop, calls=%fused_computation.24 | loop fusion | flops 270336 | bytes 1081348 | tf_op jit(solution)/shard_map/jit(_roll_dynamic)/concatenate | solution.py:89
  119.0 4.7 %fusion.13 = bf16[64,2,8,4,66]{4,1,2,3,0:T(2,128)(2,1)S(1)} fusion(s32[]{:T(128)S(6)} %select_n.94, bf16[64,4,8,2,66]{4,3,2,1,0:T(2,128)(2,1)S(1)} %fusion.10), kind=kLoop, calls=%fused_computation.27 | loop fusion | flops 1081344 | bytes 1081348 | tf_op jit(solution)/shard_map/transpose | solution.py:118
  123.7 1.6 copy.11
  125.3 3.1 %reshape.521 = bf16[64,4224]{1,0:T(8,128)(2,1)} reshape(bf16[64,2,8,4,66]{4,3,2,1,0:T(4,128)(2,1)} %copy.11) | data formatting | bytes 1081344 | tf_op jit(solution)/shard_map/reshape | solution.py:118
  128.4 5.1 %all-to-all-done = bf16[64,64,66]{2,0,1:T(8,128)(2,1)} async-done(((bf16[64,64,66]{2,0,1:T(8,128)(2,1)}), bf16[64,64,66]{2,0,1:T(8,128)(2,1)}, u32[]{:S(2)}, u32[]{:S(2)}) %all-to-all-start) | async-done | bytes 540704 | tf_op jit(solution)/shard_map/all_to_all | solution.py:116
  133.5 2.3 copy.15
  135.8 3.4 %reduce_sum.74 = f32[352]{0:T(512)S(1)} reduce(f32[1,4096,352]{2,1,0:T(8,128)} %all-gather.3.cloned.1.call-done, f32[]{:T(128)} %constant.137.clone.1), dimensions={0,1}, to_apply=%region_2.0 | reduce | flops 1441440 | bytes 5768580 | tf_op jit(solution)/shard_map/reduce_sum | solution.py:104
  139.1 3.7 %multiply_reduce_fusion = f32[352]{0:T(512)S(1)} fusion(f32[1,4096,352]{2,1,0:T(8,128)} %all-gather.3.cloned.1.call-done, f32[352]{0:T(512)S(1)} %broadcast_multiply_fusion), kind=kLoop, calls=%fused_computation.2 | loop fusion | flops 4325024 | bytes 5769984 | tf_op jit(solution)/shard_map/reduce_sum | solution.py:106
  142.9 0.8 copy-done.1
  143.7 1.9 select_convert_fusion
  145.6 3.8 %collective-permute-start.7 = (bf16[66,352]{1,0:T(8,128)(2,1)S(1)}, bf16[66,352]{1,0:T(8,128)(2,1)S(1)}, u32[]{:S(2)}, u32[]{:S(2)}) collective-permute-start(bf16[66,352]{1,0:T(8,128)(2,1)S(1)} %select_convert_fusion), channel_id=1, source_target_pairs={{0,576},{192,0},{384,192},{576,384},{1,577},{193,1},{385,193},{577... | collective-permute-start | bytes 139400 | tf_op jit(solution)/shard_map/ppermute | solution.py:20
  149.4 2.3 collective-permute-start.8
  151.7 2.6 %collective-permute-start.9 = (bf16[66,352]{1,0:T(8,128)(2,1)S(1)}, bf16[66,352]{1,0:T(8,128)(2,1)S(1)}, u32[]{:S(2)}, u32[]{:S(2)}) collective-permute-start(bf16[66,352]{1,0:T(8,128)(2,1)S(1)} %select_convert_fusion), channel_id=1, source_target_pairs={{0,192},{192,384},{384,576},{576,0},{1,193},{193,385},{385,577},{5... | collective-permute-start | bytes 139400 | tf_op jit(solution)/shard_map/ppermute | solution.py:20
  154.3 2.3 %collective-permute-done.8 = bf16[66,352]{1,0:T(8,128)(2,1)S(1)} collective-permute-done((bf16[66,352]{1,0:T(8,128)(2,1)S(1)}, bf16[66,352]{1,0:T(8,128)(2,1)S(1)}, u32[]{:S(2)}, u32[]{:S(2)}) %collective-permute-start.8) | collective-permute-done | bytes 46496 | tf_op jit(solution)/shard_map/ppermute | solution.py:20
  156.7 1.7 collective-permute-done.9
  158.4 0.1 pad_maximum_fusion
  158.5 1.9 collective-permute-start.10
  160.4 3.4 %collective-permute-start.13 = (bf16[4,66,352]{2,1,0:T(8,128)(2,1)S(1)}, bf16[4,66,352]{2,1,0:T(8,128)(2,1)S(1)}, u32[]{:S(2)}, u32[]{:S(2)}) collective-permute-start(bf16[4,66,352]{2,1,0:T(8,128)(2,1)S(1)} %pad_maximum_fusion), channel_id=1, source_target_pairs={{0,24},{24,48},{48,72},{72,96},{96,120},{120,144},{144,168},{168,0... | collective-permute-start | bytes 557576 | tf_op jit(solution)/shard_map/ppermute | solution.py:13
  163.8 2.8 %collective-permute-done.10 = bf16[4,66,352]{2,1,0:T(8,128)(2,1)S(1)} collective-permute-done((bf16[4,66,352]{2,1,0:T(8,128)(2,1)S(1)}, bf16[4,66,352]{2,1,0:T(8,128)(2,1)S(1)}, u32[]{:S(2)}, u32[]{:S(2)}) %collective-permute-start.10) | collective-permute-done | bytes 185888 | tf_op jit(solution)/shard_map/ppermute | solution.py:13
  166.6 2.0 collective-permute-start.11
  168.6 3.3 %collective-permute-start.14 = (bf16[4,66,352]{2,1,0:T(8,128)(2,1)S(1)}, bf16[4,66,352]{2,1,0:T(8,128)(2,1)S(1)}, u32[]{:S(2)}, u32[]{:S(2)}) collective-permute-start(bf16[4,66,352]{2,1,0:T(8,128)(2,1)S(1)} %collective-permute-done.13), channel_id=1, source_target_pairs={{0,24},{24,48},{48,72},{72,96},{96,120},{120,144},{144,168},{168,0... | collective-permute-start | bytes 557576 | tf_op jit(solution)/shard_map/ppermute | solution.py:13
  172.0 1.9 collective-permute-done.11
  173.9 2.6 %collective-permute-start.12 = (bf16[4,66,352]{2,1,0:T(8,128)(2,1)S(1)}, bf16[4,66,352]{2,1,0:T(8,128)(2,1)S(1)}, u32[]{:S(2)}, u32[]{:S(2)}) collective-permute-start(bf16[4,66,352]{2,1,0:T(8,128)(2,1)S(1)} %collective-permute-done.11), channel_id=1, source_target_pairs={{0,168},{24,0},{48,24},{72,48},{96,72},{120,96},{144,120},{168,144... | collective-permute-start | bytes 557576 | tf_op jit(solution)/shard_map/ppermute | solution.py:13
  176.5 0.0 collective-permute-done.14
  176.5 2.6 %collective-permute-start.15 = (bf16[4,66,352]{2,1,0:T(8,128)(2,1)S(1)}, bf16[4,66,352]{2,1,0:T(8,128)(2,1)S(1)}, u32[]{:S(2)}, u32[]{:S(2)}) collective-permute-start(bf16[4,66,352]{2,1,0:T(8,128)(2,1)S(1)} %collective-permute-done.14), channel_id=1, source_target_pairs={{0,24},{24,48},{48,72},{72,96},{96,120},{120,144},{144,168},{168,0... | collective-permute-start | bytes 557576 | tf_op jit(solution)/shard_map/ppermute | solution.py:13
  179.2 5.2 %collective-permute-done.15 = bf16[4,66,352]{2,1,0:T(8,128)(2,1)S(1)} collective-permute-done((bf16[4,66,352]{2,1,0:T(8,128)(2,1)S(1)}, bf16[4,66,352]{2,1,0:T(8,128)(2,1)S(1)}, u32[]{:S(2)}, u32[]{:S(2)}) %collective-permute-start.15) | collective-permute-done | bytes 185888 | tf_op jit(solution)/shard_map/ppermute | solution.py:13
  184.4 1.9 collective-permute-start.16
  186.4 5.9 %collective-permute-done.16 = bf16[4,66,352]{2,1,0:T(8,128)(2,1)S(1)} collective-permute-done((bf16[4,66,352]{2,1,0:T(8,128)(2,1)S(1)}, bf16[4,66,352]{2,1,0:T(8,128)(2,1)S(1)}, u32[]{:S(2)}, u32[]{:S(2)}) %collective-permute-start.16) | collective-permute-done | bytes 185888 | tf_op jit(solution)/shard_map/ppermute | solution.py:13
  192.5 1.2 copy-done.2
  193.7 1.7 copy.12
  195.4 8.3 %collective-permute-start.17 = (bf16[8,4,66,352]{3,0,2,1:T(8,128)(2,1)}, bf16[8,4,66,352]{3,0,2,1:T(8,128)(2,1)}, u32[]{:S(2)}, u32[]{:S(2)}) collective-permute-start(bf16[8,4,66,352]{3,0,2,1:T(8,128)(2,1)} %copy.12), channel_id=1, source_target_pairs={{0,12},{12,0},{1,13},{13,1},{2,14},{14,2},{3,15},{15,3},{4,16},{16... | collective-permute-start | bytes 4460552 | tf_op jit(solution)/shard_map/ppermute | solution.py:13
  203.8 0.1 add_multiply_fusion
  203.9 0.1 iota_add_fusion
  204.0 3.7 %reshape.522 = bf16[2112,352]{1,0:T(8,128)(2,1)} reshape(bf16[8,4,66,352]{3,2,1,0:T(8,128)(2,1)} %copy-done.2) | data formatting | bytes 2973696 | tf_op jit(solution)/shard_map/reshape | solution.py:142
  207.6 2.9 %copy.13 = bf16[8,4,66,352]{3,2,1,0:T(8,128)(2,1)} copy(bf16[8,4,66,352]{3,0,2,1:T(8,128)(2,1)} %collective-permute-done.17) | data formatting | bytes 2973696 | tf_op jit(solution)/shard_map/ppermute | solution.py:13
  210.5 3.7 %reshape.523 = bf16[2112,352]{1,0:T(8,128)(2,1)} reshape(bf16[8,4,66,352]{3,2,1,0:T(8,128)(2,1)} %copy.13) | data formatting | bytes 2973696 | tf_op jit(solution)/shard_map/reshape | solution.py:142
  214.2 2.1 fusion.14
  216.3 3.5 %fusion.2 = (f32[352]{0:T(512)S(1)}, f32[352]{0:T(512)S(1)}, f32[352]{0:T(512)S(1)}, f32[352]{0:T(512)S(1)}) fusion(bf16[8,4,66,352]{3,0,2,1:T(8,128)(2,1)} %collective-permute-done.17, s32[352]{0:T(512)S(1)} %iota_add_fusion.2, s32[8,4,66]{2,1,0:T(4,128)S(1)} %get-tuple-element.31, s32[8,4,66]{2,1,0:T(4,128)S(1)} %get-tuple-element.32, ...), kind=kLoop, calls=%fused_computation.9 | loop fusion | flops 8919680 | bytes 2997632 | tf_op jit(solution)/shard_map/reduce_sum | solution.py:145
  219.8 1.0 fusion.9
  (53 shorter events, 0.6 us)
Async XLA Ops:
  6.5 1.8 copy-start
  6.5 129.2 %all-gather.3.cloned.1.call-start = ((), (), s32[]{:S(2)}) async-start(), calls=%async_computation.1 | async-start | bytes 6389760 | tf_op jit(solution)/shard_map/all_gather | solution.py:103
  11.4 13.2 %collective-permute-start = (f32[2,1,1,352]{3,2,1,0:T(1,128)S(1)}, f32[2,1,1,352]{3,2,1,0:T(1,128)S(1)}, u32[]{:S(2)}, u32[]{:S(2)}) collective-permute-start(f32[2,1,1,352]{3,2,1,0:T(1,128)S(1)} %pad_maximum_fusion.1), channel_id=1, source_target_pairs={{0,12},{12,0},{1,13},{13,1},{2,14},{14,2},{3,15},{15,3},{4,16},{16... | collective-permute-start | bytes 8456 | tf_op jit(solution)/shard_map/ppermute | solution.py:49
  24.7 4.3 %collective-permute-start.1 = (f32[2,1,1,352]{3,2,1,0:T(1,128)S(1)}, f32[2,1,1,352]{3,2,1,0:T(1,128)S(1)}, u32[]{:S(2)}, u32[]{:S(2)}) collective-permute-start(f32[2,1,1,352]{3,2,1,0:T(1,128)S(1)} %pad_maximum_fusion.2), channel_id=1, source_target_pairs={{0,24},{24,0},{48,72},{72,48},{96,120},{120,96},{144,168},{168,144... | collective-permute-start | bytes 8456 | tf_op jit(solution)/shard_map/ppermute | solution.py:49
  29.1 5.2 %collective-permute-start.2 = (f32[2,1,1,352]{3,2,1,0:T(1,128)S(1)}, f32[2,1,1,352]{3,2,1,0:T(1,128)S(1)}, u32[]{:S(2)}, u32[]{:S(2)}) collective-permute-start(f32[2,1,1,352]{3,2,1,0:T(1,128)S(1)} %pad_maximum_fusion.3), channel_id=1, source_target_pairs={{0,48},{24,72},{48,0},{72,24},{96,144},{120,168},{144,96},{168,120... | collective-permute-start | bytes 8456 | tf_op jit(solution)/shard_map/ppermute | solution.py:49
  34.3 8.3 %collective-permute-start.3 = (f32[2,1,1,352]{3,2,1,0:T(1,128)S(1)}, f32[2,1,1,352]{3,2,1,0:T(1,128)S(1)}, u32[]{:S(2)}, u32[]{:S(2)}) collective-permute-start(f32[2,1,1,352]{3,2,1,0:T(1,128)S(1)} %pad_maximum_fusion.4), channel_id=1, source_target_pairs={{0,96},{24,120},{48,144},{72,168},{96,0},{120,24},{144,48},{168,72... | collective-permute-start | bytes 8456 | tf_op jit(solution)/shard_map/ppermute | solution.py:49
  42.6 7.2 %collective-permute-start.4 = (f32[2,1,1,352]{3,2,1,0:T(1,128)S(1)}, f32[2,1,1,352]{3,2,1,0:T(1,128)S(1)}, u32[]{:S(2)}, u32[]{:S(2)}) collective-permute-start(f32[2,1,1,352]{3,2,1,0:T(1,128)S(1)} %pad_maximum_fusion.5), channel_id=1, source_target_pairs={{0,576},{192,0},{384,192},{576,384},{1,577},{193,1},{385,193},{577... | collective-permute-start | bytes 8456 | tf_op jit(solution)/shard_map/ppermute | solution.py:20
  44.6 5.9 %collective-permute-start.5 = (f32[2,1,1,352]{3,2,1,0:T(1,128)S(1)}, f32[2,1,1,352]{3,2,1,0:T(1,128)S(1)}, u32[]{:S(2)}, u32[]{:S(2)}) collective-permute-start(f32[2,1,1,352]{3,2,1,0:T(1,128)S(1)} %pad_maximum_fusion.5), channel_id=1, source_target_pairs={{0,384},{192,576},{384,0},{576,192},{1,385},{193,577},{385,1},{577... | collective-permute-start | bytes 8456 | tf_op jit(solution)/shard_map/ppermute | solution.py:20
  46.5 6.9 %collective-permute-start.6 = (f32[2,1,1,352]{3,2,1,0:T(1,128)S(1)}, f32[2,1,1,352]{3,2,1,0:T(1,128)S(1)}, u32[]{:S(2)}, u32[]{:S(2)}) collective-permute-start(f32[2,1,1,352]{3,2,1,0:T(1,128)S(1)} %pad_maximum_fusion.5), channel_id=1, source_target_pairs={{0,192},{192,384},{384,576},{576,0},{1,193},{193,385},{385,577},{5... | collective-permute-start | bytes 8456 | tf_op jit(solution)/shard_map/ppermute | solution.py:20
  85.1 48.4 %all-to-all-start = ((bf16[64,64,66]{2,0,1:T(8,128)(2,1)}), bf16[64,64,66]{2,0,1:T(8,128)(2,1)}, u32[]{:S(2)}, u32[]{:S(2)}) async-start(bf16[64,64,66]{2,0,1:T(8,128)(2,1)} %copy.8), calls=%async_computation | async-start | bytes 2097152 | tf_op jit(solution)/shard_map/all_to_all | solution.py:116
  139.1 4.6 %copy-start.1 = (f32[1,4096,352]{2,1,0:T(8,128)S(1)}, f32[1,4096,352]{2,1,0:T(8,128)}, u32[]{:S(2)}) copy-start(f32[1,4096,352]{2,1,0:T(8,128)} %all-gather.3.cloned.1.call-done) | copy-start | bytes 17301508
  145.6 8.7 %collective-permute-start.7 = (bf16[66,352]{1,0:T(8,128)(2,1)S(1)}, bf16[66,352]{1,0:T(8,128)(2,1)S(1)}, u32[]{:S(2)}, u32[]{:S(2)}) collective-permute-start(bf16[66,352]{1,0:T(8,128)(2,1)S(1)} %select_convert_fusion), channel_id=1, source_target_pairs={{0,576},{192,0},{384,192},{576,384},{1,577},{193,1},{385,193},{577... | collective-permute-start | bytes 139400 | tf_op jit(solution)/shard_map/ppermute | solution.py:20
  149.4 7.3 %collective-permute-start.8 = (bf16[66,352]{1,0:T(8,128)(2,1)S(1)}, bf16[66,352]{1,0:T(8,128)(2,1)S(1)}, u32[]{:S(2)}, u32[]{:S(2)}) collective-permute-start(bf16[66,352]{1,0:T(8,128)(2,1)S(1)} %select_convert_fusion), channel_id=1, source_target_pairs={{0,384},{192,576},{384,0},{576,192},{1,385},{193,577},{385,1},{577... | collective-permute-start | bytes 139400 | tf_op jit(solution)/shard_map/ppermute | solution.py:20
  151.7 6.7 %collective-permute-start.9 = (bf16[66,352]{1,0:T(8,128)(2,1)S(1)}, bf16[66,352]{1,0:T(8,128)(2,1)S(1)}, u32[]{:S(2)}, u32[]{:S(2)}) collective-permute-start(bf16[66,352]{1,0:T(8,128)(2,1)S(1)} %select_convert_fusion), channel_id=1, source_target_pairs={{0,192},{192,384},{384,576},{576,0},{1,193},{193,385},{385,577},{5... | collective-permute-start | bytes 139400 | tf_op jit(solution)/shard_map/ppermute | solution.py:20
  158.5 8.2 %collective-permute-start.10 = (bf16[4,66,352]{2,1,0:T(8,128)(2,1)S(1)}, bf16[4,66,352]{2,1,0:T(8,128)(2,1)S(1)}, u32[]{:S(2)}, u32[]{:S(2)}) collective-permute-start(bf16[4,66,352]{2,1,0:T(8,128)(2,1)S(1)} %pad_maximum_fusion), channel_id=1, source_target_pairs={{0,168},{24,0},{48,24},{72,48},{96,72},{120,96},{144,120},{168,144... | collective-permute-start | bytes 557576 | tf_op jit(solution)/shard_map/ppermute | solution.py:13
  160.4 8.2 %collective-permute-start.13 = (bf16[4,66,352]{2,1,0:T(8,128)(2,1)S(1)}, bf16[4,66,352]{2,1,0:T(8,128)(2,1)S(1)}, u32[]{:S(2)}, u32[]{:S(2)}) collective-permute-start(bf16[4,66,352]{2,1,0:T(8,128)(2,1)S(1)} %pad_maximum_fusion), channel_id=1, source_target_pairs={{0,24},{24,48},{48,72},{72,96},{96,120},{120,144},{144,168},{168,0... | collective-permute-start | bytes 557576 | tf_op jit(solution)/shard_map/ppermute | solution.py:13
  166.6 7.2 %collective-permute-start.11 = (bf16[4,66,352]{2,1,0:T(8,128)(2,1)S(1)}, bf16[4,66,352]{2,1,0:T(8,128)(2,1)S(1)}, u32[]{:S(2)}, u32[]{:S(2)}) collective-permute-start(bf16[4,66,352]{2,1,0:T(8,128)(2,1)S(1)} %collective-permute-done.10), channel_id=1, source_target_pairs={{0,168},{24,0},{48,24},{72,48},{96,72},{120,96},{144,120},{168,144... | collective-permute-start | bytes 557576 | tf_op jit(solution)/shard_map/ppermute | solution.py:13
  168.6 7.9 %collective-permute-start.14 = (bf16[4,66,352]{2,1,0:T(8,128)(2,1)S(1)}, bf16[4,66,352]{2,1,0:T(8,128)(2,1)S(1)}, u32[]{:S(2)}, u32[]{:S(2)}) collective-permute-start(bf16[4,66,352]{2,1,0:T(8,128)(2,1)S(1)} %collective-permute-done.13), channel_id=1, source_target_pairs={{0,24},{24,48},{48,72},{72,96},{96,120},{120,144},{144,168},{168,0... | collective-permute-start | bytes 557576 | tf_op jit(solution)/shard_map/ppermute | solution.py:13
  173.9 12.5 %collective-permute-start.12 = (bf16[4,66,352]{2,1,0:T(8,128)(2,1)S(1)}, bf16[4,66,352]{2,1,0:T(8,128)(2,1)S(1)}, u32[]{:S(2)}, u32[]{:S(2)}) collective-permute-start(bf16[4,66,352]{2,1,0:T(8,128)(2,1)S(1)} %collective-permute-done.11), channel_id=1, source_target_pairs={{0,168},{24,0},{48,24},{72,48},{96,72},{120,96},{144,120},{168,144... | collective-permute-start | bytes 557576 | tf_op jit(solution)/shard_map/ppermute | solution.py:13
  176.5 7.9 %collective-permute-start.15 = (bf16[4,66,352]{2,1,0:T(8,128)(2,1)S(1)}, bf16[4,66,352]{2,1,0:T(8,128)(2,1)S(1)}, u32[]{:S(2)}, u32[]{:S(2)}) collective-permute-start(bf16[4,66,352]{2,1,0:T(8,128)(2,1)S(1)} %collective-permute-done.14), channel_id=1, source_target_pairs={{0,24},{24,48},{48,72},{72,96},{96,120},{120,144},{144,168},{168,0... | collective-permute-start | bytes 557576 | tf_op jit(solution)/shard_map/ppermute | solution.py:13
  184.4 7.9 %collective-permute-start.16 = (bf16[4,66,352]{2,1,0:T(8,128)(2,1)S(1)}, bf16[4,66,352]{2,1,0:T(8,128)(2,1)S(1)}, u32[]{:S(2)}, u32[]{:S(2)}) collective-permute-start(bf16[4,66,352]{2,1,0:T(8,128)(2,1)S(1)} %collective-permute-done.15), channel_id=1, source_target_pairs={{0,24},{24,48},{48,72},{72,96},{96,120},{120,144},{144,168},{168,0... | collective-permute-start | bytes 557576 | tf_op jit(solution)/shard_map/ppermute | solution.py:13
  192.5 1.2 copy-start.2
  195.4 12.2 %collective-permute-start.17 = (bf16[8,4,66,352]{3,0,2,1:T(8,128)(2,1)}, bf16[8,4,66,352]{3,0,2,1:T(8,128)(2,1)}, u32[]{:S(2)}, u32[]{:S(2)}) collective-permute-start(bf16[8,4,66,352]{3,0,2,1:T(8,128)(2,1)} %copy.12), channel_id=1, source_target_pairs={{0,12},{12,0},{1,13},{13,1},{2,14},{14,2},{3,15},{15,3},{4,16},{16... | collective-permute-start | bytes 4460552 | tf_op jit(solution)/shard_map/ppermute | solution.py:13
  214.2 2.1 copy-start.3
  216.3 3.5 %copy-start.4 = (bf16[2112,352]{1,0:T(8,128)(2,1)S(1)}, bf16[2112,352]{1,0:T(8,128)(2,1)}, u32[]{:S(2)}) copy-start(bf16[2112,352]{1,0:T(8,128)(2,1)} %reshape.522) | copy-start | bytes 4460548
  216.3 3.5 %copy-start.5 = (bf16[64,4224]{1,0:T(8,128)(2,1)S(1)}, bf16[64,4224]{1,0:T(8,128)(2,1)}, u32[]{:S(2)}) copy-start(bf16[64,4224]{1,0:T(8,128)(2,1)} %reshape.521) | copy-start | bytes 1622020
Sparse Core Ops, SparseCore 0:
  11.5 102.5 all-gather.2

commit v13 on v10

--- a/solution.py
+++ b/solution.py
@@ -84,12 +84,6 @@
     return mean, m2 / count
 
 
-def relative_order(v, axes):
-    for dim, axis in enumerate(axes, start=1):
-        v = jnp.roll(v, -lax.axis_index(axis), axis=dim)
-    return v
-
-
 def shards(hidden, proj_weight):
     mp_index = lax.axis_index("mp")
     dp_index = lax.axis_index(DP)
@@ -114,8 +108,14 @@
     second_full = jnp.transpose(stacked, (1, 0, 2)).reshape(local, n_mp * rows)
     width = second_full.shape[1] // dp_count
     columns = lax.all_to_all(second_full, DP, split_axis=1, concat_axis=0, tiled=True)
-    second_perm = relative_order(second_full.reshape(local, nx, ny, nc, width), ("x", "y", "c"))
-    second_perm = jnp.transpose(second_perm, (0, 3, 2, 1, 4)).reshape(local, dp_count * width)
+    pc = (lax.iota(jnp.int32, nc)[:, None, None] + ic) % nc
+    py = (lax.iota(jnp.int32, ny)[None, :, None] + iy) % ny
+    px = (lax.iota(jnp.int32, nx)[None, None, :] + ix) % nx
+    src_block = ((px * ny + py) * nc + pc).reshape(-1)
+    pick = (src_block[:, None] == lax.iota(jnp.int32, dp_count)[None, :]).astype(jnp.bfloat16)
+    second_perm = jnp.einsum(
+        "bkt,pk->bpt", second_full.reshape(local, dp_count, width), pick, preferred_element_type=jnp.float32
+    ).astype(jnp.bfloat16).reshape(local, dp_count * width)
     columns, second_perm = lax.optimization_barrier((columns, second_perm))
     corr = (
         jnp.einsum("bi,bj->ij", first_all, columns, preferred_element_type=jnp.float32)

time: 226 us -> 226 us (level)
  waiting for transfers between devices: 44.2 us -> 61.9 us
  other arithmetic: 25.5 us -> 12.6 us
  local copies, waits for them, and re-layouts: 30.9 us -> 23.3 us
  matrix products: 7.54 us -> 10.2 us
    all_to_all x1, waiting for transfers between devices: 5.08 us -> 22.9 us  [shards(): lax.all_to_all(second_full, DP, split_axis=1, concat_axis=0, tiled=True)]
    concatenate x2 -> x0, other arithmetic: 8.29 us -> none  [relative_order(): v = jnp.roll(v, -lax.axis_index(axis), axis=dim)]
    another operation x1 -> x0, local copies, waits for them, and re-layouts: 6.1 us -> none  [shards(): second_full.reshape(local, nx, ny, nc, width)]
    transpose x1 -> x0, other arithmetic: 4.66 us -> none  [shards(): jnp.transpose(second_perm, (0, 3, 2, 1, 4)).reshape(local, dp_count * width)]
    dot_general x0 -> x1, matrix products: none -> 2.7 us  [shards(): jnp.einsum('bkt,pk->bpt', second_full.reshape(local, dp_count, width), pi...]
  transfers between devices with their start and end apart: 20 -> 20, of which waited for: 14 -> 14; matrix products, arithmetic and copies ran while one was open for 14% -> 6% of each run, Pallas kernels for 0% -> 0%
where the time goes in v13:
time: 226 us; the launch traced here: 225 us
  starting transfers between devices  79.7 us (35%)
  waiting for transfers between devices  61.9 us (27%)
  blocking collectives  23.4 us (10%)
  local copies, waits for them, and re-layouts  23.3 us (10%)
  between operations  13.8 us (6%)
  other arithmetic  12.6 us (6%)
  matrix products  10.2 us (5%)
    ppermute x8, starting transfers between devices, shift(): return lax.ppermute(v, axis, [(i, (i + step) % n) for i in range(n)])  26.2 us
    all_gather x1, blocking collectives, shards(): stacked = lax.all_gather(second, 'mp', axis=0)  23.4 us
    all_to_all x1, waiting for transfers between devices, shards(): lax.all_to_all(second_full, DP, split_axis=1, concat_axis=0, tiled=True)  22.9 us
    all_to_all x1, starting transfers between devices, shards(): lax.all_to_all(second_full, DP, split_axis=1, concat_axis=0, tiled=True)  19.4 us
    ppermute x8, waiting for transfers between devices, shift(): return lax.ppermute(v, axis, [(i, (i + step) % n) for i in range(n)])  18.7 us
    ppermute x4, starting transfers between devices, combine(): other = lax.ppermute(jnp.stack([mean, m2]), axis, pairs)  18.2 us
    ppermute x6, starting transfers between devices, direct_gather(): got[t] = lax.ppermute(v, axis, [(i, (i - t) % n) for i in range(n)])  15.9 us
    ppermute x4, waiting for transfers between devices, combine(): other = lax.ppermute(jnp.stack([mean, m2]), axis, pairs)  12.8 us
  transfers between devices with their start and end apart: 20, of which 14 were waited for; matrix products, arithmetic and copies ran while one was open for 6% of the time, Pallas kernels for 0%

profile of v13, /device:TPU:1, one launch (start us, length us, event | category | flops | bytes accessed | tf_op | source)
XLA Modules:
  0.0 225.0 jit_solution(3698006335452213429)
XLA Ops:
  6.5 1.8 copy-done
  8.4 2.3 %fusion.3 = f32[2,64,352]{2,1,0:T(8,128)S(1)} fusion(bf16[2,64,4224]{2,1,0:T(8,128)(2,1)} %param.2, bf16[4224,352]{0,1:T(8,128)(2,1)S(1)} %copy-done), kind=kOutput, calls=%fused_computation.9 | convolution fusion | flops 380633088 | bytes 4235264 | tf_op jit(solution)/shard_map/vbh,hc->vbc/dot_general | solution.py:96
  10.7 0.7 fusion.28
  11.4 0.0 all-gather.3.cloned.1.call-update
  11.4 12.4 %collective-permute-start = (f32[2,1,1,352]{3,2,1,0:T(1,128)S(1)}, f32[2,1,1,352]{3,2,1,0:T(1,128)S(1)}, u32[]{:S(2)}, u32[]{:S(2)}) collective-permute-start(f32[2,1,1,352]{3,2,1,0:T(1,128)S(1)} %pad_maximum_fusion.2), channel_id=1, source_target_pairs={{0,12},{12,0},{1,13},{13,1},{2,14},{14,2},{3,15},{15,3},{4,16},{16... | collective-permute-start | bytes 8456 | tf_op jit(solution)/shard_map/ppermute | solution.py:49
  23.9 0.8 collective-permute-done
  24.7 1.9 collective-permute-start.1
  26.6 2.4 %collective-permute-done.1 = f32[2,1,1,352]{3,2,1,0:T(1,128)S(1)} collective-permute-done((f32[2,1,1,352]{3,2,1,0:T(1,128)S(1)}, f32[2,1,1,352]{3,2,1,0:T(1,128)S(1)}, u32[]{:S(2)}, u32[]{:S(2)}) %collective-permute-start.1) | collective-permute-done | bytes 2848 | tf_op jit(solution)/shard_map/ppermute | solution.py:49
  29.1 1.9 collective-permute-start.2
  31.0 3.3 %collective-permute-done.2 = f32[2,1,1,352]{3,2,1,0:T(1,128)S(1)} collective-permute-done((f32[2,1,1,352]{3,2,1,0:T(1,128)S(1)}, f32[2,1,1,352]{3,2,1,0:T(1,128)S(1)}, u32[]{:S(2)}, u32[]{:S(2)}) %collective-permute-start.2) | collective-permute-done | bytes 2848 | tf_op jit(solution)/shard_map/ppermute | solution.py:49
  34.3 1.9 collective-permute-start.3
  36.3 6.3 %collective-permute-done.3 = f32[2,1,1,352]{3,2,1,0:T(1,128)S(1)} collective-permute-done((f32[2,1,1,352]{3,2,1,0:T(1,128)S(1)}, f32[2,1,1,352]{3,2,1,0:T(1,128)S(1)}, u32[]{:S(2)}, u32[]{:S(2)}) %collective-permute-start.3) | collective-permute-done | bytes 2848 | tf_op jit(solution)/shard_map/ppermute | solution.py:49
  42.6 1.9 collective-permute-start.4
  44.6 1.9 collective-permute-start.5
  46.5 3.4 %collective-permute-start.6 = (f32[2,1,1,352]{3,2,1,0:T(1,128)S(1)}, f32[2,1,1,352]{3,2,1,0:T(1,128)S(1)}, u32[]{:S(2)}, u32[]{:S(2)}) collective-permute-start(f32[2,1,1,352]{3,2,1,0:T(1,128)S(1)} %pad_maximum_fusion.6), channel_id=1, source_target_pairs={{0,192},{192,384},{384,576},{576,0},{1,193},{193,385},{385,577},{5... | collective-permute-start | bytes 8456 | tf_op jit(solution)/shard_map/ppermute | solution.py:20
  49.9 0.0 collective-permute-done.4
  49.9 0.6 collective-permute-done.5
  50.5 2.9 %collective-permute-done.6 = f32[2,1,1,352]{3,2,1,0:T(1,128)S(1)} collective-permute-done((f32[2,1,1,352]{3,2,1,0:T(1,128)S(1)}, f32[2,1,1,352]{3,2,1,0:T(1,128)S(1)}, u32[]{:S(2)}, u32[]{:S(2)}) %collective-permute-start.6) | collective-permute-done | bytes 2848 | tf_op jit(solution)/shard_map/ppermute | solution.py:20
  53.5 0.1 multiply_reduce_fusion.2
  53.6 23.4 %all_gather.7 = bf16[12,64,352]{2,1,0:T(8,128)(2,1)S(1)} all-gather(bf16[1,64,352]{2,1,0:T(8,128)(2,1)S(1)} %divide_convert_fusion.4), channel_id=1, replica_groups=mesh['x'=4,'y'=8,'c'=2,'mp'=12] {'mp'}, dimensions={0}, use_global_device_ids=true | all-gather | bytes 585728 | tf_op jit(solution)/shard_map/all_gather | solution.py:107
  77.0 1.3 copy.5
  78.3 4.0 %all_to_all.14 = bf16[64,64,66]{2,1,0:T(8,128)(2,1)} reshape(bf16[64,12,352]{2,1,0:T(8,128)(2,1)} %copy.5) | data formatting | bytes 1081344 | tf_op jit(solution)/shard_map/all_to_all | solution.py:110
  82.3 2.9 %copy.6 = bf16[64,64,66]{2,0,1:T(8,128)(2,1)} copy(bf16[64,64,66]{2,1,0:T(8,128)(2,1)} %all_to_all.14) | data formatting | bytes 1081344 | tf_op jit(solution)/shard_map/all_to_all | solution.py:110
  85.2 19.4 %all-to-all-start = ((bf16[64,64,66]{2,0,1:T(8,128)(2,1)}), bf16[64,64,66]{2,0,1:T(8,128)(2,1)}, u32[]{:S(2)}, u32[]{:S(2)}) async-start(bf16[64,64,66]{2,0,1:T(8,128)(2,1)} %copy.6), calls=%async_computation | async-start | bytes 2097152 | tf_op jit(solution)/shard_map/all_to_all | solution.py:110
  104.6 0.1 add_multiply_fusion
  104.7 0.1 broadcast_multiply_fusion
  104.8 0.1 add.540
  104.9 2.7 %fusion.5 = bf16[64,64,66]{2,1,0:T(8,128)(2,1)} fusion(bf16[64,64,66]{2,1,0:T(8,128)(2,1)} %all_to_all.14, s32[64]{0:T(128)S(1)} %add.540), kind=kOutput, calls=%fused_computation.13 | convolution fusion | flops 34877440 | bytes 1081600 | tf_op jit(solution)/shard_map/bkt,pk->bpt/dot_general | solution.py:116
  107.6 3.1 %reshape.600 = bf16[64,4224]{1,0:T(8,128)(2,1)} reshape(bf16[64,64,66]{2,1,0:T(8,128)(2,1)} %fusion.5) | data formatting | bytes 1081344 | tf_op jit(solution)/shard_map/reshape | solution.py:118
  110.7 22.9 %all-to-all-done = bf16[64,64,66]{2,0,1:T(8,128)(2,1)} async-done(((bf16[64,64,66]{2,0,1:T(8,128)(2,1)}), bf16[64,64,66]{2,0,1:T(8,128)(2,1)}, u32[]{:S(2)}, u32[]{:S(2)}) %all-to-all-start) | async-done | bytes 540704 | tf_op jit(solution)/shard_map/all_to_all | solution.py:110
  133.6 2.3 %copy.10 = bf16[4096,66]{0,1:T(8,128)(2,1)} copy(bf16[4096,66]{1,0:T(8,128)(2,1)} %bitcast.7) | data formatting | bytes 1081344 | tf_op jit(solution)/shard_map/all_to_all | solution.py:110
  135.9 3.4 %reduce_sum.56 = f32[352]{0:T(512)S(1)} reduce(f32[1,4096,352]{2,1,0:T(8,128)} %all-gather.3.cloned.1.call-done, f32[]{:T(128)} %constant.121.clone.1), dimensions={0,1}, to_apply=%region_2.0 | reduce | flops 1441440 | bytes 5768580 | tf_op jit(solution)/shard_map/reduce_sum | solution.py:98
  139.2 3.7 %multiply_reduce_fusion = f32[352]{0:T(512)S(1)} fusion(f32[1,4096,352]{2,1,0:T(8,128)} %all-gather.3.cloned.1.call-done, f32[352]{0:T(512)S(1)} %broadcast_multiply_fusion.1), kind=kLoop, calls=%fused_computation.6 | loop fusion | flops 4325024 | bytes 5769984 | tf_op jit(solution)/shard_map/reduce_sum | solution.py:100
  143.0 0.9 copy-done.1
  143.8 1.9 select_convert_fusion
  145.7 3.8 %collective-permute-start.7 = (bf16[66,352]{1,0:T(8,128)(2,1)S(1)}, bf16[66,352]{1,0:T(8,128)(2,1)S(1)}, u32[]{:S(2)}, u32[]{:S(2)}) collective-permute-start(bf16[66,352]{1,0:T(8,128)(2,1)S(1)} %select_convert_fusion), channel_id=1, source_target_pairs={{0,576},{192,0},{384,192},{576,384},{1,577},{193,1},{385,193},{577... | collective-permute-start | bytes 139400 | tf_op jit(solution)/shard_map/ppermute | solution.py:20
  149.5 2.3 %collective-permute-start.8 = (bf16[66,352]{1,0:T(8,128)(2,1)S(1)}, bf16[66,352]{1,0:T(8,128)(2,1)S(1)}, u32[]{:S(2)}, u32[]{:S(2)}) collective-permute-start(bf16[66,352]{1,0:T(8,128)(2,1)S(1)} %select_convert_fusion), channel_id=1, source_target_pairs={{0,384},{192,576},{384,0},{576,192},{1,385},{193,577},{385,1},{577... | collective-permute-start | bytes 139400 | tf_op jit(solution)/shard_map/ppermute | solution.py:20
  151.8 2.6 %collective-permute-start.9 = (bf16[66,352]{1,0:T(8,128)(2,1)S(1)}, bf16[66,352]{1,0:T(8,128)(2,1)S(1)}, u32[]{:S(2)}, u32[]{:S(2)}) collective-permute-start(bf16[66,352]{1,0:T(8,128)(2,1)S(1)} %select_convert_fusion), channel_id=1, source_target_pairs={{0,192},{192,384},{384,576},{576,0},{1,193},{193,385},{385,577},{5... | collective-permute-start | bytes 139400 | tf_op jit(solution)/shard_map/ppermute | solution.py:20
  154.4 0.0 collective-permute-done.7
  154.4 2.4 %collective-permute-done.8 = bf16[66,352]{1,0:T(8,128)(2,1)S(1)} collective-permute-done((bf16[66,352]{1,0:T(8,128)(2,1)S(1)}, bf16[66,352]{1,0:T(8,128)(2,1)S(1)}, u32[]{:S(2)}, u32[]{:S(2)}) %collective-permute-start.8) | collective-permute-done | bytes 46496 | tf_op jit(solution)/shard_map/ppermute | solution.py:20
  156.8 1.6 collective-permute-done.9
  158.4 0.1 pad_maximum_fusion.1
  158.5 1.9 collective-permute-start.10
  160.4 3.4 %collective-permute-start.13 = (bf16[4,66,352]{2,1,0:T(8,128)(2,1)S(1)}, bf16[4,66,352]{2,1,0:T(8,128)(2,1)S(1)}, u32[]{:S(2)}, u32[]{:S(2)}) collective-permute-start(bf16[4,66,352]{2,1,0:T(8,128)(2,1)S(1)} %pad_maximum_fusion.1), channel_id=1, source_target_pairs={{0,24},{24,48},{48,72},{72,96},{96,120},{120,144},{144,168},{168,0... | collective-permute-start | bytes 557576 | tf_op jit(solution)/shard_map/ppermute | solution.py:13
  163.8 2.8 %collective-permute-done.10 = bf16[4,66,352]{2,1,0:T(8,128)(2,1)S(1)} collective-permute-done((bf16[4,66,352]{2,1,0:T(8,128)(2,1)S(1)}, bf16[4,66,352]{2,1,0:T(8,128)(2,1)S(1)}, u32[]{:S(2)}, u32[]{:S(2)}) %collective-permute-start.10) | collective-permute-done | bytes 185888 | tf_op jit(solution)/shard_map/ppermute | solution.py:13
  166.6 2.1 collective-permute-start.11
  168.7 0.0 collective-permute-done.13
  168.7 3.2 %collective-permute-start.14 = (bf16[4,66,352]{2,1,0:T(8,128)(2,1)S(1)}, bf16[4,66,352]{2,1,0:T(8,128)(2,1)S(1)}, u32[]{:S(2)}, u32[]{:S(2)}) collective-permute-start(bf16[4,66,352]{2,1,0:T(8,128)(2,1)S(1)} %collective-permute-done.13), channel_id=1, source_target_pairs={{0,24},{24,48},{48,72},{72,96},{96,120},{120,144},{144,168},{168,0... | collective-permute-start | bytes 557576 | tf_op jit(solution)/shard_map/ppermute | solution.py:13
  171.9 1.8 collective-permute-done.11
  173.8 2.8 %collective-permute-start.12 = (bf16[4,66,352]{2,1,0:T(8,128)(2,1)S(1)}, bf16[4,66,352]{2,1,0:T(8,128)(2,1)S(1)}, u32[]{:S(2)}, u32[]{:S(2)}) collective-permute-start(bf16[4,66,352]{2,1,0:T(8,128)(2,1)S(1)} %collective-permute-done.11), channel_id=1, source_target_pairs={{0,168},{24,0},{48,24},{72,48},{96,72},{120,96},{144,120},{168,144... | collective-permute-start | bytes 557576 | tf_op jit(solution)/shard_map/ppermute | solution.py:13
  176.6 0.0 collective-permute-done.14
  176.6 2.5 %collective-permute-start.15 = (bf16[4,66,352]{2,1,0:T(8,128)(2,1)S(1)}, bf16[4,66,352]{2,1,0:T(8,128)(2,1)S(1)}, u32[]{:S(2)}, u32[]{:S(2)}) collective-permute-start(bf16[4,66,352]{2,1,0:T(8,128)(2,1)S(1)} %collective-permute-done.14), channel_id=1, source_target_pairs={{0,24},{24,48},{48,72},{72,96},{96,120},{120,144},{144,168},{168,0... | collective-permute-start | bytes 557576 | tf_op jit(solution)/shard_map/ppermute | solution.py:13
  179.1 5.4 %collective-permute-done.15 = bf16[4,66,352]{2,1,0:T(8,128)(2,1)S(1)} collective-permute-done((bf16[4,66,352]{2,1,0:T(8,128)(2,1)S(1)}, bf16[4,66,352]{2,1,0:T(8,128)(2,1)S(1)}, u32[]{:S(2)}, u32[]{:S(2)}) %collective-permute-start.15) | collective-permute-done | bytes 185888 | tf_op jit(solution)/shard_map/ppermute | solution.py:13
  184.5 1.9 collective-permute-start.16
  186.4 5.9 %collective-permute-done.16 = bf16[4,66,352]{2,1,0:T(8,128)(2,1)S(1)} collective-permute-done((bf16[4,66,352]{2,1,0:T(8,128)(2,1)S(1)}, bf16[4,66,352]{2,1,0:T(8,128)(2,1)S(1)}, u32[]{:S(2)}, u32[]{:S(2)}) %collective-permute-start.16) | collective-permute-done | bytes 185888 | tf_op jit(solution)/shard_map/ppermute | solution.py:13
  192.5 0.6 copy.8
  193.1 8.5 %collective-permute-start.17 = (bf16[8,4,66,352]{3,0,2,1:T(8,128)(2,1)S(1)}, bf16[8,4,66,352]{3,0,2,1:T(8,128)(2,1)S(1)}, u32[]{:S(2)}, u32[]{:S(2)}) collective-permute-start(bf16[8,4,66,352]{3,0,2,1:T(8,128)(2,1)S(1)} %copy.8), channel_id=1, source_target_pairs={{0,12},{12,0},{1,13},{13,1},{2,14},{14,2},{3,15},{15,3},{4,16},{16... | collective-permute-start | bytes 4460552 | tf_op jit(solution)/shard_map/ppermute | solution.py:13
  201.6 0.1 iota_add_fusion
  201.7 2.8 %collective-permute-done.17 = bf16[8,4,66,352]{3,0,2,1:T(8,128)(2,1)S(1)} collective-permute-done((bf16[8,4,66,352]{3,0,2,1:T(8,128)(2,1)S(1)}, bf16[8,4,66,352]{3,0,2,1:T(8,128)(2,1)S(1)}, u32[]{:S(2)}, u32[]{:S(2)}) %collective-permute-start.17) | collective-permute-done | bytes 1486880 | tf_op jit(solution)/shard_map/ppermute | solution.py:13
  204.5 0.2 copy.12
  204.7 2.5 %pad_maximum_fusion = bf16[2,8,4,66,352]{4,3,2,1,0:T(8,128)(2,1)} fusion(bf16[1,8,4,66,352]{4,3,2,1,0:T(8,128)(2,1)S(1)} %bitcast.72, bf16[1,8,4,66,352]{4,3,2,1,0:T(8,128)(2,1)S(1)} %bitcast.70), kind=kLoop, calls=%fused_computation.7 | loop fusion | flops 1486848 | bytes 5947392 | tf_op jit(solution)/shard_map/stack | solution.py:39
  207.2 1.8 fusion
  209.0 5.8 %reshape.601 = bf16[4224,352]{1,0:T(8,128)(2,1)} reshape(bf16[2,8,4,66,352]{4,3,2,1,0:T(8,128)(2,1)} %pad_maximum_fusion) | data formatting | bytes 5947392 | tf_op jit(solution)/shard_map/reshape | solution.py:129
  214.9 3.3 %fusion.7 = bf16[64,352]{1,0:T(8,128)(2,1)} fusion(bf16[64,4224]{1,0:T(8,128)(2,1)} %reshape.600, bf16[4224,352]{1,0:T(8,128)(2,1)} %reshape.601, f32[352]{0:T(512)S(1)} %get-tuple-element.25, f32[352]{0:T(512)S(1)} %multiply_add_fusion, f32[352]{0:T(512)S(1)} %get-tuple-element.26, f32[352]{0:T(512)S(1)} %broadcast_multiply_fusion.1, ...), kind=kOutput, calls=%fused_computation.16 | convolution fusion | flops 190496768 | bytes 3655168 | tf_op jit(solution)/shard_map/dot_general | solution.py:144
  (43 shorter events, 0.6 us)
Async XLA Ops:
  6.5 1.8 copy-start
  6.5 129.3 %all-gather.3.cloned.1.call-start = ((), (), s32[]{:S(2)}) async-start(), calls=%async_computation.1 | async-start | bytes 6389760 | tf_op jit(solution)/shard_map/all_gather | solution.py:97
  11.4 13.2 %collective-permute-start = (f32[2,1,1,352]{3,2,1,0:T(1,128)S(1)}, f32[2,1,1,352]{3,2,1,0:T(1,128)S(1)}, u32[]{:S(2)}, u32[]{:S(2)}) collective-permute-start(f32[2,1,1,352]{3,2,1,0:T(1,128)S(1)} %pad_maximum_fusion.2), channel_id=1, source_target_pairs={{0,12},{12,0},{1,13},{13,1},{2,14},{14,2},{3,15},{15,3},{4,16},{16... | collective-permute-start | bytes 8456 | tf_op jit(solution)/shard_map/ppermute | solution.py:49
  24.7 4.3 %collective-permute-start.1 = (f32[2,1,1,352]{3,2,1,0:T(1,128)S(1)}, f32[2,1,1,352]{3,2,1,0:T(1,128)S(1)}, u32[]{:S(2)}, u32[]{:S(2)}) collective-permute-start(f32[2,1,1,352]{3,2,1,0:T(1,128)S(1)} %pad_maximum_fusion.3), channel_id=1, source_target_pairs={{0,24},{24,0},{48,72},{72,48},{96,120},{120,96},{144,168},{168,144... | collective-permute-start | bytes 8456 | tf_op jit(solution)/shard_map/ppermute | solution.py:49
  29.1 5.2 %collective-permute-start.2 = (f32[2,1,1,352]{3,2,1,0:T(1,128)S(1)}, f32[2,1,1,352]{3,2,1,0:T(1,128)S(1)}, u32[]{:S(2)}, u32[]{:S(2)}) collective-permute-start(f32[2,1,1,352]{3,2,1,0:T(1,128)S(1)} %pad_maximum_fusion.4), channel_id=1, source_target_pairs={{0,48},{24,72},{48,0},{72,24},{96,144},{120,168},{144,96},{168,120... | collective-permute-start | bytes 8456 | tf_op jit(solution)/shard_map/ppermute | solution.py:49
  34.3 8.3 %collective-permute-start.3 = (f32[2,1,1,352]{3,2,1,0:T(1,128)S(1)}, f32[2,1,1,352]{3,2,1,0:T(1,128)S(1)}, u32[]{:S(2)}, u32[]{:S(2)}) collective-permute-start(f32[2,1,1,352]{3,2,1,0:T(1,128)S(1)} %pad_maximum_fusion.5), channel_id=1, source_target_pairs={{0,96},{24,120},{48,144},{72,168},{96,0},{120,24},{144,48},{168,72... | collective-permute-start | bytes 8456 | tf_op jit(solution)/shard_map/ppermute | solution.py:49
  42.6 7.2 %collective-permute-start.4 = (f32[2,1,1,352]{3,2,1,0:T(1,128)S(1)}, f32[2,1,1,352]{3,2,1,0:T(1,128)S(1)}, u32[]{:S(2)}, u32[]{:S(2)}) collective-permute-start(f32[2,1,1,352]{3,2,1,0:T(1,128)S(1)} %pad_maximum_fusion.6), channel_id=1, source_target_pairs={{0,576},{192,0},{384,192},{576,384},{1,577},{193,1},{385,193},{577... | collective-permute-start | bytes 8456 | tf_op jit(solution)/shard_map/ppermute | solution.py:20
  44.6 5.9 %collective-permute-start.5 = (f32[2,1,1,352]{3,2,1,0:T(1,128)S(1)}, f32[2,1,1,352]{3,2,1,0:T(1,128)S(1)}, u32[]{:S(2)}, u32[]{:S(2)}) collective-permute-start(f32[2,1,1,352]{3,2,1,0:T(1,128)S(1)} %pad_maximum_fusion.6), channel_id=1, source_target_pairs={{0,384},{192,576},{384,0},{576,192},{1,385},{193,577},{385,1},{577... | collective-permute-start | bytes 8456 | tf_op jit(solution)/shard_map/ppermute | solution.py:20
  46.5 6.9 %collective-permute-start.6 = (f32[2,1,1,352]{3,2,1,0:T(1,128)S(1)}, f32[2,1,1,352]{3,2,1,0:T(1,128)S(1)}, u32[]{:S(2)}, u32[]{:S(2)}) collective-permute-start(f32[2,1,1,352]{3,2,1,0:T(1,128)S(1)} %pad_maximum_fusion.6), channel_id=1, source_target_pairs={{0,192},{192,384},{384,576},{576,0},{1,193},{193,385},{385,577},{5... | collective-permute-start | bytes 8456 | tf_op jit(solution)/shard_map/ppermute | solution.py:20
  85.2 48.4 %all-to-all-start = ((bf16[64,64,66]{2,0,1:T(8,128)(2,1)}), bf16[64,64,66]{2,0,1:T(8,128)(2,1)}, u32[]{:S(2)}, u32[]{:S(2)}) async-start(bf16[64,64,66]{2,0,1:T(8,128)(2,1)} %copy.6), calls=%async_computation | async-start | bytes 2097152 | tf_op jit(solution)/shard_map/all_to_all | solution.py:110
  139.2 4.6 %copy-start.1 = (f32[1,4096,352]{2,1,0:T(8,128)S(1)}, f32[1,4096,352]{2,1,0:T(8,128)}, u32[]{:S(2)}) copy-start(f32[1,4096,352]{2,1,0:T(8,128)} %all-gather.3.cloned.1.call-done) | copy-start | bytes 17301508
  145.7 8.7 %collective-permute-start.7 = (bf16[66,352]{1,0:T(8,128)(2,1)S(1)}, bf16[66,352]{1,0:T(8,128)(2,1)S(1)}, u32[]{:S(2)}, u32[]{:S(2)}) collective-permute-start(bf16[66,352]{1,0:T(8,128)(2,1)S(1)} %select_convert_fusion), channel_id=1, source_target_pairs={{0,576},{192,0},{384,192},{576,384},{1,577},{193,1},{385,193},{577... | collective-permute-start | bytes 139400 | tf_op jit(solution)/shard_map/ppermute | solution.py:20
  149.5 7.3 %collective-permute-start.8 = (bf16[66,352]{1,0:T(8,128)(2,1)S(1)}, bf16[66,352]{1,0:T(8,128)(2,1)S(1)}, u32[]{:S(2)}, u32[]{:S(2)}) collective-permute-start(bf16[66,352]{1,0:T(8,128)(2,1)S(1)} %select_convert_fusion), channel_id=1, source_target_pairs={{0,384},{192,576},{384,0},{576,192},{1,385},{193,577},{385,1},{577... | collective-permute-start | bytes 139400 | tf_op jit(solution)/shard_map/ppermute | solution.py:20
  151.8 6.6 %collective-permute-start.9 = (bf16[66,352]{1,0:T(8,128)(2,1)S(1)}, bf16[66,352]{1,0:T(8,128)(2,1)S(1)}, u32[]{:S(2)}, u32[]{:S(2)}) collective-permute-start(bf16[66,352]{1,0:T(8,128)(2,1)S(1)} %select_convert_fusion), channel_id=1, source_target_pairs={{0,192},{192,384},{384,576},{576,0},{1,193},{193,385},{385,577},{5... | collective-permute-start | bytes 139400 | tf_op jit(solution)/shard_map/ppermute | solution.py:20
  158.5 8.1 %collective-permute-start.10 = (bf16[4,66,352]{2,1,0:T(8,128)(2,1)S(1)}, bf16[4,66,352]{2,1,0:T(8,128)(2,1)S(1)}, u32[]{:S(2)}, u32[]{:S(2)}) collective-permute-start(bf16[4,66,352]{2,1,0:T(8,128)(2,1)S(1)} %pad_maximum_fusion.1), channel_id=1, source_target_pairs={{0,168},{24,0},{48,24},{72,48},{96,72},{120,96},{144,120},{168,144... | collective-permute-start | bytes 557576 | tf_op jit(solution)/shard_map/ppermute | solution.py:13
  160.4 8.3 %collective-permute-start.13 = (bf16[4,66,352]{2,1,0:T(8,128)(2,1)S(1)}, bf16[4,66,352]{2,1,0:T(8,128)(2,1)S(1)}, u32[]{:S(2)}, u32[]{:S(2)}) collective-permute-start(bf16[4,66,352]{2,1,0:T(8,128)(2,1)S(1)} %pad_maximum_fusion.1), channel_id=1, source_target_pairs={{0,24},{24,48},{48,72},{72,96},{96,120},{120,144},{144,168},{168,0... | collective-permute-start | bytes 557576 | tf_op jit(solution)/shard_map/ppermute | solution.py:13
  166.6 7.2 %collective-permute-start.11 = (bf16[4,66,352]{2,1,0:T(8,128)(2,1)S(1)}, bf16[4,66,352]{2,1,0:T(8,128)(2,1)S(1)}, u32[]{:S(2)}, u32[]{:S(2)}) collective-permute-start(bf16[4,66,352]{2,1,0:T(8,128)(2,1)S(1)} %collective-permute-done.10), channel_id=1, source_target_pairs={{0,168},{24,0},{48,24},{72,48},{96,72},{120,96},{144,120},{168,144... | collective-permute-start | bytes 557576 | tf_op jit(solution)/shard_map/ppermute | solution.py:13
  168.7 7.9 %collective-permute-start.14 = (bf16[4,66,352]{2,1,0:T(8,128)(2,1)S(1)}, bf16[4,66,352]{2,1,0:T(8,128)(2,1)S(1)}, u32[]{:S(2)}, u32[]{:S(2)}) collective-permute-start(bf16[4,66,352]{2,1,0:T(8,128)(2,1)S(1)} %collective-permute-done.13), channel_id=1, source_target_pairs={{0,24},{24,48},{48,72},{72,96},{96,120},{120,144},{144,168},{168,0... | collective-permute-start | bytes 557576 | tf_op jit(solution)/shard_map/ppermute | solution.py:13
  173.8 12.6 %collective-permute-start.12 = (bf16[4,66,352]{2,1,0:T(8,128)(2,1)S(1)}, bf16[4,66,352]{2,1,0:T(8,128)(2,1)S(1)}, u32[]{:S(2)}, u32[]{:S(2)}) collective-permute-start(bf16[4,66,352]{2,1,0:T(8,128)(2,1)S(1)} %collective-permute-done.11), channel_id=1, source_target_pairs={{0,168},{24,0},{48,24},{72,48},{96,72},{120,96},{144,120},{168,144... | collective-permute-start | bytes 557576 | tf_op jit(solution)/shard_map/ppermute | solution.py:13
  176.6 7.9 %collective-permute-start.15 = (bf16[4,66,352]{2,1,0:T(8,128)(2,1)S(1)}, bf16[4,66,352]{2,1,0:T(8,128)(2,1)S(1)}, u32[]{:S(2)}, u32[]{:S(2)}) collective-permute-start(bf16[4,66,352]{2,1,0:T(8,128)(2,1)S(1)} %collective-permute-done.14), channel_id=1, source_target_pairs={{0,24},{24,48},{48,72},{72,96},{96,120},{120,144},{144,168},{168,0... | collective-permute-start | bytes 557576 | tf_op jit(solution)/shard_map/ppermute | solution.py:13
  184.5 7.9 %collective-permute-start.16 = (bf16[4,66,352]{2,1,0:T(8,128)(2,1)S(1)}, bf16[4,66,352]{2,1,0:T(8,128)(2,1)S(1)}, u32[]{:S(2)}, u32[]{:S(2)}) collective-permute-start(bf16[4,66,352]{2,1,0:T(8,128)(2,1)S(1)} %collective-permute-done.15), channel_id=1, source_target_pairs={{0,24},{24,48},{48,72},{72,96},{96,120},{120,144},{144,168},{168,0... | collective-permute-start | bytes 557576 | tf_op jit(solution)/shard_map/ppermute | solution.py:13
  193.1 11.4 %collective-permute-start.17 = (bf16[8,4,66,352]{3,0,2,1:T(8,128)(2,1)S(1)}, bf16[8,4,66,352]{3,0,2,1:T(8,128)(2,1)S(1)}, u32[]{:S(2)}, u32[]{:S(2)}) collective-permute-start(bf16[8,4,66,352]{3,0,2,1:T(8,128)(2,1)S(1)} %copy.8), channel_id=1, source_target_pairs={{0,12},{12,0},{1,13},{13,1},{2,14},{14,2},{3,15},{15,3},{4,16},{16... | collective-permute-start | bytes 4460552 | tf_op jit(solution)/shard_map/ppermute | solution.py:13
Sparse Core Ops, SparseCore 0:
  11.5 102.4 all-gather.2

commit v14 on v13

--- a/solution.py
+++ b/solution.py
@@ -113,8 +113,9 @@
     px = (lax.iota(jnp.int32, nx)[None, None, :] + ix) % nx
     src_block = ((px * ny + py) * nc + pc).reshape(-1)
     pick = (src_block[:, None] == lax.iota(jnp.int32, dp_count)[None, :]).astype(jnp.bfloat16)
+    first_all, reorder_in = lax.optimization_barrier((first_all, second_full))
     second_perm = jnp.einsum(
-        "bkt,pk->bpt", second_full.reshape(local, dp_count, width), pick, preferred_element_type=jnp.float32
+        "bkt,pk->bpt", reorder_in.reshape(local, dp_count, width), pick, preferred_element_type=jnp.float32
     ).astype(jnp.bfloat16).reshape(local, dp_count * width)
     columns, second_perm = lax.optimization_barrier((columns, second_perm))
     corr = (

time: 226 us -> 240 us (1.062)
  local copies, waits for them, and re-layouts: 23.3 us -> 30.9 us
  waiting for transfers between devices: 61.9 us -> 64.5 us
    reshape x1 -> x3, local copies, waits for them, and re-layouts: 3.1 us -> 10.7 us  [the longest x1 5.02 us: shards(): reorder_in.reshape(local, dp_count, width)]
    all_to_all x1, waiting for transfers between devices: 22.9 us -> 26 us  [shards(): lax.all_to_all(second_full, DP, split_axis=1, concat_axis=0, tiled=True)]
  transfers between devices with their start and end apart: 20 -> 20, of which waited for: 14 -> 12; matrix products, arithmetic and copies ran while one was open for 6% -> 4% of each run, Pallas kernels for 0% -> 0%
where the time goes in v14:
time: 240 us; the launch traced here: 239 us
  starting transfers between devices  79 us (33%)
  waiting for transfers between devices  64.5 us (27%)
  local copies, waits for them, and re-layouts  30.9 us (13%)
  blocking collectives  24.6 us (10%)
  other arithmetic  14.8 us (6%)
  between operations  13.9 us (6%)
  matrix products  11 us (5%)
    all_to_all x1, waiting for transfers between devices, shards(): lax.all_to_all(second_full, DP, split_axis=1, concat_axis=0, tiled=True)  26 us
    ppermute x8, starting transfers between devices, shift(): return lax.ppermute(v, axis, [(i, (i + step) % n) for i in range(n)])  25.2 us
    all_gather x1, blocking collectives, shards(): stacked = lax.all_gather(second, 'mp', axis=0)  24.6 us
    ppermute x8, waiting for transfers between devices, shift(): return lax.ppermute(v, axis, [(i, (i + step) % n) for i in range(n)])  19.9 us
    all_to_all x1, starting transfers between devices, shards(): lax.all_to_all(second_full, DP, split_axis=1, concat_axis=0, tiled=True)  18.3 us
    ppermute x4, starting transfers between devices, combine(): other = lax.ppermute(jnp.stack([mean, m2]), axis, pairs)  18.2 us
    ppermute x6, starting transfers between devices, direct_gather(): got[t] = lax.ppermute(v, axis, [(i, (i - t) % n) for i in range(n)])  17.3 us
    ppermute x4, waiting for transfers between devices, combine(): other = lax.ppermute(jnp.stack([mean, m2]), axis, pairs)  12.9 us
  transfers between devices with their start and end apart: 20, of which 12 were waited for; matrix products, arithmetic and copies ran while one was open for 4% of the time, Pallas kernels for 0%

profile of v14, /device:TPU:1, one launch (start us, length us, event | category | flops | bytes accessed | tf_op | source)
XLA Modules:
  0.0 238.6 jit_solution(2910644468500065471)
XLA Ops:
  6.5 1.8 copy-done
  8.4 2.3 fusion.2
  10.7 0.6 fusion.27
  11.4 0.0 all-gather.3.cloned.1.call-update
  11.4 12.4 %collective-permute-start = (f32[2,1,1,352]{3,2,1,0:T(1,128)S(1)}, f32[2,1,1,352]{3,2,1,0:T(1,128)S(1)}, u32[]{:S(2)}, u32[]{:S(2)}) collective-permute-start(f32[2,1,1,352]{3,2,1,0:T(1,128)S(1)} %pad_maximum_fusion.2), channel_id=1, source_target_pairs={{0,12},{12,0},{1,13},{13,1},{2,14},{14,2},{3,15},{15,3},{4,16},{16... | collective-permute-start | bytes 8456 | tf_op jit(solution)/shard_map/ppermute | solution.py:49
  23.9 0.8 collective-permute-done
  24.7 1.9 collective-permute-start.1
  26.6 2.4 %collective-permute-done.1 = f32[2,1,1,352]{3,2,1,0:T(1,128)S(1)} collective-permute-done((f32[2,1,1,352]{3,2,1,0:T(1,128)S(1)}, f32[2,1,1,352]{3,2,1,0:T(1,128)S(1)}, u32[]{:S(2)}, u32[]{:S(2)}) %collective-permute-start.1) | collective-permute-done | bytes 2848 | tf_op jit(solution)/shard_map/ppermute | solution.py:49
  29.1 1.9 collective-permute-start.2
  31.0 3.3 %collective-permute-done.2 = f32[2,1,1,352]{3,2,1,0:T(1,128)S(1)} collective-permute-done((f32[2,1,1,352]{3,2,1,0:T(1,128)S(1)}, f32[2,1,1,352]{3,2,1,0:T(1,128)S(1)}, u32[]{:S(2)}, u32[]{:S(2)}) %collective-permute-start.2) | collective-permute-done | bytes 2848 | tf_op jit(solution)/shard_map/ppermute | solution.py:49
  34.3 1.9 collective-permute-start.3
  36.3 6.3 %collective-permute-done.3 = f32[2,1,1,352]{3,2,1,0:T(1,128)S(1)} collective-permute-done((f32[2,1,1,352]{3,2,1,0:T(1,128)S(1)}, f32[2,1,1,352]{3,2,1,0:T(1,128)S(1)}, u32[]{:S(2)}, u32[]{:S(2)}) %collective-permute-start.3) | collective-permute-done | bytes 2848 | tf_op jit(solution)/shard_map/ppermute | solution.py:49
  42.6 1.9 collective-permute-start.5
  44.5 1.9 collective-permute-start.4
  46.5 3.4 %collective-permute-start.6 = (f32[2,1,1,352]{3,2,1,0:T(1,128)S(1)}, f32[2,1,1,352]{3,2,1,0:T(1,128)S(1)}, u32[]{:S(2)}, u32[]{:S(2)}) collective-permute-start(f32[2,1,1,352]{3,2,1,0:T(1,128)S(1)} %pad_maximum_fusion.6), channel_id=1, source_target_pairs={{0,192},{192,384},{384,576},{576,0},{1,193},{193,385},{385,577},{5... | collective-permute-start | bytes 8456 | tf_op jit(solution)/shard_map/ppermute | solution.py:20
  49.9 0.0 collective-permute-done.4
  49.9 0.0 collective-permute-done.5
  49.9 3.0 %collective-permute-done.6 = f32[2,1,1,352]{3,2,1,0:T(1,128)S(1)} collective-permute-done((f32[2,1,1,352]{3,2,1,0:T(1,128)S(1)}, f32[2,1,1,352]{3,2,1,0:T(1,128)S(1)}, u32[]{:S(2)}, u32[]{:S(2)}) %collective-permute-start.6) | collective-permute-done | bytes 2848 | tf_op jit(solution)/shard_map/ppermute | solution.py:20
  52.9 0.1 multiply_reduce_fusion.2
  53.0 24.6 %all_gather.7 = bf16[12,64,352]{2,1,0:T(8,128)(2,1)S(1)} all-gather(bf16[1,64,352]{2,1,0:T(8,128)(2,1)S(1)} %divide_convert_fusion.1), channel_id=1, replica_groups=mesh['x'=4,'y'=8,'c'=2,'mp'=12] {'mp'}, dimensions={0}, use_global_device_ids=true | all-gather | bytes 585728 | tf_op jit(solution)/shard_map/all_gather | solution.py:107
  77.6 1.3 copy.6
  78.9 4.0 %all_to_all.14 = bf16[64,64,66]{2,1,0:T(8,128)(2,1)} reshape(bf16[64,12,352]{2,1,0:T(8,128)(2,1)} %copy.6) | data formatting | bytes 1081344 | tf_op jit(solution)/shard_map/all_to_all | solution.py:110
  82.8 2.9 %copy.7 = bf16[64,64,66]{2,0,1:T(8,128)(2,1)} copy(bf16[64,64,66]{2,1,0:T(8,128)(2,1)} %all_to_all.14) | data formatting | bytes 1081344 | tf_op jit(solution)/shard_map/all_to_all | solution.py:110
  85.8 18.3 %all-to-all-start = ((bf16[64,64,66]{2,0,1:T(8,128)(2,1)}), bf16[64,64,66]{2,0,1:T(8,128)(2,1)}, u32[]{:S(2)}, u32[]{:S(2)}) async-start(bf16[64,64,66]{2,0,1:T(8,128)(2,1)} %copy.7), calls=%async_computation | async-start | bytes 2097152 | tf_op jit(solution)/shard_map/all_to_all | solution.py:110
  104.2 0.1 add_multiply_fusion
  104.3 0.1 broadcast_multiply_fusion
  104.3 0.1 add.540
  104.5 2.5 %reshape.605 = bf16[64,4224]{1,0:T(8,128)(2,1)} reshape(bf16[64,12,352]{2,1,0:T(8,128)(2,1)} %copy.6) | data formatting | bytes 1081344 | tf_op jit(solution)/shard_map/reshape | solution.py:108
  107.0 26.0 %all-to-all-done = bf16[64,64,66]{2,0,1:T(8,128)(2,1)} async-done(((bf16[64,64,66]{2,0,1:T(8,128)(2,1)}), bf16[64,64,66]{2,0,1:T(8,128)(2,1)}, u32[]{:S(2)}, u32[]{:S(2)}) %all-to-all-start) | async-done | bytes 540704 | tf_op jit(solution)/shard_map/all_to_all | solution.py:110
  133.0 2.3 copy.12
  135.3 3.4 %reduce_sum.56 = f32[352]{0:T(512)S(1)} reduce(f32[1,4096,352]{2,1,0:T(8,128)} %all-gather.3.cloned.1.call-done, f32[]{:T(128)} %constant.121.clone.1), dimensions={0,1}, to_apply=%region_2.0 | reduce | flops 1441440 | bytes 5768580 | tf_op jit(solution)/shard_map/reduce_sum | solution.py:98
  138.7 3.7 %multiply_reduce_fusion = f32[352]{0:T(512)S(1)} fusion(f32[1,4096,352]{2,1,0:T(8,128)} %all-gather.3.cloned.1.call-done, f32[352]{0:T(512)S(1)} %broadcast_multiply_fusion.1), kind=kLoop, calls=%fused_computation.6 | loop fusion | flops 4325024 | bytes 5769984 | tf_op jit(solution)/shard_map/reduce_sum | solution.py:100
  142.4 0.9 copy-done.1
  143.3 2.3 divide_convert_fusion
  145.5 5.0 %reshape.606 = bf16[64,64,66]{2,1,0:T(8,128)(2,1)} reshape(bf16[64,4224]{1,0:T(8,128)(2,1)} %reshape.605) | data formatting | bytes 1081344 | tf_op jit(solution)/shard_map/reshape | solution.py:118
  150.5 2.7 %fusion.4 = bf16[64,64,66]{2,1,0:T(8,128)(2,1)} fusion(bf16[64,64,66]{2,1,0:T(8,128)(2,1)} %reshape.606, s32[64]{0:T(128)S(1)} %add.540), kind=kOutput, calls=%fused_computation.12 | convolution fusion | flops 34877440 | bytes 1081600 | tf_op jit(solution)/shard_map/bkt,pk->bpt/dot_general | solution.py:117
  153.2 3.1 %reshape.607 = bf16[64,4224]{1,0:T(8,128)(2,1)} reshape(bf16[64,64,66]{2,1,0:T(8,128)(2,1)} %fusion.4) | data formatting | bytes 1081344 | tf_op jit(solution)/shard_map/reshape | solution.py:119
  156.3 2.7 %select_convert_fusion = bf16[66,352]{1,0:T(8,128)(2,1)S(1)} fusion(s32[352]{0:T(512)S(1)} %iota_add_fusion.1, s32[66]{0:T(128)S(1)} %iota_add_fusion.2, bf16[4096,66]{0,1:T(8,128)(2,1)} %copy.12, bf16[4096,352]{1,0:T(8,128)(2,1)} %divide_convert_fusion), kind=kOutput, calls=%fused_computation.25 | convolution fusion | flops 190479168 | bytes 3472392 | tf_op jit(solution)/shard_map/bi,bj->ij/dot_general | solution.py:122
  159.0 2.3 collective-permute-start.9
  161.3 4.8 %collective-permute-start.8 = (bf16[66,352]{1,0:T(8,128)(2,1)S(1)}, bf16[66,352]{1,0:T(8,128)(2,1)S(1)}, u32[]{:S(2)}, u32[]{:S(2)}) collective-permute-start(bf16[66,352]{1,0:T(8,128)(2,1)S(1)} %select_convert_fusion), channel_id=1, source_target_pairs={{0,384},{192,576},{384,0},{576,192},{1,385},{193,577},{385,1},{577... | collective-permute-start | bytes 139400 | tf_op jit(solution)/shard_map/ppermute | solution.py:20
  166.1 3.0 %collective-permute-start.7 = (bf16[66,352]{1,0:T(8,128)(2,1)S(1)}, bf16[66,352]{1,0:T(8,128)(2,1)S(1)}, u32[]{:S(2)}, u32[]{:S(2)}) collective-permute-start(bf16[66,352]{1,0:T(8,128)(2,1)S(1)} %select_convert_fusion), channel_id=1, source_target_pairs={{0,576},{192,0},{384,192},{576,384},{1,577},{193,1},{385,193},{577... | collective-permute-start | bytes 139400 | tf_op jit(solution)/shard_map/ppermute | solution.py:20
  169.1 0.0 collective-permute-done.9
  169.1 2.7 %collective-permute-done.7 = bf16[66,352]{1,0:T(8,128)(2,1)S(1)} collective-permute-done((bf16[66,352]{1,0:T(8,128)(2,1)S(1)}, bf16[66,352]{1,0:T(8,128)(2,1)S(1)}, u32[]{:S(2)}, u32[]{:S(2)}) %collective-permute-start.7) | collective-permute-done | bytes 46496 | tf_op jit(solution)/shard_map/ppermute | solution.py:20
  171.9 0.1 pad_maximum_fusion.1
  171.9 1.9 collective-permute-start.10
  173.8 3.4 %collective-permute-start.13 = (bf16[4,66,352]{2,1,0:T(8,128)(2,1)S(1)}, bf16[4,66,352]{2,1,0:T(8,128)(2,1)S(1)}, u32[]{:S(2)}, u32[]{:S(2)}) collective-permute-start(bf16[4,66,352]{2,1,0:T(8,128)(2,1)S(1)} %pad_maximum_fusion.1), channel_id=1, source_target_pairs={{0,24},{24,48},{48,72},{72,96},{96,120},{120,144},{144,168},{168,0... | collective-permute-start | bytes 557576 | tf_op jit(solution)/shard_map/ppermute | solution.py:13
  177.3 3.1 %collective-permute-done.10 = bf16[4,66,352]{2,1,0:T(8,128)(2,1)S(1)} collective-permute-done((bf16[4,66,352]{2,1,0:T(8,128)(2,1)S(1)}, bf16[4,66,352]{2,1,0:T(8,128)(2,1)S(1)}, u32[]{:S(2)}, u32[]{:S(2)}) %collective-permute-start.10) | collective-permute-done | bytes 185888 | tf_op jit(solution)/shard_map/ppermute | solution.py:13
  180.4 2.6 %collective-permute-start.11 = (bf16[4,66,352]{2,1,0:T(8,128)(2,1)S(1)}, bf16[4,66,352]{2,1,0:T(8,128)(2,1)S(1)}, u32[]{:S(2)}, u32[]{:S(2)}) collective-permute-start(bf16[4,66,352]{2,1,0:T(8,128)(2,1)S(1)} %collective-permute-done.10), channel_id=1, source_target_pairs={{0,168},{24,0},{48,24},{72,48},{96,72},{120,96},{144,120},{168,144... | collective-permute-start | bytes 557576 | tf_op jit(solution)/shard_map/ppermute | solution.py:13
  183.0 2.6 %collective-permute-start.14 = (bf16[4,66,352]{2,1,0:T(8,128)(2,1)S(1)}, bf16[4,66,352]{2,1,0:T(8,128)(2,1)S(1)}, u32[]{:S(2)}, u32[]{:S(2)}) collective-permute-start(bf16[4,66,352]{2,1,0:T(8,128)(2,1)S(1)} %collective-permute-done.13), channel_id=1, source_target_pairs={{0,24},{24,48},{48,72},{72,96},{96,120},{120,144},{144,168},{168,0... | collective-permute-start | bytes 557576 | tf_op jit(solution)/shard_map/ppermute | solution.py:13
  185.7 2.2 collective-permute-done.11
  187.9 3.4 %collective-permute-start.12 = (bf16[4,66,352]{2,1,0:T(8,128)(2,1)S(1)}, bf16[4,66,352]{2,1,0:T(8,128)(2,1)S(1)}, u32[]{:S(2)}, u32[]{:S(2)}) collective-permute-start(bf16[4,66,352]{2,1,0:T(8,128)(2,1)S(1)} %collective-permute-done.11), channel_id=1, source_target_pairs={{0,168},{24,0},{48,24},{72,48},{96,72},{120,96},{144,120},{168,144... | collective-permute-start | bytes 557576 | tf_op jit(solution)/shard_map/ppermute | solution.py:13
  191.3 1.9 collective-permute-start.15
  193.2 5.9 %collective-permute-done.15 = bf16[4,66,352]{2,1,0:T(8,128)(2,1)S(1)} collective-permute-done((bf16[4,66,352]{2,1,0:T(8,128)(2,1)S(1)}, bf16[4,66,352]{2,1,0:T(8,128)(2,1)S(1)}, u32[]{:S(2)}, u32[]{:S(2)}) %collective-permute-start.15) | collective-permute-done | bytes 185888 | tf_op jit(solution)/shard_map/ppermute | solution.py:13
  199.1 1.9 collective-permute-start.16
  201.1 5.9 %collective-permute-done.16 = bf16[4,66,352]{2,1,0:T(8,128)(2,1)S(1)} collective-permute-done((bf16[4,66,352]{2,1,0:T(8,128)(2,1)S(1)}, bf16[4,66,352]{2,1,0:T(8,128)(2,1)S(1)}, u32[]{:S(2)}, u32[]{:S(2)}) %collective-permute-start.16) | collective-permute-done | bytes 185888 | tf_op jit(solution)/shard_map/ppermute | solution.py:13
  207.2 0.6 copy.10
  207.8 7.4 %collective-permute-start.17 = (bf16[8,4,66,352]{3,0,2,1:T(8,128)(2,1)S(1)}, bf16[8,4,66,352]{3,0,2,1:T(8,128)(2,1)S(1)}, u32[]{:S(2)}, u32[]{:S(2)}) collective-permute-start(bf16[8,4,66,352]{3,0,2,1:T(8,128)(2,1)S(1)} %copy.10), channel_id=1, source_target_pairs={{0,12},{12,0},{1,13},{13,1},{2,14},{14,2},{3,15},{15,3},{4,16},{16... | collective-permute-start | bytes 4460552 | tf_op jit(solution)/shard_map/ppermute | solution.py:13
  215.2 0.1 iota_add_fusion
  215.3 2.8 %collective-permute-done.17 = bf16[8,4,66,352]{3,0,2,1:T(8,128)(2,1)S(1)} collective-permute-done((bf16[8,4,66,352]{3,0,2,1:T(8,128)(2,1)S(1)}, bf16[8,4,66,352]{3,0,2,1:T(8,128)(2,1)S(1)}, u32[]{:S(2)}, u32[]{:S(2)}) %collective-permute-start.17) | collective-permute-done | bytes 1486880 | tf_op jit(solution)/shard_map/ppermute | solution.py:13
  218.1 0.2 copy.14
  218.3 2.5 %pad_maximum_fusion = bf16[2,8,4,66,352]{4,3,2,1,0:T(8,128)(2,1)} fusion(bf16[1,8,4,66,352]{4,3,2,1,0:T(8,128)(2,1)S(1)} %bitcast.70, bf16[1,8,4,66,352]{4,3,2,1,0:T(8,128)(2,1)S(1)} %bitcast.68), kind=kLoop, calls=%fused_computation.7 | loop fusion | flops 1486848 | bytes 5947392 | tf_op jit(solution)/shard_map/stack | solution.py:39
  220.8 1.8 fusion
  222.6 5.8 %reshape.608 = bf16[4224,352]{1,0:T(8,128)(2,1)} reshape(bf16[2,8,4,66,352]{4,3,2,1,0:T(8,128)(2,1)} %pad_maximum_fusion) | data formatting | bytes 5947392 | tf_op jit(solution)/shard_map/reshape | solution.py:130
  228.4 3.3 %fusion.6 = bf16[64,352]{1,0:T(8,128)(2,1)} fusion(bf16[64,4224]{1,0:T(8,128)(2,1)} %reshape.607, bf16[4224,352]{1,0:T(8,128)(2,1)} %reshape.608, f32[352]{0:T(512)S(1)} %get-tuple-element.29, f32[352]{0:T(512)S(1)} %multiply_add_fusion, f32[352]{0:T(512)S(1)} %get-tuple-element.30, f32[352]{0:T(512)S(1)} %broadcast_multiply_fusion.1, ...), kind=kOutput, calls=%fused_computation.15 | convolution fusion | flops 190496768 | bytes 3655168 | tf_op jit(solution)/shard_map/dot_general | solution.py:145
  (46 shorter events, 0.6 us)
Async XLA Ops:
  6.5 1.8 copy-start
  6.5 128.7 %all-gather.3.cloned.1.call-start = ((), (), s32[]{:S(2)}) async-start(), calls=%async_computation.1 | async-start | bytes 6389760 | tf_op jit(solution)/shard_map/all_gather | solution.py:97
  11.4 13.2 %collective-permute-start = (f32[2,1,1,352]{3,2,1,0:T(1,128)S(1)}, f32[2,1,1,352]{3,2,1,0:T(1,128)S(1)}, u32[]{:S(2)}, u32[]{:S(2)}) collective-permute-start(f32[2,1,1,352]{3,2,1,0:T(1,128)S(1)} %pad_maximum_fusion.2), channel_id=1, source_target_pairs={{0,12},{12,0},{1,13},{13,1},{2,14},{14,2},{3,15},{15,3},{4,16},{16... | collective-permute-start | bytes 8456 | tf_op jit(solution)/shard_map/ppermute | solution.py:49
  24.7 4.3 %collective-permute-start.1 = (f32[2,1,1,352]{3,2,1,0:T(1,128)S(1)}, f32[2,1,1,352]{3,2,1,0:T(1,128)S(1)}, u32[]{:S(2)}, u32[]{:S(2)}) collective-permute-start(f32[2,1,1,352]{3,2,1,0:T(1,128)S(1)} %pad_maximum_fusion.3), channel_id=1, source_target_pairs={{0,24},{24,0},{48,72},{72,48},{96,120},{120,96},{144,168},{168,144... | collective-permute-start | bytes 8456 | tf_op jit(solution)/shard_map/ppermute | solution.py:49
  29.1 5.2 %collective-permute-start.2 = (f32[2,1,1,352]{3,2,1,0:T(1,128)S(1)}, f32[2,1,1,352]{3,2,1,0:T(1,128)S(1)}, u32[]{:S(2)}, u32[]{:S(2)}) collective-permute-start(f32[2,1,1,352]{3,2,1,0:T(1,128)S(1)} %pad_maximum_fusion.4), channel_id=1, source_target_pairs={{0,48},{24,72},{48,0},{72,24},{96,144},{120,168},{144,96},{168,120... | collective-permute-start | bytes 8456 | tf_op jit(solution)/shard_map/ppermute | solution.py:49
  34.3 8.3 %collective-permute-start.3 = (f32[2,1,1,352]{3,2,1,0:T(1,128)S(1)}, f32[2,1,1,352]{3,2,1,0:T(1,128)S(1)}, u32[]{:S(2)}, u32[]{:S(2)}) collective-permute-start(f32[2,1,1,352]{3,2,1,0:T(1,128)S(1)} %pad_maximum_fusion.5), channel_id=1, source_target_pairs={{0,96},{24,120},{48,144},{72,168},{96,0},{120,24},{144,48},{168,72... | collective-permute-start | bytes 8456 | tf_op jit(solution)/shard_map/ppermute | solution.py:49
  42.6 7.3 %collective-permute-start.5 = (f32[2,1,1,352]{3,2,1,0:T(1,128)S(1)}, f32[2,1,1,352]{3,2,1,0:T(1,128)S(1)}, u32[]{:S(2)}, u32[]{:S(2)}) collective-permute-start(f32[2,1,1,352]{3,2,1,0:T(1,128)S(1)} %pad_maximum_fusion.6), channel_id=1, source_target_pairs={{0,384},{192,576},{384,0},{576,192},{1,385},{193,577},{385,1},{577... | collective-permute-start | bytes 8456 | tf_op jit(solution)/shard_map/ppermute | solution.py:20
  44.5 5.3 %collective-permute-start.4 = (f32[2,1,1,352]{3,2,1,0:T(1,128)S(1)}, f32[2,1,1,352]{3,2,1,0:T(1,128)S(1)}, u32[]{:S(2)}, u32[]{:S(2)}) collective-permute-start(f32[2,1,1,352]{3,2,1,0:T(1,128)S(1)} %pad_maximum_fusion.6), channel_id=1, source_target_pairs={{0,576},{192,0},{384,192},{576,384},{1,577},{193,1},{385,193},{577... | collective-permute-start | bytes 8456 | tf_op jit(solution)/shard_map/ppermute | solution.py:20
  46.5 6.4 %collective-permute-start.6 = (f32[2,1,1,352]{3,2,1,0:T(1,128)S(1)}, f32[2,1,1,352]{3,2,1,0:T(1,128)S(1)}, u32[]{:S(2)}, u32[]{:S(2)}) collective-permute-start(f32[2,1,1,352]{3,2,1,0:T(1,128)S(1)} %pad_maximum_fusion.6), channel_id=1, source_target_pairs={{0,192},{192,384},{384,576},{576,0},{1,193},{193,385},{385,577},{5... | collective-permute-start | bytes 8456 | tf_op jit(solution)/shard_map/ppermute | solution.py:20
  85.8 47.2 %all-to-all-start = ((bf16[64,64,66]{2,0,1:T(8,128)(2,1)}), bf16[64,64,66]{2,0,1:T(8,128)(2,1)}, u32[]{:S(2)}, u32[]{:S(2)}) async-start(bf16[64,64,66]{2,0,1:T(8,128)(2,1)} %copy.7), calls=%async_computation | async-start | bytes 2097152 | tf_op jit(solution)/shard_map/all_to_all | solution.py:110
  138.7 4.6 %copy-start.1 = (f32[1,4096,352]{2,1,0:T(8,128)S(1)}, f32[1,4096,352]{2,1,0:T(8,128)}, u32[]{:S(2)}) copy-start(f32[1,4096,352]{2,1,0:T(8,128)} %all-gather.3.cloned.1.call-done) | copy-start | bytes 17301508
  159.0 10.1 %collective-permute-start.9 = (bf16[66,352]{1,0:T(8,128)(2,1)S(1)}, bf16[66,352]{1,0:T(8,128)(2,1)S(1)}, u32[]{:S(2)}, u32[]{:S(2)}) collective-permute-start(bf16[66,352]{1,0:T(8,128)(2,1)S(1)} %select_convert_fusion), channel_id=1, source_target_pairs={{0,192},{192,384},{384,576},{576,0},{1,193},{193,385},{385,577},{5... | collective-permute-start | bytes 139400 | tf_op jit(solution)/shard_map/ppermute | solution.py:20
  161.3 7.8 %collective-permute-start.8 = (bf16[66,352]{1,0:T(8,128)(2,1)S(1)}, bf16[66,352]{1,0:T(8,128)(2,1)S(1)}, u32[]{:S(2)}, u32[]{:S(2)}) collective-permute-start(bf16[66,352]{1,0:T(8,128)(2,1)S(1)} %select_convert_fusion), channel_id=1, source_target_pairs={{0,384},{192,576},{384,0},{576,192},{1,385},{193,577},{385,1},{577... | collective-permute-start | bytes 139400 | tf_op jit(solution)/shard_map/ppermute | solution.py:20
  166.1 5.7 %collective-permute-start.7 = (bf16[66,352]{1,0:T(8,128)(2,1)S(1)}, bf16[66,352]{1,0:T(8,128)(2,1)S(1)}, u32[]{:S(2)}, u32[]{:S(2)}) collective-permute-start(bf16[66,352]{1,0:T(8,128)(2,1)S(1)} %select_convert_fusion), channel_id=1, source_target_pairs={{0,576},{192,0},{384,192},{576,384},{1,577},{193,1},{385,193},{577... | collective-permute-start | bytes 139400 | tf_op jit(solution)/shard_map/ppermute | solution.py:20
  171.9 8.4 %collective-permute-start.10 = (bf16[4,66,352]{2,1,0:T(8,128)(2,1)S(1)}, bf16[4,66,352]{2,1,0:T(8,128)(2,1)S(1)}, u32[]{:S(2)}, u32[]{:S(2)}) collective-permute-start(bf16[4,66,352]{2,1,0:T(8,128)(2,1)S(1)} %pad_maximum_fusion.1), channel_id=1, source_target_pairs={{0,168},{24,0},{48,24},{72,48},{96,72},{120,96},{144,120},{168,144... | collective-permute-start | bytes 557576 | tf_op jit(solution)/shard_map/ppermute | solution.py:13
  173.8 9.2 %collective-permute-start.13 = (bf16[4,66,352]{2,1,0:T(8,128)(2,1)S(1)}, bf16[4,66,352]{2,1,0:T(8,128)(2,1)S(1)}, u32[]{:S(2)}, u32[]{:S(2)}) collective-permute-start(bf16[4,66,352]{2,1,0:T(8,128)(2,1)S(1)} %pad_maximum_fusion.1), channel_id=1, source_target_pairs={{0,24},{24,48},{48,72},{72,96},{96,120},{120,144},{144,168},{168,0... | collective-permute-start | bytes 557576 | tf_op jit(solution)/shard_map/ppermute | solution.py:13
  180.4 7.5 %collective-permute-start.11 = (bf16[4,66,352]{2,1,0:T(8,128)(2,1)S(1)}, bf16[4,66,352]{2,1,0:T(8,128)(2,1)S(1)}, u32[]{:S(2)}, u32[]{:S(2)}) collective-permute-start(bf16[4,66,352]{2,1,0:T(8,128)(2,1)S(1)} %collective-permute-done.10), channel_id=1, source_target_pairs={{0,168},{24,0},{48,24},{72,48},{96,72},{120,96},{144,120},{168,144... | collective-permute-start | bytes 557576 | tf_op jit(solution)/shard_map/ppermute | solution.py:13
  183.0 8.2 %collective-permute-start.14 = (bf16[4,66,352]{2,1,0:T(8,128)(2,1)S(1)}, bf16[4,66,352]{2,1,0:T(8,128)(2,1)S(1)}, u32[]{:S(2)}, u32[]{:S(2)}) collective-permute-start(bf16[4,66,352]{2,1,0:T(8,128)(2,1)S(1)} %collective-permute-done.13), channel_id=1, source_target_pairs={{0,24},{24,48},{48,72},{72,96},{96,120},{120,144},{144,168},{168,0... | collective-permute-start | bytes 557576 | tf_op jit(solution)/shard_map/ppermute | solution.py:13
  187.9 13.2 %collective-permute-start.12 = (bf16[4,66,352]{2,1,0:T(8,128)(2,1)S(1)}, bf16[4,66,352]{2,1,0:T(8,128)(2,1)S(1)}, u32[]{:S(2)}, u32[]{:S(2)}) collective-permute-start(bf16[4,66,352]{2,1,0:T(8,128)(2,1)S(1)} %collective-permute-done.11), channel_id=1, source_target_pairs={{0,168},{24,0},{48,24},{72,48},{96,72},{120,96},{144,120},{168,144... | collective-permute-start | bytes 557576 | tf_op jit(solution)/shard_map/ppermute | solution.py:13
  191.3 7.9 %collective-permute-start.15 = (bf16[4,66,352]{2,1,0:T(8,128)(2,1)S(1)}, bf16[4,66,352]{2,1,0:T(8,128)(2,1)S(1)}, u32[]{:S(2)}, u32[]{:S(2)}) collective-permute-start(bf16[4,66,352]{2,1,0:T(8,128)(2,1)S(1)} %collective-permute-done.14), channel_id=1, source_target_pairs={{0,24},{24,48},{48,72},{72,96},{96,120},{120,144},{144,168},{168,0... | collective-permute-start | bytes 557576 | tf_op jit(solution)/shard_map/ppermute | solution.py:13
  199.1 7.9 %collective-permute-start.16 = (bf16[4,66,352]{2,1,0:T(8,128)(2,1)S(1)}, bf16[4,66,352]{2,1,0:T(8,128)(2,1)S(1)}, u32[]{:S(2)}, u32[]{:S(2)}) collective-permute-start(bf16[4,66,352]{2,1,0:T(8,128)(2,1)S(1)} %collective-permute-done.15), channel_id=1, source_target_pairs={{0,24},{24,48},{48,72},{72,96},{96,120},{120,144},{144,168},{168,0... | collective-permute-start | bytes 557576 | tf_op jit(solution)/shard_map/ppermute | solution.py:13
  207.8 10.3 %collective-permute-start.17 = (bf16[8,4,66,352]{3,0,2,1:T(8,128)(2,1)S(1)}, bf16[8,4,66,352]{3,0,2,1:T(8,128)(2,1)S(1)}, u32[]{:S(2)}, u32[]{:S(2)}) collective-permute-start(bf16[8,4,66,352]{3,0,2,1:T(8,128)(2,1)S(1)} %copy.10), channel_id=1, source_target_pairs={{0,12},{12,0},{1,13},{13,1},{2,14},{14,2},{3,15},{15,3},{4,16},{16... | collective-permute-start | bytes 4460552 | tf_op jit(solution)/shard_map/ppermute | solution.py:13
Sparse Core Ops, SparseCore 0:
  11.5 102.6 all-gather.2

commit v15 on v13

--- a/solution.py
+++ b/solution.py
@@ -104,7 +104,9 @@
     mean1, var1 = dp_stats(feats[1:])
     second = ((feats[1] - mean1[0]) / jnp.sqrt(var1[0] + eps)).astype(jnp.bfloat16)
     n_mp = lax.axis_size("mp")
-    stacked = lax.all_gather(second, "mp", axis=0)
+    stacked = lax.all_to_all(
+        jnp.broadcast_to(second[None], (n_mp,) + second.shape), "mp", split_axis=0, concat_axis=0, tiled=True
+    )
     second_full = jnp.transpose(stacked, (1, 0, 2)).reshape(local, n_mp * rows)
     width = second_full.shape[1] // dp_count
     columns = lax.all_to_all(second_full, DP, split_axis=1, concat_axis=0, tiled=True)

time: 226 us -> 229 us (1.013)
  blocking collectives: 23.4 us -> 0 us
  waiting for transfers between devices: 61.9 us -> 80.8 us
  starting transfers between devices: 79.7 us -> 85.3 us
    all_gather x1 -> x0, blocking collectives: 23.4 us -> none  [shards(): stacked = lax.all_gather(second, 'mp', axis=0)]
    all_to_all x0 -> x1, waiting for transfers between devices: none -> 18.8 us  [shards(): lax.all_to_all(jnp.broadcast_to(second[None], (n_mp,) + second.shape), 'm...]
    all_to_all x0 -> x1, starting transfers between devices: none -> 7.64 us  [shards(): lax.all_to_all(jnp.broadcast_to(second[None], (n_mp,) + second.shape), 'm...]
    all_to_all x1, starting transfers between devices: 19.4 us -> 16.8 us  [shards(): lax.all_to_all(second_full, DP, split_axis=1, concat_axis=0, tiled=True)]
  transfers between devices with their start and end apart: 20 -> 21, of which waited for: 14 -> 15; matrix products, arithmetic and copies ran while one was open for 6% -> 7% of each run, Pallas kernels for 0% -> 0%
where the time goes in v15:
time: 229 us; the launch traced here: 228 us
  starting transfers between devices  85.3 us (37%)
  waiting for transfers between devices  80.8 us (35%)
  local copies, waits for them, and re-layouts  25.4 us (11%)
  between operations  13.9 us (6%)
  other arithmetic  12.6 us (6%)
  matrix products  10.2 us (4%)
    ppermute x8, starting transfers between devices, shift(): return lax.ppermute(v, axis, [(i, (i + step) % n) for i in range(n)])  26 us
    all_to_all x1, waiting for transfers between devices, shards(): lax.all_to_all(second_full, DP, split_axis=1, concat_axis=0, tiled=True)  22.4 us
    ppermute x8, waiting for transfers between devices, shift(): return lax.ppermute(v, axis, [(i, (i + step) % n) for i in range(n)])  18.9 us
    all_to_all x1, waiting for transfers between devices, shards(): lax.all_to_all(jnp.broadcast_to(second[None], (n_mp,) + second.shape), 'm...  18.8 us
    ppermute x4, starting transfers between devices, combine(): other = lax.ppermute(jnp.stack([mean, m2]), axis, pairs)  18.2 us
    all_to_all x1, starting transfers between devices, shards(): lax.all_to_all(second_full, DP, split_axis=1, concat_axis=0, tiled=True)  16.8 us
    ppermute x6, starting transfers between devices, direct_gather(): got[t] = lax.ppermute(v, axis, [(i, (i - t) % n) for i in range(n)])  16.6 us
    ppermute x4, waiting for transfers between devices, combine(): other = lax.ppermute(jnp.stack([mean, m2]), axis, pairs)  12.9 us
  transfers between devices with their start and end apart: 21, of which 15 were waited for; matrix products, arithmetic and copies ran while one was open for 7% of the time, Pallas kernels for 0%

profile of v15, /device:TPU:1, one launch (start us, length us, event | category | flops | bytes accessed | tf_op | source)
XLA Modules:
  0.0 228.1 jit_solution(10587401626562038776)
XLA Ops:
  6.5 1.8 copy-done
  8.4 2.3 %fusion.3 = f32[2,64,352]{2,1,0:T(8,128)S(1)} fusion(bf16[2,64,4224]{2,1,0:T(8,128)(2,1)} %param.2, bf16[4224,352]{0,1:T(8,128)(2,1)S(1)} %copy-done), kind=kOutput, calls=%fused_computation.9 | convolution fusion | flops 380633088 | bytes 4235264 | tf_op jit(solution)/shard_map/vbh,hc->vbc/dot_general | solution.py:96
  10.7 0.7 fusion.29
  11.4 0.0 all-gather.3.cloned.1.call-update
  11.4 12.4 %collective-permute-start = (f32[2,1,1,352]{3,2,1,0:T(1,128)S(1)}, f32[2,1,1,352]{3,2,1,0:T(1,128)S(1)}, u32[]{:S(2)}, u32[]{:S(2)}) collective-permute-start(f32[2,1,1,352]{3,2,1,0:T(1,128)S(1)} %pad_maximum_fusion.2), channel_id=1, source_target_pairs={{0,12},{12,0},{1,13},{13,1},{2,14},{14,2},{3,15},{15,3},{4,16},{16... | collective-permute-start | bytes 8456 | tf_op jit(solution)/shard_map/ppermute | solution.py:49
  23.9 0.8 collective-permute-done
  24.7 1.9 collective-permute-start.1
  26.6 2.4 %collective-permute-done.1 = f32[2,1,1,352]{3,2,1,0:T(1,128)S(1)} collective-permute-done((f32[2,1,1,352]{3,2,1,0:T(1,128)S(1)}, f32[2,1,1,352]{3,2,1,0:T(1,128)S(1)}, u32[]{:S(2)}, u32[]{:S(2)}) %collective-permute-start.1) | collective-permute-done | bytes 2848 | tf_op jit(solution)/shard_map/ppermute | solution.py:49
  29.1 1.9 collective-permute-start.2
  31.0 3.3 %collective-permute-done.2 = f32[2,1,1,352]{3,2,1,0:T(1,128)S(1)} collective-permute-done((f32[2,1,1,352]{3,2,1,0:T(1,128)S(1)}, f32[2,1,1,352]{3,2,1,0:T(1,128)S(1)}, u32[]{:S(2)}, u32[]{:S(2)}) %collective-permute-start.2) | collective-permute-done | bytes 2848 | tf_op jit(solution)/shard_map/ppermute | solution.py:49
  34.3 1.9 collective-permute-start.3
  36.3 6.3 %collective-permute-done.3 = f32[2,1,1,352]{3,2,1,0:T(1,128)S(1)} collective-permute-done((f32[2,1,1,352]{3,2,1,0:T(1,128)S(1)}, f32[2,1,1,352]{3,2,1,0:T(1,128)S(1)}, u32[]{:S(2)}, u32[]{:S(2)}) %collective-permute-start.3) | collective-permute-done | bytes 2848 | tf_op jit(solution)/shard_map/ppermute | solution.py:49
  42.6 1.9 collective-permute-start.4
  44.6 1.9 collective-permute-start.5
  46.5 3.4 %collective-permute-start.6 = (f32[2,1,1,352]{3,2,1,0:T(1,128)S(1)}, f32[2,1,1,352]{3,2,1,0:T(1,128)S(1)}, u32[]{:S(2)}, u32[]{:S(2)}) collective-permute-start(f32[2,1,1,352]{3,2,1,0:T(1,128)S(1)} %pad_maximum_fusion.6), channel_id=1, source_target_pairs={{0,192},{192,384},{384,576},{576,0},{1,193},{193,385},{385,577},{5... | collective-permute-start | bytes 8456 | tf_op jit(solution)/shard_map/ppermute | solution.py:20
  49.9 0.6 collective-permute-done.5
  50.5 2.9 %collective-permute-done.6 = f32[2,1,1,352]{3,2,1,0:T(1,128)S(1)} collective-permute-done((f32[2,1,1,352]{3,2,1,0:T(1,128)S(1)}, f32[2,1,1,352]{3,2,1,0:T(1,128)S(1)}, u32[]{:S(2)}, u32[]{:S(2)}) %collective-permute-start.6) | collective-permute-done | bytes 2848 | tf_op jit(solution)/shard_map/ppermute | solution.py:20
  53.5 0.1 multiply_reduce_fusion.2
  53.5 0.9 broadcast_in_dim.8
  54.4 7.6 %all-to-all-start = ((bf16[12,64,352]{2,1,0:T(8,128)(2,1)}), bf16[12,64,352]{2,1,0:T(8,128)(2,1)}, u32[]{:S(2)}, u32[]{:S(2)}) async-start(bf16[12,64,352]{2,1,0:T(8,128)(2,1)} %broadcast_in_dim.8), calls=%async_computation | async-start | bytes 1179648 | tf_op jit(solution)/shard_map/all_to_all | solution.py:107
  62.1 18.8 %all-to-all-done = bf16[12,64,352]{2,1,0:T(8,128)(2,1)} async-done(((bf16[12,64,352]{2,1,0:T(8,128)(2,1)}), bf16[12,64,352]{2,1,0:T(8,128)(2,1)}, u32[]{:S(2)}, u32[]{:S(2)}) %all-to-all-start) | async-done | bytes 540704 | tf_op jit(solution)/shard_map/all_to_all | solution.py:107
  80.9 2.3 %copy.4 = bf16[64,12,352]{2,1,0:T(8,128)(2,1)} copy(bf16[64,12,352]{2,0,1:T(8,128)(2,1)} %bitcast.6) | data formatting | bytes 1081344 | tf_op jit(solution)/shard_map/transpose | solution.py:110
  83.3 4.0 %all_to_all.18 = bf16[64,64,66]{2,1,0:T(8,128)(2,1)} reshape(bf16[64,12,352]{2,1,0:T(8,128)(2,1)} %copy.4) | data formatting | bytes 1081344 | tf_op jit(solution)/shard_map/all_to_all | solution.py:112
  87.3 3.0 %copy.5 = bf16[64,64,66]{2,0,1:T(8,128)(2,1)} copy(bf16[64,64,66]{2,1,0:T(8,128)(2,1)} %all_to_all.18) | data formatting | bytes 1081344 | tf_op jit(solution)/shard_map/all_to_all | solution.py:112
  90.3 16.8 %all-to-all-start.1 = ((bf16[64,64,66]{2,0,1:T(8,128)(2,1)}), bf16[64,64,66]{2,0,1:T(8,128)(2,1)}, u32[]{:S(2)}, u32[]{:S(2)}) async-start(bf16[64,64,66]{2,0,1:T(8,128)(2,1)} %copy.5), calls=%async_computation.1 | async-start | bytes 2097152 | tf_op jit(solution)/shard_map/all_to_all | solution.py:112
  107.1 0.1 add_multiply_fusion
  107.2 0.1 broadcast_multiply_fusion
  107.3 0.1 add.540
  107.4 2.7 %fusion.5 = bf16[64,64,66]{2,1,0:T(8,128)(2,1)} fusion(bf16[64,64,66]{2,1,0:T(8,128)(2,1)} %all_to_all.18, s32[64]{0:T(128)S(1)} %add.540), kind=kOutput, calls=%fused_computation.13 | convolution fusion | flops 34877440 | bytes 1081600 | tf_op jit(solution)/shard_map/bkt,pk->bpt/dot_general | solution.py:118
  110.1 3.1 %reshape.600 = bf16[64,4224]{1,0:T(8,128)(2,1)} reshape(bf16[64,64,66]{2,1,0:T(8,128)(2,1)} %fusion.5) | data formatting | bytes 1081344 | tf_op jit(solution)/shard_map/reshape | solution.py:120
  113.2 22.4 %all-to-all-done.1 = bf16[64,64,66]{2,0,1:T(8,128)(2,1)} async-done(((bf16[64,64,66]{2,0,1:T(8,128)(2,1)}), bf16[64,64,66]{2,0,1:T(8,128)(2,1)}, u32[]{:S(2)}, u32[]{:S(2)}) %all-to-all-start.1) | async-done | bytes 540704 | tf_op jit(solution)/shard_map/all_to_all | solution.py:112
  135.6 2.3 copy.9
  137.8 3.4 %reduce_sum.56 = f32[352]{0:T(512)S(1)} reduce(f32[1,4096,352]{2,1,0:T(8,128)} %all-gather.3.cloned.1.call-done, f32[]{:T(128)} %constant.121.clone.1), dimensions={0,1}, to_apply=%region_2.0 | reduce | flops 1441440 | bytes 5768580 | tf_op jit(solution)/shard_map/reduce_sum | solution.py:98
  141.2 3.7 %multiply_reduce_fusion = f32[352]{0:T(512)S(1)} fusion(f32[1,4096,352]{2,1,0:T(8,128)} %all-gather.3.cloned.1.call-done, f32[352]{0:T(512)S(1)} %broadcast_multiply_fusion.1), kind=kLoop, calls=%fused_computation.6 | loop fusion | flops 4325024 | bytes 5769984 | tf_op jit(solution)/shard_map/reduce_sum | solution.py:100
  145.0 0.9 copy-done.1
  145.8 1.9 select_convert_fusion
  147.7 4.6 %collective-permute-start.7 = (bf16[66,352]{1,0:T(8,128)(2,1)S(1)}, bf16[66,352]{1,0:T(8,128)(2,1)S(1)}, u32[]{:S(2)}, u32[]{:S(2)}) collective-permute-start(bf16[66,352]{1,0:T(8,128)(2,1)S(1)} %select_convert_fusion), channel_id=1, source_target_pairs={{0,576},{192,0},{384,192},{576,384},{1,577},{193,1},{385,193},{577... | collective-permute-start | bytes 139400 | tf_op jit(solution)/shard_map/ppermute | solution.py:20
  152.3 2.3 collective-permute-start.8
  154.6 2.6 %collective-permute-start.9 = (bf16[66,352]{1,0:T(8,128)(2,1)S(1)}, bf16[66,352]{1,0:T(8,128)(2,1)S(1)}, u32[]{:S(2)}, u32[]{:S(2)}) collective-permute-start(bf16[66,352]{1,0:T(8,128)(2,1)S(1)} %select_convert_fusion), channel_id=1, source_target_pairs={{0,192},{192,384},{384,576},{576,0},{1,193},{193,385},{385,577},{5... | collective-permute-start | bytes 139400 | tf_op jit(solution)/shard_map/ppermute | solution.py:20
  157.2 0.0 collective-permute-done.7
  157.2 1.5 collective-permute-done.8
  158.7 2.7 %collective-permute-done.9 = bf16[66,352]{1,0:T(8,128)(2,1)S(1)} collective-permute-done((bf16[66,352]{1,0:T(8,128)(2,1)S(1)}, bf16[66,352]{1,0:T(8,128)(2,1)S(1)}, u32[]{:S(2)}, u32[]{:S(2)}) %collective-permute-start.9) | collective-permute-done | bytes 46496 | tf_op jit(solution)/shard_map/ppermute | solution.py:20
  161.4 0.1 pad_maximum_fusion.1
  161.5 1.9 collective-permute-start.10
  163.4 3.4 %collective-permute-start.13 = (bf16[4,66,352]{2,1,0:T(8,128)(2,1)S(1)}, bf16[4,66,352]{2,1,0:T(8,128)(2,1)S(1)}, u32[]{:S(2)}, u32[]{:S(2)}) collective-permute-start(bf16[4,66,352]{2,1,0:T(8,128)(2,1)S(1)} %pad_maximum_fusion.1), channel_id=1, source_target_pairs={{0,24},{24,48},{48,72},{72,96},{96,120},{120,144},{144,168},{168,0... | collective-permute-start | bytes 557576 | tf_op jit(solution)/shard_map/ppermute | solution.py:13
  166.8 3.0 %collective-permute-done.10 = bf16[4,66,352]{2,1,0:T(8,128)(2,1)S(1)} collective-permute-done((bf16[4,66,352]{2,1,0:T(8,128)(2,1)S(1)}, bf16[4,66,352]{2,1,0:T(8,128)(2,1)S(1)}, u32[]{:S(2)}, u32[]{:S(2)}) %collective-permute-start.10) | collective-permute-done | bytes 185888 | tf_op jit(solution)/shard_map/ppermute | solution.py:13
  169.9 2.1 collective-permute-start.11
  172.0 3.2 %collective-permute-start.14 = (bf16[4,66,352]{2,1,0:T(8,128)(2,1)S(1)}, bf16[4,66,352]{2,1,0:T(8,128)(2,1)S(1)}, u32[]{:S(2)}, u32[]{:S(2)}) collective-permute-start(bf16[4,66,352]{2,1,0:T(8,128)(2,1)S(1)} %collective-permute-done.13), channel_id=1, source_target_pairs={{0,24},{24,48},{48,72},{72,96},{96,120},{120,144},{144,168},{168,0... | collective-permute-start | bytes 557576 | tf_op jit(solution)/shard_map/ppermute | solution.py:13
  175.2 2.1 collective-permute-done.11
  177.3 2.5 %collective-permute-start.12 = (bf16[4,66,352]{2,1,0:T(8,128)(2,1)S(1)}, bf16[4,66,352]{2,1,0:T(8,128)(2,1)S(1)}, u32[]{:S(2)}, u32[]{:S(2)}) collective-permute-start(bf16[4,66,352]{2,1,0:T(8,128)(2,1)S(1)} %collective-permute-done.11), channel_id=1, source_target_pairs={{0,168},{24,0},{48,24},{72,48},{96,72},{120,96},{144,120},{168,144... | collective-permute-start | bytes 557576 | tf_op jit(solution)/shard_map/ppermute | solution.py:13
  179.8 0.0 collective-permute-done.14
  179.9 2.8 %collective-permute-start.15 = (bf16[4,66,352]{2,1,0:T(8,128)(2,1)S(1)}, bf16[4,66,352]{2,1,0:T(8,128)(2,1)S(1)}, u32[]{:S(2)}, u32[]{:S(2)}) collective-permute-start(bf16[4,66,352]{2,1,0:T(8,128)(2,1)S(1)} %collective-permute-done.14), channel_id=1, source_target_pairs={{0,24},{24,48},{48,72},{72,96},{96,120},{120,144},{144,168},{168,0... | collective-permute-start | bytes 557576 | tf_op jit(solution)/shard_map/ppermute | solution.py:13
  182.7 5.1 %collective-permute-done.15 = bf16[4,66,352]{2,1,0:T(8,128)(2,1)S(1)} collective-permute-done((bf16[4,66,352]{2,1,0:T(8,128)(2,1)S(1)}, bf16[4,66,352]{2,1,0:T(8,128)(2,1)S(1)}, u32[]{:S(2)}, u32[]{:S(2)}) %collective-permute-start.15) | collective-permute-done | bytes 185888 | tf_op jit(solution)/shard_map/ppermute | solution.py:13
  187.7 1.9 collective-permute-start.16
  189.7 5.9 %collective-permute-done.16 = bf16[4,66,352]{2,1,0:T(8,128)(2,1)S(1)} collective-permute-done((bf16[4,66,352]{2,1,0:T(8,128)(2,1)S(1)}, bf16[4,66,352]{2,1,0:T(8,128)(2,1)S(1)}, u32[]{:S(2)}, u32[]{:S(2)}) %collective-permute-start.16) | collective-permute-done | bytes 185888 | tf_op jit(solution)/shard_map/ppermute | solution.py:13
  195.8 0.6 copy.7
  196.4 8.2 %collective-permute-start.17 = (bf16[8,4,66,352]{3,0,2,1:T(8,128)(2,1)S(1)}, bf16[8,4,66,352]{3,0,2,1:T(8,128)(2,1)S(1)}, u32[]{:S(2)}, u32[]{:S(2)}) collective-permute-start(bf16[8,4,66,352]{3,0,2,1:T(8,128)(2,1)S(1)} %copy.7), channel_id=1, source_target_pairs={{0,12},{12,0},{1,13},{13,1},{2,14},{14,2},{3,15},{15,3},{4,16},{16... | collective-permute-start | bytes 4460552 | tf_op jit(solution)/shard_map/ppermute | solution.py:13
  204.6 0.1 iota_add_fusion
  204.7 2.8 %collective-permute-done.17 = bf16[8,4,66,352]{3,0,2,1:T(8,128)(2,1)S(1)} collective-permute-done((bf16[8,4,66,352]{3,0,2,1:T(8,128)(2,1)S(1)}, bf16[8,4,66,352]{3,0,2,1:T(8,128)(2,1)S(1)}, u32[]{:S(2)}, u32[]{:S(2)}) %collective-permute-start.17) | collective-permute-done | bytes 1486880 | tf_op jit(solution)/shard_map/ppermute | solution.py:13
  207.5 0.2 copy.11
  207.8 2.5 %pad_maximum_fusion = bf16[2,8,4,66,352]{4,3,2,1,0:T(8,128)(2,1)} fusion(bf16[1,8,4,66,352]{4,3,2,1,0:T(8,128)(2,1)S(1)} %bitcast.74, bf16[1,8,4,66,352]{4,3,2,1,0:T(8,128)(2,1)S(1)} %bitcast.72), kind=kLoop, calls=%fused_computation.7 | loop fusion | flops 1486848 | bytes 5947392 | tf_op jit(solution)/shard_map/stack | solution.py:39
  210.2 1.8 fusion
  212.0 5.8 %reshape.601 = bf16[4224,352]{1,0:T(8,128)(2,1)} reshape(bf16[2,8,4,66,352]{4,3,2,1,0:T(8,128)(2,1)} %pad_maximum_fusion) | data formatting | bytes 5947392 | tf_op jit(solution)/shard_map/reshape | solution.py:131
  217.9 3.3 %fusion.7 = bf16[64,352]{1,0:T(8,128)(2,1)} fusion(bf16[64,4224]{1,0:T(8,128)(2,1)} %reshape.600, bf16[4224,352]{1,0:T(8,128)(2,1)} %reshape.601, f32[352]{0:T(512)S(1)} %get-tuple-element.25, f32[352]{0:T(512)S(1)} %multiply_add_fusion, f32[352]{0:T(512)S(1)} %get-tuple-element.26, f32[352]{0:T(512)S(1)} %broadcast_multiply_fusion.1, ...), kind=kOutput, calls=%fused_computation.16 | convolution fusion | flops 190496768 | bytes 3655168 | tf_op jit(solution)/shard_map/dot_general | solution.py:146
  (45 shorter events, 0.6 us)
Async XLA Ops:
  6.5 1.8 copy-start
  6.5 131.3 %all-gather.3.cloned.1.call-start = ((), (), s32[]{:S(2)}) async-start(), calls=%async_computation.2 | async-start | bytes 6389760 | tf_op jit(solution)/shard_map/all_gather | solution.py:97
  11.4 13.2 %collective-permute-start = (f32[2,1,1,352]{3,2,1,0:T(1,128)S(1)}, f32[2,1,1,352]{3,2,1,0:T(1,128)S(1)}, u32[]{:S(2)}, u32[]{:S(2)}) collective-permute-start(f32[2,1,1,352]{3,2,1,0:T(1,128)S(1)} %pad_maximum_fusion.2), channel_id=1, source_target_pairs={{0,12},{12,0},{1,13},{13,1},{2,14},{14,2},{3,15},{15,3},{4,16},{16... | collective-permute-start | bytes 8456 | tf_op jit(solution)/shard_map/ppermute | solution.py:49
  24.7 4.3 %collective-permute-start.1 = (f32[2,1,1,352]{3,2,1,0:T(1,128)S(1)}, f32[2,1,1,352]{3,2,1,0:T(1,128)S(1)}, u32[]{:S(2)}, u32[]{:S(2)}) collective-permute-start(f32[2,1,1,352]{3,2,1,0:T(1,128)S(1)} %pad_maximum_fusion.3), channel_id=1, source_target_pairs={{0,24},{24,0},{48,72},{72,48},{96,120},{120,96},{144,168},{168,144... | collective-permute-start | bytes 8456 | tf_op jit(solution)/shard_map/ppermute | solution.py:49
  29.1 5.2 %collective-permute-start.2 = (f32[2,1,1,352]{3,2,1,0:T(1,128)S(1)}, f32[2,1,1,352]{3,2,1,0:T(1,128)S(1)}, u32[]{:S(2)}, u32[]{:S(2)}) collective-permute-start(f32[2,1,1,352]{3,2,1,0:T(1,128)S(1)} %pad_maximum_fusion.4), channel_id=1, source_target_pairs={{0,48},{24,72},{48,0},{72,24},{96,144},{120,168},{144,96},{168,120... | collective-permute-start | bytes 8456 | tf_op jit(solution)/shard_map/ppermute | solution.py:49
  34.3 8.3 %collective-permute-start.3 = (f32[2,1,1,352]{3,2,1,0:T(1,128)S(1)}, f32[2,1,1,352]{3,2,1,0:T(1,128)S(1)}, u32[]{:S(2)}, u32[]{:S(2)}) collective-permute-start(f32[2,1,1,352]{3,2,1,0:T(1,128)S(1)} %pad_maximum_fusion.5), channel_id=1, source_target_pairs={{0,96},{24,120},{48,144},{72,168},{96,0},{120,24},{144,48},{168,72... | collective-permute-start | bytes 8456 | tf_op jit(solution)/shard_map/ppermute | solution.py:49
  42.6 7.2 %collective-permute-start.4 = (f32[2,1,1,352]{3,2,1,0:T(1,128)S(1)}, f32[2,1,1,352]{3,2,1,0:T(1,128)S(1)}, u32[]{:S(2)}, u32[]{:S(2)}) collective-permute-start(f32[2,1,1,352]{3,2,1,0:T(1,128)S(1)} %pad_maximum_fusion.6), channel_id=1, source_target_pairs={{0,576},{192,0},{384,192},{576,384},{1,577},{193,1},{385,193},{577... | collective-permute-start | bytes 8456 | tf_op jit(solution)/shard_map/ppermute | solution.py:20
  44.6 5.9 %collective-permute-start.5 = (f32[2,1,1,352]{3,2,1,0:T(1,128)S(1)}, f32[2,1,1,352]{3,2,1,0:T(1,128)S(1)}, u32[]{:S(2)}, u32[]{:S(2)}) collective-permute-start(f32[2,1,1,352]{3,2,1,0:T(1,128)S(1)} %pad_maximum_fusion.6), channel_id=1, source_target_pairs={{0,384},{192,576},{384,0},{576,192},{1,385},{193,577},{385,1},{577... | collective-permute-start | bytes 8456 | tf_op jit(solution)/shard_map/ppermute | solution.py:20
  46.5 6.9 %collective-permute-start.6 = (f32[2,1,1,352]{3,2,1,0:T(1,128)S(1)}, f32[2,1,1,352]{3,2,1,0:T(1,128)S(1)}, u32[]{:S(2)}, u32[]{:S(2)}) collective-permute-start(f32[2,1,1,352]{3,2,1,0:T(1,128)S(1)} %pad_maximum_fusion.6), channel_id=1, source_target_pairs={{0,192},{192,384},{384,576},{576,0},{1,193},{193,385},{385,577},{5... | collective-permute-start | bytes 8456 | tf_op jit(solution)/shard_map/ppermute | solution.py:20
  54.4 26.5 %all-to-all-start = ((bf16[12,64,352]{2,1,0:T(8,128)(2,1)}), bf16[12,64,352]{2,1,0:T(8,128)(2,1)}, u32[]{:S(2)}, u32[]{:S(2)}) async-start(bf16[12,64,352]{2,1,0:T(8,128)(2,1)} %broadcast_in_dim.8), calls=%async_computation | async-start | bytes 1179648 | tf_op jit(solution)/shard_map/all_to_all | solution.py:107
  90.3 45.3 %all-to-all-start.1 = ((bf16[64,64,66]{2,0,1:T(8,128)(2,1)}), bf16[64,64,66]{2,0,1:T(8,128)(2,1)}, u32[]{:S(2)}, u32[]{:S(2)}) async-start(bf16[64,64,66]{2,0,1:T(8,128)(2,1)} %copy.5), calls=%async_computation.1 | async-start | bytes 2097152 | tf_op jit(solution)/shard_map/all_to_all | solution.py:112
  141.2 4.6 %copy-start.1 = (f32[1,4096,352]{2,1,0:T(8,128)S(1)}, f32[1,4096,352]{2,1,0:T(8,128)}, u32[]{:S(2)}) copy-start(f32[1,4096,352]{2,1,0:T(8,128)} %all-gather.3.cloned.1.call-done) | copy-start | bytes 17301508
  147.7 9.5 %collective-permute-start.7 = (bf16[66,352]{1,0:T(8,128)(2,1)S(1)}, bf16[66,352]{1,0:T(8,128)(2,1)S(1)}, u32[]{:S(2)}, u32[]{:S(2)}) collective-permute-start(bf16[66,352]{1,0:T(8,128)(2,1)S(1)} %select_convert_fusion), channel_id=1, source_target_pairs={{0,576},{192,0},{384,192},{576,384},{1,577},{193,1},{385,193},{577... | collective-permute-start | bytes 139400 | tf_op jit(solution)/shard_map/ppermute | solution.py:20
  152.3 6.4 %collective-permute-start.8 = (bf16[66,352]{1,0:T(8,128)(2,1)S(1)}, bf16[66,352]{1,0:T(8,128)(2,1)S(1)}, u32[]{:S(2)}, u32[]{:S(2)}) collective-permute-start(bf16[66,352]{1,0:T(8,128)(2,1)S(1)} %select_convert_fusion), channel_id=1, source_target_pairs={{0,384},{192,576},{384,0},{576,192},{1,385},{193,577},{385,1},{577... | collective-permute-start | bytes 139400 | tf_op jit(solution)/shard_map/ppermute | solution.py:20
  154.6 6.9 %collective-permute-start.9 = (bf16[66,352]{1,0:T(8,128)(2,1)S(1)}, bf16[66,352]{1,0:T(8,128)(2,1)S(1)}, u32[]{:S(2)}, u32[]{:S(2)}) collective-permute-start(bf16[66,352]{1,0:T(8,128)(2,1)S(1)} %select_convert_fusion), channel_id=1, source_target_pairs={{0,192},{192,384},{384,576},{576,0},{1,193},{193,385},{385,577},{5... | collective-permute-start | bytes 139400 | tf_op jit(solution)/shard_map/ppermute | solution.py:20
  161.5 8.4 %collective-permute-start.10 = (bf16[4,66,352]{2,1,0:T(8,128)(2,1)S(1)}, bf16[4,66,352]{2,1,0:T(8,128)(2,1)S(1)}, u32[]{:S(2)}, u32[]{:S(2)}) collective-permute-start(bf16[4,66,352]{2,1,0:T(8,128)(2,1)S(1)} %pad_maximum_fusion.1), channel_id=1, source_target_pairs={{0,168},{24,0},{48,24},{72,48},{96,72},{120,96},{144,120},{168,144... | collective-permute-start | bytes 557576 | tf_op jit(solution)/shard_map/ppermute | solution.py:13
  163.4 8.5 %collective-permute-start.13 = (bf16[4,66,352]{2,1,0:T(8,128)(2,1)S(1)}, bf16[4,66,352]{2,1,0:T(8,128)(2,1)S(1)}, u32[]{:S(2)}, u32[]{:S(2)}) collective-permute-start(bf16[4,66,352]{2,1,0:T(8,128)(2,1)S(1)} %pad_maximum_fusion.1), channel_id=1, source_target_pairs={{0,24},{24,48},{48,72},{72,96},{96,120},{120,144},{144,168},{168,0... | collective-permute-start | bytes 557576 | tf_op jit(solution)/shard_map/ppermute | solution.py:13
  169.9 7.4 %collective-permute-start.11 = (bf16[4,66,352]{2,1,0:T(8,128)(2,1)S(1)}, bf16[4,66,352]{2,1,0:T(8,128)(2,1)S(1)}, u32[]{:S(2)}, u32[]{:S(2)}) collective-permute-start(bf16[4,66,352]{2,1,0:T(8,128)(2,1)S(1)} %collective-permute-done.10), channel_id=1, source_target_pairs={{0,168},{24,0},{48,24},{72,48},{96,72},{120,96},{144,120},{168,144... | collective-permute-start | bytes 557576 | tf_op jit(solution)/shard_map/ppermute | solution.py:13
  172.0 7.9 %collective-permute-start.14 = (bf16[4,66,352]{2,1,0:T(8,128)(2,1)S(1)}, bf16[4,66,352]{2,1,0:T(8,128)(2,1)S(1)}, u32[]{:S(2)}, u32[]{:S(2)}) collective-permute-start(bf16[4,66,352]{2,1,0:T(8,128)(2,1)S(1)} %collective-permute-done.13), channel_id=1, source_target_pairs={{0,24},{24,48},{48,72},{72,96},{96,120},{120,144},{144,168},{168,0... | collective-permute-start | bytes 557576 | tf_op jit(solution)/shard_map/ppermute | solution.py:13
  177.3 12.3 %collective-permute-start.12 = (bf16[4,66,352]{2,1,0:T(8,128)(2,1)S(1)}, bf16[4,66,352]{2,1,0:T(8,128)(2,1)S(1)}, u32[]{:S(2)}, u32[]{:S(2)}) collective-permute-start(bf16[4,66,352]{2,1,0:T(8,128)(2,1)S(1)} %collective-permute-done.11), channel_id=1, source_target_pairs={{0,168},{24,0},{48,24},{72,48},{96,72},{120,96},{144,120},{168,144... | collective-permute-start | bytes 557576 | tf_op jit(solution)/shard_map/ppermute | solution.py:13
  179.9 7.9 %collective-permute-start.15 = (bf16[4,66,352]{2,1,0:T(8,128)(2,1)S(1)}, bf16[4,66,352]{2,1,0:T(8,128)(2,1)S(1)}, u32[]{:S(2)}, u32[]{:S(2)}) collective-permute-start(bf16[4,66,352]{2,1,0:T(8,128)(2,1)S(1)} %collective-permute-done.14), channel_id=1, source_target_pairs={{0,24},{24,48},{48,72},{72,96},{96,120},{120,144},{144,168},{168,0... | collective-permute-start | bytes 557576 | tf_op jit(solution)/shard_map/ppermute | solution.py:13
  187.7 7.9 %collective-permute-start.16 = (bf16[4,66,352]{2,1,0:T(8,128)(2,1)S(1)}, bf16[4,66,352]{2,1,0:T(8,128)(2,1)S(1)}, u32[]{:S(2)}, u32[]{:S(2)}) collective-permute-start(bf16[4,66,352]{2,1,0:T(8,128)(2,1)S(1)} %collective-permute-done.15), channel_id=1, source_target_pairs={{0,24},{24,48},{48,72},{72,96},{96,120},{120,144},{144,168},{168,0... | collective-permute-start | bytes 557576 | tf_op jit(solution)/shard_map/ppermute | solution.py:13
  196.4 11.2 %collective-permute-start.17 = (bf16[8,4,66,352]{3,0,2,1:T(8,128)(2,1)S(1)}, bf16[8,4,66,352]{3,0,2,1:T(8,128)(2,1)S(1)}, u32[]{:S(2)}, u32[]{:S(2)}) collective-permute-start(bf16[8,4,66,352]{3,0,2,1:T(8,128)(2,1)S(1)} %copy.7), channel_id=1, source_target_pairs={{0,12},{12,0},{1,13},{13,1},{2,14},{14,2},{3,15},{15,3},{4,16},{16... | collective-permute-start | bytes 4460552 | tf_op jit(solution)/shard_map/ppermute | solution.py:13
Sparse Core Ops, SparseCore 0:
  11.5 99.9 all-gather.2

commit v16 on v13

--- a/solution.py
+++ b/solution.py
@@ -107,7 +107,9 @@
     stacked = lax.all_gather(second, "mp", axis=0)
     second_full = jnp.transpose(stacked, (1, 0, 2)).reshape(local, n_mp * rows)
     width = second_full.shape[1] // dp_count
-    columns = lax.all_to_all(second_full, DP, split_axis=1, concat_axis=0, tiled=True)
+    chips = lax.all_to_all(second_full, ("x", "y"), split_axis=1, concat_axis=0, tiled=True)
+    columns = lax.all_to_all(chips, "c", split_axis=1, concat_axis=0, tiled=True)
+    columns = jnp.transpose(columns.reshape(nc, nx * ny, local, width), (1, 0, 2, 3)).reshape(total, width)
     pc = (lax.iota(jnp.int32, nc)[:, None, None] + ic) % nc
     py = (lax.iota(jnp.int32, ny)[None, :, None] + iy) % ny
     px = (lax.iota(jnp.int32, nx)[None, None, :] + ix) % nx

time: 226 us -> 243 us (1.075)
  local copies, waits for them, and re-layouts: 23.3 us -> 42.6 us
  blocking collectives: 23.4 us -> 36.3 us
  starting transfers between devices: 79.7 us -> 71.5 us
  waiting for transfers between devices: 61.9 us -> 54.5 us
    all_to_all x0 -> x1, blocking collectives: none -> 12.9 us  [shards(): lax.all_to_all(chips, 'c', split_axis=1, concat_axis=0, tiled=True)]
    all_to_all x1, starting transfers between devices: 19.4 us -> 8.43 us  [shards(): lax.all_to_all(second_full, ('x', 'y'), split_axis=1, concat_axis=0, tile...]
    reshape x0 -> x2, local copies, waits for them, and re-layouts: none -> 7.17 us  [the longest x1 4.1 us: shards(): jnp.transpose(columns.reshape(nc, nx * ny, local, width), (1, 0, 2, 3))]
    all_to_all x1, waiting for transfers between devices: 22.9 us -> 16.6 us  [shards(): lax.all_to_all(second_full, ('x', 'y'), split_axis=1, concat_axis=0, tile...]
    all_to_all x3 -> x5, local copies, waits for them, and re-layouts: 9.21 us -> 13.9 us  [the longest x3 7.61 us: shards(): lax.all_to_all(chips, 'c', split_axis=1, concat_axis=0, tiled=True)]
    another operation x0 -> x1, local copies, waits for them, and re-layouts: none -> 4.04 us  [shards(): second_full.reshape(local, dp_count, width)]
    ppermute x8, starting transfers between devices: 26.2 us -> 29.7 us  [shift(): return lax.ppermute(v, axis, [(i, (i + step) % n) for i in range(n)])]
    transpose x0 -> x1, local copies, waits for them, and re-layouts: none -> 3.39 us  [shards(): jnp.transpose(columns.reshape(nc, nx * ny, local, width), (1, 0, 2, 3))]
  transfers between devices with their start and end apart: 20 -> 20, of which waited for: 14 -> 14; matrix products, arithmetic and copies ran while one was open for 6% -> 14% of each run, Pallas kernels for 0% -> 0%
where the time goes in v16:
time: 243 us; the launch traced here: 242 us
  starting transfers between devices  71.5 us (29%)
  waiting for transfers between devices  54.5 us (22%)
  local copies, waits for them, and re-layouts  42.6 us (18%)
  blocking collectives  36.3 us (15%)
  between operations  13.8 us (6%)
  other arithmetic  12.6 us (5%)
  matrix products  10.2 us (4%)
    ppermute x8, starting transfers between devices, shift(): return lax.ppermute(v, axis, [(i, (i + step) % n) for i in range(n)])  29.7 us
    all_gather x1, blocking collectives, shards(): stacked = lax.all_gather(second, 'mp', axis=0)  23.4 us
    ppermute x4, starting transfers between devices, combine(): other = lax.ppermute(jnp.stack([mean, m2]), axis, pairs)  18.2 us
    ppermute x8, waiting for transfers between devices, shift(): return lax.ppermute(v, axis, [(i, (i + step) % n) for i in range(n)])  17.5 us
    all_to_all x1, waiting for transfers between devices, shards(): lax.all_to_all(second_full, ('x', 'y'), split_axis=1, concat_axis=0, tile...  16.6 us
    ppermute x6, starting transfers between devices, direct_gather(): got[t] = lax.ppermute(v, axis, [(i, (i - t) % n) for i in range(n)])  15.2 us
    all_to_all x1, blocking collectives, shards(): lax.all_to_all(chips, 'c', split_axis=1, concat_axis=0, tiled=True)  12.9 us
    ppermute x4, waiting for transfers between devices, combine(): other = lax.ppermute(jnp.stack([mean, m2]), axis, pairs)  12.8 us
  transfers between devices with their start and end apart: 20, of which 14 were waited for; matrix products, arithmetic and copies ran while one was open for 14% of the time, Pallas kernels for 0%

profile of v16, /device:TPU:1, one launch (start us, length us, event | category | flops | bytes accessed | tf_op | source)
XLA Modules:
  0.0 241.6 jit_solution(5516761093978975306)
XLA Ops:
  6.5 1.8 copy-done
  8.4 2.3 fusion.3
  10.7 0.7 fusion.28
  11.4 12.4 %collective-permute-start = (f32[2,1,1,352]{3,2,1,0:T(1,128)S(1)}, f32[2,1,1,352]{3,2,1,0:T(1,128)S(1)}, u32[]{:S(2)}, u32[]{:S(2)}) collective-permute-start(f32[2,1,1,352]{3,2,1,0:T(1,128)S(1)} %pad_maximum_fusion.2), channel_id=1, source_target_pairs={{0,12},{12,0},{1,13},{13,1},{2,14},{14,2},{3,15},{15,3},{4,16},{16... | collective-permute-start | bytes 8456 | tf_op jit(solution)/shard_map/ppermute | solution.py:49
  23.9 0.8 collective-permute-done
  24.7 1.9 collective-permute-start.1
  26.6 2.4 collective-permute-done.1
  29.1 1.9 collective-permute-start.2
  31.0 3.3 %collective-permute-done.2 = f32[2,1,1,352]{3,2,1,0:T(1,128)S(1)} collective-permute-done((f32[2,1,1,352]{3,2,1,0:T(1,128)S(1)}, f32[2,1,1,352]{3,2,1,0:T(1,128)S(1)}, u32[]{:S(2)}, u32[]{:S(2)}) %collective-permute-start.2) | collective-permute-done | bytes 2848 | tf_op jit(solution)/shard_map/ppermute | solution.py:49
  34.3 1.9 collective-permute-start.3
  36.3 6.3 %collective-permute-done.3 = f32[2,1,1,352]{3,2,1,0:T(1,128)S(1)} collective-permute-done((f32[2,1,1,352]{3,2,1,0:T(1,128)S(1)}, f32[2,1,1,352]{3,2,1,0:T(1,128)S(1)}, u32[]{:S(2)}, u32[]{:S(2)}) %collective-permute-start.3) | collective-permute-done | bytes 2848 | tf_op jit(solution)/shard_map/ppermute | solution.py:49
  42.6 1.9 collective-permute-start.4
  44.6 1.9 collective-permute-start.5
  46.5 3.4 %collective-permute-start.6 = (f32[2,1,1,352]{3,2,1,0:T(1,128)S(1)}, f32[2,1,1,352]{3,2,1,0:T(1,128)S(1)}, u32[]{:S(2)}, u32[]{:S(2)}) collective-permute-start(f32[2,1,1,352]{3,2,1,0:T(1,128)S(1)} %pad_maximum_fusion.6), channel_id=1, source_target_pairs={{0,192},{192,384},{384,576},{576,0},{1,193},{193,385},{385,577},{5... | collective-permute-start | bytes 8456 | tf_op jit(solution)/shard_map/ppermute | solution.py:20
  49.9 0.6 collective-permute-done.5
  50.5 2.9 %collective-permute-done.6 = f32[2,1,1,352]{3,2,1,0:T(1,128)S(1)} collective-permute-done((f32[2,1,1,352]{3,2,1,0:T(1,128)S(1)}, f32[2,1,1,352]{3,2,1,0:T(1,128)S(1)}, u32[]{:S(2)}, u32[]{:S(2)}) %collective-permute-start.6) | collective-permute-done | bytes 2848 | tf_op jit(solution)/shard_map/ppermute | solution.py:20
  53.6 23.4 %all_gather.7 = bf16[12,64,352]{2,1,0:T(8,128)(2,1)S(1)} all-gather(bf16[1,64,352]{2,1,0:T(8,128)(2,1)S(1)} %divide_convert_fusion.4), channel_id=1, replica_groups=mesh['x'=4,'y'=8,'c'=2,'mp'=12] {'mp'}, dimensions={0}, use_global_device_ids=true | all-gather | bytes 585728 | tf_op jit(solution)/shard_map/all_gather | solution.py:107
  77.0 1.2 copy.12
  78.2 3.5 %all_to_all.24 = bf16[64,32,132]{2,1,0:T(8,128)(2,1)} reshape(bf16[64,12,352]{2,1,0:T(8,128)(2,1)} %copy.12) | data formatting | bytes 1081344 | tf_op jit(solution)/shard_map/all_to_all | solution.py:110
  81.7 2.8 %copy.13 = bf16[64,32,132]{2,0,1:T(8,128)(2,1)} copy(bf16[64,32,132]{2,1,0:T(8,128)(2,1)} %all_to_all.24) | data formatting | bytes 1081344 | tf_op jit(solution)/shard_map/all_to_all | solution.py:110
  84.5 8.4 %all-to-all-start = ((bf16[64,32,132]{2,0,1:T(8,128)(2,1)}), bf16[64,32,132]{2,0,1:T(8,128)(2,1)}, u32[]{:S(2)}, u32[]{:S(2)}) async-start(bf16[64,32,132]{2,0,1:T(8,128)(2,1)} %copy.13), calls=%async_computation | async-start | bytes 2097152 | tf_op jit(solution)/shard_map/all_to_all | solution.py:110
  93.0 0.1 add_multiply_fusion
  93.1 0.1 broadcast_multiply_fusion
  93.1 0.1 add.540
  93.3 4.0 %reshape_reshape.3 = bf16[64,64,66]{2,1,0:T(8,128)(2,1)} reshape(bf16[64,12,352]{2,1,0:T(8,128)(2,1)} %copy.12) | data formatting | bytes 1081344 | tf_op jit(solution)/shard_map/reshape;reshape | solution.py:119
  97.3 2.7 %fusion.5 = bf16[64,64,66]{2,1,0:T(8,128)(2,1)} fusion(bf16[64,64,66]{2,1,0:T(8,128)(2,1)} %reshape_reshape.3, s32[64]{0:T(128)S(1)} %add.540), kind=kOutput, calls=%fused_computation.13 | convolution fusion | flops 34877440 | bytes 1081600 | tf_op jit(solution)/shard_map/bkt,pk->bpt/dot_general | solution.py:118
  100.0 3.1 %reshape.613 = bf16[64,4224]{1,0:T(8,128)(2,1)} reshape(bf16[64,64,66]{2,1,0:T(8,128)(2,1)} %fusion.5) | data formatting | bytes 1081344 | tf_op jit(solution)/shard_map/reshape | solution.py:120
  103.1 16.6 %all-to-all-done = bf16[64,32,132]{2,0,1:T(8,128)(2,1)} async-done(((bf16[64,32,132]{2,0,1:T(8,128)(2,1)}), bf16[64,32,132]{2,0,1:T(8,128)(2,1)}, u32[]{:S(2)}, u32[]{:S(2)}) %all-to-all-start) | async-done | bytes 540704 | tf_op jit(solution)/shard_map/all_to_all | solution.py:110
  119.7 2.5 %reshape.627 = bf16[2048,2,66]{2,1,0:T(2,128)(2,1)} reshape(bf16[32,64,132]{2,1,0:T(8,128)(2,1)} %bitcast.6) | data formatting | bytes 1081344 | tf_op jit(solution)/shard_map/all_to_all | solution.py:111
  122.2 3.8 %copy.20 = bf16[2048,2,66]{0,2,1:T(8,128)(2,1)} copy(bf16[2048,2,66]{2,1,0:T(2,128)(2,1)} %reshape.627) | data formatting | bytes 1081344 | tf_op jit(solution)/shard_map/all_to_all | solution.py:111
  125.9 12.9 %all_to_all.32 = bf16[2048,2,66]{0,2,1:T(8,128)(2,1)S(1)} all-to-all(bf16[2048,2,66]{0,2,1:T(8,128)(2,1)} %copy.20), channel_id=1, replica_groups=mesh['x'=4,'y'=8,'c'=2,'mp'=12] {'c'}, dimensions={1} | all-to-all | bytes 1081344 | tf_op jit(solution)/shard_map/all_to_all | solution.py:111
  138.8 1.3 copy.15
  140.1 3.1 %reshape.611 = bf16[2,32,64,66]{2,1,0,3:T(8,128)(2,1)} reshape(bf16[2,2048,66]{1,0,2:T(2,128)(2,1)} %copy.15) | data formatting | bytes 1081344 | tf_op jit(solution)/shard_map/reshape | solution.py:112
  143.2 3.4 %copy.16 = bf16[32,2,64,66]{2,1,0,3:T(2,128)(2,1)} copy(bf16[32,2,64,66]{2,0,1,3:T(8,128)(2,1)} %bitcast.78) | data formatting | bytes 1081344 | tf_op jit(solution)/shard_map/transpose | solution.py:112
  146.6 4.1 %reshape.612 = bf16[4096,66]{0,1:T(8,128)(2,1)} reshape(bf16[32,2,64,66]{2,1,0,3:T(2,128)(2,1)} %copy.16) | data formatting | bytes 1081344 | tf_op jit(solution)/shard_map/reshape | solution.py:112
  150.7 3.4 %reduce_sum.56 = f32[352]{0:T(512)S(1)} reduce(f32[1,4096,352]{2,1,0:T(8,128)} %all-gather.3.cloned.1.call-done, f32[]{:T(128)} %constant.121.clone.1), dimensions={0,1}, to_apply=%region_2.0 | reduce | flops 1441440 | bytes 5768580 | tf_op jit(solution)/shard_map/reduce_sum | solution.py:98
  154.1 3.7 %multiply_reduce_fusion = f32[352]{0:T(512)S(1)} fusion(f32[1,4096,352]{2,1,0:T(8,128)} %all-gather.3.cloned.1.call-done, f32[352]{0:T(512)S(1)} %broadcast_multiply_fusion.1), kind=kLoop, calls=%fused_computation.6 | loop fusion | flops 4325024 | bytes 5769984 | tf_op jit(solution)/shard_map/reduce_sum | solution.py:100
  157.8 0.9 copy-done.1
  158.7 1.9 select_convert_fusion
  160.6 3.3 %collective-permute-start.7 = (bf16[66,352]{1,0:T(8,128)(2,1)S(1)}, bf16[66,352]{1,0:T(8,128)(2,1)S(1)}, u32[]{:S(2)}, u32[]{:S(2)}) collective-permute-start(bf16[66,352]{1,0:T(8,128)(2,1)S(1)} %select_convert_fusion), channel_id=1, source_target_pairs={{0,576},{192,0},{384,192},{576,384},{1,577},{193,1},{385,193},{577... | collective-permute-start | bytes 139400 | tf_op jit(solution)/shard_map/ppermute | solution.py:20
  163.9 2.8 %collective-permute-start.8 = (bf16[66,352]{1,0:T(8,128)(2,1)S(1)}, bf16[66,352]{1,0:T(8,128)(2,1)S(1)}, u32[]{:S(2)}, u32[]{:S(2)}) collective-permute-start(bf16[66,352]{1,0:T(8,128)(2,1)S(1)} %select_convert_fusion), channel_id=1, source_target_pairs={{0,384},{192,576},{384,0},{576,192},{1,385},{193,577},{385,1},{577... | collective-permute-start | bytes 139400 | tf_op jit(solution)/shard_map/ppermute | solution.py:20
  166.6 2.0 collective-permute-start.9
  168.6 1.7 collective-permute-done.8
  170.3 2.5 %collective-permute-done.9 = bf16[66,352]{1,0:T(8,128)(2,1)S(1)} collective-permute-done((bf16[66,352]{1,0:T(8,128)(2,1)S(1)}, bf16[66,352]{1,0:T(8,128)(2,1)S(1)}, u32[]{:S(2)}, u32[]{:S(2)}) %collective-permute-start.9) | collective-permute-done | bytes 46496 | tf_op jit(solution)/shard_map/ppermute | solution.py:20
  172.8 4.1 %collective-permute-start.10 = (bf16[4,66,352]{2,1,0:T(8,128)(2,1)S(1)}, bf16[4,66,352]{2,1,0:T(8,128)(2,1)S(1)}, u32[]{:S(2)}, u32[]{:S(2)}) collective-permute-start(bf16[4,66,352]{2,1,0:T(8,128)(2,1)S(1)} %pad_maximum_fusion.1), channel_id=1, source_target_pairs={{0,168},{24,0},{48,24},{72,48},{96,72},{120,96},{144,120},{168,144... | collective-permute-start | bytes 557576 | tf_op jit(solution)/shard_map/ppermute | solution.py:13
  176.9 2.0 collective-permute-start.13
  178.9 1.7 collective-permute-done.10
  180.7 4.1 %collective-permute-start.11 = (bf16[4,66,352]{2,1,0:T(8,128)(2,1)S(1)}, bf16[4,66,352]{2,1,0:T(8,128)(2,1)S(1)}, u32[]{:S(2)}, u32[]{:S(2)}) collective-permute-start(bf16[4,66,352]{2,1,0:T(8,128)(2,1)S(1)} %collective-permute-done.10), channel_id=1, source_target_pairs={{0,168},{24,0},{48,24},{72,48},{96,72},{120,96},{144,120},{168,144... | collective-permute-start | bytes 557576 | tf_op jit(solution)/shard_map/ppermute | solution.py:13
  184.8 1.9 collective-permute-start.14
  186.7 0.9 collective-permute-done.11
  187.6 5.0 %collective-permute-start.12 = (bf16[4,66,352]{2,1,0:T(8,128)(2,1)S(1)}, bf16[4,66,352]{2,1,0:T(8,128)(2,1)S(1)}, u32[]{:S(2)}, u32[]{:S(2)}) collective-permute-start(bf16[4,66,352]{2,1,0:T(8,128)(2,1)S(1)} %collective-permute-done.11), channel_id=1, source_target_pairs={{0,168},{24,0},{48,24},{72,48},{96,72},{120,96},{144,120},{168,144... | collective-permute-start | bytes 557576 | tf_op jit(solution)/shard_map/ppermute | solution.py:13
  192.7 1.9 collective-permute-start.15
  194.6 5.9 %collective-permute-done.15 = bf16[4,66,352]{2,1,0:T(8,128)(2,1)S(1)} collective-permute-done((bf16[4,66,352]{2,1,0:T(8,128)(2,1)S(1)}, bf16[4,66,352]{2,1,0:T(8,128)(2,1)S(1)}, u32[]{:S(2)}, u32[]{:S(2)}) %collective-permute-start.15) | collective-permute-done | bytes 185888 | tf_op jit(solution)/shard_map/ppermute | solution.py:13
  200.5 1.9 collective-permute-start.16
  202.5 5.9 %collective-permute-done.16 = bf16[4,66,352]{2,1,0:T(8,128)(2,1)S(1)} collective-permute-done((bf16[4,66,352]{2,1,0:T(8,128)(2,1)S(1)}, bf16[4,66,352]{2,1,0:T(8,128)(2,1)S(1)}, u32[]{:S(2)}, u32[]{:S(2)}) %collective-permute-start.16) | collective-permute-done | bytes 185888 | tf_op jit(solution)/shard_map/ppermute | solution.py:13
  208.6 0.6 copy.18
  209.2 8.8 %collective-permute-start.17 = (bf16[8,4,66,352]{3,0,2,1:T(8,128)(2,1)S(1)}, bf16[8,4,66,352]{3,0,2,1:T(8,128)(2,1)S(1)}, u32[]{:S(2)}, u32[]{:S(2)}) collective-permute-start(bf16[8,4,66,352]{3,0,2,1:T(8,128)(2,1)S(1)} %copy.18), channel_id=1, source_target_pairs={{0,12},{12,0},{1,13},{13,1},{2,14},{14,2},{3,15},{15,3},{4,16},{16... | collective-permute-start | bytes 4460552 | tf_op jit(solution)/shard_map/ppermute | solution.py:13
  218.0 0.1 iota_add_fusion
  218.1 3.0 %collective-permute-done.17 = bf16[8,4,66,352]{3,0,2,1:T(8,128)(2,1)S(1)} collective-permute-done((bf16[8,4,66,352]{3,0,2,1:T(8,128)(2,1)S(1)}, bf16[8,4,66,352]{3,0,2,1:T(8,128)(2,1)S(1)}, u32[]{:S(2)}, u32[]{:S(2)}) %collective-permute-start.17) | collective-permute-done | bytes 1486880 | tf_op jit(solution)/shard_map/ppermute | solution.py:13
  221.1 0.2 copy.22
  221.3 2.5 %pad_maximum_fusion = bf16[2,8,4,66,352]{4,3,2,1,0:T(8,128)(2,1)} fusion(bf16[1,8,4,66,352]{4,3,2,1,0:T(8,128)(2,1)S(1)} %bitcast.76, bf16[1,8,4,66,352]{4,3,2,1,0:T(8,128)(2,1)S(1)} %bitcast.74), kind=kLoop, calls=%fused_computation.7 | loop fusion | flops 1486848 | bytes 5947392 | tf_op jit(solution)/shard_map/stack | solution.py:39
  223.8 1.8 fusion
  225.6 5.8 %reshape.614 = bf16[4224,352]{1,0:T(8,128)(2,1)} reshape(bf16[2,8,4,66,352]{4,3,2,1,0:T(8,128)(2,1)} %pad_maximum_fusion) | data formatting | bytes 5947392 | tf_op jit(solution)/shard_map/reshape | solution.py:131
  231.4 3.3 %fusion.7 = bf16[64,352]{1,0:T(8,128)(2,1)} fusion(bf16[64,4224]{1,0:T(8,128)(2,1)} %reshape.613, bf16[4224,352]{1,0:T(8,128)(2,1)} %reshape.614, f32[352]{0:T(512)S(1)} %get-tuple-element.25, f32[352]{0:T(512)S(1)} %multiply_add_fusion, f32[352]{0:T(512)S(1)} %get-tuple-element.26, f32[352]{0:T(512)S(1)} %broadcast_multiply_fusion.1, ...), kind=kOutput, calls=%fused_computation.16 | convolution fusion | flops 190496768 | bytes 3655168 | tf_op jit(solution)/shard_map/dot_general | solution.py:146
  (50 shorter events, 0.7 us)
Async XLA Ops:
  6.5 1.8 copy-start
  6.5 144.2 %all-gather.3.cloned.1.call-start = ((), (), s32[]{:S(2)}) async-start(), calls=%async_computation.2 | async-start | bytes 6389760 | tf_op jit(solution)/shard_map/all_gather | solution.py:97
  11.4 13.2 %collective-permute-start = (f32[2,1,1,352]{3,2,1,0:T(1,128)S(1)}, f32[2,1,1,352]{3,2,1,0:T(1,128)S(1)}, u32[]{:S(2)}, u32[]{:S(2)}) collective-permute-start(f32[2,1,1,352]{3,2,1,0:T(1,128)S(1)} %pad_maximum_fusion.2), channel_id=1, source_target_pairs={{0,12},{12,0},{1,13},{13,1},{2,14},{14,2},{3,15},{15,3},{4,16},{16... | collective-permute-start | bytes 8456 | tf_op jit(solution)/shard_map/ppermute | solution.py:49
  24.7 4.3 %collective-permute-start.1 = (f32[2,1,1,352]{3,2,1,0:T(1,128)S(1)}, f32[2,1,1,352]{3,2,1,0:T(1,128)S(1)}, u32[]{:S(2)}, u32[]{:S(2)}) collective-permute-start(f32[2,1,1,352]{3,2,1,0:T(1,128)S(1)} %pad_maximum_fusion.3), channel_id=1, source_target_pairs={{0,24},{24,0},{48,72},{72,48},{96,120},{120,96},{144,168},{168,144... | collective-permute-start | bytes 8456 | tf_op jit(solution)/shard_map/ppermute | solution.py:49
  29.1 5.2 %collective-permute-start.2 = (f32[2,1,1,352]{3,2,1,0:T(1,128)S(1)}, f32[2,1,1,352]{3,2,1,0:T(1,128)S(1)}, u32[]{:S(2)}, u32[]{:S(2)}) collective-permute-start(f32[2,1,1,352]{3,2,1,0:T(1,128)S(1)} %pad_maximum_fusion.4), channel_id=1, source_target_pairs={{0,48},{24,72},{48,0},{72,24},{96,144},{120,168},{144,96},{168,120... | collective-permute-start | bytes 8456 | tf_op jit(solution)/shard_map/ppermute | solution.py:49
  34.3 8.3 %collective-permute-start.3 = (f32[2,1,1,352]{3,2,1,0:T(1,128)S(1)}, f32[2,1,1,352]{3,2,1,0:T(1,128)S(1)}, u32[]{:S(2)}, u32[]{:S(2)}) collective-permute-start(f32[2,1,1,352]{3,2,1,0:T(1,128)S(1)} %pad_maximum_fusion.5), channel_id=1, source_target_pairs={{0,96},{24,120},{48,144},{72,168},{96,0},{120,24},{144,48},{168,72... | collective-permute-start | bytes 8456 | tf_op jit(solution)/shard_map/ppermute | solution.py:49
  42.6 7.2 %collective-permute-start.4 = (f32[2,1,1,352]{3,2,1,0:T(1,128)S(1)}, f32[2,1,1,352]{3,2,1,0:T(1,128)S(1)}, u32[]{:S(2)}, u32[]{:S(2)}) collective-permute-start(f32[2,1,1,352]{3,2,1,0:T(1,128)S(1)} %pad_maximum_fusion.6), channel_id=1, source_target_pairs={{0,576},{192,0},{384,192},{576,384},{1,577},{193,1},{385,193},{577... | collective-permute-start | bytes 8456 | tf_op jit(solution)/shard_map/ppermute | solution.py:20
  44.6 5.9 %collective-permute-start.5 = (f32[2,1,1,352]{3,2,1,0:T(1,128)S(1)}, f32[2,1,1,352]{3,2,1,0:T(1,128)S(1)}, u32[]{:S(2)}, u32[]{:S(2)}) collective-permute-start(f32[2,1,1,352]{3,2,1,0:T(1,128)S(1)} %pad_maximum_fusion.6), channel_id=1, source_target_pairs={{0,384},{192,576},{384,0},{576,192},{1,385},{193,577},{385,1},{577... | collective-permute-start | bytes 8456 | tf_op jit(solution)/shard_map/ppermute | solution.py:20
  46.5 6.9 %collective-permute-start.6 = (f32[2,1,1,352]{3,2,1,0:T(1,128)S(1)}, f32[2,1,1,352]{3,2,1,0:T(1,128)S(1)}, u32[]{:S(2)}, u32[]{:S(2)}) collective-permute-start(f32[2,1,1,352]{3,2,1,0:T(1,128)S(1)} %pad_maximum_fusion.6), channel_id=1, source_target_pairs={{0,192},{192,384},{384,576},{576,0},{1,193},{193,385},{385,577},{5... | collective-permute-start | bytes 8456 | tf_op jit(solution)/shard_map/ppermute | solution.py:20
  84.5 35.2 %all-to-all-start = ((bf16[64,32,132]{2,0,1:T(8,128)(2,1)}), bf16[64,32,132]{2,0,1:T(8,128)(2,1)}, u32[]{:S(2)}, u32[]{:S(2)}) async-start(bf16[64,32,132]{2,0,1:T(8,128)(2,1)} %copy.13), calls=%async_computation | async-start | bytes 2097152 | tf_op jit(solution)/shard_map/all_to_all | solution.py:110
  154.1 4.6 %copy-start.1 = (f32[1,4096,352]{2,1,0:T(8,128)S(1)}, f32[1,4096,352]{2,1,0:T(8,128)}, u32[]{:S(2)}) copy-start(f32[1,4096,352]{2,1,0:T(8,128)} %all-gather.3.cloned.1.call-done) | copy-start | bytes 17301508
  160.6 8.0 %collective-permute-start.7 = (bf16[66,352]{1,0:T(8,128)(2,1)S(1)}, bf16[66,352]{1,0:T(8,128)(2,1)S(1)}, u32[]{:S(2)}, u32[]{:S(2)}) collective-permute-start(bf16[66,352]{1,0:T(8,128)(2,1)S(1)} %select_convert_fusion), channel_id=1, source_target_pairs={{0,576},{192,0},{384,192},{576,384},{1,577},{193,1},{385,193},{577... | collective-permute-start | bytes 139400 | tf_op jit(solution)/shard_map/ppermute | solution.py:20
  163.9 6.4 %collective-permute-start.8 = (bf16[66,352]{1,0:T(8,128)(2,1)S(1)}, bf16[66,352]{1,0:T(8,128)(2,1)S(1)}, u32[]{:S(2)}, u32[]{:S(2)}) collective-permute-start(bf16[66,352]{1,0:T(8,128)(2,1)S(1)} %select_convert_fusion), channel_id=1, source_target_pairs={{0,384},{192,576},{384,0},{576,192},{1,385},{193,577},{385,1},{577... | collective-permute-start | bytes 139400 | tf_op jit(solution)/shard_map/ppermute | solution.py:20
  166.6 6.1 %collective-permute-start.9 = (bf16[66,352]{1,0:T(8,128)(2,1)S(1)}, bf16[66,352]{1,0:T(8,128)(2,1)S(1)}, u32[]{:S(2)}, u32[]{:S(2)}) collective-permute-start(bf16[66,352]{1,0:T(8,128)(2,1)S(1)} %select_convert_fusion), channel_id=1, source_target_pairs={{0,192},{192,384},{384,576},{576,0},{1,193},{193,385},{385,577},{5... | collective-permute-start | bytes 139400 | tf_op jit(solution)/shard_map/ppermute | solution.py:20
  172.8 7.9 %collective-permute-start.10 = (bf16[4,66,352]{2,1,0:T(8,128)(2,1)S(1)}, bf16[4,66,352]{2,1,0:T(8,128)(2,1)S(1)}, u32[]{:S(2)}, u32[]{:S(2)}) collective-permute-start(bf16[4,66,352]{2,1,0:T(8,128)(2,1)S(1)} %pad_maximum_fusion.1), channel_id=1, source_target_pairs={{0,168},{24,0},{48,24},{72,48},{96,72},{120,96},{144,120},{168,144... | collective-permute-start | bytes 557576 | tf_op jit(solution)/shard_map/ppermute | solution.py:13
  176.9 7.9 %collective-permute-start.13 = (bf16[4,66,352]{2,1,0:T(8,128)(2,1)S(1)}, bf16[4,66,352]{2,1,0:T(8,128)(2,1)S(1)}, u32[]{:S(2)}, u32[]{:S(2)}) collective-permute-start(bf16[4,66,352]{2,1,0:T(8,128)(2,1)S(1)} %pad_maximum_fusion.1), channel_id=1, source_target_pairs={{0,24},{24,48},{48,72},{72,96},{96,120},{120,144},{144,168},{168,0... | collective-permute-start | bytes 557576 | tf_op jit(solution)/shard_map/ppermute | solution.py:13
  180.7 7.0 %collective-permute-start.11 = (bf16[4,66,352]{2,1,0:T(8,128)(2,1)S(1)}, bf16[4,66,352]{2,1,0:T(8,128)(2,1)S(1)}, u32[]{:S(2)}, u32[]{:S(2)}) collective-permute-start(bf16[4,66,352]{2,1,0:T(8,128)(2,1)S(1)} %collective-permute-done.10), channel_id=1, source_target_pairs={{0,168},{24,0},{48,24},{72,48},{96,72},{120,96},{144,120},{168,144... | collective-permute-start | bytes 557576 | tf_op jit(solution)/shard_map/ppermute | solution.py:13
  184.8 7.9 %collective-permute-start.14 = (bf16[4,66,352]{2,1,0:T(8,128)(2,1)S(1)}, bf16[4,66,352]{2,1,0:T(8,128)(2,1)S(1)}, u32[]{:S(2)}, u32[]{:S(2)}) collective-permute-start(bf16[4,66,352]{2,1,0:T(8,128)(2,1)S(1)} %collective-permute-done.13), channel_id=1, source_target_pairs={{0,24},{24,48},{48,72},{72,96},{96,120},{120,144},{144,168},{168,0... | collective-permute-start | bytes 557576 | tf_op jit(solution)/shard_map/ppermute | solution.py:13
  187.6 14.8 %collective-permute-start.12 = (bf16[4,66,352]{2,1,0:T(8,128)(2,1)S(1)}, bf16[4,66,352]{2,1,0:T(8,128)(2,1)S(1)}, u32[]{:S(2)}, u32[]{:S(2)}) collective-permute-start(bf16[4,66,352]{2,1,0:T(8,128)(2,1)S(1)} %collective-permute-done.11), channel_id=1, source_target_pairs={{0,168},{24,0},{48,24},{72,48},{96,72},{120,96},{144,120},{168,144... | collective-permute-start | bytes 557576 | tf_op jit(solution)/shard_map/ppermute | solution.py:13
  192.7 7.9 %collective-permute-start.15 = (bf16[4,66,352]{2,1,0:T(8,128)(2,1)S(1)}, bf16[4,66,352]{2,1,0:T(8,128)(2,1)S(1)}, u32[]{:S(2)}, u32[]{:S(2)}) collective-permute-start(bf16[4,66,352]{2,1,0:T(8,128)(2,1)S(1)} %collective-permute-done.14), channel_id=1, source_target_pairs={{0,24},{24,48},{48,72},{72,96},{96,120},{120,144},{144,168},{168,0... | collective-permute-start | bytes 557576 | tf_op jit(solution)/shard_map/ppermute | solution.py:13
  200.5 7.9 %collective-permute-start.16 = (bf16[4,66,352]{2,1,0:T(8,128)(2,1)S(1)}, bf16[4,66,352]{2,1,0:T(8,128)(2,1)S(1)}, u32[]{:S(2)}, u32[]{:S(2)}) collective-permute-start(bf16[4,66,352]{2,1,0:T(8,128)(2,1)S(1)} %collective-permute-done.15), channel_id=1, source_target_pairs={{0,24},{24,48},{48,72},{72,96},{96,120},{120,144},{144,168},{168,0... | collective-permute-start | bytes 557576 | tf_op jit(solution)/shard_map/ppermute | solution.py:13
  209.2 11.9 %collective-permute-start.17 = (bf16[8,4,66,352]{3,0,2,1:T(8,128)(2,1)S(1)}, bf16[8,4,66,352]{3,0,2,1:T(8,128)(2,1)S(1)}, u32[]{:S(2)}, u32[]{:S(2)}) collective-permute-start(bf16[8,4,66,352]{3,0,2,1:T(8,128)(2,1)S(1)} %copy.18), channel_id=1, source_target_pairs={{0,12},{12,0},{1,13},{13,1},{2,14},{14,2},{3,15},{15,3},{4,16},{16... | collective-permute-start | bytes 4460552 | tf_op jit(solution)/shard_map/ppermute | solution.py:13
Sparse Core Ops, SparseCore 0:
  11.5 107.8 all-gather.2

commit v17 on v16

--- a/solution.py
+++ b/solution.py
@@ -108,8 +108,6 @@
     second_full = jnp.transpose(stacked, (1, 0, 2)).reshape(local, n_mp * rows)
     width = second_full.shape[1] // dp_count
     chips = lax.all_to_all(second_full, ("x", "y"), split_axis=1, concat_axis=0, tiled=True)
-    columns = lax.all_to_all(chips, "c", split_axis=1, concat_axis=0, tiled=True)
-    columns = jnp.transpose(columns.reshape(nc, nx * ny, local, width), (1, 0, 2, 3)).reshape(total, width)
     pc = (lax.iota(jnp.int32, nc)[:, None, None] + ic) % nc
     py = (lax.iota(jnp.int32, ny)[None, :, None] + iy) % ny
     px = (lax.iota(jnp.int32, nx)[None, None, :] + ix) % nx
@@ -118,11 +116,14 @@
     second_perm = jnp.einsum(
         "bkt,pk->bpt", second_full.reshape(local, dp_count, width), pick, preferred_element_type=jnp.float32
     ).astype(jnp.bfloat16).reshape(local, dp_count * width)
-    columns, second_perm = lax.optimization_barrier((columns, second_perm))
-    corr = (
-        jnp.einsum("bi,bj->ij", first_all, columns, preferred_element_type=jnp.float32)
-        / total
+    chips, second_perm = lax.optimization_barrier((chips, second_perm))
+    first_c = lax.dynamic_index_in_dim(first_all.reshape(nx * ny, nc, local, rows), ic, axis=1, keepdims=False)
+    part = jnp.einsum(
+        "bi,bj->ij", first_c.reshape(total // nc, rows), chips, preferred_element_type=jnp.float32
     )
+    mine = lax.dynamic_slice_in_dim(part, ic * width, width, axis=1)
+    theirs = lax.dynamic_slice_in_dim(part, (1 - ic) * width, width, axis=1)
+    corr = (mine + shift(theirs, "c", nc, 1)) / total
     row_ids = mp_index * rows + lax.iota(jnp.int32, rows)[:, None]
     col_ids = dp_index * width + lax.iota(jnp.int32, width)[None, :]
     grad_block = jnp.where(row_ids == col_ids, 2.0 * (corr - 1.0), 2.0 * off_weight * corr).astype(

time: 243 us -> 225 us (0.926)
  local copies, waits for them, and re-layouts: 42.6 us -> 27.6 us
  blocking collectives: 36.3 us -> 24.6 us
  starting transfers between devices: 71.5 us -> 79.3 us
    all_to_all x1 -> x0, blocking collectives: 12.9 us -> none  [shards(): lax.all_to_all(chips, 'c', split_axis=1, concat_axis=0, tiled=True)]
    ppermute x8 -> x9, starting transfers between devices: 29.7 us -> 37.4 us  [shift(): return lax.ppermute(v, axis, [(i, (i + step) % n) for i in range(n)])]
    all_to_all x3 -> x0, local copies, waits for them, and re-layouts: 7.61 us -> none  [shards(): lax.all_to_all(chips, 'c', split_axis=1, concat_axis=0, tiled=True)]
    reshape x2 -> x0, local copies, waits for them, and re-layouts: 7.17 us -> none  [the longest x1 4.1 us: shards(): jnp.transpose(columns.reshape(nc, nx * ny, local, width), (1, 0, 2, 3))]
    transpose x1 -> x0, local copies, waits for them, and re-layouts: 3.39 us -> none  [shards(): jnp.transpose(columns.reshape(nc, nx * ny, local, width), (1, 0, 2, 3))]
    all_to_all x2 -> x3, local copies, waits for them, and re-layouts: 6.28 us -> 8.39 us  [shards(): lax.all_to_all(second_full, ('x', 'y'), split_axis=1, concat_axis=0, tile...]
    ppermute x8 -> x9, waiting for transfers between devices: 17.5 us -> 18.3 us  [shift(): return lax.ppermute(v, axis, [(i, (i + step) % n) for i in range(n)])]
  transfers between devices with their start and end apart: 20 -> 21, of which waited for: 14 -> 14; matrix products, arithmetic and copies ran while one was open for 14% -> 7% of each run, Pallas kernels for 0% -> 0%
where the time goes in v17:
time: 225 us; the launch traced here: 223 us
  starting transfers between devices  79.3 us (35%)
  waiting for transfers between devices  55.9 us (25%)
  local copies, waits for them, and re-layouts  27.6 us (12%)
  blocking collectives  24.6 us (11%)
  between operations  13.9 us (6%)
  other arithmetic  13.3 us (6%)
  matrix products  8.77 us (4%)
    ppermute x9, starting transfers between devices, shift(): return lax.ppermute(v, axis, [(i, (i + step) % n) for i in range(n)])  37.4 us
    all_gather x1, blocking collectives, shards(): stacked = lax.all_gather(second, 'mp', axis=0)  24.6 us
    ppermute x9, waiting for transfers between devices, shift(): return lax.ppermute(v, axis, [(i, (i + step) % n) for i in range(n)])  18.3 us
    ppermute x4, starting transfers between devices, combine(): other = lax.ppermute(jnp.stack([mean, m2]), axis, pairs)  18.2 us
    all_to_all x1, waiting for transfers between devices, shards(): lax.all_to_all(second_full, ('x', 'y'), split_axis=1, concat_axis=0, tile...  17.6 us
    ppermute x6, starting transfers between devices, direct_gather(): got[t] = lax.ppermute(v, axis, [(i, (i - t) % n) for i in range(n)])  16.4 us
    ppermute x4, waiting for transfers between devices, combine(): other = lax.ppermute(jnp.stack([mean, m2]), axis, pairs)  12.8 us
    all_to_all x3, local copies, waits for them, and re-layouts, shards(): lax.all_to_all(second_full, ('x', 'y'), split_axis=1, concat_axis=0, tile...  8.39 us
  transfers between devices with their start and end apart: 21, of which 14 were waited for; matrix products, arithmetic and copies ran while one was open for 7% of the time, Pallas kernels for 0%

profile of v17, /device:TPU:1, one launch (start us, length us, event | category | flops | bytes accessed | tf_op | source)
XLA Modules:
  0.0 223.3 jit_solution(14583438786671508397)
XLA Ops:
  6.5 1.8 copy-done
  8.4 2.3 %fusion.2 = f32[2,64,352]{2,1,0:T(8,128)S(1)} fusion(bf16[2,64,4224]{2,1,0:T(8,128)(2,1)} %param.2, bf16[4224,352]{0,1:T(8,128)(2,1)S(1)} %copy-done), kind=kOutput, calls=%fused_computation.8 | convolution fusion | flops 380633088 | bytes 4235264 | tf_op jit(solution)/shard_map/vbh,hc->vbc/dot_general | solution.py:96
  10.7 0.7 fusion.27
  11.4 12.4 %collective-permute-start = (f32[2,1,1,352]{3,2,1,0:T(1,128)S(1)}, f32[2,1,1,352]{3,2,1,0:T(1,128)S(1)}, u32[]{:S(2)}, u32[]{:S(2)}) collective-permute-start(f32[2,1,1,352]{3,2,1,0:T(1,128)S(1)} %pad_maximum_fusion.2), channel_id=1, source_target_pairs={{0,12},{12,0},{1,13},{13,1},{2,14},{14,2},{3,15},{15,3},{4,16},{16... | collective-permute-start | bytes 8456 | tf_op jit(solution)/shard_map/ppermute | solution.py:49
  23.9 0.8 collective-permute-done
  24.7 1.9 collective-permute-start.1
  26.6 2.4 %collective-permute-done.1 = f32[2,1,1,352]{3,2,1,0:T(1,128)S(1)} collective-permute-done((f32[2,1,1,352]{3,2,1,0:T(1,128)S(1)}, f32[2,1,1,352]{3,2,1,0:T(1,128)S(1)}, u32[]{:S(2)}, u32[]{:S(2)}) %collective-permute-start.1) | collective-permute-done | bytes 2848 | tf_op jit(solution)/shard_map/ppermute | solution.py:49
  29.1 1.9 collective-permute-start.2
  31.0 3.3 %collective-permute-done.2 = f32[2,1,1,352]{3,2,1,0:T(1,128)S(1)} collective-permute-done((f32[2,1,1,352]{3,2,1,0:T(1,128)S(1)}, f32[2,1,1,352]{3,2,1,0:T(1,128)S(1)}, u32[]{:S(2)}, u32[]{:S(2)}) %collective-permute-start.2) | collective-permute-done | bytes 2848 | tf_op jit(solution)/shard_map/ppermute | solution.py:49
  34.3 1.9 collective-permute-start.3
  36.3 6.3 %collective-permute-done.3 = f32[2,1,1,352]{3,2,1,0:T(1,128)S(1)} collective-permute-done((f32[2,1,1,352]{3,2,1,0:T(1,128)S(1)}, f32[2,1,1,352]{3,2,1,0:T(1,128)S(1)}, u32[]{:S(2)}, u32[]{:S(2)}) %collective-permute-start.3) | collective-permute-done | bytes 2848 | tf_op jit(solution)/shard_map/ppermute | solution.py:49
  42.6 1.9 collective-permute-start.5
  44.6 1.9 collective-permute-start.4
  46.5 3.4 %collective-permute-start.6 = (f32[2,1,1,352]{3,2,1,0:T(1,128)S(1)}, f32[2,1,1,352]{3,2,1,0:T(1,128)S(1)}, u32[]{:S(2)}, u32[]{:S(2)}) collective-permute-start(f32[2,1,1,352]{3,2,1,0:T(1,128)S(1)} %pad_maximum_fusion.6), channel_id=1, source_target_pairs={{0,192},{192,384},{384,576},{576,0},{1,193},{193,385},{385,577},{5... | collective-permute-start | bytes 8456 | tf_op jit(solution)/shard_map/ppermute | solution.py:20
  49.9 3.0 %collective-permute-done.6 = f32[2,1,1,352]{3,2,1,0:T(1,128)S(1)} collective-permute-done((f32[2,1,1,352]{3,2,1,0:T(1,128)S(1)}, f32[2,1,1,352]{3,2,1,0:T(1,128)S(1)}, u32[]{:S(2)}, u32[]{:S(2)}) %collective-permute-start.6) | collective-permute-done | bytes 2848 | tf_op jit(solution)/shard_map/ppermute | solution.py:20
  53.0 24.6 %all_gather.7 = bf16[12,64,352]{2,1,0:T(8,128)(2,1)S(1)} all-gather(bf16[1,64,352]{2,1,0:T(8,128)(2,1)S(1)} %divide_convert_fusion.1), channel_id=1, replica_groups=mesh['x'=4,'y'=8,'c'=2,'mp'=12] {'mp'}, dimensions={0}, use_global_device_ids=true | all-gather | bytes 585728 | tf_op jit(solution)/shard_map/all_gather | solution.py:107
  77.6 1.2 copy.6
  78.8 3.4 %all_to_all.14 = bf16[64,32,132]{2,1,0:T(8,128)(2,1)} reshape(bf16[64,12,352]{2,1,0:T(8,128)(2,1)} %copy.6) | data formatting | bytes 1081344 | tf_op jit(solution)/shard_map/all_to_all | solution.py:110
  82.3 2.8 %copy.7 = bf16[64,32,132]{2,0,1:T(8,128)(2,1)} copy(bf16[64,32,132]{2,1,0:T(8,128)(2,1)} %all_to_all.14) | data formatting | bytes 1081344 | tf_op jit(solution)/shard_map/all_to_all | solution.py:110
  85.1 7.3 %all-to-all-start = ((bf16[64,32,132]{2,0,1:T(8,128)(2,1)}), bf16[64,32,132]{2,0,1:T(8,128)(2,1)}, u32[]{:S(2)}, u32[]{:S(2)}) async-start(bf16[64,32,132]{2,0,1:T(8,128)(2,1)} %copy.7), calls=%async_computation | async-start | bytes 2097152 | tf_op jit(solution)/shard_map/all_to_all | solution.py:110
  92.4 0.1 add_multiply_fusion
  92.5 0.1 broadcast_multiply_fusion
  92.6 0.1 add.552
  92.7 4.0 %reshape_reshape.3 = bf16[64,64,66]{2,1,0:T(8,128)(2,1)} reshape(bf16[64,12,352]{2,1,0:T(8,128)(2,1)} %copy.6) | data formatting | bytes 1081344 | tf_op jit(solution)/shard_map/reshape;reshape | solution.py:117
  96.7 2.7 %fusion.4 = bf16[64,64,66]{2,1,0:T(8,128)(2,1)} fusion(bf16[64,64,66]{2,1,0:T(8,128)(2,1)} %reshape_reshape.3, s32[64]{0:T(128)S(1)} %add.552), kind=kOutput, calls=%fused_computation.12 | convolution fusion | flops 34877440 | bytes 1081600 | tf_op jit(solution)/shard_map/bkt,pk->bpt/dot_general | solution.py:116
  99.4 3.1 %reshape.607 = bf16[64,4224]{1,0:T(8,128)(2,1)} reshape(bf16[64,64,66]{2,1,0:T(8,128)(2,1)} %fusion.4) | data formatting | bytes 1081344 | tf_op jit(solution)/shard_map/reshape | solution.py:118
  102.5 17.6 %all-to-all-done = bf16[64,32,132]{2,0,1:T(8,128)(2,1)} async-done(((bf16[64,32,132]{2,0,1:T(8,128)(2,1)}), bf16[64,32,132]{2,0,1:T(8,128)(2,1)}, u32[]{:S(2)}, u32[]{:S(2)}) %all-to-all-start) | async-done | bytes 540704 | tf_op jit(solution)/shard_map/all_to_all | solution.py:110
  120.1 2.1 copy.12
  122.2 3.4 %reduce_sum.56 = f32[352]{0:T(512)S(1)} reduce(f32[1,4096,352]{2,1,0:T(8,128)} %all-gather.3.cloned.1.call-done, f32[]{:T(128)} %constant.85.clone.1), dimensions={0,1}, to_apply=%region_2.0 | reduce | flops 1441440 | bytes 5768580 | tf_op jit(solution)/shard_map/reduce_sum | solution.py:98
  125.6 3.7 %multiply_reduce_fusion = f32[352]{0:T(512)S(1)} fusion(f32[1,4096,352]{2,1,0:T(8,128)} %all-gather.3.cloned.1.call-done, f32[352]{0:T(512)S(1)} %broadcast_multiply_fusion.1), kind=kLoop, calls=%fused_computation.6 | loop fusion | flops 4325024 | bytes 5769984 | tf_op jit(solution)/shard_map/reduce_sum | solution.py:100
  129.3 0.9 copy-done.1
  130.2 0.6 divide_convert_fusion
  130.8 0.2 constant_dynamic-slice_fusion.8
  131.0 0.8 copy-done.2
  131.9 0.5 fusion.28
  132.4 9.6 %collective-permute-start.7 = (f32[352,66]{0,1:T(8,128)S(1)}, f32[352,66]{0,1:T(8,128)S(1)}, u32[]{:S(2)}, u32[]{:S(2)}) collective-permute-start(f32[352,66]{0,1:T(8,128)S(1)} %constant_dynamic-slice_fusion.7), channel_id=1, source_target_pairs={{0,12},{12,0},{1,13},{13,1},{2,14},{14,2},{3,15},{15,3},{4,16},{16... | collective-permute-start | bytes 278792 | tf_op jit(solution)/shard_map/ppermute | solution.py:13
  142.0 0.9 collective-permute-done.7
  142.9 0.1 select_convert_fusion
  143.0 3.0 %collective-permute-start.9 = (bf16[66,352]{1,0:T(8,128)(2,1)S(1)}, bf16[66,352]{1,0:T(8,128)(2,1)S(1)}, u32[]{:S(2)}, u32[]{:S(2)}) collective-permute-start(bf16[66,352]{1,0:T(8,128)(2,1)S(1)} %bitcast.79), channel_id=1, source_target_pairs={{0,384},{192,576},{384,0},{576,192},{1,385},{193,577},{385,1},{577... | collective-permute-start | bytes 139400 | tf_op jit(solution)/shard_map/ppermute | solution.py:20
  146.0 4.3 %collective-permute-start.8 = (bf16[66,352]{1,0:T(8,128)(2,1)S(1)}, bf16[66,352]{1,0:T(8,128)(2,1)S(1)}, u32[]{:S(2)}, u32[]{:S(2)}) collective-permute-start(bf16[66,352]{1,0:T(8,128)(2,1)S(1)} %bitcast.80), channel_id=1, source_target_pairs={{0,576},{192,0},{384,192},{576,384},{1,577},{193,1},{385,193},{577... | collective-permute-start | bytes 139400 | tf_op jit(solution)/shard_map/ppermute | solution.py:20
  150.3 1.9 collective-permute-start.10
  152.2 4.2 %collective-permute-done.10 = bf16[66,352]{1,0:T(8,128)(2,1)S(1)} collective-permute-done((bf16[66,352]{1,0:T(8,128)(2,1)S(1)}, bf16[66,352]{1,0:T(8,128)(2,1)S(1)}, u32[]{:S(2)}, u32[]{:S(2)}) %collective-permute-start.10) | collective-permute-done | bytes 46496 | tf_op jit(solution)/shard_map/ppermute | solution.py:20
  156.4 0.1 pad_maximum_fusion.1
  156.5 1.9 collective-permute-start.11
  158.4 3.4 %collective-permute-start.14 = (bf16[4,66,352]{2,1,0:T(8,128)(2,1)S(1)}, bf16[4,66,352]{2,1,0:T(8,128)(2,1)S(1)}, u32[]{:S(2)}, u32[]{:S(2)}) collective-permute-start(bf16[4,66,352]{2,1,0:T(8,128)(2,1)S(1)} %pad_maximum_fusion.1), channel_id=1, source_target_pairs={{0,24},{24,48},{48,72},{72,96},{96,120},{120,144},{144,168},{168,0... | collective-permute-start | bytes 557576 | tf_op jit(solution)/shard_map/ppermute | solution.py:13
  161.8 1.3 collective-permute-done.11
  163.1 3.1 %collective-permute-start.12 = (bf16[4,66,352]{2,1,0:T(8,128)(2,1)S(1)}, bf16[4,66,352]{2,1,0:T(8,128)(2,1)S(1)}, u32[]{:S(2)}, u32[]{:S(2)}) collective-permute-start(bf16[4,66,352]{2,1,0:T(8,128)(2,1)S(1)} %collective-permute-done.11), channel_id=1, source_target_pairs={{0,168},{24,0},{48,24},{72,48},{96,72},{120,96},{144,120},{168,144... | collective-permute-start | bytes 557576 | tf_op jit(solution)/shard_map/ppermute | solution.py:13
  166.3 2.4 %collective-permute-start.15 = (bf16[4,66,352]{2,1,0:T(8,128)(2,1)S(1)}, bf16[4,66,352]{2,1,0:T(8,128)(2,1)S(1)}, u32[]{:S(2)}, u32[]{:S(2)}) collective-permute-start(bf16[4,66,352]{2,1,0:T(8,128)(2,1)S(1)} %collective-permute-done.14), channel_id=1, source_target_pairs={{0,24},{24,48},{48,72},{72,96},{96,120},{120,144},{144,168},{168,0... | collective-permute-start | bytes 557576 | tf_op jit(solution)/shard_map/ppermute | solution.py:13
  168.8 1.0 collective-permute-done.12
  169.8 4.3 %collective-permute-start.13 = (bf16[4,66,352]{2,1,0:T(8,128)(2,1)S(1)}, bf16[4,66,352]{2,1,0:T(8,128)(2,1)S(1)}, u32[]{:S(2)}, u32[]{:S(2)}) collective-permute-start(bf16[4,66,352]{2,1,0:T(8,128)(2,1)S(1)} %collective-permute-done.12), channel_id=1, source_target_pairs={{0,168},{24,0},{48,24},{72,48},{96,72},{120,96},{144,120},{168,144... | collective-permute-start | bytes 557576 | tf_op jit(solution)/shard_map/ppermute | solution.py:13
  174.1 0.2 collective-permute-done.15
  174.3 1.9 collective-permute-start.16
  176.3 5.9 %collective-permute-done.16 = bf16[4,66,352]{2,1,0:T(8,128)(2,1)S(1)} collective-permute-done((bf16[4,66,352]{2,1,0:T(8,128)(2,1)S(1)}, bf16[4,66,352]{2,1,0:T(8,128)(2,1)S(1)}, u32[]{:S(2)}, u32[]{:S(2)}) %collective-permute-start.16) | collective-permute-done | bytes 185888 | tf_op jit(solution)/shard_map/ppermute | solution.py:13
  182.2 1.9 collective-permute-start.17
  184.2 5.9 %collective-permute-done.17 = bf16[4,66,352]{2,1,0:T(8,128)(2,1)S(1)} collective-permute-done((bf16[4,66,352]{2,1,0:T(8,128)(2,1)S(1)}, bf16[4,66,352]{2,1,0:T(8,128)(2,1)S(1)}, u32[]{:S(2)}, u32[]{:S(2)}) %collective-permute-start.17) | collective-permute-done | bytes 185888 | tf_op jit(solution)/shard_map/ppermute | solution.py:13
  190.3 0.6 copy.10
  190.9 8.8 %collective-permute-start.18 = (bf16[8,4,66,352]{3,0,2,1:T(8,128)(2,1)S(1)}, bf16[8,4,66,352]{3,0,2,1:T(8,128)(2,1)S(1)}, u32[]{:S(2)}, u32[]{:S(2)}) collective-permute-start(bf16[8,4,66,352]{3,0,2,1:T(8,128)(2,1)S(1)} %copy.10), channel_id=1, source_target_pairs={{0,12},{12,0},{1,13},{13,1},{2,14},{14,2},{3,15},{15,3},{4,16},{16... | collective-permute-start | bytes 4460552 | tf_op jit(solution)/shard_map/ppermute | solution.py:13
  199.7 0.1 iota_add_fusion
  199.8 3.0 %collective-permute-done.18 = bf16[8,4,66,352]{3,0,2,1:T(8,128)(2,1)S(1)} collective-permute-done((bf16[8,4,66,352]{3,0,2,1:T(8,128)(2,1)S(1)}, bf16[8,4,66,352]{3,0,2,1:T(8,128)(2,1)S(1)}, u32[]{:S(2)}, u32[]{:S(2)}) %collective-permute-start.18) | collective-permute-done | bytes 1486880 | tf_op jit(solution)/shard_map/ppermute | solution.py:13
  202.8 0.2 copy.14
  203.0 2.5 %pad_maximum_fusion = bf16[2,8,4,66,352]{4,3,2,1,0:T(8,128)(2,1)} fusion(bf16[1,8,4,66,352]{4,3,2,1,0:T(8,128)(2,1)S(1)} %bitcast.74, bf16[1,8,4,66,352]{4,3,2,1,0:T(8,128)(2,1)S(1)} %bitcast.72), kind=kLoop, calls=%fused_computation.7 | loop fusion | flops 1486848 | bytes 5947392 | tf_op jit(solution)/shard_map/stack | solution.py:39
  205.5 1.8 fusion
  207.3 5.8 %reshape.610 = bf16[4224,352]{1,0:T(8,128)(2,1)} reshape(bf16[2,8,4,66,352]{4,3,2,1,0:T(8,128)(2,1)} %pad_maximum_fusion) | data formatting | bytes 5947392 | tf_op jit(solution)/shard_map/reshape | solution.py:132
  213.1 3.3 %fusion.6 = bf16[64,352]{1,0:T(8,128)(2,1)} fusion(bf16[64,4224]{1,0:T(8,128)(2,1)} %reshape.607, bf16[4224,352]{1,0:T(8,128)(2,1)} %reshape.610, f32[352]{0:T(512)S(1)} %get-tuple-element.25, f32[352]{0:T(512)S(1)} %multiply_add_fusion, f32[352]{0:T(512)S(1)} %get-tuple-element.26, f32[352]{0:T(512)S(1)} %broadcast_multiply_fusion.1, ...), kind=kOutput, calls=%fused_computation.15 | convolution fusion | flops 190496768 | bytes 3655168 | tf_op jit(solution)/shard_map/dot_general | solution.py:147
  (52 shorter events, 0.7 us)
Async XLA Ops:
  6.5 1.8 copy-start
  6.5 115.7 %all-gather.3.cloned.1.call-start = ((), (), s32[]{:S(2)}) async-start(), calls=%async_computation.1 | async-start | bytes 6389760 | tf_op jit(solution)/shard_map/all_gather | solution.py:97
  11.4 13.2 %collective-permute-start = (f32[2,1,1,352]{3,2,1,0:T(1,128)S(1)}, f32[2,1,1,352]{3,2,1,0:T(1,128)S(1)}, u32[]{:S(2)}, u32[]{:S(2)}) collective-permute-start(f32[2,1,1,352]{3,2,1,0:T(1,128)S(1)} %pad_maximum_fusion.2), channel_id=1, source_target_pairs={{0,12},{12,0},{1,13},{13,1},{2,14},{14,2},{3,15},{15,3},{4,16},{16... | collective-permute-start | bytes 8456 | tf_op jit(solution)/shard_map/ppermute | solution.py:49
  24.7 4.3 %collective-permute-start.1 = (f32[2,1,1,352]{3,2,1,0:T(1,128)S(1)}, f32[2,1,1,352]{3,2,1,0:T(1,128)S(1)}, u32[]{:S(2)}, u32[]{:S(2)}) collective-permute-start(f32[2,1,1,352]{3,2,1,0:T(1,128)S(1)} %pad_maximum_fusion.3), channel_id=1, source_target_pairs={{0,24},{24,0},{48,72},{72,48},{96,120},{120,96},{144,168},{168,144... | collective-permute-start | bytes 8456 | tf_op jit(solution)/shard_map/ppermute | solution.py:49
  29.1 5.2 %collective-permute-start.2 = (f32[2,1,1,352]{3,2,1,0:T(1,128)S(1)}, f32[2,1,1,352]{3,2,1,0:T(1,128)S(1)}, u32[]{:S(2)}, u32[]{:S(2)}) collective-permute-start(f32[2,1,1,352]{3,2,1,0:T(1,128)S(1)} %pad_maximum_fusion.4), channel_id=1, source_target_pairs={{0,48},{24,72},{48,0},{72,24},{96,144},{120,168},{144,96},{168,120... | collective-permute-start | bytes 8456 | tf_op jit(solution)/shard_map/ppermute | solution.py:49
  34.3 8.3 %collective-permute-start.3 = (f32[2,1,1,352]{3,2,1,0:T(1,128)S(1)}, f32[2,1,1,352]{3,2,1,0:T(1,128)S(1)}, u32[]{:S(2)}, u32[]{:S(2)}) collective-permute-start(f32[2,1,1,352]{3,2,1,0:T(1,128)S(1)} %pad_maximum_fusion.5), channel_id=1, source_target_pairs={{0,96},{24,120},{48,144},{72,168},{96,0},{120,24},{144,48},{168,72... | collective-permute-start | bytes 8456 | tf_op jit(solution)/shard_map/ppermute | solution.py:49
  42.6 7.3 %collective-permute-start.5 = (f32[2,1,1,352]{3,2,1,0:T(1,128)S(1)}, f32[2,1,1,352]{3,2,1,0:T(1,128)S(1)}, u32[]{:S(2)}, u32[]{:S(2)}) collective-permute-start(f32[2,1,1,352]{3,2,1,0:T(1,128)S(1)} %pad_maximum_fusion.6), channel_id=1, source_target_pairs={{0,384},{192,576},{384,0},{576,192},{1,385},{193,577},{385,1},{577... | collective-permute-start | bytes 8456 | tf_op jit(solution)/shard_map/ppermute | solution.py:20
  44.6 5.3 %collective-permute-start.4 = (f32[2,1,1,352]{3,2,1,0:T(1,128)S(1)}, f32[2,1,1,352]{3,2,1,0:T(1,128)S(1)}, u32[]{:S(2)}, u32[]{:S(2)}) collective-permute-start(f32[2,1,1,352]{3,2,1,0:T(1,128)S(1)} %pad_maximum_fusion.6), channel_id=1, source_target_pairs={{0,576},{192,0},{384,192},{576,384},{1,577},{193,1},{385,193},{577... | collective-permute-start | bytes 8456 | tf_op jit(solution)/shard_map/ppermute | solution.py:20
  46.5 6.4 %collective-permute-start.6 = (f32[2,1,1,352]{3,2,1,0:T(1,128)S(1)}, f32[2,1,1,352]{3,2,1,0:T(1,128)S(1)}, u32[]{:S(2)}, u32[]{:S(2)}) collective-permute-start(f32[2,1,1,352]{3,2,1,0:T(1,128)S(1)} %pad_maximum_fusion.6), channel_id=1, source_target_pairs={{0,192},{192,384},{384,576},{576,0},{1,193},{193,385},{385,577},{5... | collective-permute-start | bytes 8456 | tf_op jit(solution)/shard_map/ppermute | solution.py:20
  85.1 35.0 %all-to-all-start = ((bf16[64,32,132]{2,0,1:T(8,128)(2,1)}), bf16[64,32,132]{2,0,1:T(8,128)(2,1)}, u32[]{:S(2)}, u32[]{:S(2)}) async-start(bf16[64,32,132]{2,0,1:T(8,128)(2,1)} %copy.7), calls=%async_computation | async-start | bytes 2097152 | tf_op jit(solution)/shard_map/all_to_all | solution.py:110
  125.6 4.6 %copy-start.1 = (f32[1,4096,352]{2,1,0:T(8,128)S(1)}, f32[1,4096,352]{2,1,0:T(8,128)}, u32[]{:S(2)}) copy-start(f32[1,4096,352]{2,1,0:T(8,128)} %all-gather.3.cloned.1.call-done) | copy-start | bytes 17301508
  130.8 1.1 copy-start.2
  132.4 10.5 %collective-permute-start.7 = (f32[352,66]{0,1:T(8,128)S(1)}, f32[352,66]{0,1:T(8,128)S(1)}, u32[]{:S(2)}, u32[]{:S(2)}) collective-permute-start(f32[352,66]{0,1:T(8,128)S(1)} %constant_dynamic-slice_fusion.7), channel_id=1, source_target_pairs={{0,12},{12,0},{1,13},{13,1},{2,14},{14,2},{3,15},{15,3},{4,16},{16... | collective-permute-start | bytes 278792 | tf_op jit(solution)/shard_map/ppermute | solution.py:13
  143.0 9.2 %collective-permute-start.9 = (bf16[66,352]{1,0:T(8,128)(2,1)S(1)}, bf16[66,352]{1,0:T(8,128)(2,1)S(1)}, u32[]{:S(2)}, u32[]{:S(2)}) collective-permute-start(bf16[66,352]{1,0:T(8,128)(2,1)S(1)} %bitcast.79), channel_id=1, source_target_pairs={{0,384},{192,576},{384,0},{576,192},{1,385},{193,577},{385,1},{577... | collective-permute-start | bytes 139400 | tf_op jit(solution)/shard_map/ppermute | solution.py:20
  146.0 6.3 %collective-permute-start.8 = (bf16[66,352]{1,0:T(8,128)(2,1)S(1)}, bf16[66,352]{1,0:T(8,128)(2,1)S(1)}, u32[]{:S(2)}, u32[]{:S(2)}) collective-permute-start(bf16[66,352]{1,0:T(8,128)(2,1)S(1)} %bitcast.80), channel_id=1, source_target_pairs={{0,576},{192,0},{384,192},{576,384},{1,577},{193,1},{385,193},{577... | collective-permute-start | bytes 139400 | tf_op jit(solution)/shard_map/ppermute | solution.py:20
  150.3 6.1 %collective-permute-start.10 = (bf16[66,352]{1,0:T(8,128)(2,1)S(1)}, bf16[66,352]{1,0:T(8,128)(2,1)S(1)}, u32[]{:S(2)}, u32[]{:S(2)}) collective-permute-start(bf16[66,352]{1,0:T(8,128)(2,1)S(1)} %bitcast.81), channel_id=1, source_target_pairs={{0,192},{192,384},{384,576},{576,0},{1,193},{193,385},{385,577},{5... | collective-permute-start | bytes 139400 | tf_op jit(solution)/shard_map/ppermute | solution.py:20
  156.5 6.7 %collective-permute-start.11 = (bf16[4,66,352]{2,1,0:T(8,128)(2,1)S(1)}, bf16[4,66,352]{2,1,0:T(8,128)(2,1)S(1)}, u32[]{:S(2)}, u32[]{:S(2)}) collective-permute-start(bf16[4,66,352]{2,1,0:T(8,128)(2,1)S(1)} %pad_maximum_fusion.1), channel_id=1, source_target_pairs={{0,168},{24,0},{48,24},{72,48},{96,72},{120,96},{144,120},{168,144... | collective-permute-start | bytes 557576 | tf_op jit(solution)/shard_map/ppermute | solution.py:13
  158.4 7.9 %collective-permute-start.14 = (bf16[4,66,352]{2,1,0:T(8,128)(2,1)S(1)}, bf16[4,66,352]{2,1,0:T(8,128)(2,1)S(1)}, u32[]{:S(2)}, u32[]{:S(2)}) collective-permute-start(bf16[4,66,352]{2,1,0:T(8,128)(2,1)S(1)} %pad_maximum_fusion.1), channel_id=1, source_target_pairs={{0,24},{24,48},{48,72},{72,96},{96,120},{120,144},{144,168},{168,0... | collective-permute-start | bytes 557576 | tf_op jit(solution)/shard_map/ppermute | solution.py:13
  163.1 6.7 %collective-permute-start.12 = (bf16[4,66,352]{2,1,0:T(8,128)(2,1)S(1)}, bf16[4,66,352]{2,1,0:T(8,128)(2,1)S(1)}, u32[]{:S(2)}, u32[]{:S(2)}) collective-permute-start(bf16[4,66,352]{2,1,0:T(8,128)(2,1)S(1)} %collective-permute-done.11), channel_id=1, source_target_pairs={{0,168},{24,0},{48,24},{72,48},{96,72},{120,96},{144,120},{168,144... | collective-permute-start | bytes 557576 | tf_op jit(solution)/shard_map/ppermute | solution.py:13
  166.3 8.1 %collective-permute-start.15 = (bf16[4,66,352]{2,1,0:T(8,128)(2,1)S(1)}, bf16[4,66,352]{2,1,0:T(8,128)(2,1)S(1)}, u32[]{:S(2)}, u32[]{:S(2)}) collective-permute-start(bf16[4,66,352]{2,1,0:T(8,128)(2,1)S(1)} %collective-permute-done.14), channel_id=1, source_target_pairs={{0,24},{24,48},{48,72},{72,96},{96,120},{120,144},{144,168},{168,0... | collective-permute-start | bytes 557576 | tf_op jit(solution)/shard_map/ppermute | solution.py:13
  169.8 14.3 %collective-permute-start.13 = (bf16[4,66,352]{2,1,0:T(8,128)(2,1)S(1)}, bf16[4,66,352]{2,1,0:T(8,128)(2,1)S(1)}, u32[]{:S(2)}, u32[]{:S(2)}) collective-permute-start(bf16[4,66,352]{2,1,0:T(8,128)(2,1)S(1)} %collective-permute-done.12), channel_id=1, source_target_pairs={{0,168},{24,0},{48,24},{72,48},{96,72},{120,96},{144,120},{168,144... | collective-permute-start | bytes 557576 | tf_op jit(solution)/shard_map/ppermute | solution.py:13
  174.3 7.9 %collective-permute-start.16 = (bf16[4,66,352]{2,1,0:T(8,128)(2,1)S(1)}, bf16[4,66,352]{2,1,0:T(8,128)(2,1)S(1)}, u32[]{:S(2)}, u32[]{:S(2)}) collective-permute-start(bf16[4,66,352]{2,1,0:T(8,128)(2,1)S(1)} %collective-permute-done.15), channel_id=1, source_target_pairs={{0,24},{24,48},{48,72},{72,96},{96,120},{120,144},{144,168},{168,0... | collective-permute-start | bytes 557576 | tf_op jit(solution)/shard_map/ppermute | solution.py:13
  182.2 7.9 %collective-permute-start.17 = (bf16[4,66,352]{2,1,0:T(8,128)(2,1)S(1)}, bf16[4,66,352]{2,1,0:T(8,128)(2,1)S(1)}, u32[]{:S(2)}, u32[]{:S(2)}) collective-permute-start(bf16[4,66,352]{2,1,0:T(8,128)(2,1)S(1)} %collective-permute-done.16), channel_id=1, source_target_pairs={{0,24},{24,48},{48,72},{72,96},{96,120},{120,144},{144,168},{168,0... | collective-permute-start | bytes 557576 | tf_op jit(solution)/shard_map/ppermute | solution.py:13
  190.9 11.9 %collective-permute-start.18 = (bf16[8,4,66,352]{3,0,2,1:T(8,128)(2,1)S(1)}, bf16[8,4,66,352]{3,0,2,1:T(8,128)(2,1)S(1)}, u32[]{:S(2)}, u32[]{:S(2)}) collective-permute-start(bf16[8,4,66,352]{3,0,2,1:T(8,128)(2,1)S(1)} %copy.10), channel_id=1, source_target_pairs={{0,12},{12,0},{1,13},{13,1},{2,14},{14,2},{3,15},{15,3},{4,16},{16... | collective-permute-start | bytes 4460552 | tf_op jit(solution)/shard_map/ppermute | solution.py:13
Sparse Core Ops, SparseCore 0:
  11.5 107.9 all-gather.2

commit v18 on v17

--- a/solution.py
+++ b/solution.py
@@ -84,6 +84,11 @@
     return mean, m2 / count
 
 
+def group_sum(v, group=128):
+    part = jnp.sum(v.reshape(v.shape[0] // group, group, v.shape[1]), axis=1)
+    return jnp.sum(lax.optimization_barrier(part), axis=0, keepdims=True)
+
+
 def shards(hidden, proj_weight):
     mp_index = lax.axis_index("mp")
     dp_index = lax.axis_index(DP)
@@ -95,9 +100,9 @@
     total = local * dp_count
     feats = jnp.einsum("vbh,hc->vbc", hidden, proj_weight, preferred_element_type=jnp.float32)
     feats0_all = lax.all_gather(feats[0], DP, axis=0, tiled=True)
-    mean0 = jnp.sum(feats0_all, axis=0, keepdims=True) / total
+    mean0 = group_sum(feats0_all) / total
     centered0 = feats0_all - mean0
-    var0 = jnp.sum(centered0 * centered0, axis=0, keepdims=True) / total
+    var0 = group_sum(centered0 * centered0) / total
     first_all = (centered0 / jnp.sqrt(var0 + eps)).astype(jnp.bfloat16)
     first = ((feats[0] - mean0) / jnp.sqrt(var0 + eps)).astype(jnp.bfloat16)
     inv_std0 = 1.0 / jnp.sqrt(var0 + eps)

time: 225 us -> 226 us (level)
  other arithmetic: 13.3 us -> 15.9 us
    convert_element_type x1, other arithmetic: 0.64 us -> 3.43 us  [shards(): first_all = (centered0 / jnp.sqrt(var0 + eps)).astype(jnp.bfloat16)]
    reduce_sum x2 -> x4, other arithmetic: 7.09 us -> 6.95 us  [the longest x2 6.9 us: group_sum(): part = jnp.sum(v.reshape(v.shape[0] // group, group, v.shape[1]), axis=1)]
  transfers between devices with their start and end apart: 21 -> 21, of which waited for: 14 -> 13; matrix products, arithmetic and copies ran while one was open for 7% -> 7% of each run, Pallas kernels for 0% -> 0%
where the time goes in v18:
time: 226 us; the launch traced here: 225 us
  starting transfers between devices  79 us (35%)
  waiting for transfers between devices  56 us (25%)
  local copies, waits for them, and re-layouts  26.7 us (12%)
  blocking collectives  24.6 us (11%)
  other arithmetic  15.9 us (7%)
  between operations  13.9 us (6%)
  matrix products  8.77 us (4%)
    ppermute x9, starting transfers between devices, shift(): return lax.ppermute(v, axis, [(i, (i + step) % n) for i in range(n)])  37.1 us
    all_gather x1, blocking collectives, shards(): stacked = lax.all_gather(second, 'mp', axis=0)  24.6 us
    ppermute x4, starting transfers between devices, combine(): other = lax.ppermute(jnp.stack([mean, m2]), axis, pairs)  18.2 us
    ppermute x9, waiting for transfers between devices, shift(): return lax.ppermute(v, axis, [(i, (i + step) % n) for i in range(n)])  18.2 us
    all_to_all x1, waiting for transfers between devices, shards(): lax.all_to_all(second_full, ('x', 'y'), split_axis=1, concat_axis=0, tile...  17.8 us
    ppermute x6, starting transfers between devices, direct_gather(): got[t] = lax.ppermute(v, axis, [(i, (i - t) % n) for i in range(n)])  16.4 us
    ppermute x4, waiting for transfers between devices, combine(): other = lax.ppermute(jnp.stack([mean, m2]), axis, pairs)  12.8 us
    all_to_all x3, local copies, waits for them, and re-layouts, shards(): lax.all_to_all(second_full, ('x', 'y'), split_axis=1, concat_axis=0, tile...  8.39 us
  transfers between devices with their start and end apart: 21, of which 13 were waited for; matrix products, arithmetic and copies ran while one was open for 7% of the time, Pallas kernels for 0%

profile of v18, /device:TPU:1, one launch (start us, length us, event | category | flops | bytes accessed | tf_op | source)
XLA Modules:
  0.0 224.9 jit_solution(17613168622734153602)
XLA Ops:
  6.5 1.8 copy-done
  8.4 2.3 %fusion.3 = f32[2,64,352]{2,1,0:T(8,128)S(1)} fusion(bf16[2,64,4224]{2,1,0:T(8,128)(2,1)} %param.2, bf16[4224,352]{0,1:T(8,128)(2,1)S(1)} %copy-done), kind=kOutput, calls=%fused_computation.9 | convolution fusion | flops 380633088 | bytes 4235264 | tf_op jit(solution)/shard_map/vbh,hc->vbc/dot_general | solution.py:101
  10.7 0.7 fusion.28
  11.4 12.4 %collective-permute-start = (f32[2,1,1,352]{3,2,1,0:T(1,128)S(1)}, f32[2,1,1,352]{3,2,1,0:T(1,128)S(1)}, u32[]{:S(2)}, u32[]{:S(2)}) collective-permute-start(f32[2,1,1,352]{3,2,1,0:T(1,128)S(1)} %pad_maximum_fusion.2), channel_id=1, source_target_pairs={{0,12},{12,0},{1,13},{13,1},{2,14},{14,2},{3,15},{15,3},{4,16},{16... | collective-permute-start | bytes 8456 | tf_op jit(solution)/shard_map/ppermute | solution.py:49
  23.9 0.8 collective-permute-done
  24.7 1.9 collective-permute-start.1
  26.6 2.4 %collective-permute-done.1 = f32[2,1,1,352]{3,2,1,0:T(1,128)S(1)} collective-permute-done((f32[2,1,1,352]{3,2,1,0:T(1,128)S(1)}, f32[2,1,1,352]{3,2,1,0:T(1,128)S(1)}, u32[]{:S(2)}, u32[]{:S(2)}) %collective-permute-start.1) | collective-permute-done | bytes 2848 | tf_op jit(solution)/shard_map/ppermute | solution.py:49
  29.1 1.9 collective-permute-start.2
  31.0 3.3 %collective-permute-done.2 = f32[2,1,1,352]{3,2,1,0:T(1,128)S(1)} collective-permute-done((f32[2,1,1,352]{3,2,1,0:T(1,128)S(1)}, f32[2,1,1,352]{3,2,1,0:T(1,128)S(1)}, u32[]{:S(2)}, u32[]{:S(2)}) %collective-permute-start.2) | collective-permute-done | bytes 2848 | tf_op jit(solution)/shard_map/ppermute | solution.py:49
  34.3 1.9 collective-permute-start.3
  36.3 6.3 %collective-permute-done.3 = f32[2,1,1,352]{3,2,1,0:T(1,128)S(1)} collective-permute-done((f32[2,1,1,352]{3,2,1,0:T(1,128)S(1)}, f32[2,1,1,352]{3,2,1,0:T(1,128)S(1)}, u32[]{:S(2)}, u32[]{:S(2)}) %collective-permute-start.3) | collective-permute-done | bytes 2848 | tf_op jit(solution)/shard_map/ppermute | solution.py:49
  42.6 1.9 collective-permute-start.5
  44.6 1.9 collective-permute-start.4
  46.5 3.4 %collective-permute-start.6 = (f32[2,1,1,352]{3,2,1,0:T(1,128)S(1)}, f32[2,1,1,352]{3,2,1,0:T(1,128)S(1)}, u32[]{:S(2)}, u32[]{:S(2)}) collective-permute-start(f32[2,1,1,352]{3,2,1,0:T(1,128)S(1)} %pad_maximum_fusion.6), channel_id=1, source_target_pairs={{0,192},{192,384},{384,576},{576,0},{1,193},{193,385},{385,577},{5... | collective-permute-start | bytes 8456 | tf_op jit(solution)/shard_map/ppermute | solution.py:20
  49.9 3.0 %collective-permute-done.6 = f32[2,1,1,352]{3,2,1,0:T(1,128)S(1)} collective-permute-done((f32[2,1,1,352]{3,2,1,0:T(1,128)S(1)}, f32[2,1,1,352]{3,2,1,0:T(1,128)S(1)}, u32[]{:S(2)}, u32[]{:S(2)}) %collective-permute-start.6) | collective-permute-done | bytes 2848 | tf_op jit(solution)/shard_map/ppermute | solution.py:20
  52.9 0.1 multiply_reduce_fusion.1
  53.0 24.6 %all_gather.7 = bf16[12,64,352]{2,1,0:T(8,128)(2,1)S(1)} all-gather(bf16[1,64,352]{2,1,0:T(8,128)(2,1)S(1)} %divide_convert_fusion.1), channel_id=1, replica_groups=mesh['x'=4,'y'=8,'c'=2,'mp'=12] {'mp'}, dimensions={0}, use_global_device_ids=true | all-gather | bytes 585728 | tf_op jit(solution)/shard_map/all_gather | solution.py:112
  77.6 1.2 copy.6
  78.8 3.5 %all_to_all.14 = bf16[64,32,132]{2,1,0:T(8,128)(2,1)} reshape(bf16[64,12,352]{2,1,0:T(8,128)(2,1)} %copy.6) | data formatting | bytes 1081344 | tf_op jit(solution)/shard_map/all_to_all | solution.py:115
  82.3 2.8 %copy.7 = bf16[64,32,132]{2,0,1:T(8,128)(2,1)} copy(bf16[64,32,132]{2,1,0:T(8,128)(2,1)} %all_to_all.14) | data formatting | bytes 1081344 | tf_op jit(solution)/shard_map/all_to_all | solution.py:115
  85.1 7.3 %all-to-all-start = ((bf16[64,32,132]{2,0,1:T(8,128)(2,1)}), bf16[64,32,132]{2,0,1:T(8,128)(2,1)}, u32[]{:S(2)}, u32[]{:S(2)}) async-start(bf16[64,32,132]{2,0,1:T(8,128)(2,1)} %copy.7), calls=%async_computation | async-start | bytes 2097152 | tf_op jit(solution)/shard_map/all_to_all | solution.py:115
  92.4 0.1 add_multiply_fusion
  92.5 0.1 broadcast_multiply_fusion
  92.6 0.1 add.552
  92.7 4.0 %reshape_reshape.3 = bf16[64,64,66]{2,1,0:T(8,128)(2,1)} reshape(bf16[64,12,352]{2,1,0:T(8,128)(2,1)} %copy.6) | data formatting | bytes 1081344 | tf_op jit(solution)/shard_map/reshape;reshape | solution.py:122
  96.7 2.7 %fusion.5 = bf16[64,64,66]{2,1,0:T(8,128)(2,1)} fusion(bf16[64,64,66]{2,1,0:T(8,128)(2,1)} %reshape_reshape.3, s32[64]{0:T(128)S(1)} %add.552), kind=kOutput, calls=%fused_computation.13 | convolution fusion | flops 34877440 | bytes 1081600 | tf_op jit(solution)/shard_map/bkt,pk->bpt/dot_general | solution.py:121
  99.4 3.1 %reshape.613 = bf16[64,4224]{1,0:T(8,128)(2,1)} reshape(bf16[64,64,66]{2,1,0:T(8,128)(2,1)} %fusion.5) | data formatting | bytes 1081344 | tf_op jit(solution)/shard_map/reshape | solution.py:123
  102.5 17.8 %all-to-all-done = bf16[64,32,132]{2,0,1:T(8,128)(2,1)} async-done(((bf16[64,32,132]{2,0,1:T(8,128)(2,1)}), bf16[64,32,132]{2,0,1:T(8,128)(2,1)}, u32[]{:S(2)}, u32[]{:S(2)}) %all-to-all-start) | async-done | bytes 540704 | tf_op jit(solution)/shard_map/all_to_all | solution.py:115
  120.3 2.1 copy.12
  122.5 3.3 %reduce_sum.74 = f32[32,352]{1,0:T(8,128)S(1)} reduce(f32[32,128,352]{2,1,0:T(8,128)} %bitcast.77, f32[]{:T(128)} %constant.85.clone.1), dimensions={1}, to_apply=%region_2.0 | reduce | flops 1430528 | bytes 5812228 | tf_op jit(solution)/shard_map/reduce_sum | solution.py:88
  125.8 3.6 %bitcast_reduce_fusion = f32[32,352]{1,0:T(8,128)S(1)} fusion(f32[1,4096,352]{2,1,0:T(8,128)} %all-gather.3.cloned.1.call-done, f32[352]{0:T(512)S(1)} %broadcast_multiply_fusion.1), kind=kLoop, calls=%fused_computation.4 | loop fusion | flops 4314112 | bytes 5813632 | tf_op jit(solution)/shard_map/reduce_sum | solution.py:88
  129.4 3.4 %divide_convert_fusion = bf16[4096,352]{1,0:T(8,128)(2,1)S(1)} fusion(f32[1,4096,352]{2,1,0:T(8,128)} %all-gather.3.cloned.1.call-done, f32[352]{0:T(512)S(1)} %get-tuple-element.26, f32[352]{0:T(512)S(1)} %broadcast_multiply_fusion.1), kind=kLoop, calls=%fused_computation.6 | loop fusion | flops 4325376 | bytes 8653568 | tf_op jit(solution)/shard_map/convert_element_type | solution.py:106
  132.9 0.2 constant_dynamic-slice_fusion.8
  133.1 0.8 copy-done.1
  133.9 0.5 fusion.29
  134.4 9.3 %collective-permute-start.7 = (f32[352,66]{0,1:T(8,128)S(1)}, f32[352,66]{0,1:T(8,128)S(1)}, u32[]{:S(2)}, u32[]{:S(2)}) collective-permute-start(f32[352,66]{0,1:T(8,128)S(1)} %constant_dynamic-slice_fusion.7), channel_id=1, source_target_pairs={{0,12},{12,0},{1,13},{13,1},{2,14},{14,2},{3,15},{15,3},{4,16},{16... | collective-permute-start | bytes 278792 | tf_op jit(solution)/shard_map/ppermute | solution.py:13
  143.7 0.9 collective-permute-done.7
  144.7 0.1 select_convert_fusion
  144.7 3.0 %collective-permute-start.9 = (bf16[66,352]{1,0:T(8,128)(2,1)S(1)}, bf16[66,352]{1,0:T(8,128)(2,1)S(1)}, u32[]{:S(2)}, u32[]{:S(2)}) collective-permute-start(bf16[66,352]{1,0:T(8,128)(2,1)S(1)} %bitcast.85), channel_id=1, source_target_pairs={{0,384},{192,576},{384,0},{576,192},{1,385},{193,577},{385,1},{577... | collective-permute-start | bytes 139400 | tf_op jit(solution)/shard_map/ppermute | solution.py:20
  147.7 4.3 %collective-permute-start.8 = (bf16[66,352]{1,0:T(8,128)(2,1)S(1)}, bf16[66,352]{1,0:T(8,128)(2,1)S(1)}, u32[]{:S(2)}, u32[]{:S(2)}) collective-permute-start(bf16[66,352]{1,0:T(8,128)(2,1)S(1)} %bitcast.86), channel_id=1, source_target_pairs={{0,576},{192,0},{384,192},{576,384},{1,577},{193,1},{385,193},{577... | collective-permute-start | bytes 139400 | tf_op jit(solution)/shard_map/ppermute | solution.py:20
  152.0 1.9 collective-permute-start.10
  154.0 4.2 %collective-permute-done.10 = bf16[66,352]{1,0:T(8,128)(2,1)S(1)} collective-permute-done((bf16[66,352]{1,0:T(8,128)(2,1)S(1)}, bf16[66,352]{1,0:T(8,128)(2,1)S(1)}, u32[]{:S(2)}, u32[]{:S(2)}) %collective-permute-start.10) | collective-permute-done | bytes 46496 | tf_op jit(solution)/shard_map/ppermute | solution.py:20
  158.2 0.1 pad_maximum_fusion.1
  158.2 1.9 collective-permute-start.11
  160.2 3.4 %collective-permute-start.14 = (bf16[4,66,352]{2,1,0:T(8,128)(2,1)S(1)}, bf16[4,66,352]{2,1,0:T(8,128)(2,1)S(1)}, u32[]{:S(2)}, u32[]{:S(2)}) collective-permute-start(bf16[4,66,352]{2,1,0:T(8,128)(2,1)S(1)} %pad_maximum_fusion.1), channel_id=1, source_target_pairs={{0,24},{24,48},{48,72},{72,96},{96,120},{120,144},{144,168},{168,0... | collective-permute-start | bytes 557576 | tf_op jit(solution)/shard_map/ppermute | solution.py:13
  163.6 1.3 collective-permute-done.11
  164.9 3.1 %collective-permute-start.12 = (bf16[4,66,352]{2,1,0:T(8,128)(2,1)S(1)}, bf16[4,66,352]{2,1,0:T(8,128)(2,1)S(1)}, u32[]{:S(2)}, u32[]{:S(2)}) collective-permute-start(bf16[4,66,352]{2,1,0:T(8,128)(2,1)S(1)} %collective-permute-done.11), channel_id=1, source_target_pairs={{0,168},{24,0},{48,24},{72,48},{96,72},{120,96},{144,120},{168,144... | collective-permute-start | bytes 557576 | tf_op jit(solution)/shard_map/ppermute | solution.py:13
  168.0 2.4 %collective-permute-start.15 = (bf16[4,66,352]{2,1,0:T(8,128)(2,1)S(1)}, bf16[4,66,352]{2,1,0:T(8,128)(2,1)S(1)}, u32[]{:S(2)}, u32[]{:S(2)}) collective-permute-start(bf16[4,66,352]{2,1,0:T(8,128)(2,1)S(1)} %collective-permute-done.14), channel_id=1, source_target_pairs={{0,24},{24,48},{48,72},{72,96},{96,120},{120,144},{144,168},{168,0... | collective-permute-start | bytes 557576 | tf_op jit(solution)/shard_map/ppermute | solution.py:13
  170.5 1.0 collective-permute-done.12
  171.6 4.3 %collective-permute-start.13 = (bf16[4,66,352]{2,1,0:T(8,128)(2,1)S(1)}, bf16[4,66,352]{2,1,0:T(8,128)(2,1)S(1)}, u32[]{:S(2)}, u32[]{:S(2)}) collective-permute-start(bf16[4,66,352]{2,1,0:T(8,128)(2,1)S(1)} %collective-permute-done.12), channel_id=1, source_target_pairs={{0,168},{24,0},{48,24},{72,48},{96,72},{120,96},{144,120},{168,144... | collective-permute-start | bytes 557576 | tf_op jit(solution)/shard_map/ppermute | solution.py:13
  175.9 0.0 collective-permute-done.15
  175.9 1.9 collective-permute-start.16
  177.9 5.9 %collective-permute-done.16 = bf16[4,66,352]{2,1,0:T(8,128)(2,1)S(1)} collective-permute-done((bf16[4,66,352]{2,1,0:T(8,128)(2,1)S(1)}, bf16[4,66,352]{2,1,0:T(8,128)(2,1)S(1)}, u32[]{:S(2)}, u32[]{:S(2)}) %collective-permute-start.16) | collective-permute-done | bytes 185888 | tf_op jit(solution)/shard_map/ppermute | solution.py:13
  183.8 1.9 collective-permute-start.17
  185.8 5.9 %collective-permute-done.17 = bf16[4,66,352]{2,1,0:T(8,128)(2,1)S(1)} collective-permute-done((bf16[4,66,352]{2,1,0:T(8,128)(2,1)S(1)}, bf16[4,66,352]{2,1,0:T(8,128)(2,1)S(1)}, u32[]{:S(2)}, u32[]{:S(2)}) %collective-permute-start.17) | collective-permute-done | bytes 185888 | tf_op jit(solution)/shard_map/ppermute | solution.py:13
  191.9 0.6 copy.10
  192.4 8.8 %collective-permute-start.18 = (bf16[8,4,66,352]{3,0,2,1:T(8,128)(2,1)S(1)}, bf16[8,4,66,352]{3,0,2,1:T(8,128)(2,1)S(1)}, u32[]{:S(2)}, u32[]{:S(2)}) collective-permute-start(bf16[8,4,66,352]{3,0,2,1:T(8,128)(2,1)S(1)} %copy.10), channel_id=1, source_target_pairs={{0,12},{12,0},{1,13},{13,1},{2,14},{14,2},{3,15},{15,3},{4,16},{16... | collective-permute-start | bytes 4460552 | tf_op jit(solution)/shard_map/ppermute | solution.py:13
  201.3 0.1 iota_add_fusion
  201.4 3.0 %collective-permute-done.18 = bf16[8,4,66,352]{3,0,2,1:T(8,128)(2,1)S(1)} collective-permute-done((bf16[8,4,66,352]{3,0,2,1:T(8,128)(2,1)S(1)}, bf16[8,4,66,352]{3,0,2,1:T(8,128)(2,1)S(1)}, u32[]{:S(2)}, u32[]{:S(2)}) %collective-permute-start.18) | collective-permute-done | bytes 1486880 | tf_op jit(solution)/shard_map/ppermute | solution.py:13
  204.4 0.2 copy.14
  204.6 2.5 %pad_maximum_fusion = bf16[2,8,4,66,352]{4,3,2,1,0:T(8,128)(2,1)} fusion(bf16[1,8,4,66,352]{4,3,2,1,0:T(8,128)(2,1)S(1)} %bitcast.80, bf16[1,8,4,66,352]{4,3,2,1,0:T(8,128)(2,1)S(1)} %bitcast.78), kind=kLoop, calls=%fused_computation.8 | loop fusion | flops 1486848 | bytes 5947392 | tf_op jit(solution)/shard_map/stack | solution.py:39
  207.1 1.8 fusion
  208.9 5.8 %reshape.618 = bf16[4224,352]{1,0:T(8,128)(2,1)} reshape(bf16[2,8,4,66,352]{4,3,2,1,0:T(8,128)(2,1)} %pad_maximum_fusion) | data formatting | bytes 5947392 | tf_op jit(solution)/shard_map/reshape | solution.py:137
  214.7 3.3 %fusion.7 = bf16[64,352]{1,0:T(8,128)(2,1)} fusion(bf16[64,4224]{1,0:T(8,128)(2,1)} %reshape.613, bf16[4224,352]{1,0:T(8,128)(2,1)} %reshape.618, f32[352]{0:T(512)S(1)} %get-tuple-element.25, f32[352]{0:T(512)S(1)} %multiply_add_fusion, f32[352]{0:T(512)S(1)} %get-tuple-element.26, f32[352]{0:T(512)S(1)} %broadcast_multiply_fusion.1, ...), kind=kOutput, calls=%fused_computation.16 | convolution fusion | flops 190496768 | bytes 3655168 | tf_op jit(solution)/shard_map/dot_general | solution.py:152
  (52 shorter events, 0.7 us)
Async XLA Ops:
  6.5 1.8 copy-start
  6.5 115.9 %all-gather.3.cloned.1.call-start = ((), (), s32[]{:S(2)}) async-start(), calls=%async_computation.1 | async-start | bytes 6389760 | tf_op jit(solution)/shard_map/all_gather | solution.py:102
  11.4 13.2 %collective-permute-start = (f32[2,1,1,352]{3,2,1,0:T(1,128)S(1)}, f32[2,1,1,352]{3,2,1,0:T(1,128)S(1)}, u32[]{:S(2)}, u32[]{:S(2)}) collective-permute-start(f32[2,1,1,352]{3,2,1,0:T(1,128)S(1)} %pad_maximum_fusion.2), channel_id=1, source_target_pairs={{0,12},{12,0},{1,13},{13,1},{2,14},{14,2},{3,15},{15,3},{4,16},{16... | collective-permute-start | bytes 8456 | tf_op jit(solution)/shard_map/ppermute | solution.py:49
  24.7 4.3 %collective-permute-start.1 = (f32[2,1,1,352]{3,2,1,0:T(1,128)S(1)}, f32[2,1,1,352]{3,2,1,0:T(1,128)S(1)}, u32[]{:S(2)}, u32[]{:S(2)}) collective-permute-start(f32[2,1,1,352]{3,2,1,0:T(1,128)S(1)} %pad_maximum_fusion.3), channel_id=1, source_target_pairs={{0,24},{24,0},{48,72},{72,48},{96,120},{120,96},{144,168},{168,144... | collective-permute-start | bytes 8456 | tf_op jit(solution)/shard_map/ppermute | solution.py:49
  29.1 5.2 %collective-permute-start.2 = (f32[2,1,1,352]{3,2,1,0:T(1,128)S(1)}, f32[2,1,1,352]{3,2,1,0:T(1,128)S(1)}, u32[]{:S(2)}, u32[]{:S(2)}) collective-permute-start(f32[2,1,1,352]{3,2,1,0:T(1,128)S(1)} %pad_maximum_fusion.4), channel_id=1, source_target_pairs={{0,48},{24,72},{48,0},{72,24},{96,144},{120,168},{144,96},{168,120... | collective-permute-start | bytes 8456 | tf_op jit(solution)/shard_map/ppermute | solution.py:49
  34.3 8.3 %collective-permute-start.3 = (f32[2,1,1,352]{3,2,1,0:T(1,128)S(1)}, f32[2,1,1,352]{3,2,1,0:T(1,128)S(1)}, u32[]{:S(2)}, u32[]{:S(2)}) collective-permute-start(f32[2,1,1,352]{3,2,1,0:T(1,128)S(1)} %pad_maximum_fusion.5), channel_id=1, source_target_pairs={{0,96},{24,120},{48,144},{72,168},{96,0},{120,24},{144,48},{168,72... | collective-permute-start | bytes 8456 | tf_op jit(solution)/shard_map/ppermute | solution.py:49
  42.6 7.3 %collective-permute-start.5 = (f32[2,1,1,352]{3,2,1,0:T(1,128)S(1)}, f32[2,1,1,352]{3,2,1,0:T(1,128)S(1)}, u32[]{:S(2)}, u32[]{:S(2)}) collective-permute-start(f32[2,1,1,352]{3,2,1,0:T(1,128)S(1)} %pad_maximum_fusion.6), channel_id=1, source_target_pairs={{0,384},{192,576},{384,0},{576,192},{1,385},{193,577},{385,1},{577... | collective-permute-start | bytes 8456 | tf_op jit(solution)/shard_map/ppermute | solution.py:20
  44.6 5.3 %collective-permute-start.4 = (f32[2,1,1,352]{3,2,1,0:T(1,128)S(1)}, f32[2,1,1,352]{3,2,1,0:T(1,128)S(1)}, u32[]{:S(2)}, u32[]{:S(2)}) collective-permute-start(f32[2,1,1,352]{3,2,1,0:T(1,128)S(1)} %pad_maximum_fusion.6), channel_id=1, source_target_pairs={{0,576},{192,0},{384,192},{576,384},{1,577},{193,1},{385,193},{577... | collective-permute-start | bytes 8456 | tf_op jit(solution)/shard_map/ppermute | solution.py:20
  46.5 6.4 %collective-permute-start.6 = (f32[2,1,1,352]{3,2,1,0:T(1,128)S(1)}, f32[2,1,1,352]{3,2,1,0:T(1,128)S(1)}, u32[]{:S(2)}, u32[]{:S(2)}) collective-permute-start(f32[2,1,1,352]{3,2,1,0:T(1,128)S(1)} %pad_maximum_fusion.6), channel_id=1, source_target_pairs={{0,192},{192,384},{384,576},{576,0},{1,193},{193,385},{385,577},{5... | collective-permute-start | bytes 8456 | tf_op jit(solution)/shard_map/ppermute | solution.py:20
  85.1 35.3 %all-to-all-start = ((bf16[64,32,132]{2,0,1:T(8,128)(2,1)}), bf16[64,32,132]{2,0,1:T(8,128)(2,1)}, u32[]{:S(2)}, u32[]{:S(2)}) async-start(bf16[64,32,132]{2,0,1:T(8,128)(2,1)} %copy.7), calls=%async_computation | async-start | bytes 2097152 | tf_op jit(solution)/shard_map/all_to_all | solution.py:115
  132.9 1.1 copy-start.1
  134.4 10.3 %collective-permute-start.7 = (f32[352,66]{0,1:T(8,128)S(1)}, f32[352,66]{0,1:T(8,128)S(1)}, u32[]{:S(2)}, u32[]{:S(2)}) collective-permute-start(f32[352,66]{0,1:T(8,128)S(1)} %constant_dynamic-slice_fusion.7), channel_id=1, source_target_pairs={{0,12},{12,0},{1,13},{13,1},{2,14},{14,2},{3,15},{15,3},{4,16},{16... | collective-permute-start | bytes 278792 | tf_op jit(solution)/shard_map/ppermute | solution.py:13
  144.7 9.2 %collective-permute-start.9 = (bf16[66,352]{1,0:T(8,128)(2,1)S(1)}, bf16[66,352]{1,0:T(8,128)(2,1)S(1)}, u32[]{:S(2)}, u32[]{:S(2)}) collective-permute-start(bf16[66,352]{1,0:T(8,128)(2,1)S(1)} %bitcast.85), channel_id=1, source_target_pairs={{0,384},{192,576},{384,0},{576,192},{1,385},{193,577},{385,1},{577... | collective-permute-start | bytes 139400 | tf_op jit(solution)/shard_map/ppermute | solution.py:20
  147.7 6.3 %collective-permute-start.8 = (bf16[66,352]{1,0:T(8,128)(2,1)S(1)}, bf16[66,352]{1,0:T(8,128)(2,1)S(1)}, u32[]{:S(2)}, u32[]{:S(2)}) collective-permute-start(bf16[66,352]{1,0:T(8,128)(2,1)S(1)} %bitcast.86), channel_id=1, source_target_pairs={{0,576},{192,0},{384,192},{576,384},{1,577},{193,1},{385,193},{577... | collective-permute-start | bytes 139400 | tf_op jit(solution)/shard_map/ppermute | solution.py:20
  152.0 6.1 %collective-permute-start.10 = (bf16[66,352]{1,0:T(8,128)(2,1)S(1)}, bf16[66,352]{1,0:T(8,128)(2,1)S(1)}, u32[]{:S(2)}, u32[]{:S(2)}) collective-permute-start(bf16[66,352]{1,0:T(8,128)(2,1)S(1)} %bitcast.87), channel_id=1, source_target_pairs={{0,192},{192,384},{384,576},{576,0},{1,193},{193,385},{385,577},{5... | collective-permute-start | bytes 139400 | tf_op jit(solution)/shard_map/ppermute | solution.py:20
  158.2 6.7 %collective-permute-start.11 = (bf16[4,66,352]{2,1,0:T(8,128)(2,1)S(1)}, bf16[4,66,352]{2,1,0:T(8,128)(2,1)S(1)}, u32[]{:S(2)}, u32[]{:S(2)}) collective-permute-start(bf16[4,66,352]{2,1,0:T(8,128)(2,1)S(1)} %pad_maximum_fusion.1), channel_id=1, source_target_pairs={{0,168},{24,0},{48,24},{72,48},{96,72},{120,96},{144,120},{168,144... | collective-permute-start | bytes 557576 | tf_op jit(solution)/shard_map/ppermute | solution.py:13
  160.2 7.9 %collective-permute-start.14 = (bf16[4,66,352]{2,1,0:T(8,128)(2,1)S(1)}, bf16[4,66,352]{2,1,0:T(8,128)(2,1)S(1)}, u32[]{:S(2)}, u32[]{:S(2)}) collective-permute-start(bf16[4,66,352]{2,1,0:T(8,128)(2,1)S(1)} %pad_maximum_fusion.1), channel_id=1, source_target_pairs={{0,24},{24,48},{48,72},{72,96},{96,120},{120,144},{144,168},{168,0... | collective-permute-start | bytes 557576 | tf_op jit(solution)/shard_map/ppermute | solution.py:13
  164.9 6.7 %collective-permute-start.12 = (bf16[4,66,352]{2,1,0:T(8,128)(2,1)S(1)}, bf16[4,66,352]{2,1,0:T(8,128)(2,1)S(1)}, u32[]{:S(2)}, u32[]{:S(2)}) collective-permute-start(bf16[4,66,352]{2,1,0:T(8,128)(2,1)S(1)} %collective-permute-done.11), channel_id=1, source_target_pairs={{0,168},{24,0},{48,24},{72,48},{96,72},{120,96},{144,120},{168,144... | collective-permute-start | bytes 557576 | tf_op jit(solution)/shard_map/ppermute | solution.py:13
  168.0 7.9 %collective-permute-start.15 = (bf16[4,66,352]{2,1,0:T(8,128)(2,1)S(1)}, bf16[4,66,352]{2,1,0:T(8,128)(2,1)S(1)}, u32[]{:S(2)}, u32[]{:S(2)}) collective-permute-start(bf16[4,66,352]{2,1,0:T(8,128)(2,1)S(1)} %collective-permute-done.14), channel_id=1, source_target_pairs={{0,24},{24,48},{48,72},{72,96},{96,120},{120,144},{144,168},{168,0... | collective-permute-start | bytes 557576 | tf_op jit(solution)/shard_map/ppermute | solution.py:13
  171.6 14.2 %collective-permute-start.13 = (bf16[4,66,352]{2,1,0:T(8,128)(2,1)S(1)}, bf16[4,66,352]{2,1,0:T(8,128)(2,1)S(1)}, u32[]{:S(2)}, u32[]{:S(2)}) collective-permute-start(bf16[4,66,352]{2,1,0:T(8,128)(2,1)S(1)} %collective-permute-done.12), channel_id=1, source_target_pairs={{0,168},{24,0},{48,24},{72,48},{96,72},{120,96},{144,120},{168,144... | collective-permute-start | bytes 557576 | tf_op jit(solution)/shard_map/ppermute | solution.py:13
  175.9 7.9 %collective-permute-start.16 = (bf16[4,66,352]{2,1,0:T(8,128)(2,1)S(1)}, bf16[4,66,352]{2,1,0:T(8,128)(2,1)S(1)}, u32[]{:S(2)}, u32[]{:S(2)}) collective-permute-start(bf16[4,66,352]{2,1,0:T(8,128)(2,1)S(1)} %collective-permute-done.15), channel_id=1, source_target_pairs={{0,24},{24,48},{48,72},{72,96},{96,120},{120,144},{144,168},{168,0... | collective-permute-start | bytes 557576 | tf_op jit(solution)/shard_map/ppermute | solution.py:13
  183.8 7.9 %collective-permute-start.17 = (bf16[4,66,352]{2,1,0:T(8,128)(2,1)S(1)}, bf16[4,66,352]{2,1,0:T(8,128)(2,1)S(1)}, u32[]{:S(2)}, u32[]{:S(2)}) collective-permute-start(bf16[4,66,352]{2,1,0:T(8,128)(2,1)S(1)} %collective-permute-done.16), channel_id=1, source_target_pairs={{0,24},{24,48},{48,72},{72,96},{96,120},{120,144},{144,168},{168,0... | collective-permute-start | bytes 557576 | tf_op jit(solution)/shard_map/ppermute | solution.py:13
  192.4 11.9 %collective-permute-start.18 = (bf16[8,4,66,352]{3,0,2,1:T(8,128)(2,1)S(1)}, bf16[8,4,66,352]{3,0,2,1:T(8,128)(2,1)S(1)}, u32[]{:S(2)}, u32[]{:S(2)}) collective-permute-start(bf16[8,4,66,352]{3,0,2,1:T(8,128)(2,1)S(1)} %copy.10), channel_id=1, source_target_pairs={{0,12},{12,0},{1,13},{13,1},{2,14},{14,2},{3,15},{15,3},{4,16},{16... | collective-permute-start | bytes 4460552 | tf_op jit(solution)/shard_map/ppermute | solution.py:13
Sparse Core Ops, SparseCore 0:
  11.5 107.9 all-gather.2
